TPU v7x, 256 devices: a whole 4x4x8 slice. The times are simulated.
256 devices in a mesh: gx: 8 (over z_hi, y), gy: 8 (over x, core), gz: 4 (over z_lo).
Axes of the slice: x: 4, y: 4, z: 8 (z_hi: 2, z_lo: 4; z = z_hi * 4 + z_lo), core: 2. Of those that a mesh axis runs over, the one named last changes fastest.
Arguments:
- gas_state: float32 [5, 64, 128, 512], P(None, 'gx', 'gy', 'gz'), may hold values from -3 to 3, as said below
- parcels: float32 [8192, 5, 128], P(('gx', 'gy', 'gz')), may hold values from -4 to 5, as said below
- parcel_cells: int32 [8192, 128], P(('gx', 'gy', 'gz')), may hold values from 2471 to 20928, as said below
- offsets: float32 [8192, 3, 128], P(('gx', 'gy', 'gz')), may hold values from -0.5 to 0.5
- destination: int32 [8192], P(('gx', 'gy', 'gz')), may hold values from 0 to 26, as said below
- live_blocks: int32 [256], P(('gx', 'gy', 'gz')), may hold values from 4 to 32, as said below
Outputs:
- gas_next: float32 [5, 64, 128, 512], P(None, 'gx', 'gy', 'gz')
- kept: float32 [8192, 5, 128], P(('gx', 'gy', 'gz'))
- arrived: float32 [27648, 5, 128], P(('gx', 'gy', 'gz'))
Inputs may be any that keep to these rules, and one draw needn't show every extreme that they name: `gas_state`: field 0 is a vapour fraction within 0 and 0.6, field 1 a temperature within 0.6 and 1.4, fields 2 to 4 velocities. `parcels`: field 0 is a mass within 0.2 and 5, field 1 a temperature within 0.6 and 1.4, fields 2 to 4 velocities. `parcel_cells`: every index is that of an owned cell of the padded brick, 1 to 8, 1 to 16 and 1 to 128 along the three dimensions. Among the blocks of one brick at most 4 name any one destination other than 13; in every draw some brick sends exactly 4 live blocks to one neighbour inside the grid. Destinations of blocks that are not live carry no meaning. Block slots 0 to live_blocks[d] - 1 of brick d are live; in every draw some brick is full.
All inputs are finite; a program needn't handle non-finite values.
Results may differ from a plain program's by a relative error of at most 0.0003.
Values sent between devices are 32-bit elements; how exact they have to be, the bound alone decides.
No kernel may reach another device: no remote copies, remote signals or barrier semaphores. Data moves between devices by JAX's collectives and lax.ppermute only.
A program may use at most 64 MiB of HBM per device.

v0:
```python
import jax
import jax.numpy as jnp
from jax import lax
from jax.sharding import PartitionSpec as P

SLOTS = 4


DIFFUSION = (0.06, 0.1, 0.12, 0.12, 0.12)
TIME_STEP = 0.5
COUPLING = 0.5
PHASE_CHANGE_COST = 0.5
GROUP_BLOCKS = 8


def with_halo(block, sides, width):
    for axis, dim in sides:
        count = lax.axis_size(axis)
        forward = [(i, i + 1) for i in range(count - 1)]
        backward = [(target, source) for source, target in forward]
        low = lax.ppermute(
            lax.slice_in_dim(block, block.shape[dim] - width, None, axis=dim), axis, forward
        )
        high = lax.ppermute(lax.slice_in_dim(block, 0, width, axis=dim), axis, backward)
        block = jnp.concatenate([low, block, high], axis=dim)
    return block


def parcel_update(current_condition, local_air_sample):
    particle_weights_list = current_condition[:, 0]
    parcel_hotness_measure = current_condition[:, 1]
    particle_speed_vector = current_condition[:, 2:5]
    relax_time = 0.4 * particle_weights_list ** (2.0 / 3.0)
    keep_velocity = jnp.exp(-TIME_STEP / relax_time)
    residual_heat_content = jnp.exp(-TIME_STEP / (1.5 * relax_time))
    equilibrium_steam_load = 0.4 * jnp.exp(2.0 * (parcel_hotness_measure - 1.0))
    evaporated_share = 1.0 - jnp.exp(
        -0.3 * jax.nn.softplus(4.0 * (equilibrium_steam_load - local_air_sample[:, 0]))
    )
    evaporated = particle_weights_list * evaporated_share
    ambient_heat_content = local_air_sample[:, 1]
    gas_velocity = local_air_sample[:, 2:5]
    adjusted_heat_content = (
        ambient_heat_content
        + (parcel_hotness_measure - ambient_heat_content) * residual_heat_content
        - PHASE_CHANGE_COST * evaporated_share
    )
    velocity_new = gas_velocity + (particle_speed_vector - gas_velocity) * keep_velocity[:, None]
    enthalpy_injection = (
        0.5 * particle_weights_list * (parcel_hotness_measure - adjusted_heat_content)
    )
    push_source = particle_weights_list[:, None] * (particle_speed_vector - velocity_new)
    updated = jnp.concatenate(
        [
            (particle_weights_list - evaporated)[:, None],
            adjusted_heat_content[:, None],
            velocity_new,
        ],
        axis=1,
    )
    sources = jnp.concatenate(
        [evaporated[:, None], enthalpy_injection[:, None], push_source], axis=1
    )
    return (updated, sources)


def laplacian(padded):
    centre = padded[:, 1:-1, 1:-1, 1:-1]
    beside = padded[:, 2:, 1:-1, 1:-1] + padded[:, :-2, 1:-1, 1:-1]
    beside = beside + padded[:, 1:-1, 2:, 1:-1] + padded[:, 1:-1, :-2, 1:-1]
    beside = beside + padded[:, 1:-1, 1:-1, 2:] + padded[:, 1:-1, 1:-1, :-2]
    return beside - 6.0 * centre


def local(gas_state, parcels, parcel_cells, offsets, destination, live_blocks):
    fields, size_x, size_y, size_z = gas_state.shape
    blocks, parcel_fields, block_parcels = parcels.shape
    padded = with_halo(gas_state, (("gx", 1), ("gy", 2), ("gz", 3)), 1)
    span_x = size_x + 2
    span_y = size_y + 2
    span_z = size_z + 2
    pair_count = span_x * span_y
    plane_size = span_y * span_z
    table = jnp.transpose(padded.reshape(fields, pair_count, span_z), (1, 0, 2)).reshape(
        pair_count, fields * span_z
    )
    alive_mask = jnp.arange(blocks, dtype=jnp.int32) < live_blocks[0]
    turns = blocks // GROUP_BLOCKS
    rows = GROUP_BLOCKS * block_parcels
    pair_iota = jnp.arange(pair_count, dtype=jnp.int32)
    depth_iota = jnp.arange(span_z, dtype=jnp.int32)

    def group_step(total, item):
        group_parcels, group_cells, group_offsets, group_alive = item
        cells = group_cells.reshape(rows)
        shifts = jnp.transpose(group_offsets, (1, 0, 2)).reshape(3, rows)
        cell_x = cells // plane_size
        cell_y = cells // span_z % span_y
        cell_z = cells % span_z
        step_sign = jnp.where(shifts >= 0.0, 1, -1).astype(jnp.int32)
        far_share = jnp.abs(shifts)
        near_share = 1.0 - far_share
        pair_weights = jnp.zeros((rows, pair_count), jnp.float32)
        for bit_x in range(2):
            for bit_y in range(2):
                share = (far_share[0] if bit_x else near_share[0]) * (
                    far_share[1] if bit_y else near_share[1]
                )
                target = (cell_x + bit_x * step_sign[0]) * span_y + cell_y + bit_y * step_sign[1]
                pair_weights = pair_weights + jnp.where(
                    pair_iota[None, :] == target[:, None], share[:, None], 0.0
                )
        depth_weights = jnp.where(
            depth_iota[None, :] == cell_z[:, None], near_share[2][:, None], 0.0
        )
        depth_weights = depth_weights + jnp.where(
            depth_iota[None, :] == (cell_z + step_sign[2])[:, None], far_share[2][:, None], 0.0
        )
        mixed = jnp.dot(pair_weights, table, precision=lax.Precision.HIGHEST).reshape(
            rows, fields, span_z
        )
        sample = jnp.sum(mixed * depth_weights[:, None, :], axis=2)
        sample_blocks = jnp.transpose(
            sample.reshape(GROUP_BLOCKS, block_parcels, fields), (0, 2, 1)
        )
        updated, sources = parcel_update(group_parcels, sample_blocks)
        sources = jnp.where(group_alive[:, None, None], sources, 0.0)
        source_rows = jnp.transpose(sources, (0, 2, 1)).reshape(rows, fields)
        spread = (source_rows[:, :, None] * depth_weights[:, None, :]).reshape(
            rows, fields * span_z
        )
        total = total + lax.dot_general(
            pair_weights, spread, (((0,), (0,)), ((), ())), precision=lax.Precision.HIGHEST
        )
        return (total, updated)

    inputs = (
        parcels.reshape(turns, GROUP_BLOCKS, parcel_fields, block_parcels),
        parcel_cells.reshape(turns, GROUP_BLOCKS, block_parcels),
        offsets.reshape(turns, GROUP_BLOCKS, 3, block_parcels),
        alive_mask.reshape(turns, GROUP_BLOCKS),
    )
    deposit_rows, updated = lax.scan(
        group_step, jnp.zeros((pair_count, fields * span_z), jnp.float32), inputs
    )
    updated = updated.reshape(blocks, parcel_fields, block_parcels)
    deposit = jnp.transpose(deposit_rows.reshape(span_x, span_y, fields, span_z), (2, 0, 1, 3))
    ghost_shell = deposit.at[:, 1:-1, 1:-1, 1:-1].set(0.0)
    extended = with_halo(ghost_shell, (("gx", 1), ("gy", 2), ("gz", 3)), 1)
    extended = extended.at[:, 2].add(extended[:, 0]).at[:, -3].add(extended[:, -1])
    extended = extended.at[:, :, 2].add(extended[:, :, 0]).at[:, :, -3].add(extended[:, :, -1])
    extended = (
        extended.at[:, :, :, 2].add(extended[:, :, :, 0]).at[:, :, :, -3].add(extended[:, :, :, -1])
    )
    cell_sources = deposit[:, 1:-1, 1:-1, 1:-1] + extended[:, 2:-2, 2:-2, 2:-2]
    kappa = jnp.array(DIFFUSION, jnp.float32)[:, None, None, None]
    gas_next = gas_state + kappa * laplacian(padded) + COUPLING * cell_sources
    kept = jnp.where((alive_mask & (destination == 13))[:, None, None], updated, 0.0)
    leaving = alive_mask & (destination != 13)
    one_hot = (
        (destination[:, None] == jnp.arange(27, dtype=jnp.int32)[None, :]) & leaving[:, None]
    ).astype(jnp.int32)
    slot_rank = jnp.sum(jnp.cumsum(one_hot, axis=0) * one_hot, axis=1) - 1
    slot_index = jnp.where(leaving, destination * SLOTS + slot_rank, -1)
    selector = (jnp.arange(27 * SLOTS, dtype=jnp.int32)[:, None] == slot_index[None, :]).astype(
        jnp.float32
    )
    outbox = jnp.dot(selector, updated.reshape(blocks, -1), precision=lax.Precision.HIGHEST)
    outbox = outbox.reshape((3, 3, 3, SLOTS) + parcels.shape[1:])
    widened = with_halo(outbox, (("gx", 0), ("gy", 1), ("gz", 2)), 1)
    arrived_boxes = widened[0::2, 0::2, 0::2]
    arrived = arrived_boxes.reshape((27 * SLOTS,) + parcels.shape[1:])
    return (gas_next, kept, arrived)


def solution(mesh):
    placed = (
        P(None, "gx", "gy", "gz"),
        P(("gx", "gy", "gz"), None, None),
        P(("gx", "gy", "gz"), None),
        P(("gx", "gy", "gz"), None, None),
        P(("gx", "gy", "gz")),
        P(("gx", "gy", "gz")),
    )
    return jax.shard_map(
        local,
        mesh=mesh,
        in_specs=placed,
        out_specs=(
            P(None, "gx", "gy", "gz"),
            P(("gx", "gy", "gz"), None, None),
            P(("gx", "gy", "gz"), None, None),
        ),
        check_vma=False,
    )
```

profile of v0, /device:TPU:58, one launch (start us, length us, event | category | flops | bytes accessed | tf_op | source)
XLA Modules:
  0.0 301.7 jit_solution(9534212255292930902)
XLA Ops:
  2.6 7.9 %collective-permute-start.1 = (f32[5,1,16,128]{3,0,2,1:T(8,128)S(1)}, f32[5,1,16,128]{3,0,2,1:T(8,128)S(1)}, u32[]{:S(2)}, u32[]{:S(2)}) collective-permute-start(f32[5,1,16,128]{3,0,2,1:T(8,128)S(1)} %get-tuple-element.423), channel_id=1, source_target_pairs={{0,32},{32,64},{64,96},{96,128},{128,160},{160,192},{192,224},{1,3... | collective-permute-start | bytes 122888 | tf_op jit(solution)/shard_map/ppermute | solution.py:21
  17.2 5.7 %collective-permute-done = f32[5,1,16,128]{3,0,2,1:T(8,128)S(1)} collective-permute-done((f32[5,1,16,128]{3,0,2,1:T(8,128)S(1)}, f32[5,1,16,128]{3,0,2,1:T(8,128)S(1)}, u32[]{:S(2)}, u32[]{:S(2)}) %collective-permute-start) | collective-permute-done | bytes 40992 | tf_op jit(solution)/shard_map/ppermute | solution.py:24
  24.9 2.4 collective-permute-start.3
  27.8 2.4 collective-permute-done.3
  30.9 2.7 collective-permute-start.4
  34.1 3.1 %collective-permute-start.5 = (f32[5,10,18,1]{2,3,1,0:T(1,128)S(1)}, f32[5,10,18,1]{2,3,1,0:T(1,128)S(1)}, u32[]{:S(2)}, u32[]{:S(2)}) collective-permute-start(f32[5,10,18,1]{2,3,1,0:T(1,128)S(1)} %copy.36), channel_id=1, source_target_pairs={{0,1},{1,2},{2,3},{4,5},{5,6},{6,7},{8,9},{9,10},{10,11},{12,13},{... | collective-permute-start | bytes 10808 | tf_op jit(solution)/shard_map/ppermute | solution.py:21
  44.0 97.1 %while.24 = (s32[]{:T(128)}, f32[180,650]{1,0:T(8,128)}, f32[4,8,5,128]{3,1,2,0:T(8,128)S(1)}, s32[4,8,128]{2,1,0:T(8,128)}, f32[4,8,3,128]{3,2,1,0:T(4,128)S(1)...) while((s32[]{:T(128)}, f32[180,650]{1,0:T(8,128)}, ...), condition=%wide.region_2.3_spmd.clone.clone, body=%wide.region_0.2_spmd.clone.clone.sunk | while | flops 2882474496 | bytes 25044612 | solution.py:143
  47.0 7.5 %fusion.83 = f32[1024,650]{0,1:T(8,128)} fusion(f32[180,650]{1,0:T(8,128)S(1)} %get-tuple-element.556, f32[1024]{0:T(1024)S(1)} %bitcast.187, s32[1024]{0:T(1024)S(1)} %get-tuple-element.510, f32[1024]{0:T(1024)S(1)} %bitcast.183, s32[1024]{0:T(1024)S(1)} %get-tuple-element.512, f32[1024]{0:T(1024)S(1)} %bitcast.185, ...), kind=kOutput, calls=%fused_computation.10.clone.1 | convolution fusion | flops 1439723520 | bytes 3163168 | tf_op jit(solution)/shard_map/while/body/eval_jaxpr/dot_general | solution.py:119
  59.3 9.0 %convolution_add_fusion.2 = f32[180,650]{1,0:T(8,128)} fusion(f32[1024,650]{0,1:T(8,128)} %mul.506, f32[180,650]{1,0:T(8,128)} %get-tuple-element.540, f32[1024]{0:T(1024)S(1)} %bitcast.188, s32[1024]{0:T(1024)S(1)} %copy-done.25, f32[1024]{0:T(1024)S(1)} %bitcast.184, s32[1024]{0:T(1024)S(1)} %copy-done.27, f32[1024]{0:T(1024)S(1)} %bitcast.186, ...), kind=kOutput, calls=%fused_computation.8.clone.1 | convolution fusion | flops 1439957504 | bytes 3631169 | tf_op jit(solution)/shard_map/while/body/eval_jaxpr/dot_general | solution.py:132
  71.1 7.5 %fusion.83 = f32[1024,650]{0,1:T(8,128)} fusion(f32[180,650]{1,0:T(8,128)S(1)} %get-tuple-element.556, f32[1024]{0:T(1024)S(1)} %bitcast.187, s32[1024]{0:T(1024)S(1)} %get-tuple-element.510, f32[1024]{0:T(1024)S(1)} %bitcast.183, s32[1024]{0:T(1024)S(1)} %get-tuple-element.512, f32[1024]{0:T(1024)S(1)} %bitcast.185, ...), kind=kOutput, calls=%fused_computation.10.clone.1 | convolution fusion | flops 1439723520 | bytes 3163168 | tf_op jit(solution)/shard_map/while/body/eval_jaxpr/dot_general | solution.py:119
  83.4 9.1 %convolution_add_fusion.2 = f32[180,650]{1,0:T(8,128)} fusion(f32[1024,650]{0,1:T(8,128)} %mul.506, f32[180,650]{1,0:T(8,128)} %get-tuple-element.540, f32[1024]{0:T(1024)S(1)} %bitcast.188, s32[1024]{0:T(1024)S(1)} %copy-done.25, f32[1024]{0:T(1024)S(1)} %bitcast.184, s32[1024]{0:T(1024)S(1)} %copy-done.27, f32[1024]{0:T(1024)S(1)} %bitcast.186, ...), kind=kOutput, calls=%fused_computation.8.clone.1 | convolution fusion | flops 1439957504 | bytes 3631169 | tf_op jit(solution)/shard_map/while/body/eval_jaxpr/dot_general | solution.py:132
  95.4 7.5 %fusion.83 = f32[1024,650]{0,1:T(8,128)} fusion(f32[180,650]{1,0:T(8,128)S(1)} %get-tuple-element.556, f32[1024]{0:T(1024)S(1)} %bitcast.187, s32[1024]{0:T(1024)S(1)} %get-tuple-element.510, f32[1024]{0:T(1024)S(1)} %bitcast.183, s32[1024]{0:T(1024)S(1)} %get-tuple-element.512, f32[1024]{0:T(1024)S(1)} %bitcast.185, ...), kind=kOutput, calls=%fused_computation.10.clone.1 | convolution fusion | flops 1439723520 | bytes 3163168 | tf_op jit(solution)/shard_map/while/body/eval_jaxpr/dot_general | solution.py:119
  107.7 9.1 %convolution_add_fusion.2 = f32[180,650]{1,0:T(8,128)} fusion(f32[1024,650]{0,1:T(8,128)} %mul.506, f32[180,650]{1,0:T(8,128)} %get-tuple-element.540, f32[1024]{0:T(1024)S(1)} %bitcast.188, s32[1024]{0:T(1024)S(1)} %copy-done.25, f32[1024]{0:T(1024)S(1)} %bitcast.184, s32[1024]{0:T(1024)S(1)} %copy-done.27, f32[1024]{0:T(1024)S(1)} %bitcast.186, ...), kind=kOutput, calls=%fused_computation.8.clone.1 | convolution fusion | flops 1439957504 | bytes 3631169 | tf_op jit(solution)/shard_map/while/body/eval_jaxpr/dot_general | solution.py:132
  119.6 7.5 %fusion.83 = f32[1024,650]{0,1:T(8,128)} fusion(f32[180,650]{1,0:T(8,128)S(1)} %get-tuple-element.556, f32[1024]{0:T(1024)S(1)} %bitcast.187, s32[1024]{0:T(1024)S(1)} %get-tuple-element.510, f32[1024]{0:T(1024)S(1)} %bitcast.183, s32[1024]{0:T(1024)S(1)} %get-tuple-element.512, f32[1024]{0:T(1024)S(1)} %bitcast.185, ...), kind=kOutput, calls=%fused_computation.10.clone.1 | convolution fusion | flops 1439723520 | bytes 3163168 | tf_op jit(solution)/shard_map/while/body/eval_jaxpr/dot_general | solution.py:119
  131.9 9.1 %convolution_add_fusion.2 = f32[180,650]{1,0:T(8,128)} fusion(f32[1024,650]{0,1:T(8,128)} %mul.506, f32[180,650]{1,0:T(8,128)} %get-tuple-element.540, f32[1024]{0:T(1024)S(1)} %bitcast.188, s32[1024]{0:T(1024)S(1)} %copy-done.25, f32[1024]{0:T(1024)S(1)} %bitcast.184, s32[1024]{0:T(1024)S(1)} %copy-done.27, f32[1024]{0:T(1024)S(1)} %bitcast.186, ...), kind=kOutput, calls=%fused_computation.8.clone.1 | convolution fusion | flops 1439957504 | bytes 3631169 | tf_op jit(solution)/shard_map/while/body/eval_jaxpr/dot_general | solution.py:132
  142.9 20.9 %scatter.4 = f32[5,10,18,130]{3,0,2,1:T(8,128)S(1)} dynamic-update-slice(f32[5,10,18,130]{3,0,2,1:T(8,128)S(1)} %copy.82, f32[5,8,16,128]{3,0,2,1:T(8,128)S(1)} %broadcast.844, s32[]{:T(128)} %constant.359.clone.1, s32[]{:T(128)} %constant.362.clone.1, s32[]{:T(128)} %constant.362.clone.1, s32[]{:T(128)} %constant.362.clone.1) | dynamic-update-slice | bytes 655364 | tf_op jit(solution)/shard_map/scatter | solution.py:148
  165.7 9.9 %collective-permute-start.6 = (f32[5,1,18,130]{3,0,2,1:T(8,128)S(1)}, f32[5,1,18,130]{3,0,2,1:T(8,128)S(1)}, u32[]{:S(2)}, u32[]{:S(2)}) collective-permute-start(f32[5,1,18,130]{3,0,2,1:T(8,128)S(1)} %get-tuple-element.412), channel_id=1, source_target_pairs={{0,32},{32,64},{64,96},{96,128},{128,160},{160,192},{192,224},{1,3... | collective-permute-start | bytes 140408 | tf_op jit(solution)/shard_map/ppermute | solution.py:21
  181.8 2.6 collective-permute-start.8
  185.2 2.6 collective-permute-done.8
  190.1 2.3 copy.48
  196.5 3.9 %collective-permute-start.10 = (f32[5,12,20,1]{2,3,1,0:T(1,128)}, f32[5,12,20,1]{2,3,1,0:T(1,128)}, u32[]{:S(2)}, u32[]{:S(2)}) collective-permute-start(f32[5,12,20,1]{2,3,1,0:T(1,128)} %copy.47), channel_id=1, source_target_pairs={{0,1},{1,2},{2,3},{4,5},{5,6},{6,7},{8,9},{9,10},{10,11},{12,13},{... | collective-permute-start | bytes 14408 | tf_op jit(solution)/shard_map/ppermute | solution.py:21
  204.5 10.4 %collective-permute-start.12 = (f32[1,3,3,4,5,128]{5,4,3,2,1,0:T(8,128)}, f32[1,3,3,4,5,128]{5,4,3,2,1,0:T(8,128)}, u32[]{:S(2)}, u32[]{:S(2)}) collective-permute-start(f32[1,3,3,4,5,128]{5,4,3,2,1,0:T(8,128)} %slice.459), channel_id=1, source_target_pairs={{0,32},{32,64},{64,96},{96,128},{128,160},{160,192},{192,224},{1,3... | collective-permute-start | bytes 276488 | tf_op jit(solution)/shard_map/ppermute | solution.py:21
  218.4 2.4 copy.50
  220.8 2.4 copy.49
  223.2 2.3 pad_maximum_fusion.2
  228.7 20.9 %scatter-add.26 = f32[5,12,20,132]{3,0,2,1:T(8,128)} dynamic-update-slice(f32[5,12,20,132]{3,0,2,1:T(8,128)} %copy.87, f32[5,12,20,1]{3,0,2,1:T(8,128)} %slice_add_fusion.1, s32[]{:T(128)} %constant.359.clone.1, s32[]{:T(128)} %constant.359.clone.1, s32[]{:T(128)} %constant.359.clone.1, s32[]{:T(128)} %constant.363.clone.1) | dynamic-update-slice | bytes 9604 | tf_op jit(solution)/shard_map/scatter-add | solution.py:153
  256.3 2.4 collective-permute-start.14
  260.3 21.1 %scatter-add.29 = f32[5,12,20,132]{3,0,2,1:T(8,128)} dynamic-update-slice(f32[5,12,20,132]{3,0,2,1:T(8,128)} %scatter-add.26, f32[5,12,20,1]{3,0,2,1:T(8,128)} %slice_add_fusion, s32[]{:T(128)} %constant.359.clone.1, s32[]{:T(128)} %constant.359.clone.1, s32[]{:T(128)} %constant.359.clone.1, s32[]{:T(128)} %constant.366.clone.1) | dynamic-update-slice | bytes 9604 | tf_op jit(solution)/shard_map/scatter-add | solution.py:153
  282.8 2.5 collective-permute-start.17
  285.3 3.5 %collective-permute-start.16 = (f32[5,5,1,4,5,128]{5,4,3,2,1,0:T(8,128)S(1)}, f32[5,5,1,4,5,128]{5,4,3,2,1,0:T(8,128)S(1)}, u32[]{:S(2)}, u32[]{:S(2)}) collective-permute-start(f32[5,5,1,4,5,128]{5,4,3,2,1,0:T(8,128)S(1)} %get-tuple-element.414), channel_id=1, source_target_pairs={{0,1},{1,2},{2,3},{4,5},{5,6},{6,7},{8,9},{9,10},{10,11},{12,13},{... | collective-permute-start | bytes 768008 | tf_op jit(solution)/shard_map/ppermute | solution.py:21
  291.7 5.2 %collective-permute-done.17 = f32[5,5,1,4,5,128]{5,4,3,2,1,0:T(8,128)S(1)} collective-permute-done((f32[5,5,1,4,5,128]{5,4,3,2,1,0:T(8,128)S(1)}, f32[5,5,1,4,5,128]{5,4,3,2,1,0:T(8,128)S(1)}, u32[]{:S(2)}, u32[]{:S(2)}) %collective-permute-start.17) | collective-permute-done | bytes 256032 | tf_op jit(solution)/shard_map/ppermute | solution.py:24
  296.9 2.7 collective-permute-done.16
  (284 shorter events, 90.7 us)
Async XLA Ops:
  0.6 26.6 %copy-start.33 = (s32[32]{0:T(128)S(1)}, s32[32]{0:T(128)}, u32[]{:S(2)}) copy-start(s32[32]{0:T(128)} %param.27) | copy-start | bytes 388
  2.6 13.3 %collective-permute-start.1 = (f32[5,1,16,128]{3,0,2,1:T(8,128)S(1)}, f32[5,1,16,128]{3,0,2,1:T(8,128)S(1)}, u32[]{:S(2)}, u32[]{:S(2)}) collective-permute-start(f32[5,1,16,128]{3,0,2,1:T(8,128)S(1)} %get-tuple-element.423), channel_id=1, source_target_pairs={{0,32},{32,64},{64,96},{96,128},{128,160},{160,192},{192,224},{1,3... | collective-permute-start | bytes 122888 | tf_op jit(solution)/shard_map/ppermute | solution.py:21
  10.5 12.4 %collective-permute-start = (f32[5,1,16,128]{3,0,2,1:T(8,128)S(1)}, f32[5,1,16,128]{3,0,2,1:T(8,128)S(1)}, u32[]{:S(2)}, u32[]{:S(2)}) collective-permute-start(f32[5,1,16,128]{3,0,2,1:T(8,128)S(1)} %get-tuple-element.422), channel_id=1, source_target_pairs={{32,0},{64,32},{96,64},{128,96},{160,128},{192,160},{224,192},{33,... | collective-permute-start | bytes 122888 | tf_op jit(solution)/shard_map/ppermute | solution.py:24
  16.0 14.2 %copy-start.20 = (f32[5,1,16,128]{3,0,2,1:T(8,128)}, f32[5,1,16,128]{3,0,2,1:T(8,128)S(1)}, u32[]{:S(2)}) copy-start(f32[5,1,16,128]{3,0,2,1:T(8,128)S(1)} %collective-permute-done.1) | copy-start | bytes 122884
  22.9 17.5 %copy-start = (f32[5,10,16,128]{3,0,2,1:T(8,128)}, f32[5,10,16,128]{3,0,2,1:T(8,128)S(1)}, u32[]{:S(2)}) copy-start(f32[5,10,16,128]{3,0,2,1:T(8,128)S(1)} %constant_dynamic-update-slice_fusion) | copy-start | bytes 1228804
  22.9 4.9 %collective-permute-start.2 = (f32[5,10,1,128]{3,0,2,1:T(8,128)S(1)}, f32[5,10,1,128]{3,0,2,1:T(8,128)S(1)}, u32[]{:S(2)}, u32[]{:S(2)}) collective-permute-start(f32[5,10,1,128]{3,0,2,1:T(8,128)S(1)} %get-tuple-element.421), channel_id=1, source_target_pairs={{4,0},{8,4},{12,8},{16,12},{20,16},{24,20},{28,24},{5,1},{9,5},{13... | collective-permute-start | bytes 76808 | tf_op jit(solution)/shard_map/ppermute | solution.py:24
  24.9 5.3 %collective-permute-start.3 = (f32[5,10,1,128]{3,0,2,1:T(8,128)S(1)}, f32[5,10,1,128]{3,0,2,1:T(8,128)S(1)}, u32[]{:S(2)}, u32[]{:S(2)}) collective-permute-start(f32[5,10,1,128]{3,0,2,1:T(8,128)S(1)} %get-tuple-element.420), channel_id=1, source_target_pairs={{0,4},{4,8},{8,12},{12,16},{16,20},{20,24},{24,28},{1,5},{5,9},{9,... | collective-permute-start | bytes 76808 | tf_op jit(solution)/shard_map/ppermute | solution.py:21
  30.9 6.8 %collective-permute-start.4 = (f32[5,10,18,1]{2,3,1,0:T(1,128)S(1)}, f32[5,10,18,1]{2,3,1,0:T(1,128)S(1)}, u32[]{:S(2)}, u32[]{:S(2)}) collective-permute-start(f32[5,10,18,1]{2,3,1,0:T(1,128)S(1)} %copy.34), channel_id=1, source_target_pairs={{1,0},{2,1},{3,2},{5,4},{6,5},{7,6},{9,8},{10,9},{11,10},{13,12},{... | collective-permute-start | bytes 10808 | tf_op jit(solution)/shard_map/ppermute | solution.py:24
  34.1 5.7 %collective-permute-start.5 = (f32[5,10,18,1]{2,3,1,0:T(1,128)S(1)}, f32[5,10,18,1]{2,3,1,0:T(1,128)S(1)}, u32[]{:S(2)}, u32[]{:S(2)}) collective-permute-start(f32[5,10,18,1]{2,3,1,0:T(1,128)S(1)} %copy.36), channel_id=1, source_target_pairs={{0,1},{1,2},{2,3},{4,5},{5,6},{6,7},{8,9},{9,10},{10,11},{12,13},{... | collective-permute-start | bytes 10808 | tf_op jit(solution)/shard_map/ppermute | solution.py:21
  142.7 32.9 %copy-start.35 = (s32[32]{0:T(128)S(1)}, s32[32]{0:T(128)}, u32[]{:S(2)}) copy-start(s32[32]{0:T(128)} %add_select_fusion.4) | copy-start | bytes 388
  163.8 14.7 %collective-permute-start.7 = (f32[5,1,18,130]{3,0,2,1:T(8,128)S(1)}, f32[5,1,18,130]{3,0,2,1:T(8,128)S(1)}, u32[]{:S(2)}, u32[]{:S(2)}) collective-permute-start(f32[5,1,18,130]{3,0,2,1:T(8,128)S(1)} %get-tuple-element.413), channel_id=1, source_target_pairs={{32,0},{64,32},{96,64},{128,96},{160,128},{192,160},{224,192},{33,... | collective-permute-start | bytes 140408 | tf_op jit(solution)/shard_map/ppermute | solution.py:24
  165.7 14.2 %collective-permute-start.6 = (f32[5,1,18,130]{3,0,2,1:T(8,128)S(1)}, f32[5,1,18,130]{3,0,2,1:T(8,128)S(1)}, u32[]{:S(2)}, u32[]{:S(2)}) collective-permute-start(f32[5,1,18,130]{3,0,2,1:T(8,128)S(1)} %get-tuple-element.412), channel_id=1, source_target_pairs={{0,32},{32,64},{64,96},{96,128},{128,160},{160,192},{192,224},{1,3... | collective-permute-start | bytes 140408 | tf_op jit(solution)/shard_map/ppermute | solution.py:21
  179.9 5.3 %collective-permute-start.9 = (f32[5,12,1,130]{3,0,2,1:T(8,128)S(1)}, f32[5,12,1,130]{3,0,2,1:T(8,128)S(1)}, u32[]{:S(2)}, u32[]{:S(2)}) collective-permute-start(f32[5,12,1,130]{3,0,2,1:T(8,128)S(1)} %get-tuple-element.411), channel_id=1, source_target_pairs={{4,0},{8,4},{12,8},{16,12},{20,16},{24,20},{28,24},{5,1},{9,5},{13... | collective-permute-start | bytes 93608 | tf_op jit(solution)/shard_map/ppermute | solution.py:24
  181.8 5.9 %collective-permute-start.8 = (f32[5,12,1,130]{3,0,2,1:T(8,128)S(1)}, f32[5,12,1,130]{3,0,2,1:T(8,128)S(1)}, u32[]{:S(2)}, u32[]{:S(2)}) collective-permute-start(f32[5,12,1,130]{3,0,2,1:T(8,128)S(1)} %get-tuple-element.410), channel_id=1, source_target_pairs={{0,4},{4,8},{8,12},{12,16},{16,20},{20,24},{24,28},{1,5},{5,9},{9,... | collective-permute-start | bytes 93608 | tf_op jit(solution)/shard_map/ppermute | solution.py:21
  192.3 26.0 %collective-permute-start.11 = (f32[5,12,20,1]{2,3,1,0:T(1,128)}, f32[5,12,20,1]{2,3,1,0:T(1,128)}, u32[]{:S(2)}, u32[]{:S(2)}) collective-permute-start(f32[5,12,20,1]{2,3,1,0:T(1,128)} %copy.48), channel_id=1, source_target_pairs={{1,0},{2,1},{3,2},{5,4},{6,5},{7,6},{9,8},{10,9},{11,10},{13,12},{... | collective-permute-start | bytes 14408 | tf_op jit(solution)/shard_map/ppermute | solution.py:24
  196.5 24.3 %collective-permute-start.10 = (f32[5,12,20,1]{2,3,1,0:T(1,128)}, f32[5,12,20,1]{2,3,1,0:T(1,128)}, u32[]{:S(2)}, u32[]{:S(2)}) collective-permute-start(f32[5,12,20,1]{2,3,1,0:T(1,128)} %copy.47), channel_id=1, source_target_pairs={{0,1},{1,2},{2,3},{4,5},{5,6},{6,7},{8,9},{9,10},{10,11},{12,13},{... | collective-permute-start | bytes 14408 | tf_op jit(solution)/shard_map/ppermute | solution.py:21
  202.9 20.3 %copy-start.12 = (f32[5,12,1,130]{3,0,2,1:T(8,128)S(1)}, f32[5,12,1,130]{3,0,2,1:T(8,128)}, u32[]{:S(2)}) copy-start(f32[5,12,1,130]{3,0,2,1:T(8,128)} %copy-done.11) | copy-start | bytes 93604
  202.9 20.3 %copy-start.14 = (f32[5,12,1,130]{3,0,2,1:T(8,128)S(1)}, f32[5,12,1,130]{3,0,2,1:T(8,128)}, u32[]{:S(2)}) copy-start(f32[5,12,1,130]{3,0,2,1:T(8,128)} %copy-done.13) | copy-start | bytes 93604
  204.5 45.1 %collective-permute-start.12 = (f32[1,3,3,4,5,128]{5,4,3,2,1,0:T(8,128)}, f32[1,3,3,4,5,128]{5,4,3,2,1,0:T(8,128)}, u32[]{:S(2)}, u32[]{:S(2)}) collective-permute-start(f32[1,3,3,4,5,128]{5,4,3,2,1,0:T(8,128)} %slice.459), channel_id=1, source_target_pairs={{0,32},{32,64},{64,96},{96,128},{128,160},{160,192},{192,224},{1,3... | collective-permute-start | bytes 276488 | tf_op jit(solution)/shard_map/ppermute | solution.py:21
  216.4 35.3 %collective-permute-start.13 = (f32[1,3,3,4,5,128]{5,4,3,2,1,0:T(8,128)}, f32[1,3,3,4,5,128]{5,4,3,2,1,0:T(8,128)}, u32[]{:S(2)}, u32[]{:S(2)}) collective-permute-start(f32[1,3,3,4,5,128]{5,4,3,2,1,0:T(8,128)} %slice.461), channel_id=1, source_target_pairs={{32,0},{64,32},{96,64},{128,96},{160,128},{192,160},{224,192},{33,... | collective-permute-start | bytes 276488 | tf_op jit(solution)/shard_map/ppermute | solution.py:24
  254.4 27.0 %collective-permute-start.15 = (f32[5,1,3,4,5,128]{5,4,3,2,1,0:T(8,128)}, f32[5,1,3,4,5,128]{5,4,3,2,1,0:T(8,128)}, u32[]{:S(2)}, u32[]{:S(2)}) collective-permute-start(f32[5,1,3,4,5,128]{5,4,3,2,1,0:T(8,128)} %get-tuple-element.417), channel_id=1, source_target_pairs={{4,0},{8,4},{12,8},{16,12},{20,16},{24,20},{28,24},{5,1},{9,5},{13... | collective-permute-start | bytes 460808 | tf_op jit(solution)/shard_map/ppermute | solution.py:24
  256.3 25.1 %collective-permute-start.14 = (f32[5,1,3,4,5,128]{5,4,3,2,1,0:T(8,128)}, f32[5,1,3,4,5,128]{5,4,3,2,1,0:T(8,128)}, u32[]{:S(2)}, u32[]{:S(2)}) collective-permute-start(f32[5,1,3,4,5,128]{5,4,3,2,1,0:T(8,128)} %get-tuple-element.416), channel_id=1, source_target_pairs={{0,4},{4,8},{8,12},{12,16},{16,20},{20,24},{24,28},{1,5},{5,9},{9,... | collective-permute-start | bytes 460808 | tf_op jit(solution)/shard_map/ppermute | solution.py:21
  260.2 28.5 %copy-start.1 = (f32[5,10,16,128]{3,0,2,1:T(8,128)S(1)}, f32[5,10,16,128]{3,0,2,1:T(8,128)}, u32[]{:S(2)}) copy-start(f32[5,10,16,128]{3,0,2,1:T(8,128)} %copy-done) | copy-start | bytes 1228804
  260.2 28.5 %copy-start.3 = (f32[5,10,18,1]{3,0,2,1:T(8,128)S(1)}, f32[5,10,18,1]{3,0,2,1:T(8,128)}, u32[]{:S(2)}) copy-start(f32[5,10,18,1]{3,0,2,1:T(8,128)} %copy-done.2) | copy-start | bytes 10804
  260.2 28.6 %copy-start.10 = (f32[5,8,16,128]{3,0,2,1:T(8,128)S(1)}, f32[5,8,16,128]{3,0,2,1:T(8,128)}, u32[]{:S(2)}) copy-start(f32[5,8,16,128]{3,0,2,1:T(8,128)} %copy-done.9) | copy-start | bytes 983044
  260.3 28.6 %copy-start.16 = (f32[5,10,1,128]{3,0,2,1:T(8,128)S(1)}, f32[5,10,1,128]{3,0,2,1:T(8,128)}, u32[]{:S(2)}) copy-start(f32[5,10,1,128]{3,0,2,1:T(8,128)} %copy-done.15) | copy-start | bytes 76804
  260.3 28.6 %copy-start.18 = (f32[5,10,1,128]{3,0,2,1:T(8,128)S(1)}, f32[5,10,1,128]{3,0,2,1:T(8,128)}, u32[]{:S(2)}) copy-start(f32[5,10,1,128]{3,0,2,1:T(8,128)} %copy-done.17) | copy-start | bytes 76804
  260.3 28.6 %copy-start.21 = (f32[5,1,16,128]{3,0,2,1:T(8,128)S(1)}, f32[5,1,16,128]{3,0,2,1:T(8,128)}, u32[]{:S(2)}) copy-start(f32[5,1,16,128]{3,0,2,1:T(8,128)} %copy-done.20) | copy-start | bytes 122884
  260.3 28.6 %copy-start.36 = (f32[5]{0:T(128)S(1)}, f32[5]{0:T(128)}, u32[]{:S(2)}) copy-start(f32[5]{0:T(128)} %constant.371.clone) | copy-start | bytes 64
  282.8 14.1 %collective-permute-start.17 = (f32[5,5,1,4,5,128]{5,4,3,2,1,0:T(8,128)S(1)}, f32[5,5,1,4,5,128]{5,4,3,2,1,0:T(8,128)S(1)}, u32[]{:S(2)}, u32[]{:S(2)}) collective-permute-start(f32[5,5,1,4,5,128]{5,4,3,2,1,0:T(8,128)S(1)} %get-tuple-element.415), channel_id=1, source_target_pairs={{1,0},{2,1},{3,2},{5,4},{6,5},{7,6},{9,8},{10,9},{11,10},{13,12},{... | collective-permute-start | bytes 768008 | tf_op jit(solution)/shard_map/ppermute | solution.py:24
  285.3 14.2 %copy-start.8 = (f32[5,3,3,4,5,128]{5,4,3,2,1,0:T(8,128)S(1)}, f32[5,3,3,4,5,128]{5,4,3,2,1,0:T(8,128)}, u32[]{:S(2)}) copy-start(f32[5,3,3,4,5,128]{5,4,3,2,1,0:T(8,128)} %copy-done.7) | copy-start | bytes 1382404
  285.3 14.2 %collective-permute-start.16 = (f32[5,5,1,4,5,128]{5,4,3,2,1,0:T(8,128)S(1)}, f32[5,5,1,4,5,128]{5,4,3,2,1,0:T(8,128)S(1)}, u32[]{:S(2)}, u32[]{:S(2)}) collective-permute-start(f32[5,5,1,4,5,128]{5,4,3,2,1,0:T(8,128)S(1)} %get-tuple-element.414), channel_id=1, source_target_pairs={{0,1},{1,2},{2,3},{4,5},{5,6},{6,7},{8,9},{9,10},{10,11},{12,13},{... | collective-permute-start | bytes 768008 | tf_op jit(solution)/shard_map/ppermute | solution.py:21
  (51 other events, 158.3 us)
where the time goes:
time: 306 us; the launch traced here: 302 us
  local copies, waits for them, and re-layouts  117 us (38%)
  matrix products  67.2 us (22%)
  starting transfers between devices  64.7 us (21%)
  other arithmetic  27.3 us (9%)
  waiting for transfers between devices  23.1 us (8%)
    ppermute x9, starting transfers between devices, with_halo(): lax.ppermute(lax.slice_in_dim(block, block.shape[dim] - width, None, axis...  46.1 us
    scatter-add x2, local copies, waits for them, and re-layouts, local(): extended.at[:, :, :, 2].add(extended[:, :, :, 0]).at[:, :, :, -3]  42 us
    dot_general x4, matrix products, group_step(): lax.dot_general(pair_weights, spread, (((0,), (0,)), ((), ())), precision...  36.2 us
    dot_general x4, matrix products, group_step(): jnp.dot(pair_weights, table, precision=lax.Precision.HIGHEST)  29.8 us
    scatter x1, local copies, waits for them, and re-layouts, local(): ghost_shell = deposit.at[:, 1:-1, 1:-1, 1:-1].set(0.0)  20.9 us
    ppermute x9, starting transfers between devices, with_halo(): lax.ppermute(lax.slice_in_dim(block, 0, width, axis=dim), axis, backward)  18.6 us
    ppermute x9, waiting for transfers between devices, with_halo(): lax.ppermute(lax.slice_in_dim(block, 0, width, axis=dim), axis, backward)  12.6 us
    ppermute x9, waiting for transfers between devices, with_halo(): lax.ppermute(lax.slice_in_dim(block, block.shape[dim] - width, None, axis...  10.5 us
  transfers between devices with their start and end apart: 18, of which 8 were waited for; matrix products, arithmetic and copies ran while one was open for 25% of the time, Pallas kernels for 0%

commit v1 on v0

--- a/solution.py
+++ b/solution.py
@@ -23,6 +23,23 @@
         )
         high = lax.ppermute(lax.slice_in_dim(block, 0, width, axis=dim), axis, backward)
         block = jnp.concatenate([low, block, high], axis=dim)
+    return block
+
+
+def fold_ghosts(block, sides):
+    for axis, dim in sides:
+        count = lax.axis_size(axis)
+        forward = [(i, i + 1) for i in range(count - 1)]
+        backward = [(target, source) for source, target in forward]
+        span = block.shape[dim]
+        below = lax.ppermute(lax.slice_in_dim(block, span - 1, span, axis=dim), axis, forward)
+        above = lax.ppermute(lax.slice_in_dim(block, 0, 1, axis=dim), axis, backward)
+        inner = lax.slice_in_dim(block, 1, span - 1, axis=dim)
+        low_pad = [(0, 0)] * block.ndim
+        high_pad = [(0, 0)] * block.ndim
+        low_pad[dim] = (0, span - 3)
+        high_pad[dim] = (span - 3, 0)
+        block = inner + jnp.pad(below, low_pad) + jnp.pad(above, high_pad)
     return block
 
 
@@ -145,14 +162,7 @@
     )
     updated = updated.reshape(blocks, parcel_fields, block_parcels)
     deposit = jnp.transpose(deposit_rows.reshape(span_x, span_y, fields, span_z), (2, 0, 1, 3))
-    ghost_shell = deposit.at[:, 1:-1, 1:-1, 1:-1].set(0.0)
-    extended = with_halo(ghost_shell, (("gx", 1), ("gy", 2), ("gz", 3)), 1)
-    extended = extended.at[:, 2].add(extended[:, 0]).at[:, -3].add(extended[:, -1])
-    extended = extended.at[:, :, 2].add(extended[:, :, 0]).at[:, :, -3].add(extended[:, :, -1])
-    extended = (
-        extended.at[:, :, :, 2].add(extended[:, :, :, 0]).at[:, :, :, -3].add(extended[:, :, :, -1])
-    )
-    cell_sources = deposit[:, 1:-1, 1:-1, 1:-1] + extended[:, 2:-2, 2:-2, 2:-2]
+    cell_sources = fold_ghosts(deposit, (("gx", 1), ("gy", 2), ("gz", 3)))
     kappa = jnp.array(DIFFUSION, jnp.float32)[:, None, None, None]
     gas_next = gas_state + kappa * laplacian(padded) + COUPLING * cell_sources
     kept = jnp.where((alive_mask & (destination == 13))[:, None, None], updated, 0.0)

time: 306 us -> 212 us (0.69)
  local copies, waits for them, and re-layouts: 117 us -> 32.8 us
  other arithmetic: 27.3 us -> 21.1 us
  starting transfers between devices: 64.7 us -> 61.1 us
    scatter-add x4 -> x0, local copies, waits for them, and re-layouts: 42 us -> none  [the longest x2 42 us: local(): extended.at[:, :, :, 2].add(extended[:, :, :, 0]).at[:, :, :, -3]]
    scatter x1 -> x0, local copies, waits for them, and re-layouts: 20.9 us -> none  [local(): ghost_shell = deposit.at[:, 1:-1, 1:-1, 1:-1].set(0.0)]
    ppermute x9 -> x6, starting transfers between devices: 46.1 us -> 27.7 us  [with_halo(): lax.ppermute(lax.slice_in_dim(block, block.shape[dim] - width, None, axis...]
    ppermute x0 -> x6, starting transfers between devices: none -> 17.8 us  [the longest x3 8.91 us: fold_ghosts(): lax.ppermute(lax.slice_in_dim(block, 0, 1, axis=dim), axis, backward)]
    ppermute x0 -> x6, waiting for transfers between devices: none -> 7.49 us  [the longest x3 4.8 us: fold_ghosts(): lax.ppermute(lax.slice_in_dim(block, span - 1, span, axis=dim), axis, for...]
    slice x8 -> x5, local copies, waits for them, and re-layouts: 7.03 us -> 1.41 us  [with_halo(): lax.slice_in_dim(block, block.shape[dim] - width, None, axis=dim)]
    slice x5 -> x4, local copies, waits for them, and re-layouts: 4.94 us -> 1.13 us  [with_halo(): lax.slice_in_dim(block, 0, width, axis=dim)]
    unnamed x70 -> x52, local copies, waits for them, and re-layouts: 10 us -> 6.37 us
  transfers between devices with their start and end apart: 18 -> 18, of which waited for: 8 -> 9; matrix products, arithmetic and copies ran while one was open for 25% -> 6% of each run, Pallas kernels for 0% -> 0%
where the time goes in v1:
time: 212 us; the launch traced here: 209 us
  matrix products  66.5 us (31%)
  starting transfers between devices  61.1 us (29%)
  local copies, waits for them, and re-layouts  32.8 us (15%)
  waiting for transfers between devices  25.5 us (12%)
  other arithmetic  21.1 us (10%)
    dot_general x4, matrix products, group_step(): lax.dot_general(pair_weights, spread, (((0,), (0,)), ((), ())), precision...  36.3 us
    dot_general x4, matrix products, group_step(): jnp.dot(pair_weights, table, precision=lax.Precision.HIGHEST)  30 us
    ppermute x6, starting transfers between devices, with_halo(): lax.ppermute(lax.slice_in_dim(block, block.shape[dim] - width, None, axis...  27.7 us
    ppermute x6, starting transfers between devices, with_halo(): lax.ppermute(lax.slice_in_dim(block, 0, width, axis=dim), axis, backward)  15.6 us
    ppermute x6, waiting for transfers between devices, with_halo(): lax.ppermute(lax.slice_in_dim(block, 0, width, axis=dim), axis, backward)  10.7 us
    ppermute x3, starting transfers between devices, fold_ghosts(): lax.ppermute(lax.slice_in_dim(block, 0, 1, axis=dim), axis, backward)  8.91 us
    ppermute x3, starting transfers between devices, fold_ghosts(): lax.ppermute(lax.slice_in_dim(block, span - 1, span, axis=dim), axis, for...  8.88 us
    reshape x4, local copies, waits for them, and re-layouts, group_step(): jnp.dot(pair_weights, table, precision=lax.Precision.HIGHEST)  7.71 us
  transfers between devices with their start and end apart: 18, of which 9 were waited for; matrix products, arithmetic and copies ran while one was open for 6% of the time, Pallas kernels for 0%

profile of v1, /device:TPU:58, one launch (start us, length us, event | category | flops | bytes accessed | tf_op | source)
XLA Modules:
  0.0 209.3 jit_solution(11204151778321435606)
XLA Ops:
  1.9 7.9 %collective-permute-start.1 = (f32[5,1,16,128]{3,0,2,1:T(8,128)S(1)}, f32[5,1,16,128]{3,0,2,1:T(8,128)S(1)}, u32[]{:S(2)}, u32[]{:S(2)}) collective-permute-start(f32[5,1,16,128]{3,0,2,1:T(8,128)S(1)} %get-tuple-element.339), channel_id=1, source_target_pairs={{0,32},{32,64},{64,96},{96,128},{128,160},{160,192},{192,224},{1,3... | collective-permute-start | bytes 122888 | tf_op jit(solution)/shard_map/ppermute | solution.py:21
  16.4 5.7 %collective-permute-done = f32[5,1,16,128]{3,0,2,1:T(8,128)S(1)} collective-permute-done((f32[5,1,16,128]{3,0,2,1:T(8,128)S(1)}, f32[5,1,16,128]{3,0,2,1:T(8,128)S(1)}, u32[]{:S(2)}, u32[]{:S(2)}) %collective-permute-start) | collective-permute-done | bytes 40992 | tf_op jit(solution)/shard_map/ppermute | solution.py:24
  24.0 2.4 %collective-permute-start.3 = (f32[5,10,1,128]{3,0,2,1:T(8,128)S(1)}, f32[5,10,1,128]{3,0,2,1:T(8,128)S(1)}, u32[]{:S(2)}, u32[]{:S(2)}) collective-permute-start(f32[5,10,1,128]{3,0,2,1:T(8,128)S(1)} %get-tuple-element.336), channel_id=1, source_target_pairs={{0,4},{4,8},{8,12},{12,16},{16,20},{20,24},{24,28},{1,5},{5,9},{9,... | collective-permute-start | bytes 76808 | tf_op jit(solution)/shard_map/ppermute | solution.py:21
  27.0 2.4 %collective-permute-done.3 = f32[5,10,1,128]{3,0,2,1:T(8,128)S(1)} collective-permute-done((f32[5,10,1,128]{3,0,2,1:T(8,128)S(1)}, f32[5,10,1,128]{3,0,2,1:T(8,128)S(1)}, u32[]{:S(2)}, u32[]{:S(2)}) %collective-permute-start.3) | collective-permute-done | bytes 25632 | tf_op jit(solution)/shard_map/ppermute | solution.py:21
  30.1 2.7 %collective-permute-start.4 = (f32[5,10,18,1]{2,3,1,0:T(1,128)S(1)}, f32[5,10,18,1]{2,3,1,0:T(1,128)S(1)}, u32[]{:S(2)}, u32[]{:S(2)}) collective-permute-start(f32[5,10,18,1]{2,3,1,0:T(1,128)S(1)} %copy.34), channel_id=1, source_target_pairs={{1,0},{2,1},{3,2},{5,4},{6,5},{7,6},{9,8},{10,9},{11,10},{13,12},{... | collective-permute-start | bytes 10808 | tf_op jit(solution)/shard_map/ppermute | solution.py:24
  33.3 3.1 %collective-permute-start.5 = (f32[5,10,18,1]{2,3,1,0:T(1,128)S(1)}, f32[5,10,18,1]{2,3,1,0:T(1,128)S(1)}, u32[]{:S(2)}, u32[]{:S(2)}) collective-permute-start(f32[5,10,18,1]{2,3,1,0:T(1,128)S(1)} %copy.36), channel_id=1, source_target_pairs={{0,1},{1,2},{2,3},{4,5},{5,6},{6,7},{8,9},{9,10},{10,11},{12,13},{... | collective-permute-start | bytes 10808 | tf_op jit(solution)/shard_map/ppermute | solution.py:21
  43.2 97.0 %while.17 = (s32[]{:T(128)}, f32[180,650]{1,0:T(8,128)}, f32[4,8,5,128]{3,1,2,0:T(8,128)}, s32[4,8,128]{2,1,0:T(8,128)}, f32[4,8,3,128]{3,2,1,0:T(4,128)S(1)}, /...) while((s32[]{:T(128)}, f32[180,650]{1,0:T(8,128)}, ...), condition=%wide.region_2.3_spmd.clone.clone, body=%wide.region_0.2_spmd.clone.clone.sunk | while | flops 2882474496 | bytes 28657872 | solution.py:160
  44.8 7.5 %fusion.85 = f32[1024,650]{0,1:T(8,128)} fusion(f32[180,650]{1,0:T(8,128)S(1)} %get-tuple-element.472, f32[1024]{0:T(1024)S(1)} %bitcast.187, s32[1024]{0:T(1024)S(1)} %get-tuple-element.426, f32[1024]{0:T(1024)S(1)} %bitcast.183, s32[1024]{0:T(1024)S(1)} %get-tuple-element.428, f32[1024]{0:T(1024)S(1)} %bitcast.185, ...), kind=kOutput, calls=%fused_computation.10.clone.1 | convolution fusion | flops 1439723520 | bytes 3163168 | tf_op jit(solution)/shard_map/while/body/eval_jaxpr/dot_general | solution.py:136
  52.2 1.9 reshape.476
  58.4 9.0 %convolution_add_fusion.2 = f32[180,650]{1,0:T(8,128)} fusion(f32[1024,650]{0,1:T(8,128)} %mul.506, f32[180,650]{1,0:T(8,128)} %get-tuple-element.456, f32[1024]{0:T(1024)S(1)} %bitcast.188, s32[1024]{0:T(1024)S(1)} %get-tuple-element.426, f32[1024]{0:T(1024)S(1)} %bitcast.184, s32[1024]{0:T(1024)S(1)} %get-tuple-element.428, ...), kind=kOutput, calls=%fused_computation.8.clone.1 | convolution fusion | flops 1439957504 | bytes 3631169 | tf_op jit(solution)/shard_map/while/body/eval_jaxpr/dot_general | solution.py:149
  68.9 7.5 %fusion.85 = f32[1024,650]{0,1:T(8,128)} fusion(f32[180,650]{1,0:T(8,128)S(1)} %get-tuple-element.472, f32[1024]{0:T(1024)S(1)} %bitcast.187, s32[1024]{0:T(1024)S(1)} %get-tuple-element.426, f32[1024]{0:T(1024)S(1)} %bitcast.183, s32[1024]{0:T(1024)S(1)} %get-tuple-element.428, f32[1024]{0:T(1024)S(1)} %bitcast.185, ...), kind=kOutput, calls=%fused_computation.10.clone.1 | convolution fusion | flops 1439723520 | bytes 3163168 | tf_op jit(solution)/shard_map/while/body/eval_jaxpr/dot_general | solution.py:136
  76.4 1.9 reshape.476
  82.5 9.1 %convolution_add_fusion.2 = f32[180,650]{1,0:T(8,128)} fusion(f32[1024,650]{0,1:T(8,128)} %mul.506, f32[180,650]{1,0:T(8,128)} %get-tuple-element.456, f32[1024]{0:T(1024)S(1)} %bitcast.188, s32[1024]{0:T(1024)S(1)} %get-tuple-element.426, f32[1024]{0:T(1024)S(1)} %bitcast.184, s32[1024]{0:T(1024)S(1)} %get-tuple-element.428, ...), kind=kOutput, calls=%fused_computation.8.clone.1 | convolution fusion | flops 1439957504 | bytes 3631169 | tf_op jit(solution)/shard_map/while/body/eval_jaxpr/dot_general | solution.py:149
  93.2 7.5 %fusion.85 = f32[1024,650]{0,1:T(8,128)} fusion(f32[180,650]{1,0:T(8,128)S(1)} %get-tuple-element.472, f32[1024]{0:T(1024)S(1)} %bitcast.187, s32[1024]{0:T(1024)S(1)} %get-tuple-element.426, f32[1024]{0:T(1024)S(1)} %bitcast.183, s32[1024]{0:T(1024)S(1)} %get-tuple-element.428, f32[1024]{0:T(1024)S(1)} %bitcast.185, ...), kind=kOutput, calls=%fused_computation.10.clone.1 | convolution fusion | flops 1439723520 | bytes 3163168 | tf_op jit(solution)/shard_map/while/body/eval_jaxpr/dot_general | solution.py:136
  100.7 1.9 reshape.476
  106.8 9.1 %convolution_add_fusion.2 = f32[180,650]{1,0:T(8,128)} fusion(f32[1024,650]{0,1:T(8,128)} %mul.506, f32[180,650]{1,0:T(8,128)} %get-tuple-element.456, f32[1024]{0:T(1024)S(1)} %bitcast.188, s32[1024]{0:T(1024)S(1)} %get-tuple-element.426, f32[1024]{0:T(1024)S(1)} %bitcast.184, s32[1024]{0:T(1024)S(1)} %get-tuple-element.428, ...), kind=kOutput, calls=%fused_computation.8.clone.1 | convolution fusion | flops 1439957504 | bytes 3631169 | tf_op jit(solution)/shard_map/while/body/eval_jaxpr/dot_general | solution.py:149
  117.5 7.5 %fusion.85 = f32[1024,650]{0,1:T(8,128)} fusion(f32[180,650]{1,0:T(8,128)S(1)} %get-tuple-element.472, f32[1024]{0:T(1024)S(1)} %bitcast.187, s32[1024]{0:T(1024)S(1)} %get-tuple-element.426, f32[1024]{0:T(1024)S(1)} %bitcast.183, s32[1024]{0:T(1024)S(1)} %get-tuple-element.428, f32[1024]{0:T(1024)S(1)} %bitcast.185, ...), kind=kOutput, calls=%fused_computation.10.clone.1 | convolution fusion | flops 1439723520 | bytes 3163168 | tf_op jit(solution)/shard_map/while/body/eval_jaxpr/dot_general | solution.py:136
  125.0 1.9 reshape.476
  131.1 9.1 %convolution_add_fusion.2 = f32[180,650]{1,0:T(8,128)} fusion(f32[1024,650]{0,1:T(8,128)} %mul.506, f32[180,650]{1,0:T(8,128)} %get-tuple-element.456, f32[1024]{0:T(1024)S(1)} %bitcast.188, s32[1024]{0:T(1024)S(1)} %get-tuple-element.426, f32[1024]{0:T(1024)S(1)} %bitcast.184, s32[1024]{0:T(1024)S(1)} %get-tuple-element.428, ...), kind=kOutput, calls=%fused_computation.8.clone.1 | convolution fusion | flops 1439957504 | bytes 3631169 | tf_op jit(solution)/shard_map/while/body/eval_jaxpr/dot_general | solution.py:149
  141.9 4.4 %collective-permute-start.6 = (f32[5,1,18,130]{3,0,2,1:T(8,128)S(1)}, f32[5,1,18,130]{3,0,2,1:T(8,128)S(1)}, u32[]{:S(2)}, u32[]{:S(2)}) collective-permute-start(f32[5,1,18,130]{3,0,2,1:T(8,128)S(1)} %get-tuple-element.324), channel_id=1, source_target_pairs={{0,32},{32,64},{64,96},{96,128},{128,160},{160,192},{192,224},{1,3... | collective-permute-start | bytes 140408 | tf_op jit(solution)/shard_map/ppermute | solution.py:35
  150.0 9.9 %collective-permute-start.12 = (f32[1,3,3,4,5,128]{5,4,3,2,1,0:T(8,128)}, f32[1,3,3,4,5,128]{5,4,3,2,1,0:T(8,128)}, u32[]{:S(2)}, u32[]{:S(2)}) collective-permute-start(f32[1,3,3,4,5,128]{5,4,3,2,1,0:T(8,128)} %slice.238), channel_id=1, source_target_pairs={{0,32},{32,64},{64,96},{96,128},{128,160},{160,192},{192,224},{1,3... | collective-permute-start | bytes 276488 | tf_op jit(solution)/shard_map/ppermute | solution.py:21
  166.3 3.6 %collective-permute-start.9 = (f32[5,8,1,130]{3,0,2,1:T(8,128)S(1)}, f32[5,8,1,130]{3,0,2,1:T(8,128)S(1)}, u32[]{:S(2)}, u32[]{:S(2)}) collective-permute-start(f32[5,8,1,130]{3,0,2,1:T(8,128)S(1)} %get-tuple-element.329), channel_id=1, source_target_pairs={{4,0},{8,4},{12,8},{16,12},{20,16},{24,20},{28,24},{5,1},{9,5},{13... | collective-permute-start | bytes 62408 | tf_op jit(solution)/shard_map/ppermute | solution.py:36
  172.9 2.7 %collective-permute-done.13 = f32[1,3,3,4,5,128]{5,4,3,2,1,0:T(8,128)S(1)} collective-permute-done((f32[1,3,3,4,5,128]{5,4,3,2,1,0:T(8,128)}, f32[1,3,3,4,5,128]{5,4,3,2,1,0:T(8,128)S(1)}, u32[]{:S(2)}, u32[]{:S(2)}) %collective-permute-start.13) | collective-permute-done | bytes 92192 | tf_op jit(solution)/shard_map/ppermute | solution.py:24
  177.6 3.8 %collective-permute-start.15 = (f32[5,1,3,4,5,128]{5,4,3,2,1,0:T(8,128)S(1)}, f32[5,1,3,4,5,128]{5,4,3,2,1,0:T(8,128)S(1)}, u32[]{:S(2)}, u32[]{:S(2)}) collective-permute-start(f32[5,1,3,4,5,128]{5,4,3,2,1,0:T(8,128)S(1)} %get-tuple-element.333), channel_id=1, source_target_pairs={{4,0},{8,4},{12,8},{16,12},{20,16},{24,20},{28,24},{5,1},{9,5},{13... | collective-permute-start | bytes 460808 | tf_op jit(solution)/shard_map/ppermute | solution.py:24
  181.6 2.5 %collective-permute-start.10 = (f32[5,8,16,1]{3,0,2,1:T(8,128)S(1)}, f32[5,8,16,1]{3,0,2,1:T(8,128)S(1)}, u32[]{:S(2)}, u32[]{:S(2)}) collective-permute-start(f32[5,8,16,1]{3,0,2,1:T(8,128)S(1)} %get-tuple-element.330), channel_id=1, source_target_pairs={{0,1},{1,2},{2,3},{4,5},{5,6},{6,7},{8,9},{9,10},{10,11},{12,13},{... | collective-permute-start | bytes 7688 | tf_op jit(solution)/shard_map/ppermute | solution.py:35
  184.2 3.3 %collective-permute-start.11 = (f32[5,8,16,1]{3,0,2,1:T(8,128)S(1)}, f32[5,8,16,1]{3,0,2,1:T(8,128)S(1)}, u32[]{:S(2)}, u32[]{:S(2)}) collective-permute-start(f32[5,8,16,1]{3,0,2,1:T(8,128)S(1)} %get-tuple-element.331), channel_id=1, source_target_pairs={{1,0},{2,1},{3,2},{5,4},{6,5},{7,6},{9,8},{10,9},{11,10},{13,12},{... | collective-permute-start | bytes 7688 | tf_op jit(solution)/shard_map/ppermute | solution.py:36
  187.6 2.5 %collective-permute-start.16 = (f32[5,5,1,4,5,128]{5,4,3,2,1,0:T(8,128)S(1)}, f32[5,5,1,4,5,128]{5,4,3,2,1,0:T(8,128)S(1)}, u32[]{:S(2)}, u32[]{:S(2)}) collective-permute-start(f32[5,5,1,4,5,128]{5,4,3,2,1,0:T(8,128)S(1)} %get-tuple-element.326), channel_id=1, source_target_pairs={{0,1},{1,2},{2,3},{4,5},{5,6},{6,7},{8,9},{9,10},{10,11},{12,13},{... | collective-permute-start | bytes 768008 | tf_op jit(solution)/shard_map/ppermute | solution.py:21
  190.1 3.4 %collective-permute-start.17 = (f32[5,5,1,4,5,128]{5,4,3,2,1,0:T(8,128)S(1)}, f32[5,5,1,4,5,128]{5,4,3,2,1,0:T(8,128)S(1)}, u32[]{:S(2)}, u32[]{:S(2)}) collective-permute-start(f32[5,5,1,4,5,128]{5,4,3,2,1,0:T(8,128)S(1)} %get-tuple-element.327), channel_id=1, source_target_pairs={{1,0},{2,1},{3,2},{5,4},{6,5},{7,6},{9,8},{10,9},{11,10},{13,12},{... | collective-permute-start | bytes 768008 | tf_op jit(solution)/shard_map/ppermute | solution.py:24
  193.5 4.8 %collective-permute-done.10 = f32[5,8,16,1]{3,0,2,1:T(8,128)S(1)} collective-permute-done((f32[5,8,16,1]{3,0,2,1:T(8,128)S(1)}, f32[5,8,16,1]{3,0,2,1:T(8,128)S(1)}, u32[]{:S(2)}, u32[]{:S(2)}) %collective-permute-start.10) | collective-permute-done | bytes 2592 | tf_op jit(solution)/shard_map/ppermute | solution.py:35
  198.3 2.5 %collective-permute-done.11 = f32[5,8,16,1]{3,0,2,1:T(8,128)S(1)} collective-permute-done((f32[5,8,16,1]{3,0,2,1:T(8,128)S(1)}, f32[5,8,16,1]{3,0,2,1:T(8,128)S(1)}, u32[]{:S(2)}, u32[]{:S(2)}) %collective-permute-start.11) | collective-permute-done | bytes 2592 | tf_op jit(solution)/shard_map/ppermute | solution.py:36
  202.5 3.5 %collective-permute-done.16 = f32[5,5,1,4,5,128]{5,4,3,2,1,0:T(8,128)S(1)} collective-permute-done((f32[5,5,1,4,5,128]{5,4,3,2,1,0:T(8,128)S(1)}, f32[5,5,1,4,5,128]{5,4,3,2,1,0:T(8,128)S(1)}, u32[]{:S(2)}, u32[]{:S(2)}) %collective-permute-start.16) | collective-permute-done | bytes 256032 | tf_op jit(solution)/shard_map/ppermute | solution.py:21
  206.0 2.3 %collective-permute-done.17 = f32[5,5,1,4,5,128]{5,4,3,2,1,0:T(8,128)S(1)} collective-permute-done((f32[5,5,1,4,5,128]{5,4,3,2,1,0:T(8,128)S(1)}, f32[5,5,1,4,5,128]{5,4,3,2,1,0:T(8,128)S(1)}, u32[]{:S(2)}, u32[]{:S(2)}) %collective-permute-start.17) | collective-permute-done | bytes 256032 | tf_op jit(solution)/shard_map/ppermute | solution.py:24
  (202 shorter events, 59.5 us)
Async XLA Ops:
  0.6 25.8 %copy-start.20 = (s32[32]{0:T(128)S(1)}, s32[32]{0:T(128)}, u32[]{:S(2)}) copy-start(s32[32]{0:T(128)} %param.13) | copy-start | bytes 388
  1.8 13.3 %copy-start.4 = (f32[5,8,16,128]{3,0,2,1:T(8,128)}, f32[5,8,16,128]{3,0,2,1:T(8,128)S(1)}, u32[]{:S(2)}) copy-start(f32[5,8,16,128]{3,0,2,1:T(8,128)S(1)} %copy.39) | copy-start | bytes 983044
  1.9 13.3 %collective-permute-start.1 = (f32[5,1,16,128]{3,0,2,1:T(8,128)S(1)}, f32[5,1,16,128]{3,0,2,1:T(8,128)S(1)}, u32[]{:S(2)}, u32[]{:S(2)}) collective-permute-start(f32[5,1,16,128]{3,0,2,1:T(8,128)S(1)} %get-tuple-element.339), channel_id=1, source_target_pairs={{0,32},{32,64},{64,96},{96,128},{128,160},{160,192},{192,224},{1,3... | collective-permute-start | bytes 122888 | tf_op jit(solution)/shard_map/ppermute | solution.py:21
  9.7 12.4 %collective-permute-start = (f32[5,1,16,128]{3,0,2,1:T(8,128)S(1)}, f32[5,1,16,128]{3,0,2,1:T(8,128)S(1)}, u32[]{:S(2)}, u32[]{:S(2)}) collective-permute-start(f32[5,1,16,128]{3,0,2,1:T(8,128)S(1)} %get-tuple-element.338), channel_id=1, source_target_pairs={{32,0},{64,32},{96,64},{128,96},{160,128},{192,160},{224,192},{33,... | collective-permute-start | bytes 122888 | tf_op jit(solution)/shard_map/ppermute | solution.py:24
  15.1 14.2 %copy-start.14 = (f32[5,1,16,128]{3,0,2,1:T(8,128)}, f32[5,1,16,128]{3,0,2,1:T(8,128)S(1)}, u32[]{:S(2)}) copy-start(f32[5,1,16,128]{3,0,2,1:T(8,128)S(1)} %collective-permute-done.1) | copy-start | bytes 122884
  22.1 4.9 %collective-permute-start.2 = (f32[5,10,1,128]{3,0,2,1:T(8,128)S(1)}, f32[5,10,1,128]{3,0,2,1:T(8,128)S(1)}, u32[]{:S(2)}, u32[]{:S(2)}) collective-permute-start(f32[5,10,1,128]{3,0,2,1:T(8,128)S(1)} %get-tuple-element.337), channel_id=1, source_target_pairs={{4,0},{8,4},{12,8},{16,12},{20,16},{24,20},{28,24},{5,1},{9,5},{13... | collective-permute-start | bytes 76808 | tf_op jit(solution)/shard_map/ppermute | solution.py:24
  24.0 5.3 %collective-permute-start.3 = (f32[5,10,1,128]{3,0,2,1:T(8,128)S(1)}, f32[5,10,1,128]{3,0,2,1:T(8,128)S(1)}, u32[]{:S(2)}, u32[]{:S(2)}) collective-permute-start(f32[5,10,1,128]{3,0,2,1:T(8,128)S(1)} %get-tuple-element.336), channel_id=1, source_target_pairs={{0,4},{4,8},{8,12},{12,16},{16,20},{20,24},{24,28},{1,5},{5,9},{9,... | collective-permute-start | bytes 76808 | tf_op jit(solution)/shard_map/ppermute | solution.py:21
  27.0 12.6 %copy-start.9 = (f32[5,10,1,128]{3,0,2,1:T(8,128)}, f32[5,10,1,128]{3,0,2,1:T(8,128)S(1)}, u32[]{:S(2)}) copy-start(f32[5,10,1,128]{3,0,2,1:T(8,128)S(1)} %collective-permute-done.2) | copy-start | bytes 76804
  29.4 10.2 %copy-start.11 = (f32[5,10,1,128]{3,0,2,1:T(8,128)}, f32[5,10,1,128]{3,0,2,1:T(8,128)S(1)}, u32[]{:S(2)}) copy-start(f32[5,10,1,128]{3,0,2,1:T(8,128)S(1)} %collective-permute-done.3) | copy-start | bytes 76804
  30.1 6.8 %collective-permute-start.4 = (f32[5,10,18,1]{2,3,1,0:T(1,128)S(1)}, f32[5,10,18,1]{2,3,1,0:T(1,128)S(1)}, u32[]{:S(2)}, u32[]{:S(2)}) collective-permute-start(f32[5,10,18,1]{2,3,1,0:T(1,128)S(1)} %copy.34), channel_id=1, source_target_pairs={{1,0},{2,1},{3,2},{5,4},{6,5},{7,6},{9,8},{10,9},{11,10},{13,12},{... | collective-permute-start | bytes 10808 | tf_op jit(solution)/shard_map/ppermute | solution.py:24
  33.3 5.7 %collective-permute-start.5 = (f32[5,10,18,1]{2,3,1,0:T(1,128)S(1)}, f32[5,10,18,1]{2,3,1,0:T(1,128)S(1)}, u32[]{:S(2)}, u32[]{:S(2)}) collective-permute-start(f32[5,10,18,1]{2,3,1,0:T(1,128)S(1)} %copy.36), channel_id=1, source_target_pairs={{0,1},{1,2},{2,3},{4,5},{5,6},{6,7},{8,9},{9,10},{10,11},{12,13},{... | collective-permute-start | bytes 10808 | tf_op jit(solution)/shard_map/ppermute | solution.py:21
  141.9 20.6 %collective-permute-start.6 = (f32[5,1,18,130]{3,0,2,1:T(8,128)S(1)}, f32[5,1,18,130]{3,0,2,1:T(8,128)S(1)}, u32[]{:S(2)}, u32[]{:S(2)}) collective-permute-start(f32[5,1,18,130]{3,0,2,1:T(8,128)S(1)} %get-tuple-element.324), channel_id=1, source_target_pairs={{0,32},{32,64},{64,96},{96,128},{128,160},{160,192},{192,224},{1,3... | collective-permute-start | bytes 140408 | tf_op jit(solution)/shard_map/ppermute | solution.py:35
  146.4 16.9 %collective-permute-start.7 = (f32[5,1,18,130]{3,0,2,1:T(8,128)S(1)}, f32[5,1,18,130]{3,0,2,1:T(8,128)}, u32[]{:S(2)}, u32[]{:S(2)}) collective-permute-start(f32[5,1,18,130]{3,0,2,1:T(8,128)S(1)} %get-tuple-element.325), channel_id=1, source_target_pairs={{32,0},{64,32},{96,64},{128,96},{160,128},{192,160},{224,192},{33,... | collective-permute-start | bytes 140408 | tf_op jit(solution)/shard_map/ppermute | solution.py:36
  148.3 21.6 %copy-start.21 = (pred[32]{0:T(512)(128)(4,1)S(1)}, pred[32]{0:T(512)(128)(4,1)}, u32[]{:S(2)}) copy-start(pred[32]{0:T(512)(128)(4,1)} %get-tuple-element.343) | copy-start | bytes 100
  150.0 21.9 %collective-permute-start.12 = (f32[1,3,3,4,5,128]{5,4,3,2,1,0:T(8,128)}, f32[1,3,3,4,5,128]{5,4,3,2,1,0:T(8,128)}, u32[]{:S(2)}, u32[]{:S(2)}) collective-permute-start(f32[1,3,3,4,5,128]{5,4,3,2,1,0:T(8,128)} %slice.238), channel_id=1, source_target_pairs={{0,32},{32,64},{64,96},{96,128},{128,160},{160,192},{192,224},{1,3... | collective-permute-start | bytes 276488 | tf_op jit(solution)/shard_map/ppermute | solution.py:21
  160.6 14.9 %collective-permute-start.13 = (f32[1,3,3,4,5,128]{5,4,3,2,1,0:T(8,128)}, f32[1,3,3,4,5,128]{5,4,3,2,1,0:T(8,128)S(1)}, u32[]{:S(2)}, u32[]{:S(2)}) collective-permute-start(f32[1,3,3,4,5,128]{5,4,3,2,1,0:T(8,128)} %slice.240), channel_id=1, source_target_pairs={{32,0},{64,32},{96,64},{128,96},{160,128},{192,160},{224,192},{33,... | collective-permute-start | bytes 276488 | tf_op jit(solution)/shard_map/ppermute | solution.py:24
  164.3 7.3 %collective-permute-start.8 = (f32[5,8,1,130]{3,0,2,1:T(8,128)S(1)}, f32[5,8,1,130]{3,0,2,1:T(8,128)S(1)}, u32[]{:S(2)}, u32[]{:S(2)}) collective-permute-start(f32[5,8,1,130]{3,0,2,1:T(8,128)S(1)} %get-tuple-element.328), channel_id=1, source_target_pairs={{0,4},{4,8},{8,12},{12,16},{16,20},{20,24},{24,28},{1,5},{5,9},{9,... | collective-permute-start | bytes 62408 | tf_op jit(solution)/shard_map/ppermute | solution.py:35
  166.3 5.5 %collective-permute-start.9 = (f32[5,8,1,130]{3,0,2,1:T(8,128)S(1)}, f32[5,8,1,130]{3,0,2,1:T(8,128)S(1)}, u32[]{:S(2)}, u32[]{:S(2)}) collective-permute-start(f32[5,8,1,130]{3,0,2,1:T(8,128)S(1)} %get-tuple-element.329), channel_id=1, source_target_pairs={{4,0},{8,4},{12,8},{16,12},{20,16},{24,20},{28,24},{5,1},{9,5},{13... | collective-permute-start | bytes 62408 | tf_op jit(solution)/shard_map/ppermute | solution.py:36
  175.6 11.9 %collective-permute-start.14 = (f32[5,1,3,4,5,128]{5,4,3,2,1,0:T(8,128)S(1)}, f32[5,1,3,4,5,128]{5,4,3,2,1,0:T(8,128)S(1)}, u32[]{:S(2)}, u32[]{:S(2)}) collective-permute-start(f32[5,1,3,4,5,128]{5,4,3,2,1,0:T(8,128)S(1)} %get-tuple-element.332), channel_id=1, source_target_pairs={{0,4},{4,8},{8,12},{12,16},{16,20},{20,24},{24,28},{1,5},{5,9},{9,... | collective-permute-start | bytes 460808 | tf_op jit(solution)/shard_map/ppermute | solution.py:21
  177.6 23.3 %copy-start.1 = (f32[5,10,18,1]{3,0,2,1:T(8,128)S(1)}, f32[5,10,18,1]{3,0,2,1:T(8,128)}, u32[]{:S(2)}) copy-start(f32[5,10,18,1]{3,0,2,1:T(8,128)} %copy-done) | copy-start | bytes 10804
  177.6 23.3 %copy-start.3 = (f32[5,10,18,1]{3,0,2,1:T(8,128)S(1)}, f32[5,10,18,1]{3,0,2,1:T(8,128)}, u32[]{:S(2)}) copy-start(f32[5,10,18,1]{3,0,2,1:T(8,128)} %copy-done.2) | copy-start | bytes 10804
  177.6 23.3 %copy-start.5 = (f32[5,8,16,128]{3,0,2,1:T(8,128)S(1)}, f32[5,8,16,128]{3,0,2,1:T(8,128)}, u32[]{:S(2)}) copy-start(f32[5,8,16,128]{3,0,2,1:T(8,128)} %copy-done.4) | copy-start | bytes 983044
  177.6 23.3 %copy-start.10 = (f32[5,10,1,128]{3,0,2,1:T(8,128)S(1)}, f32[5,10,1,128]{3,0,2,1:T(8,128)}, u32[]{:S(2)}) copy-start(f32[5,10,1,128]{3,0,2,1:T(8,128)} %copy-done.9) | copy-start | bytes 76804
  177.6 23.3 %copy-start.12 = (f32[5,10,1,128]{3,0,2,1:T(8,128)S(1)}, f32[5,10,1,128]{3,0,2,1:T(8,128)}, u32[]{:S(2)}) copy-start(f32[5,10,1,128]{3,0,2,1:T(8,128)} %copy-done.11) | copy-start | bytes 76804
  177.6 23.3 %copy-start.15 = (f32[5,1,16,128]{3,0,2,1:T(8,128)S(1)}, f32[5,1,16,128]{3,0,2,1:T(8,128)}, u32[]{:S(2)}) copy-start(f32[5,1,16,128]{3,0,2,1:T(8,128)} %copy-done.14) | copy-start | bytes 122884
  177.6 23.3 %copy-start.17 = (f32[5,1,16,128]{3,0,2,1:T(8,128)S(1)}, f32[5,1,16,128]{3,0,2,1:T(8,128)}, u32[]{:S(2)}) copy-start(f32[5,1,16,128]{3,0,2,1:T(8,128)} %copy-done.16) | copy-start | bytes 122884
  177.6 23.3 %copy-start.23 = (f32[5]{0:T(128)S(1)}, f32[5]{0:T(128)}, u32[]{:S(2)}) copy-start(f32[5]{0:T(128)} %constant.176.clone) | copy-start | bytes 64
  177.6 9.9 %collective-permute-start.15 = (f32[5,1,3,4,5,128]{5,4,3,2,1,0:T(8,128)S(1)}, f32[5,1,3,4,5,128]{5,4,3,2,1,0:T(8,128)S(1)}, u32[]{:S(2)}, u32[]{:S(2)}) collective-permute-start(f32[5,1,3,4,5,128]{5,4,3,2,1,0:T(8,128)S(1)} %get-tuple-element.333), channel_id=1, source_target_pairs={{4,0},{8,4},{12,8},{16,12},{20,16},{24,20},{28,24},{5,1},{9,5},{13... | collective-permute-start | bytes 460808 | tf_op jit(solution)/shard_map/ppermute | solution.py:24
  181.6 16.7 %collective-permute-start.10 = (f32[5,8,16,1]{3,0,2,1:T(8,128)S(1)}, f32[5,8,16,1]{3,0,2,1:T(8,128)S(1)}, u32[]{:S(2)}, u32[]{:S(2)}) collective-permute-start(f32[5,8,16,1]{3,0,2,1:T(8,128)S(1)} %get-tuple-element.330), channel_id=1, source_target_pairs={{0,1},{1,2},{2,3},{4,5},{5,6},{6,7},{8,9},{9,10},{10,11},{12,13},{... | collective-permute-start | bytes 7688 | tf_op jit(solution)/shard_map/ppermute | solution.py:35
  184.2 16.7 %collective-permute-start.11 = (f32[5,8,16,1]{3,0,2,1:T(8,128)S(1)}, f32[5,8,16,1]{3,0,2,1:T(8,128)S(1)}, u32[]{:S(2)}, u32[]{:S(2)}) collective-permute-start(f32[5,8,16,1]{3,0,2,1:T(8,128)S(1)} %get-tuple-element.331), channel_id=1, source_target_pairs={{1,0},{2,1},{3,2},{5,4},{6,5},{7,6},{9,8},{10,9},{11,10},{13,12},{... | collective-permute-start | bytes 7688 | tf_op jit(solution)/shard_map/ppermute | solution.py:36
  187.6 18.4 %collective-permute-start.16 = (f32[5,5,1,4,5,128]{5,4,3,2,1,0:T(8,128)S(1)}, f32[5,5,1,4,5,128]{5,4,3,2,1,0:T(8,128)S(1)}, u32[]{:S(2)}, u32[]{:S(2)}) collective-permute-start(f32[5,5,1,4,5,128]{5,4,3,2,1,0:T(8,128)S(1)} %get-tuple-element.326), channel_id=1, source_target_pairs={{0,1},{1,2},{2,3},{4,5},{5,6},{6,7},{8,9},{9,10},{10,11},{12,13},{... | collective-permute-start | bytes 768008 | tf_op jit(solution)/shard_map/ppermute | solution.py:21
  190.1 18.1 %collective-permute-start.17 = (f32[5,5,1,4,5,128]{5,4,3,2,1,0:T(8,128)S(1)}, f32[5,5,1,4,5,128]{5,4,3,2,1,0:T(8,128)S(1)}, u32[]{:S(2)}, u32[]{:S(2)}) collective-permute-start(f32[5,5,1,4,5,128]{5,4,3,2,1,0:T(8,128)S(1)} %get-tuple-element.327), channel_id=1, source_target_pairs={{1,0},{2,1},{3,2},{5,4},{6,5},{7,6},{9,8},{10,9},{11,10},{13,12},{... | collective-permute-start | bytes 768008 | tf_op jit(solution)/shard_map/ppermute | solution.py:24
  (20 other events, 90.1 us)

commit v2 on v1

--- a/solution.py
+++ b/solution.py
@@ -2,6 +2,8 @@
 import jax.numpy as jnp
 from jax import lax
 from jax.sharding import PartitionSpec as P
+from jax.experimental import pallas as pl
+from jax.experimental.pallas import tpu as pltpu
 
 SLOTS = 4
 
@@ -10,7 +12,6 @@
 TIME_STEP = 0.5
 COUPLING = 0.5
 PHASE_CHANGE_COST = 0.5
-GROUP_BLOCKS = 8
 
 
 def with_halo(block, sides, width):
@@ -89,6 +90,86 @@
     return beside - 6.0 * centre
 
 
+PAIR_LANES = 256
+DEPTH_ROWS = 136
+
+
+def split_bf16(value):
+    high = value.astype(jnp.bfloat16)
+    low = (value - high.astype(jnp.float32)).astype(jnp.bfloat16)
+    return high, low
+
+
+def three_pass(a, b, dims):
+    a_high, a_low = split_bf16(a)
+    b_high, b_low = split_bf16(b)
+    out = None
+    for x, y in ((a_high, b_high), (a_high, b_low), (a_low, b_high)):
+        part = lax.dot_general(x, y, (dims, ((), ())), preferred_element_type=jnp.float32)
+        out = part if out is None else out + part
+    return out
+
+
+def coupling_kernel(
+    live_ref, table_ref, parcel_ref, pair_ref, pair_share_ref, depth_ref, depth_share_ref,
+    factor_ref, updated_ref, deposit_ref,
+):
+    fields = parcel_ref.shape[1]
+    blocks = parcel_ref.shape[0]
+    lanes = parcel_ref.shape[2]
+    deposit_ref[...] = jnp.zeros(deposit_ref.shape, jnp.float32)
+    live = live_ref[0]
+    pair_iota = lax.broadcasted_iota(jnp.int32, (PAIR_LANES, lanes), 0)
+    depth_iota = lax.broadcasted_iota(jnp.int32, (DEPTH_ROWS, lanes), 0)
+
+    def body(b, carry):
+        pair = pair_ref[b]
+        pair_share = pair_share_ref[b]
+        weights = jnp.zeros((PAIR_LANES, lanes), jnp.float32)
+        for c in range(4):
+            weights = weights + jnp.where(pair_iota == pair[c:c + 1], pair_share[c:c + 1], 0.0)
+        depth = depth_ref[b]
+        depth_share = depth_share_ref[b]
+        depth_weights = jnp.where(depth_iota == depth[0:1], depth_share[0:1], 0.0)
+        depth_weights = depth_weights + jnp.where(
+            depth_iota == depth[1:2], depth_share[1:2], 0.0
+        )
+        mixed = three_pass(table_ref[...], weights, ((1,), (0,)))
+        sample = [
+            jnp.sum(
+                mixed[f * DEPTH_ROWS:(f + 1) * DEPTH_ROWS] * depth_weights, axis=0, keepdims=True
+            )
+            for f in range(fields)
+        ]
+        current = parcel_ref[b]
+        factors = factor_ref[b]
+        mass = current[0:1]
+        heat = current[1:2]
+        keep_velocity = factors[0:1]
+        residual_heat = factors[1:2]
+        equilibrium = factors[2:3]
+        x = 4.0 * (equilibrium - sample[0])
+        soft = jnp.maximum(x, 0.0) + jnp.log1p(jnp.exp(-jnp.abs(x)))
+        share = 1.0 - jnp.exp(-0.3 * soft)
+        evaporated = mass * share
+        ambient = sample[1]
+        adjusted = ambient + (heat - ambient) * residual_heat - PHASE_CHANGE_COST * share
+        velocity = [
+            sample[2 + d] + (current[2 + d:3 + d] - sample[2 + d]) * keep_velocity
+            for d in range(3)
+        ]
+        enthalpy = 0.5 * mass * (heat - adjusted)
+        push = [mass * (current[2 + d:3 + d] - velocity[d]) for d in range(3)]
+        updated_ref[b] = jnp.concatenate([mass - evaporated, adjusted] + velocity, axis=0)
+        alive = b < live
+        sources = [jnp.where(alive, s, 0.0) for s in [evaporated, enthalpy] + push]
+        spread = jnp.concatenate([s * depth_weights for s in sources], axis=0)
+        deposit_ref[...] += three_pass(spread, weights, ((1,), (1,)))
+        return carry
+
+    lax.fori_loop(0, blocks, body, 0)
+
+
 def local(gas_state, parcels, parcel_cells, offsets, destination, live_blocks):
     fields, size_x, size_y, size_z = gas_state.shape
     blocks, parcel_fields, block_parcels = parcels.shape
@@ -98,70 +179,52 @@
     span_z = size_z + 2
     pair_count = span_x * span_y
     plane_size = span_y * span_z
-    table = jnp.transpose(padded.reshape(fields, pair_count, span_z), (1, 0, 2)).reshape(
-        pair_count, fields * span_z
-    )
+    table = jnp.transpose(padded, (0, 3, 1, 2)).reshape(fields, span_z, pair_count)
+    table = jnp.pad(table, ((0, 0), (0, DEPTH_ROWS - span_z), (0, PAIR_LANES - pair_count)))
+    table = table.reshape(fields * DEPTH_ROWS, PAIR_LANES)
     alive_mask = jnp.arange(blocks, dtype=jnp.int32) < live_blocks[0]
-    turns = blocks // GROUP_BLOCKS
-    rows = GROUP_BLOCKS * block_parcels
-    pair_iota = jnp.arange(pair_count, dtype=jnp.int32)
-    depth_iota = jnp.arange(span_z, dtype=jnp.int32)
-
-    def group_step(total, item):
-        group_parcels, group_cells, group_offsets, group_alive = item
-        cells = group_cells.reshape(rows)
-        shifts = jnp.transpose(group_offsets, (1, 0, 2)).reshape(3, rows)
-        cell_x = cells // plane_size
-        cell_y = cells // span_z % span_y
-        cell_z = cells % span_z
-        step_sign = jnp.where(shifts >= 0.0, 1, -1).astype(jnp.int32)
-        far_share = jnp.abs(shifts)
-        near_share = 1.0 - far_share
-        pair_weights = jnp.zeros((rows, pair_count), jnp.float32)
-        for bit_x in range(2):
-            for bit_y in range(2):
-                share = (far_share[0] if bit_x else near_share[0]) * (
-                    far_share[1] if bit_y else near_share[1]
-                )
-                target = (cell_x + bit_x * step_sign[0]) * span_y + cell_y + bit_y * step_sign[1]
-                pair_weights = pair_weights + jnp.where(
-                    pair_iota[None, :] == target[:, None], share[:, None], 0.0
-                )
-        depth_weights = jnp.where(
-            depth_iota[None, :] == cell_z[:, None], near_share[2][:, None], 0.0
-        )
-        depth_weights = depth_weights + jnp.where(
-            depth_iota[None, :] == (cell_z + step_sign[2])[:, None], far_share[2][:, None], 0.0
-        )
-        mixed = jnp.dot(pair_weights, table, precision=lax.Precision.HIGHEST).reshape(
-            rows, fields, span_z
-        )
-        sample = jnp.sum(mixed * depth_weights[:, None, :], axis=2)
-        sample_blocks = jnp.transpose(
-            sample.reshape(GROUP_BLOCKS, block_parcels, fields), (0, 2, 1)
-        )
-        updated, sources = parcel_update(group_parcels, sample_blocks)
-        sources = jnp.where(group_alive[:, None, None], sources, 0.0)
-        source_rows = jnp.transpose(sources, (0, 2, 1)).reshape(rows, fields)
-        spread = (source_rows[:, :, None] * depth_weights[:, None, :]).reshape(
-            rows, fields * span_z
-        )
-        total = total + lax.dot_general(
-            pair_weights, spread, (((0,), (0,)), ((), ())), precision=lax.Precision.HIGHEST
-        )
-        return (total, updated)
-
-    inputs = (
-        parcels.reshape(turns, GROUP_BLOCKS, parcel_fields, block_parcels),
-        parcel_cells.reshape(turns, GROUP_BLOCKS, block_parcels),
-        offsets.reshape(turns, GROUP_BLOCKS, 3, block_parcels),
-        alive_mask.reshape(turns, GROUP_BLOCKS),
-    )
-    deposit_rows, updated = lax.scan(
-        group_step, jnp.zeros((pair_count, fields * span_z), jnp.float32), inputs
-    )
-    updated = updated.reshape(blocks, parcel_fields, block_parcels)
-    deposit = jnp.transpose(deposit_rows.reshape(span_x, span_y, fields, span_z), (2, 0, 1, 3))
+    cell_x = parcel_cells // plane_size
+    cell_y = parcel_cells // span_z % span_y
+    cell_z = parcel_cells % span_z
+    step_sign = jnp.where(offsets >= 0.0, 1, -1).astype(jnp.int32)
+    far_share = jnp.abs(offsets)
+    near_share = 1.0 - far_share
+    pairs = []
+    pair_shares = []
+    for bit_x in range(2):
+        for bit_y in range(2):
+            pair_shares.append(
+                (far_share[:, 0] if bit_x else near_share[:, 0])
+                * (far_share[:, 1] if bit_y else near_share[:, 1])
+            )
+            pairs.append(
+                (cell_x + bit_x * step_sign[:, 0]) * span_y + cell_y + bit_y * step_sign[:, 1]
+            )
+    pairs = jnp.stack(pairs, axis=1)
+    pair_shares = jnp.stack(pair_shares, axis=1)
+    depths = jnp.stack([cell_z, cell_z + step_sign[:, 2]], axis=1)
+    depth_shares = jnp.stack([near_share[:, 2], far_share[:, 2]], axis=1)
+    relax_time = 0.4 * parcels[:, 0] ** (2.0 / 3.0)
+    factors = jnp.stack(
+        [
+            jnp.exp(-TIME_STEP / relax_time),
+            jnp.exp(-TIME_STEP / (1.5 * relax_time)),
+            0.4 * jnp.exp(2.0 * (parcels[:, 1] - 1.0)),
+        ],
+        axis=1,
+    )
+    vmem = pl.BlockSpec(memory_space=pltpu.VMEM)
+    updated, deposit_rows = pl.pallas_call(
+        coupling_kernel,
+        out_shape=(
+            jax.ShapeDtypeStruct(parcels.shape, jnp.float32),
+            jax.ShapeDtypeStruct((fields * DEPTH_ROWS, PAIR_LANES), jnp.float32),
+        ),
+        in_specs=[pl.BlockSpec(memory_space=pltpu.SMEM)] + [vmem] * 7,
+        out_specs=(vmem, vmem),
+    )(live_blocks, table, parcels, pairs, pair_shares, depths, depth_shares, factors)
+    deposit = deposit_rows.reshape(fields, DEPTH_ROWS, PAIR_LANES)[:, :span_z, :pair_count]
+    deposit = jnp.transpose(deposit.reshape(fields, span_z, span_x, span_y), (0, 2, 3, 1))
     cell_sources = fold_ghosts(deposit, (("gx", 1), ("gy", 2), ("gz", 3)))
     kappa = jnp.array(DIFFUSION, jnp.float32)[:, None, None, None]
     gas_next = gas_state + kappa * laplacian(padded) + COUPLING * cell_sources

time: 212 us -> 175 us (0.83)
  matrix products: 66.5 us -> 1.17 us
  Pallas kernels: 0 us -> 43.4 us
  local copies, waits for them, and re-layouts: 32.8 us -> 20.5 us
  other arithmetic: 21.1 us -> 12.8 us
  waiting for transfers between devices: 25.5 us -> 29.2 us
  starting transfers between devices: 61.1 us -> 64.8 us
    dot_general x8 -> x0, matrix products: 66.3 us -> none  [the longest x4 36.3 us: group_step(): lax.dot_general(pair_weights, spread, (((0,), (0,)), ((), ())), precision...]
    pallas_call x0 -> x1, Pallas kernels: none -> 43.4 us  [local(): pl.pallas_call(coupling_kernel, out_shape=(jax.ShapeDtypeStruct(parcels.s...]
    reshape x6 -> x2, local copies, waits for them, and re-layouts: 11.1 us -> 2.39 us  [the longest x1 1.3 us: local(): deposit.reshape(fields, span_z, span_x, span_y)]
    ppermute x3, starting transfers between devices: 8.88 us -> 16.4 us  [fold_ghosts(): lax.ppermute(lax.slice_in_dim(block, span - 1, span, axis=dim), axis, for...]
    mul x4 -> x0, local copies, waits for them, and re-layouts: 7.14 us -> none  [group_step(): source_rows[:, :, None] * depth_weights[:, None, :]]
    ppermute x6, waiting for transfers between devices: 10.7 us -> 17.7 us  [with_halo(): lax.ppermute(lax.slice_in_dim(block, 0, width, axis=dim), axis, backward)]
    add x12 -> x1, other arithmetic: 6.25 us -> 0.77 us  [local(): depths = jnp.stack([cell_z, cell_z + step_sign[:, 2]], axis=1)]
    ppermute x6, starting transfers between devices: 15.6 us -> 12.5 us  [with_halo(): lax.ppermute(lax.slice_in_dim(block, 0, width, axis=dim), axis, backward)]
  transfers between devices with their start and end apart: 18 -> 18, of which waited for: 9 -> 10; matrix products, arithmetic and copies ran while one was open for 6% -> 12% of each run, Pallas kernels for 0% -> 0%
where the time goes in v2:
time: 175 us; the launch traced here: 173 us
  starting transfers between devices  64.8 us (37%)
  Pallas kernels  43.4 us (25%)
  waiting for transfers between devices  29.2 us (17%)
  local copies, waits for them, and re-layouts  20.5 us (12%)
  other arithmetic  12.8 us (7%)
    pallas_call x1, Pallas kernels, local(): pl.pallas_call(coupling_kernel, out_shape=(jax.ShapeDtypeStruct(parcels.s...  43.4 us
    ppermute x6, starting transfers between devices, with_halo(): lax.ppermute(lax.slice_in_dim(block, block.shape[dim] - width, None, axis...  29.8 us
    ppermute x6, waiting for transfers between devices, with_halo(): lax.ppermute(lax.slice_in_dim(block, 0, width, axis=dim), axis, backward)  17.7 us
    ppermute x3, starting transfers between devices, fold_ghosts(): lax.ppermute(lax.slice_in_dim(block, span - 1, span, axis=dim), axis, for...  16.4 us
    ppermute x6, starting transfers between devices, with_halo(): lax.ppermute(lax.slice_in_dim(block, 0, width, axis=dim), axis, backward)  12.5 us
    unnamed x31, local copies, waits for them, and re-layouts  8.08 us
    ppermute x6, waiting for transfers between devices, with_halo(): lax.ppermute(lax.slice_in_dim(block, block.shape[dim] - width, None, axis...  7.46 us
    ppermute x3, starting transfers between devices, fold_ghosts(): lax.ppermute(lax.slice_in_dim(block, 0, 1, axis=dim), axis, backward)  6.01 us
  transfers between devices with their start and end apart: 18, of which 10 were waited for; matrix products, arithmetic and copies ran while one was open for 12% of the time, Pallas kernels for 0%

profile of v2, /device:TPU:58, one launch (start us, length us, event | category | flops | bytes accessed | tf_op | source)
XLA Modules:
  0.0 173.5 jit_solution(5436416206605825177)
XLA Ops:
  1.5 7.8 %collective-permute-start.1 = (f32[5,1,16,128]{3,2,1,0:T(8,128)S(1)}, f32[5,1,16,128]{3,2,1,0:T(8,128)S(1)}, u32[]{:S(2)}, u32[]{:S(2)}) collective-permute-start(f32[5,1,16,128]{3,2,1,0:T(8,128)S(1)} %get-tuple-element.34), channel_id=1, source_target_pairs={{0,32},{32,64},{64,96},{96,128},{128,160},{160,192},{192,224},{1,3... | collective-permute-start | bytes 122888 | tf_op jit(solution)/shard_map/ppermute | solution.py:22
  9.3 1.9 %collective-permute-start = (f32[5,1,16,128]{3,2,1,0:T(8,128)S(1)}, f32[5,1,16,128]{3,2,1,0:T(8,128)S(1)}, u32[]{:S(2)}, u32[]{:S(2)}) collective-permute-start(f32[5,1,16,128]{3,2,1,0:T(8,128)S(1)} %get-tuple-element.33), channel_id=1, source_target_pairs={{32,0},{64,32},{96,64},{128,96},{160,128},{192,160},{224,192},{33,... | collective-permute-start | bytes 122888 | tf_op jit(solution)/shard_map/ppermute | solution.py:25
  19.8 1.5 collective-permute-done
  21.3 1.9 %collective-permute-start.2 = (f32[5,10,1,128]{3,2,1,0:T(1,128)S(1)}, f32[5,10,1,128]{3,2,1,0:T(1,128)S(1)}, u32[]{:S(2)}, u32[]{:S(2)}) collective-permute-start(f32[5,10,1,128]{3,2,1,0:T(1,128)S(1)} %get-tuple-element.32), channel_id=1, source_target_pairs={{4,0},{8,4},{12,8},{16,12},{20,16},{24,20},{28,24},{5,1},{9,5},{13... | collective-permute-start | bytes 76808 | tf_op jit(solution)/shard_map/ppermute | solution.py:25
  23.2 2.4 %collective-permute-start.3 = (f32[5,10,1,128]{3,2,1,0:T(1,128)S(1)}, f32[5,10,1,128]{3,2,1,0:T(1,128)S(1)}, u32[]{:S(2)}, u32[]{:S(2)}) collective-permute-start(f32[5,10,1,128]{3,2,1,0:T(1,128)S(1)} %get-tuple-element.31), channel_id=1, source_target_pairs={{0,4},{4,8},{8,12},{12,16},{16,20},{20,24},{24,28},{1,5},{5,9},{9,... | collective-permute-start | bytes 76808 | tf_op jit(solution)/shard_map/ppermute | solution.py:22
  26.3 2.1 %collective-permute-done.3 = f32[5,10,1,128]{3,2,1,0:T(1,128)S(1)} collective-permute-done((f32[5,10,1,128]{3,2,1,0:T(1,128)S(1)}, f32[5,10,1,128]{3,2,1,0:T(1,128)S(1)}, u32[]{:S(2)}, u32[]{:S(2)}) %collective-permute-start.3) | collective-permute-done | bytes 25632 | tf_op jit(solution)/shard_map/ppermute | solution.py:22
  29.1 2.9 %collective-permute-start.4 = (f32[5,10,18,1]{2,3,1,0:T(1,128)S(1)}, f32[5,10,18,1]{2,3,1,0:T(1,128)S(1)}, u32[]{:S(2)}, u32[]{:S(2)}) collective-permute-start(f32[5,10,18,1]{2,3,1,0:T(1,128)S(1)} %copy.55), channel_id=1, source_target_pairs={{1,0},{2,1},{3,2},{5,4},{6,5},{7,6},{9,8},{10,9},{11,10},{13,12},{... | collective-permute-start | bytes 10808 | tf_op jit(solution)/shard_map/ppermute | solution.py:25
  32.4 2.9 %collective-permute-start.5 = (f32[5,10,18,1]{2,3,1,0:T(1,128)S(1)}, f32[5,10,18,1]{2,3,1,0:T(1,128)S(1)}, u32[]{:S(2)}, u32[]{:S(2)}) collective-permute-start(f32[5,10,18,1]{2,3,1,0:T(1,128)S(1)} %copy.57), channel_id=1, source_target_pairs={{0,1},{1,2},{2,3},{4,5},{5,6},{6,7},{8,9},{9,10},{10,11},{12,13},{... | collective-permute-start | bytes 10808 | tf_op jit(solution)/shard_map/ppermute | solution.py:22
  40.4 1.6 copy.75
  42.9 43.4 %shard_map.94 = (f32[32,5,128]{2,1,0:T(8,128)}, f32[680,256]{1,0:T(8,128)}) custom-call(s32[1]{0:T(128)} %copy.88.live_ref, f32[680,256]{1,0:T(8,128)} %bitcast.59, f32[32,5,128]{2,1,0:T(8,128)} %copy.69.parcel_ref, s32[32,4,128]{2,1,0:T(4,128)} %copy.70.pair_ref, f32[32,4,128]{2,1,0:T(4,128)} %pad_maximum_fusion.15.pair_share_ref, ...), custom_call_target="tpu_custom_call" | custom-call | tf_op jit(solution)/shard_map/pallas_call | solution.py:217
  86.3 2.4 %copy.74 = f32[5,130,180]{1,2,0:T(8,128)} copy(f32[5,130,180]{2,1,0:T(8,128)} %bitcast.61) | data formatting | bytes 936000
  90.1 1.9 %collective-permute-start.7 = (f32[5,1,18,130]{3,2,1,0:T(8,128)S(1)}, f32[5,1,18,130]{3,2,1,0:T(8,128)S(1)}, u32[]{:S(2)}, u32[]{:S(2)}) collective-permute-start(f32[5,1,18,130]{3,2,1,0:T(8,128)S(1)} %get-tuple-element.22), channel_id=1, source_target_pairs={{32,0},{64,32},{96,64},{128,96},{160,128},{192,160},{224,192},{33,... | collective-permute-start | bytes 140408 | tf_op jit(solution)/shard_map/ppermute | solution.py:37
  92.0 9.9 %collective-permute-start.6 = (f32[5,1,18,130]{3,2,1,0:T(8,128)S(1)}, f32[5,1,18,130]{3,2,1,0:T(8,128)S(1)}, u32[]{:S(2)}, u32[]{:S(2)}) collective-permute-start(f32[5,1,18,130]{3,2,1,0:T(8,128)S(1)} %get-tuple-element.21), channel_id=1, source_target_pairs={{0,32},{32,64},{64,96},{96,128},{128,160},{160,192},{192,224},{1,3... | collective-permute-start | bytes 140408 | tf_op jit(solution)/shard_map/ppermute | solution.py:36
  104.2 1.4 collective-permute-done.6
  107.4 2.0 %collective-permute-start.9 = (f32[5,8,1,130]{3,2,1,0:T(1,128)}, f32[5,8,1,130]{3,2,1,0:T(1,128)}, u32[]{:S(2)}, u32[]{:S(2)}) collective-permute-start(f32[5,8,1,130]{3,2,1,0:T(1,128)} %get-tuple-element.24), channel_id=1, source_target_pairs={{4,0},{8,4},{12,8},{16,12},{20,16},{24,20},{28,24},{5,1},{9,5},{13... | collective-permute-start | bytes 62408 | tf_op jit(solution)/shard_map/ppermute | solution.py:37
  109.5 2.4 %collective-permute-start.8 = (f32[5,8,1,130]{3,2,1,0:T(1,128)}, f32[5,8,1,130]{3,2,1,0:T(1,128)}, u32[]{:S(2)}, u32[]{:S(2)}) collective-permute-start(f32[5,8,1,130]{3,2,1,0:T(1,128)} %get-tuple-element.23), channel_id=1, source_target_pairs={{0,4},{4,8},{8,12},{12,16},{16,20},{20,24},{24,28},{1,5},{5,9},{9,... | collective-permute-start | bytes 62408 | tf_op jit(solution)/shard_map/ppermute | solution.py:36
  113.4 1.6 slice.172
  115.0 10.4 %collective-permute-start.12 = (f32[1,3,3,4,5,128]{5,4,3,2,1,0:T(8,128)}, f32[1,3,3,4,5,128]{5,4,3,2,1,0:T(8,128)}, u32[]{:S(2)}, u32[]{:S(2)}) collective-permute-start(f32[1,3,3,4,5,128]{5,4,3,2,1,0:T(8,128)} %slice.172), channel_id=1, source_target_pairs={{0,32},{32,64},{64,96},{96,128},{128,160},{160,192},{192,224},{1,3... | collective-permute-start | bytes 276488 | tf_op jit(solution)/shard_map/ppermute | solution.py:22
  125.4 1.6 slice.174
  127.0 1.9 %collective-permute-start.13 = (f32[1,3,3,4,5,128]{5,4,3,2,1,0:T(8,128)}, f32[1,3,3,4,5,128]{5,4,3,2,1,0:T(8,128)S(1)}, u32[]{:S(2)}, u32[]{:S(2)}) collective-permute-start(f32[1,3,3,4,5,128]{5,4,3,2,1,0:T(8,128)} %slice.174), channel_id=1, source_target_pairs={{32,0},{64,32},{96,64},{128,96},{160,128},{192,160},{224,192},{33,... | collective-permute-start | bytes 276488 | tf_op jit(solution)/shard_map/ppermute | solution.py:25
  129.9 2.9 %collective-permute-done.12 = f32[1,3,3,4,5,128]{5,4,3,2,1,0:T(8,128)} collective-permute-done((f32[1,3,3,4,5,128]{5,4,3,2,1,0:T(8,128)}, f32[1,3,3,4,5,128]{5,4,3,2,1,0:T(8,128)}, u32[]{:S(2)}, u32[]{:S(2)}) %collective-permute-start.12) | collective-permute-done | bytes 92192 | tf_op jit(solution)/shard_map/ppermute | solution.py:22
  133.8 10.9 %collective-permute-done.13 = f32[1,3,3,4,5,128]{5,4,3,2,1,0:T(8,128)S(1)} collective-permute-done((f32[1,3,3,4,5,128]{5,4,3,2,1,0:T(8,128)}, f32[1,3,3,4,5,128]{5,4,3,2,1,0:T(8,128)S(1)}, u32[]{:S(2)}, u32[]{:S(2)}) %collective-permute-start.13) | collective-permute-done | bytes 92192 | tf_op jit(solution)/shard_map/ppermute | solution.py:25
  144.7 1.9 %collective-permute-start.15 = (f32[5,1,3,4,5,128]{5,4,3,2,1,0:T(8,128)S(1)}, f32[5,1,3,4,5,128]{5,4,3,2,1,0:T(8,128)S(1)}, u32[]{:S(2)}, u32[]{:S(2)}) collective-permute-start(f32[5,1,3,4,5,128]{5,4,3,2,1,0:T(8,128)S(1)} %get-tuple-element.26), channel_id=1, source_target_pairs={{4,0},{8,4},{12,8},{16,12},{20,16},{24,20},{28,24},{5,1},{9,5},{13... | collective-permute-start | bytes 460808 | tf_op jit(solution)/shard_map/ppermute | solution.py:25
  146.6 2.4 %collective-permute-start.14 = (f32[5,1,3,4,5,128]{5,4,3,2,1,0:T(8,128)S(1)}, f32[5,1,3,4,5,128]{5,4,3,2,1,0:T(8,128)S(1)}, u32[]{:S(2)}, u32[]{:S(2)}) collective-permute-start(f32[5,1,3,4,5,128]{5,4,3,2,1,0:T(8,128)S(1)} %get-tuple-element.25), channel_id=1, source_target_pairs={{0,4},{4,8},{8,12},{12,16},{16,20},{20,24},{24,28},{1,5},{5,9},{9,... | collective-permute-start | bytes 460808 | tf_op jit(solution)/shard_map/ppermute | solution.py:22
  149.2 2.1 %collective-permute-start.11 = (f32[5,8,16,1]{3,2,1,0:T(8,128)S(1)}, f32[5,8,16,1]{3,2,1,0:T(8,128)S(1)}, u32[]{:S(2)}, u32[]{:S(2)}) collective-permute-start(f32[5,8,16,1]{3,2,1,0:T(8,128)S(1)} %get-tuple-element.28), channel_id=1, source_target_pairs={{1,0},{2,1},{3,2},{5,4},{6,5},{7,6},{9,8},{10,9},{11,10},{13,12},{... | collective-permute-start | bytes 7688 | tf_op jit(solution)/shard_map/ppermute | solution.py:37
  151.3 4.1 %collective-permute-start.10 = (f32[5,8,16,1]{3,2,1,0:T(8,128)S(1)}, f32[5,8,16,1]{3,2,1,0:T(8,128)S(1)}, u32[]{:S(2)}, u32[]{:S(2)}) collective-permute-start(f32[5,8,16,1]{3,2,1,0:T(8,128)S(1)} %get-tuple-element.27), channel_id=1, source_target_pairs={{0,1},{1,2},{2,3},{4,5},{5,6},{6,7},{8,9},{9,10},{10,11},{12,13},{... | collective-permute-start | bytes 7688 | tf_op jit(solution)/shard_map/ppermute | solution.py:36
  155.5 1.9 %collective-permute-start.17 = (f32[5,5,1,4,5,128]{5,4,3,2,1,0:T(8,128)S(1)}, f32[5,5,1,4,5,128]{5,4,3,2,1,0:T(8,128)S(1)}, u32[]{:S(2)}, u32[]{:S(2)}) collective-permute-start(f32[5,5,1,4,5,128]{5,4,3,2,1,0:T(8,128)S(1)} %get-tuple-element.20), channel_id=1, source_target_pairs={{1,0},{2,1},{3,2},{5,4},{6,5},{7,6},{9,8},{10,9},{11,10},{13,12},{... | collective-permute-start | bytes 768008 | tf_op jit(solution)/shard_map/ppermute | solution.py:25
  157.4 3.9 %collective-permute-start.16 = (f32[5,5,1,4,5,128]{5,4,3,2,1,0:T(8,128)S(1)}, f32[5,5,1,4,5,128]{5,4,3,2,1,0:T(8,128)S(1)}, u32[]{:S(2)}, u32[]{:S(2)}) collective-permute-start(f32[5,5,1,4,5,128]{5,4,3,2,1,0:T(8,128)S(1)} %get-tuple-element.19), channel_id=1, source_target_pairs={{0,1},{1,2},{2,3},{4,5},{5,6},{6,7},{8,9},{9,10},{10,11},{12,13},{... | collective-permute-start | bytes 768008 | tf_op jit(solution)/shard_map/ppermute | solution.py:22
  162.1 1.5 collective-permute-done.10
  163.6 1.4 fusion.4
  165.0 5.3 %collective-permute-done.17 = f32[5,5,1,4,5,128]{5,4,3,2,1,0:T(8,128)S(1)} collective-permute-done((f32[5,5,1,4,5,128]{5,4,3,2,1,0:T(8,128)S(1)}, f32[5,5,1,4,5,128]{5,4,3,2,1,0:T(8,128)S(1)}, u32[]{:S(2)}, u32[]{:S(2)}) %collective-permute-start.17) | collective-permute-done | bytes 256032 | tf_op jit(solution)/shard_map/ppermute | solution.py:25
  170.3 2.1 %collective-permute-done.16 = f32[5,5,1,4,5,128]{5,4,3,2,1,0:T(8,128)S(1)} collective-permute-done((f32[5,5,1,4,5,128]{5,4,3,2,1,0:T(8,128)S(1)}, f32[5,5,1,4,5,128]{5,4,3,2,1,0:T(8,128)S(1)}, u32[]{:S(2)}, u32[]{:S(2)}) %collective-permute-start.16) | collective-permute-done | bytes 256032 | tf_op jit(solution)/shard_map/ppermute | solution.py:22
  (85 shorter events, 27.4 us)
Async XLA Ops:
  0.6 19.1 %copy-start.3 = (f32[5,8,16,128]{3,2,1,0:T(8,128)S(1)}, f32[5,8,16,128]{3,2,1,0:T(8,128)}, u32[]{:S(2)}) copy-start(f32[5,8,16,128]{3,2,1,0:T(8,128)} %param.7) | copy-start | bytes 983044
  1.5 18.2 %collective-permute-start.1 = (f32[5,1,16,128]{3,2,1,0:T(8,128)S(1)}, f32[5,1,16,128]{3,2,1,0:T(8,128)S(1)}, u32[]{:S(2)}, u32[]{:S(2)}) collective-permute-start(f32[5,1,16,128]{3,2,1,0:T(8,128)S(1)} %get-tuple-element.34), channel_id=1, source_target_pairs={{0,32},{32,64},{64,96},{96,128},{128,160},{160,192},{192,224},{1,3... | collective-permute-start | bytes 122888 | tf_op jit(solution)/shard_map/ppermute | solution.py:22
  9.3 11.9 %collective-permute-start = (f32[5,1,16,128]{3,2,1,0:T(8,128)S(1)}, f32[5,1,16,128]{3,2,1,0:T(8,128)S(1)}, u32[]{:S(2)}, u32[]{:S(2)}) collective-permute-start(f32[5,1,16,128]{3,2,1,0:T(8,128)S(1)} %get-tuple-element.33), channel_id=1, source_target_pairs={{32,0},{64,32},{96,64},{128,96},{160,128},{192,160},{224,192},{33,... | collective-permute-start | bytes 122888 | tf_op jit(solution)/shard_map/ppermute | solution.py:25
  19.7 8.7 %copy-start.5 = (f32[5,1,16,128]{3,2,1,0:T(8,128)}, f32[5,1,16,128]{3,2,1,0:T(8,128)S(1)}, u32[]{:S(2)}) copy-start(f32[5,1,16,128]{3,2,1,0:T(8,128)S(1)} %collective-permute-done.1) | copy-start | bytes 122884
  21.3 7.1 %copy-start.7 = (f32[5,1,16,128]{3,2,1,0:T(8,128)}, f32[5,1,16,128]{3,2,1,0:T(8,128)S(1)}, u32[]{:S(2)}) copy-start(f32[5,1,16,128]{3,2,1,0:T(8,128)S(1)} %collective-permute-done) | copy-start | bytes 122884
  21.3 5.0 %collective-permute-start.2 = (f32[5,10,1,128]{3,2,1,0:T(1,128)S(1)}, f32[5,10,1,128]{3,2,1,0:T(1,128)S(1)}, u32[]{:S(2)}, u32[]{:S(2)}) collective-permute-start(f32[5,10,1,128]{3,2,1,0:T(1,128)S(1)} %get-tuple-element.32), channel_id=1, source_target_pairs={{4,0},{8,4},{12,8},{16,12},{20,16},{24,20},{28,24},{5,1},{9,5},{13... | collective-permute-start | bytes 76808 | tf_op jit(solution)/shard_map/ppermute | solution.py:25
  23.2 5.2 %collective-permute-start.3 = (f32[5,10,1,128]{3,2,1,0:T(1,128)S(1)}, f32[5,10,1,128]{3,2,1,0:T(1,128)S(1)}, u32[]{:S(2)}, u32[]{:S(2)}) collective-permute-start(f32[5,10,1,128]{3,2,1,0:T(1,128)S(1)} %get-tuple-element.31), channel_id=1, source_target_pairs={{0,4},{4,8},{8,12},{12,16},{16,20},{20,24},{24,28},{1,5},{5,9},{9,... | collective-permute-start | bytes 76808 | tf_op jit(solution)/shard_map/ppermute | solution.py:22
  28.7 7.3 %copy-start.9 = (f32[32,5,128]{2,0,1:T(8,128)S(1)}, f32[32,5,128]{2,0,1:T(8,128)}, u32[]{:S(2)}) copy-start(f32[32,5,128]{2,0,1:T(8,128)} %param.8) | copy-start | bytes 245764
  29.1 8.3 %collective-permute-start.4 = (f32[5,10,18,1]{2,3,1,0:T(1,128)S(1)}, f32[5,10,18,1]{2,3,1,0:T(1,128)S(1)}, u32[]{:S(2)}, u32[]{:S(2)}) collective-permute-start(f32[5,10,18,1]{2,3,1,0:T(1,128)S(1)} %copy.55), channel_id=1, source_target_pairs={{1,0},{2,1},{3,2},{5,4},{6,5},{7,6},{9,8},{10,9},{11,10},{13,12},{... | collective-permute-start | bytes 10808 | tf_op jit(solution)/shard_map/ppermute | solution.py:25
  32.4 5.7 %collective-permute-start.5 = (f32[5,10,18,1]{2,3,1,0:T(1,128)S(1)}, f32[5,10,18,1]{2,3,1,0:T(1,128)S(1)}, u32[]{:S(2)}, u32[]{:S(2)}) collective-permute-start(f32[5,10,18,1]{2,3,1,0:T(1,128)S(1)} %copy.57), channel_id=1, source_target_pairs={{0,1},{1,2},{2,3},{4,5},{5,6},{6,7},{8,9},{9,10},{10,11},{12,13},{... | collective-permute-start | bytes 10808 | tf_op jit(solution)/shard_map/ppermute | solution.py:22
  90.1 14.2 %collective-permute-start.7 = (f32[5,1,18,130]{3,2,1,0:T(8,128)S(1)}, f32[5,1,18,130]{3,2,1,0:T(8,128)S(1)}, u32[]{:S(2)}, u32[]{:S(2)}) collective-permute-start(f32[5,1,18,130]{3,2,1,0:T(8,128)S(1)} %get-tuple-element.22), channel_id=1, source_target_pairs={{32,0},{64,32},{96,64},{128,96},{160,128},{192,160},{224,192},{33,... | collective-permute-start | bytes 140408 | tf_op jit(solution)/shard_map/ppermute | solution.py:37
  92.0 13.7 %collective-permute-start.6 = (f32[5,1,18,130]{3,2,1,0:T(8,128)S(1)}, f32[5,1,18,130]{3,2,1,0:T(8,128)S(1)}, u32[]{:S(2)}, u32[]{:S(2)}) collective-permute-start(f32[5,1,18,130]{3,2,1,0:T(8,128)S(1)} %get-tuple-element.21), channel_id=1, source_target_pairs={{0,32},{32,64},{64,96},{96,128},{128,160},{160,192},{192,224},{1,3... | collective-permute-start | bytes 140408 | tf_op jit(solution)/shard_map/ppermute | solution.py:36
  105.8 1.0 copy-start
  107.4 21.5 %copy-start.1 = (f32[5,8,18,130]{3,2,1,0:T(8,128)S(1)}, f32[5,8,18,130]{3,2,1,0:T(8,128)}, u32[]{:S(2)}) copy-start(f32[5,8,18,130]{3,2,1,0:T(8,128)} %copy-done) | copy-start | bytes 1123204
  107.4 21.5 %collective-permute-start.9 = (f32[5,8,1,130]{3,2,1,0:T(1,128)}, f32[5,8,1,130]{3,2,1,0:T(1,128)}, u32[]{:S(2)}, u32[]{:S(2)}) collective-permute-start(f32[5,8,1,130]{3,2,1,0:T(1,128)} %get-tuple-element.24), channel_id=1, source_target_pairs={{4,0},{8,4},{12,8},{16,12},{20,16},{24,20},{28,24},{5,1},{9,5},{13... | collective-permute-start | bytes 62408 | tf_op jit(solution)/shard_map/ppermute | solution.py:37
  109.5 19.4 %collective-permute-start.8 = (f32[5,8,1,130]{3,2,1,0:T(1,128)}, f32[5,8,1,130]{3,2,1,0:T(1,128)}, u32[]{:S(2)}, u32[]{:S(2)}) collective-permute-start(f32[5,8,1,130]{3,2,1,0:T(1,128)} %get-tuple-element.23), channel_id=1, source_target_pairs={{0,4},{4,8},{8,12},{12,16},{16,20},{20,24},{24,28},{1,5},{5,9},{9,... | collective-permute-start | bytes 62408 | tf_op jit(solution)/shard_map/ppermute | solution.py:36
  113.4 20.3 %copy-start.2 = (f32[3,3,3,4,5,128]{5,4,3,2,1,0:T(8,128)S(1)}, f32[3,3,3,4,5,128]{5,4,3,2,1,0:T(8,128)}, u32[]{:S(2)}) copy-start(f32[3,3,3,4,5,128]{5,4,3,2,1,0:T(8,128)} %reshape.39) | copy-start | bytes 829444
  115.0 17.7 %collective-permute-start.12 = (f32[1,3,3,4,5,128]{5,4,3,2,1,0:T(8,128)}, f32[1,3,3,4,5,128]{5,4,3,2,1,0:T(8,128)}, u32[]{:S(2)}, u32[]{:S(2)}) collective-permute-start(f32[1,3,3,4,5,128]{5,4,3,2,1,0:T(8,128)} %slice.172), channel_id=1, source_target_pairs={{0,32},{32,64},{64,96},{96,128},{128,160},{160,192},{192,224},{1,3... | collective-permute-start | bytes 276488 | tf_op jit(solution)/shard_map/ppermute | solution.py:22
  127.0 17.6 %collective-permute-start.13 = (f32[1,3,3,4,5,128]{5,4,3,2,1,0:T(8,128)}, f32[1,3,3,4,5,128]{5,4,3,2,1,0:T(8,128)S(1)}, u32[]{:S(2)}, u32[]{:S(2)}) collective-permute-start(f32[1,3,3,4,5,128]{5,4,3,2,1,0:T(8,128)} %slice.174), channel_id=1, source_target_pairs={{32,0},{64,32},{96,64},{128,96},{160,128},{192,160},{224,192},{33,... | collective-permute-start | bytes 276488 | tf_op jit(solution)/shard_map/ppermute | solution.py:25
  144.7 10.7 %collective-permute-start.15 = (f32[5,1,3,4,5,128]{5,4,3,2,1,0:T(8,128)S(1)}, f32[5,1,3,4,5,128]{5,4,3,2,1,0:T(8,128)S(1)}, u32[]{:S(2)}, u32[]{:S(2)}) collective-permute-start(f32[5,1,3,4,5,128]{5,4,3,2,1,0:T(8,128)S(1)} %get-tuple-element.26), channel_id=1, source_target_pairs={{4,0},{8,4},{12,8},{16,12},{20,16},{24,20},{28,24},{5,1},{9,5},{13... | collective-permute-start | bytes 460808 | tf_op jit(solution)/shard_map/ppermute | solution.py:25
  146.6 8.7 %collective-permute-start.14 = (f32[5,1,3,4,5,128]{5,4,3,2,1,0:T(8,128)S(1)}, f32[5,1,3,4,5,128]{5,4,3,2,1,0:T(8,128)S(1)}, u32[]{:S(2)}, u32[]{:S(2)}) collective-permute-start(f32[5,1,3,4,5,128]{5,4,3,2,1,0:T(8,128)S(1)} %get-tuple-element.25), channel_id=1, source_target_pairs={{0,4},{4,8},{8,12},{12,16},{16,20},{20,24},{24,28},{1,5},{5,9},{9,... | collective-permute-start | bytes 460808 | tf_op jit(solution)/shard_map/ppermute | solution.py:22
  149.2 12.1 %copy-start.4 = (f32[32,5,128]{2,1,0:T(8,128)S(1)}, f32[32,5,128]{2,1,0:T(8,128)}, u32[]{:S(2)}) copy-start(f32[32,5,128]{2,1,0:T(8,128)} %get-tuple-element.6) | copy-start | bytes 245764
  149.2 12.9 %collective-permute-start.11 = (f32[5,8,16,1]{3,2,1,0:T(8,128)S(1)}, f32[5,8,16,1]{3,2,1,0:T(8,128)S(1)}, u32[]{:S(2)}, u32[]{:S(2)}) collective-permute-start(f32[5,8,16,1]{3,2,1,0:T(8,128)S(1)} %get-tuple-element.28), channel_id=1, source_target_pairs={{1,0},{2,1},{3,2},{5,4},{6,5},{7,6},{9,8},{10,9},{11,10},{13,12},{... | collective-permute-start | bytes 7688 | tf_op jit(solution)/shard_map/ppermute | solution.py:37
  151.3 12.4 %copy-start.6 = (f32[5,1,16,128]{3,2,1,0:T(8,128)S(1)}, f32[5,1,16,128]{3,2,1,0:T(8,128)}, u32[]{:S(2)}) copy-start(f32[5,1,16,128]{3,2,1,0:T(8,128)} %copy-done.5) | copy-start | bytes 122884
  151.3 12.4 %copy-start.8 = (f32[5,1,16,128]{3,2,1,0:T(8,128)S(1)}, f32[5,1,16,128]{3,2,1,0:T(8,128)}, u32[]{:S(2)}) copy-start(f32[5,1,16,128]{3,2,1,0:T(8,128)} %copy-done.7) | copy-start | bytes 122884
  151.3 12.4 %copy-start.10 = (f32[5]{0:T(128)S(1)}, f32[5]{0:T(128)}, u32[]{:S(2)}) copy-start(f32[5]{0:T(128)} %constant.74.clone) | copy-start | bytes 64
  151.3 12.3 %collective-permute-start.10 = (f32[5,8,16,1]{3,2,1,0:T(8,128)S(1)}, f32[5,8,16,1]{3,2,1,0:T(8,128)S(1)}, u32[]{:S(2)}, u32[]{:S(2)}) collective-permute-start(f32[5,8,16,1]{3,2,1,0:T(8,128)S(1)} %get-tuple-element.27), channel_id=1, source_target_pairs={{0,1},{1,2},{2,3},{4,5},{5,6},{6,7},{8,9},{9,10},{10,11},{12,13},{... | collective-permute-start | bytes 7688 | tf_op jit(solution)/shard_map/ppermute | solution.py:36
  155.5 14.8 %collective-permute-start.17 = (f32[5,5,1,4,5,128]{5,4,3,2,1,0:T(8,128)S(1)}, f32[5,5,1,4,5,128]{5,4,3,2,1,0:T(8,128)S(1)}, u32[]{:S(2)}, u32[]{:S(2)}) collective-permute-start(f32[5,5,1,4,5,128]{5,4,3,2,1,0:T(8,128)S(1)} %get-tuple-element.20), channel_id=1, source_target_pairs={{1,0},{2,1},{3,2},{5,4},{6,5},{7,6},{9,8},{10,9},{11,10},{13,12},{... | collective-permute-start | bytes 768008 | tf_op jit(solution)/shard_map/ppermute | solution.py:25
  157.4 15.0 %collective-permute-start.16 = (f32[5,5,1,4,5,128]{5,4,3,2,1,0:T(8,128)S(1)}, f32[5,5,1,4,5,128]{5,4,3,2,1,0:T(8,128)S(1)}, u32[]{:S(2)}, u32[]{:S(2)}) collective-permute-start(f32[5,5,1,4,5,128]{5,4,3,2,1,0:T(8,128)S(1)} %get-tuple-element.19), channel_id=1, source_target_pairs={{0,1},{1,2},{2,3},{4,5},{5,6},{6,7},{8,9},{9,10},{10,11},{12,13},{... | collective-permute-start | bytes 768008 | tf_op jit(solution)/shard_map/ppermute | solution.py:22

commit v3 on v2

--- a/solution.py
+++ b/solution.py
@@ -42,6 +42,50 @@
         high_pad[dim] = (span - 3, 0)
         block = inner + jnp.pad(below, low_pad) + jnp.pad(above, high_pad)
     return block
+
+
+def pack_rows(parts):
+    flat = jnp.concatenate([p.reshape(-1) for p in parts])
+    extra = -flat.shape[0] % 128
+    return jnp.pad(flat, (0, extra)).reshape(-1, 128)
+
+
+def unpack_rows(rows, shapes):
+    flat = rows.reshape(-1)
+    parts = []
+    at = 0
+    for shape in shapes:
+        size = 1
+        for n in shape:
+            size *= n
+        parts.append(flat[at:at + size].reshape(shape))
+        at += size
+    return parts
+
+
+def fold_and_widen(block, boxes, sides):
+    for axis, dim, box_dim in sides:
+        count = lax.axis_size(axis)
+        forward = [(i, i + 1) for i in range(count - 1)]
+        backward = [(target, source) for source, target in forward]
+        span = block.shape[dim]
+        width = boxes.shape[box_dim]
+        up = [
+            lax.slice_in_dim(block, span - 1, span, axis=dim),
+            lax.slice_in_dim(boxes, width - 1, width, axis=box_dim),
+        ]
+        down = [lax.slice_in_dim(block, 0, 1, axis=dim), lax.slice_in_dim(boxes, 0, 1, axis=box_dim)]
+        shapes = [p.shape for p in up]
+        below = unpack_rows(lax.ppermute(pack_rows(up), axis, forward), shapes)
+        above = unpack_rows(lax.ppermute(pack_rows(down), axis, backward), shapes)
+        inner = lax.slice_in_dim(block, 1, span - 1, axis=dim)
+        low_pad = [(0, 0)] * block.ndim
+        high_pad = [(0, 0)] * block.ndim
+        low_pad[dim] = (0, span - 3)
+        high_pad[dim] = (span - 3, 0)
+        block = inner + jnp.pad(below[0], low_pad) + jnp.pad(above[0], high_pad)
+        boxes = jnp.concatenate([below[1], boxes, above[1]], axis=box_dim)
+    return block, boxes
 
 
 def parcel_update(current_condition, local_air_sample):
@@ -225,9 +269,6 @@
     )(live_blocks, table, parcels, pairs, pair_shares, depths, depth_shares, factors)
     deposit = deposit_rows.reshape(fields, DEPTH_ROWS, PAIR_LANES)[:, :span_z, :pair_count]
     deposit = jnp.transpose(deposit.reshape(fields, span_z, span_x, span_y), (0, 2, 3, 1))
-    cell_sources = fold_ghosts(deposit, (("gx", 1), ("gy", 2), ("gz", 3)))
-    kappa = jnp.array(DIFFUSION, jnp.float32)[:, None, None, None]
-    gas_next = gas_state + kappa * laplacian(padded) + COUPLING * cell_sources
     kept = jnp.where((alive_mask & (destination == 13))[:, None, None], updated, 0.0)
     leaving = alive_mask & (destination != 13)
     one_hot = (
@@ -240,7 +281,11 @@
     )
     outbox = jnp.dot(selector, updated.reshape(blocks, -1), precision=lax.Precision.HIGHEST)
     outbox = outbox.reshape((3, 3, 3, SLOTS) + parcels.shape[1:])
-    widened = with_halo(outbox, (("gx", 0), ("gy", 1), ("gz", 2)), 1)
+    cell_sources, widened = fold_and_widen(
+        deposit, outbox, (("gx", 1, 0), ("gy", 2, 1), ("gz", 3, 2))
+    )
+    kappa = jnp.array(DIFFUSION, jnp.float32)[:, None, None, None]
+    gas_next = gas_state + kappa * laplacian(padded) + COUPLING * cell_sources
     arrived_boxes = widened[0::2, 0::2, 0::2]
     arrived = arrived_boxes.reshape((27 * SLOTS,) + parcels.shape[1:])
     return (gas_next, kept, arrived)

time: 175 us -> 176 us (level)
  starting transfers between devices: 64.8 us -> 41 us
  local copies, waits for them, and re-layouts: 20.5 us -> 42.3 us
  other arithmetic: 12.8 us -> 24.2 us
  waiting for transfers between devices: 29.2 us -> 21.7 us
    reshape x0 -> x24, local copies, waits for them, and re-layouts: none -> 17 us  [the longest x12 9.8 us: unpack_rows(): parts.append(flat[at:at + size].reshape(shape))]
    ppermute x6 -> x3, waiting for transfers between devices: 17.7 us -> 0.92 us  [with_halo(): lax.ppermute(lax.slice_in_dim(block, 0, width, axis=dim), axis, backward)]
    ppermute x6 -> x3, starting transfers between devices: 29.8 us -> 13.2 us  [with_halo(): lax.ppermute(lax.slice_in_dim(block, block.shape[dim] - width, None, axis...]
    ppermute x6, waiting for transfers between devices: 4.07 us -> 18.4 us  [the longest x3 11.5 us: fold_and_widen(): above = unpack_rows(lax.ppermute(pack_rows(down), axis, backward), shapes)]
    reshape x0 -> x6, other arithmetic: none -> 6.77 us  [pack_rows(): return jnp.pad(flat, (0, extra)).reshape(-1, 128)]
    slice x3 -> x17, local copies, waits for them, and re-layouts: 0.86 us -> 7.16 us  [the longest x12 5.73 us: unpack_rows(): parts.append(flat[at:at + size].reshape(shape))]
    ppermute x6 -> x3, starting transfers between devices: 12.5 us -> 6.75 us  [with_halo(): lax.ppermute(lax.slice_in_dim(block, 0, width, axis=dim), axis, backward)]
    ppermute x6 -> x3, waiting for transfers between devices: 7.46 us -> 2.45 us  [with_halo(): lax.ppermute(lax.slice_in_dim(block, block.shape[dim] - width, None, axis...]
  transfers between devices with their start and end apart: 18 -> 12, of which waited for: 10 -> 7; matrix products, arithmetic and copies ran while one was open for 12% -> 13% of each run, Pallas kernels for 0% -> 0%
where the time goes in v3:
time: 176 us; the launch traced here: 175 us
  Pallas kernels  43.4 us (25%)
  local copies, waits for them, and re-layouts  42.3 us (24%)
  starting transfers between devices  41 us (23%)
  other arithmetic  24.2 us (14%)
  waiting for transfers between devices  21.7 us (12%)
  between operations  1.8 us (1%)
    pallas_call x1, Pallas kernels, local(): pl.pallas_call(coupling_kernel, out_shape=(jax.ShapeDtypeStruct(parcels.s...  43.4 us
    ppermute x3, starting transfers between devices, fold_and_widen(): below = unpack_rows(lax.ppermute(pack_rows(up), axis, forward), shapes)  15.4 us
    ppermute x3, starting transfers between devices, with_halo(): lax.ppermute(lax.slice_in_dim(block, block.shape[dim] - width, None, axis...  13.2 us
    ppermute x3, waiting for transfers between devices, fold_and_widen(): above = unpack_rows(lax.ppermute(pack_rows(down), axis, backward), shapes)  11.5 us
    reshape x12, local copies, waits for them, and re-layouts, unpack_rows(): parts.append(flat[at:at + size].reshape(shape))  9.8 us
    unnamed x43, local copies, waits for them, and re-layouts  9.57 us
    reshape x12, local copies, waits for them, and re-layouts, pack_rows(): flat = jnp.concatenate([p.reshape(-1) for p in parts])  7.18 us
    ppermute x3, waiting for transfers between devices, fold_and_widen(): below = unpack_rows(lax.ppermute(pack_rows(up), axis, forward), shapes)  6.87 us
  transfers between devices with their start and end apart: 12, of which 7 were waited for; matrix products, arithmetic and copies ran while one was open for 13% of the time, Pallas kernels for 0%

profile of v3, /device:TPU:58, one launch (start us, length us, event | category | flops | bytes accessed | tf_op | source)
XLA Modules:
  0.0 174.6 jit_solution(873348992236625135)
XLA Ops:
  1.5 7.8 %collective-permute-start.1 = (f32[5,1,16,128]{3,2,1,0:T(8,128)S(1)}, f32[5,1,16,128]{3,2,1,0:T(8,128)S(1)}, u32[]{:S(2)}, u32[]{:S(2)}) collective-permute-start(f32[5,1,16,128]{3,2,1,0:T(8,128)S(1)} %get-tuple-element.37), channel_id=1, source_target_pairs={{0,32},{32,64},{64,96},{96,128},{128,160},{160,192},{192,224},{1,3... | collective-permute-start | bytes 122888 | tf_op jit(solution)/shard_map/ppermute | solution.py:22
  9.3 1.9 %collective-permute-start = (f32[5,1,16,128]{3,2,1,0:T(8,128)S(1)}, f32[5,1,16,128]{3,2,1,0:T(8,128)S(1)}, u32[]{:S(2)}, u32[]{:S(2)}) collective-permute-start(f32[5,1,16,128]{3,2,1,0:T(8,128)S(1)} %get-tuple-element.36), channel_id=1, source_target_pairs={{32,0},{64,32},{96,64},{128,96},{160,128},{192,160},{224,192},{33,... | collective-permute-start | bytes 122888 | tf_op jit(solution)/shard_map/ppermute | solution.py:25
  21.3 1.9 %collective-permute-start.2 = (f32[5,10,1,128]{3,2,1,0:T(1,128)S(1)}, f32[5,10,1,128]{3,2,1,0:T(1,128)S(1)}, u32[]{:S(2)}, u32[]{:S(2)}) collective-permute-start(f32[5,10,1,128]{3,2,1,0:T(1,128)S(1)} %get-tuple-element.35), channel_id=1, source_target_pairs={{4,0},{8,4},{12,8},{16,12},{20,16},{24,20},{28,24},{5,1},{9,5},{13... | collective-permute-start | bytes 76808 | tf_op jit(solution)/shard_map/ppermute | solution.py:25
  23.3 2.4 %collective-permute-start.3 = (f32[5,10,1,128]{3,2,1,0:T(1,128)S(1)}, f32[5,10,1,128]{3,2,1,0:T(1,128)S(1)}, u32[]{:S(2)}, u32[]{:S(2)}) collective-permute-start(f32[5,10,1,128]{3,2,1,0:T(1,128)S(1)} %get-tuple-element.34), channel_id=1, source_target_pairs={{0,4},{4,8},{8,12},{12,16},{16,20},{20,24},{24,28},{1,5},{5,9},{9,... | collective-permute-start | bytes 76808 | tf_op jit(solution)/shard_map/ppermute | solution.py:22
  26.3 2.1 %collective-permute-done.3 = f32[5,10,1,128]{3,2,1,0:T(1,128)S(1)} collective-permute-done((f32[5,10,1,128]{3,2,1,0:T(1,128)S(1)}, f32[5,10,1,128]{3,2,1,0:T(1,128)S(1)}, u32[]{:S(2)}, u32[]{:S(2)}) %collective-permute-start.3) | collective-permute-done | bytes 25632 | tf_op jit(solution)/shard_map/ppermute | solution.py:22
  29.2 2.9 %collective-permute-start.4 = (f32[5,10,18,1]{2,3,1,0:T(1,128)S(1)}, f32[5,10,18,1]{2,3,1,0:T(1,128)S(1)}, u32[]{:S(2)}, u32[]{:S(2)}) collective-permute-start(f32[5,10,18,1]{2,3,1,0:T(1,128)S(1)} %copy.96), channel_id=1, source_target_pairs={{1,0},{2,1},{3,2},{5,4},{6,5},{7,6},{9,8},{10,9},{11,10},{13,12},{... | collective-permute-start | bytes 10808 | tf_op jit(solution)/shard_map/ppermute | solution.py:25
  32.5 2.9 %collective-permute-start.5 = (f32[5,10,18,1]{2,3,1,0:T(1,128)S(1)}, f32[5,10,18,1]{2,3,1,0:T(1,128)S(1)}, u32[]{:S(2)}, u32[]{:S(2)}) collective-permute-start(f32[5,10,18,1]{2,3,1,0:T(1,128)S(1)} %copy.98), channel_id=1, source_target_pairs={{0,1},{1,2},{2,3},{4,5},{5,6},{6,7},{8,9},{9,10},{10,11},{12,13},{... | collective-permute-start | bytes 10808 | tf_op jit(solution)/shard_map/ppermute | solution.py:22
  40.5 1.6 copy.126
  42.9 43.4 %shard_map.94 = (f32[32,5,128]{2,1,0:T(8,128)}, f32[680,256]{1,0:T(8,128)}) custom-call(s32[1]{0:T(128)} %copy.139.live_ref, f32[680,256]{1,0:T(8,128)} %bitcast.81, f32[32,5,128]{2,1,0:T(8,128)} %copy.110.parcel_ref, s32[32,4,128]{2,1,0:T(4,128)} %copy.111.pair_ref, f32[32,4,128]{2,1,0:T(4,128)} %pad_maximum_fusion.15.pair_share_ref, ...), custom_call_target="tpu_custom_call" | custom-call | tf_op jit(solution)/shard_map/pallas_call | solution.py:261
  86.4 2.4 %copy.125 = f32[5,130,180]{1,2,0:T(8,128)} copy(f32[5,130,180]{2,1,0:T(8,128)} %bitcast.89) | data formatting | bytes 936000
  88.8 1.3 reshape.151
  92.9 9.0 %collective-permute-start.6 = (f32[272,128]{1,0:T(8,128)}, f32[272,128]{1,0:T(8,128)S(1)}, u32[]{:S(2)}, u32[]{:S(2)}) collective-permute-start(f32[272,128]{1,0:T(8,128)} %fusion.16), channel_id=1, source_target_pairs={{0,32},{32,64},{64,96},{96,128},{128,160},{160,192},{192,224},{1,3... | collective-permute-start | bytes 417800 | tf_op jit(solution)/shard_map/ppermute | solution.py:79
  102.0 1.6 fusion.15
  103.5 1.9 %collective-permute-start.7 = (f32[272,128]{1,0:T(8,128)}, f32[272,128]{1,0:T(8,128)S(1)}, u32[]{:S(2)}, u32[]{:S(2)}) collective-permute-start(f32[272,128]{1,0:T(8,128)} %fusion.15), channel_id=1, source_target_pairs={{32,0},{64,32},{96,64},{128,96},{160,128},{192,160},{224,192},{33,... | collective-permute-start | bytes 417800 | tf_op jit(solution)/shard_map/ppermute | solution.py:80
  106.8 11.5 %collective-permute-done.7 = f32[272,128]{1,0:T(8,128)S(1)} collective-permute-done((f32[272,128]{1,0:T(8,128)}, f32[272,128]{1,0:T(8,128)S(1)}, u32[]{:S(2)}, u32[]{:S(2)}) %collective-permute-start.7) | collective-permute-done | bytes 139296 | tf_op jit(solution)/shard_map/ppermute | solution.py:80
  122.4 1.6 reshape.166
  126.7 1.6 reshape.172
  131.8 1.9 %collective-permute-start.9 = (f32[341,128]{1,0:T(8,128)S(1)}, f32[341,128]{1,0:T(8,128)S(1)}, u32[]{:S(2)}, u32[]{:S(2)}) collective-permute-start(f32[341,128]{1,0:T(8,128)S(1)} %fusion.13), channel_id=1, source_target_pairs={{4,0},{8,4},{12,8},{16,12},{20,16},{24,20},{28,24},{5,1},{9,5},{13... | collective-permute-start | bytes 523784 | tf_op jit(solution)/shard_map/ppermute | solution.py:80
  134.9 2.4 %collective-permute-start.8 = (f32[341,128]{1,0:T(8,128)S(1)}, f32[341,128]{1,0:T(8,128)S(1)}, u32[]{:S(2)}, u32[]{:S(2)}) collective-permute-start(f32[341,128]{1,0:T(8,128)S(1)} %fusion.14), channel_id=1, source_target_pairs={{0,4},{4,8},{8,12},{12,16},{16,20},{20,24},{24,28},{1,5},{5,9},{9,... | collective-permute-start | bytes 523784 | tf_op jit(solution)/shard_map/ppermute | solution.py:79
  137.5 4.2 %collective-permute-done.8 = f32[341,128]{1,0:T(8,128)S(1)} collective-permute-done((f32[341,128]{1,0:T(8,128)S(1)}, f32[341,128]{1,0:T(8,128)S(1)}, u32[]{:S(2)}, u32[]{:S(2)}) %collective-permute-start.8) | collective-permute-done | bytes 174624 | tf_op jit(solution)/shard_map/ppermute | solution.py:79
  143.9 1.3 fusion.1
  145.7 1.7 maximum_bitcast_fusion.2
  147.3 1.9 %collective-permute-start.11 = (f32[505,128]{1,0:T(8,128)}, f32[505,128]{1,0:T(8,128)}, u32[]{:S(2)}, u32[]{:S(2)}) collective-permute-start(f32[505,128]{1,0:T(8,128)} %maximum_bitcast_fusion.2), channel_id=1, source_target_pairs={{1,0},{2,1},{3,2},{5,4},{6,5},{7,6},{9,8},{10,9},{11,10},{13,12},{... | collective-permute-start | bytes 775688 | tf_op jit(solution)/shard_map/ppermute | solution.py:80
  149.2 1.7 reshape.179
  151.1 1.7 maximum_bitcast_fusion.1
  152.7 3.9 %collective-permute-start.10 = (f32[505,128]{1,0:T(8,128)}, f32[505,128]{1,0:T(8,128)}, u32[]{:S(2)}, u32[]{:S(2)}) collective-permute-start(f32[505,128]{1,0:T(8,128)} %maximum_bitcast_fusion.1), channel_id=1, source_target_pairs={{0,1},{1,2},{2,3},{4,5},{5,6},{6,7},{8,9},{9,10},{10,11},{12,13},{... | collective-permute-start | bytes 775688 | tf_op jit(solution)/shard_map/ppermute | solution.py:79
  159.9 2.2 %collective-permute-done.10 = f32[505,128]{1,0:T(8,128)} collective-permute-done((f32[505,128]{1,0:T(8,128)}, f32[505,128]{1,0:T(8,128)}, u32[]{:S(2)}, u32[]{:S(2)}) %collective-permute-start.10) | collective-permute-done | bytes 258592 | tf_op jit(solution)/shard_map/ppermute | solution.py:79
  163.8 1.7 slice.264
  165.5 1.7 reshape.187
  167.2 1.7 slice.263
  168.9 1.7 reshape.186
  170.6 1.4 pad_maximum_fusion
  (125 shorter events, 43.7 us)
Async XLA Ops:
  0.6 19.7 %copy-start.3 = (f32[5,8,16,128]{3,2,1,0:T(8,128)S(1)}, f32[5,8,16,128]{3,2,1,0:T(8,128)}, u32[]{:S(2)}) copy-start(f32[5,8,16,128]{3,2,1,0:T(8,128)} %param.7) | copy-start | bytes 983044
  1.5 18.8 %collective-permute-start.1 = (f32[5,1,16,128]{3,2,1,0:T(8,128)S(1)}, f32[5,1,16,128]{3,2,1,0:T(8,128)S(1)}, u32[]{:S(2)}, u32[]{:S(2)}) collective-permute-start(f32[5,1,16,128]{3,2,1,0:T(8,128)S(1)} %get-tuple-element.37), channel_id=1, source_target_pairs={{0,32},{32,64},{64,96},{96,128},{128,160},{160,192},{192,224},{1,3... | collective-permute-start | bytes 122888 | tf_op jit(solution)/shard_map/ppermute | solution.py:22
  9.3 11.9 %collective-permute-start = (f32[5,1,16,128]{3,2,1,0:T(8,128)S(1)}, f32[5,1,16,128]{3,2,1,0:T(8,128)S(1)}, u32[]{:S(2)}, u32[]{:S(2)}) collective-permute-start(f32[5,1,16,128]{3,2,1,0:T(8,128)S(1)} %get-tuple-element.36), channel_id=1, source_target_pairs={{32,0},{64,32},{96,64},{128,96},{160,128},{192,160},{224,192},{33,... | collective-permute-start | bytes 122888 | tf_op jit(solution)/shard_map/ppermute | solution.py:25
  20.3 3.0 %copy-start.10 = (f32[5,1,16,128]{3,2,1,0:T(8,128)}, f32[5,1,16,128]{3,2,1,0:T(8,128)S(1)}, u32[]{:S(2)}) copy-start(f32[5,1,16,128]{3,2,1,0:T(8,128)S(1)} %collective-permute-done.1) | copy-start | bytes 122884
  21.3 7.5 %copy-start.12 = (f32[5,1,16,128]{3,2,1,0:T(8,128)}, f32[5,1,16,128]{3,2,1,0:T(8,128)S(1)}, u32[]{:S(2)}) copy-start(f32[5,1,16,128]{3,2,1,0:T(8,128)S(1)} %collective-permute-done) | copy-start | bytes 122884
  21.3 17.3 %copy-start = (f32[5,10,16,128]{3,2,1,0:T(8,128)}, f32[5,10,16,128]{3,2,1,0:T(8,128)S(1)}, u32[]{:S(2)}) copy-start(f32[5,10,16,128]{3,2,1,0:T(8,128)S(1)} %constant_dynamic-update-slice_fusion) | copy-start | bytes 1228804
  21.3 5.0 %collective-permute-start.2 = (f32[5,10,1,128]{3,2,1,0:T(1,128)S(1)}, f32[5,10,1,128]{3,2,1,0:T(1,128)S(1)}, u32[]{:S(2)}, u32[]{:S(2)}) collective-permute-start(f32[5,10,1,128]{3,2,1,0:T(1,128)S(1)} %get-tuple-element.35), channel_id=1, source_target_pairs={{4,0},{8,4},{12,8},{16,12},{20,16},{24,20},{28,24},{5,1},{9,5},{13... | collective-permute-start | bytes 76808 | tf_op jit(solution)/shard_map/ppermute | solution.py:25
  23.3 5.2 %collective-permute-start.3 = (f32[5,10,1,128]{3,2,1,0:T(1,128)S(1)}, f32[5,10,1,128]{3,2,1,0:T(1,128)S(1)}, u32[]{:S(2)}, u32[]{:S(2)}) collective-permute-start(f32[5,10,1,128]{3,2,1,0:T(1,128)S(1)} %get-tuple-element.34), channel_id=1, source_target_pairs={{0,4},{4,8},{8,12},{12,16},{16,20},{20,24},{24,28},{1,5},{5,9},{9,... | collective-permute-start | bytes 76808 | tf_op jit(solution)/shard_map/ppermute | solution.py:22
  28.4 10.2 %copy-start.8 = (f32[5,10,1,128]{3,2,1,0:T(1,128)}, f32[5,10,1,128]{3,2,1,0:T(1,128)S(1)}, u32[]{:S(2)}) copy-start(f32[5,10,1,128]{3,2,1,0:T(1,128)S(1)} %collective-permute-done.3) | copy-start | bytes 76804
  28.7 7.3 %copy-start.14 = (f32[32,5,128]{2,0,1:T(8,128)S(1)}, f32[32,5,128]{2,0,1:T(8,128)}, u32[]{:S(2)}) copy-start(f32[32,5,128]{2,0,1:T(8,128)} %param.8) | copy-start | bytes 245764
  29.2 8.3 %collective-permute-start.4 = (f32[5,10,18,1]{2,3,1,0:T(1,128)S(1)}, f32[5,10,18,1]{2,3,1,0:T(1,128)S(1)}, u32[]{:S(2)}, u32[]{:S(2)}) collective-permute-start(f32[5,10,18,1]{2,3,1,0:T(1,128)S(1)} %copy.96), channel_id=1, source_target_pairs={{1,0},{2,1},{3,2},{5,4},{6,5},{7,6},{9,8},{10,9},{11,10},{13,12},{... | collective-permute-start | bytes 10808 | tf_op jit(solution)/shard_map/ppermute | solution.py:25
  32.5 5.7 %collective-permute-start.5 = (f32[5,10,18,1]{2,3,1,0:T(1,128)S(1)}, f32[5,10,18,1]{2,3,1,0:T(1,128)S(1)}, u32[]{:S(2)}, u32[]{:S(2)}) collective-permute-start(f32[5,10,18,1]{2,3,1,0:T(1,128)S(1)} %copy.98), channel_id=1, source_target_pairs={{0,1},{1,2},{2,3},{4,5},{5,6},{6,7},{8,9},{9,10},{10,11},{12,13},{... | collective-permute-start | bytes 10808 | tf_op jit(solution)/shard_map/ppermute | solution.py:22
  88.8 1.3 copy-start.7
  88.8 1.4 copy-start.15
  91.1 10.9 %copy-start.6 = (f32[23040]{0:T(1024)S(1)}, f32[23040]{0:T(1024)}, u32[]{:S(2)}) copy-start(f32[23040]{0:T(1024)} %reshape.159) | copy-start | bytes 276484
  92.9 13.8 %collective-permute-start.6 = (f32[272,128]{1,0:T(8,128)}, f32[272,128]{1,0:T(8,128)S(1)}, u32[]{:S(2)}, u32[]{:S(2)}) collective-permute-start(f32[272,128]{1,0:T(8,128)} %fusion.16), channel_id=1, source_target_pairs={{0,32},{32,64},{64,96},{96,128},{128,160},{160,192},{192,224},{1,3... | collective-permute-start | bytes 417800 | tf_op jit(solution)/shard_map/ppermute | solution.py:79
  103.5 14.8 %collective-permute-start.7 = (f32[272,128]{1,0:T(8,128)}, f32[272,128]{1,0:T(8,128)S(1)}, u32[]{:S(2)}, u32[]{:S(2)}) collective-permute-start(f32[272,128]{1,0:T(8,128)} %fusion.15), channel_id=1, source_target_pairs={{32,0},{64,32},{96,64},{128,96},{160,128},{192,160},{224,192},{33,... | collective-permute-start | bytes 417800 | tf_op jit(solution)/shard_map/ppermute | solution.py:80
  129.4 1.0 copy-start.2
  131.8 5.6 %collective-permute-start.9 = (f32[341,128]{1,0:T(8,128)S(1)}, f32[341,128]{1,0:T(8,128)S(1)}, u32[]{:S(2)}, u32[]{:S(2)}) collective-permute-start(f32[341,128]{1,0:T(8,128)S(1)} %fusion.13), channel_id=1, source_target_pairs={{4,0},{8,4},{12,8},{16,12},{20,16},{24,20},{28,24},{5,1},{9,5},{13... | collective-permute-start | bytes 523784 | tf_op jit(solution)/shard_map/ppermute | solution.py:80
  134.9 6.8 %collective-permute-start.8 = (f32[341,128]{1,0:T(8,128)S(1)}, f32[341,128]{1,0:T(8,128)S(1)}, u32[]{:S(2)}, u32[]{:S(2)}) collective-permute-start(f32[341,128]{1,0:T(8,128)S(1)} %fusion.14), channel_id=1, source_target_pairs={{0,4},{4,8},{8,12},{12,16},{16,20},{20,24},{24,28},{1,5},{5,9},{9,... | collective-permute-start | bytes 523784 | tf_op jit(solution)/shard_map/ppermute | solution.py:79
  147.3 11.0 %collective-permute-start.11 = (f32[505,128]{1,0:T(8,128)}, f32[505,128]{1,0:T(8,128)}, u32[]{:S(2)}, u32[]{:S(2)}) collective-permute-start(f32[505,128]{1,0:T(8,128)} %maximum_bitcast_fusion.2), channel_id=1, source_target_pairs={{1,0},{2,1},{3,2},{5,4},{6,5},{7,6},{9,8},{10,9},{11,10},{13,12},{... | collective-permute-start | bytes 775688 | tf_op jit(solution)/shard_map/ppermute | solution.py:80
  152.7 9.4 %collective-permute-start.10 = (f32[505,128]{1,0:T(8,128)}, f32[505,128]{1,0:T(8,128)}, u32[]{:S(2)}, u32[]{:S(2)}) collective-permute-start(f32[505,128]{1,0:T(8,128)} %maximum_bitcast_fusion.1), channel_id=1, source_target_pairs={{0,1},{1,2},{2,3},{4,5},{5,6},{6,7},{8,9},{9,10},{10,11},{12,13},{... | collective-permute-start | bytes 775688 | tf_op jit(solution)/shard_map/ppermute | solution.py:79
  172.0 1.0 copy-start.1
  172.0 1.2 copy-start.4
  172.0 1.3 copy-start.5
  172.0 1.3 copy-start.9
  172.0 1.3 copy-start.11
  172.0 1.3 copy-start.13
  172.1 1.3 copy-start.16

commit v4 on v2

--- a/solution.py
+++ b/solution.py
@@ -110,64 +110,119 @@
     return out
 
 
+GROUP = 4
+
+
 def coupling_kernel(
-    live_ref, table_ref, parcel_ref, pair_ref, pair_share_ref, depth_ref, depth_share_ref,
-    factor_ref, updated_ref, deposit_ref,
+    live_ref, dest_ref, table_ref, parcel_ref, pair_ref, pair_share_ref,
+    depth_ref, depth_share_ref, factor_ref, kept_ref, outbox_ref, deposit_ref,
+    weight_scr, depth_scr, spread_scr, updated_scr, count_scr, table_high_ref, table_low_ref,
 ):
     fields = parcel_ref.shape[1]
     blocks = parcel_ref.shape[0]
     lanes = parcel_ref.shape[2]
     deposit_ref[...] = jnp.zeros(deposit_ref.shape, jnp.float32)
+    table_high, table_low = split_bf16(table_ref[...])
+    table_high_ref[...] = table_high
+    table_low_ref[...] = table_low
     live = live_ref[0]
     pair_iota = lax.broadcasted_iota(jnp.int32, (PAIR_LANES, lanes), 0)
     depth_iota = lax.broadcasted_iota(jnp.int32, (DEPTH_ROWS, lanes), 0)
 
-    def body(b, carry):
-        pair = pair_ref[b]
-        pair_share = pair_share_ref[b]
-        weights = jnp.zeros((PAIR_LANES, lanes), jnp.float32)
-        for c in range(4):
-            weights = weights + jnp.where(pair_iota == pair[c:c + 1], pair_share[c:c + 1], 0.0)
-        depth = depth_ref[b]
-        depth_share = depth_share_ref[b]
-        depth_weights = jnp.where(depth_iota == depth[0:1], depth_share[0:1], 0.0)
-        depth_weights = depth_weights + jnp.where(
-            depth_iota == depth[1:2], depth_share[1:2], 0.0
+    def group(g, carry):
+        for j in range(GROUP):
+            b = g * GROUP + j
+            pair = pair_ref[b]
+            pair_share = pair_share_ref[b]
+            weights = jnp.zeros((PAIR_LANES, lanes), jnp.float32)
+            for c in range(4):
+                weights = weights + jnp.where(pair_iota == pair[c:c + 1], pair_share[c:c + 1], 0.0)
+            weight_scr[:, j * lanes:(j + 1) * lanes] = weights
+            depth = depth_ref[b]
+            depth_share = depth_share_ref[b]
+            depth_weights = jnp.where(depth_iota == depth[0:1], depth_share[0:1], 0.0)
+            depth_weights = depth_weights + jnp.where(
+                depth_iota == depth[1:2], depth_share[1:2], 0.0
+            )
+            depth_scr[:, j * lanes:(j + 1) * lanes] = depth_weights
+        weight_high, weight_low = split_bf16(weight_scr[...])
+        table_high = table_high_ref[...]
+        mixed = (
+            jnp.dot(table_high, weight_high, preferred_element_type=jnp.float32)
+            + jnp.dot(table_high, weight_low, preferred_element_type=jnp.float32)
+            + jnp.dot(table_low_ref[...], weight_high, preferred_element_type=jnp.float32)
         )
-        mixed = three_pass(table_ref[...], weights, ((1,), (0,)))
-        sample = [
-            jnp.sum(
-                mixed[f * DEPTH_ROWS:(f + 1) * DEPTH_ROWS] * depth_weights, axis=0, keepdims=True
+        for j in range(GROUP):
+            b = g * GROUP + j
+            depth_weights = depth_scr[:, j * lanes:(j + 1) * lanes]
+            sample = [
+                jnp.sum(
+                    mixed[f * DEPTH_ROWS:(f + 1) * DEPTH_ROWS, j * lanes:(j + 1) * lanes]
+                    * depth_weights,
+                    axis=0,
+                    keepdims=True,
+                )
+                for f in range(fields)
+            ]
+            current = parcel_ref[b]
+            factors = factor_ref[b]
+            mass = current[0:1]
+            heat = current[1:2]
+            keep_velocity = factors[0:1]
+            residual_heat = factors[1:2]
+            equilibrium = factors[2:3]
+            x = 4.0 * (equilibrium - sample[0])
+            soft = jnp.maximum(x, 0.0) + jnp.log1p(jnp.exp(-jnp.abs(x)))
+            share = 1.0 - jnp.exp(-0.3 * soft)
+            evaporated = mass * share
+            ambient = sample[1]
+            adjusted = ambient + (heat - ambient) * residual_heat - PHASE_CHANGE_COST * share
+            velocity = [
+                sample[2 + d] + (current[2 + d:3 + d] - sample[2 + d]) * keep_velocity
+                for d in range(3)
+            ]
+            enthalpy = 0.5 * mass * (heat - adjusted)
+            push = [mass * (current[2 + d:3 + d] - velocity[d]) for d in range(3)]
+            updated_scr[b] = jnp.concatenate([mass - evaporated, adjusted] + velocity, axis=0)
+            alive = b < live
+            sources = [jnp.where(alive, s, 0.0) for s in [evaporated, enthalpy] + push]
+            spread_scr[:, j * lanes:(j + 1) * lanes] = jnp.concatenate(
+                [s * depth_weights for s in sources], axis=0
             )
-            for f in range(fields)
-        ]
-        current = parcel_ref[b]
-        factors = factor_ref[b]
-        mass = current[0:1]
-        heat = current[1:2]
-        keep_velocity = factors[0:1]
-        residual_heat = factors[1:2]
-        equilibrium = factors[2:3]
-        x = 4.0 * (equilibrium - sample[0])
-        soft = jnp.maximum(x, 0.0) + jnp.log1p(jnp.exp(-jnp.abs(x)))
-        share = 1.0 - jnp.exp(-0.3 * soft)
-        evaporated = mass * share
-        ambient = sample[1]
-        adjusted = ambient + (heat - ambient) * residual_heat - PHASE_CHANGE_COST * share
-        velocity = [
-            sample[2 + d] + (current[2 + d:3 + d] - sample[2 + d]) * keep_velocity
-            for d in range(3)
-        ]
-        enthalpy = 0.5 * mass * (heat - adjusted)
-        push = [mass * (current[2 + d:3 + d] - velocity[d]) for d in range(3)]
-        updated_ref[b] = jnp.concatenate([mass - evaporated, adjusted] + velocity, axis=0)
+        spread_high, spread_low = split_bf16(spread_scr[...])
+        dims = (((1,), (1,)), ((), ()))
+        deposit_ref[...] += (
+            lax.dot_general(spread_high, weight_high, dims, preferred_element_type=jnp.float32)
+            + lax.dot_general(spread_high, weight_low, dims, preferred_element_type=jnp.float32)
+            + lax.dot_general(spread_low, weight_high, dims, preferred_element_type=jnp.float32)
+        )
+        return carry
+
+    lax.fori_loop(0, blocks // GROUP, group, 0)
+
+    kept_ref[...] = jnp.zeros(kept_ref.shape, jnp.float32)
+    outbox_ref[...] = jnp.zeros(outbox_ref.shape, jnp.float32)
+    for d in range(27):
+        count_scr[d] = 0
+
+    def route(b, carry):
+        d = jnp.minimum(jnp.maximum(dest_ref[b], 0), 26)
         alive = b < live
-        sources = [jnp.where(alive, s, 0.0) for s in [evaporated, enthalpy] + push]
-        spread = jnp.concatenate([s * depth_weights for s in sources], axis=0)
-        deposit_ref[...] += three_pass(spread, weights, ((1,), (1,)))
+
+        @pl.when(alive & (d == 13))
+        def _():
+            kept_ref[b] = updated_scr[b]
+
+        rank = count_scr[d]
+
+        @pl.when(alive & (d != 13) & (rank < SLOTS))
+        def _():
+            outbox_ref[d * SLOTS + rank] = updated_scr[b]
+            count_scr[d] = rank + 1
+
         return carry
 
-    lax.fori_loop(0, blocks, body, 0)
+    lax.fori_loop(0, blocks, route, 0)
 
 
 def local(gas_state, parcels, parcel_cells, offsets, destination, live_blocks):
@@ -182,7 +237,6 @@
     table = jnp.transpose(padded, (0, 3, 1, 2)).reshape(fields, span_z, pair_count)
     table = jnp.pad(table, ((0, 0), (0, DEPTH_ROWS - span_z), (0, PAIR_LANES - pair_count)))
     table = table.reshape(fields * DEPTH_ROWS, PAIR_LANES)
-    alive_mask = jnp.arange(blocks, dtype=jnp.int32) < live_blocks[0]
     cell_x = parcel_cells // plane_size
     cell_y = parcel_cells // span_z % span_y
     cell_z = parcel_cells % span_z
@@ -214,31 +268,35 @@
         axis=1,
     )
     vmem = pl.BlockSpec(memory_space=pltpu.VMEM)
-    updated, deposit_rows = pl.pallas_call(
+    smem = pl.BlockSpec(memory_space=pltpu.SMEM)
+    lanes = GROUP * block_parcels
+    kept, outbox, deposit_rows = pl.pallas_call(
         coupling_kernel,
         out_shape=(
             jax.ShapeDtypeStruct(parcels.shape, jnp.float32),
+            jax.ShapeDtypeStruct((27 * SLOTS,) + parcels.shape[1:], jnp.float32),
             jax.ShapeDtypeStruct((fields * DEPTH_ROWS, PAIR_LANES), jnp.float32),
         ),
-        in_specs=[pl.BlockSpec(memory_space=pltpu.SMEM)] + [vmem] * 7,
-        out_specs=(vmem, vmem),
-    )(live_blocks, table, parcels, pairs, pair_shares, depths, depth_shares, factors)
+        in_specs=[smem, smem] + [vmem] * 7,
+        out_specs=(vmem, vmem, vmem),
+        scratch_shapes=[
+            pltpu.VMEM((PAIR_LANES, lanes), jnp.float32),
+            pltpu.VMEM((DEPTH_ROWS, lanes), jnp.float32),
+            pltpu.VMEM((fields * DEPTH_ROWS, lanes), jnp.float32),
+            pltpu.VMEM(parcels.shape, jnp.float32),
+            pltpu.SMEM((32,), jnp.int32),
+            pltpu.VMEM(table.shape, jnp.bfloat16),
+            pltpu.VMEM(table.shape, jnp.bfloat16),
+        ],
+    )(
+        live_blocks, destination, table, parcels, pairs, pair_shares, depths,
+        depth_shares, factors,
+    )
     deposit = deposit_rows.reshape(fields, DEPTH_ROWS, PAIR_LANES)[:, :span_z, :pair_count]
     deposit = jnp.transpose(deposit.reshape(fields, span_z, span_x, span_y), (0, 2, 3, 1))
     cell_sources = fold_ghosts(deposit, (("gx", 1), ("gy", 2), ("gz", 3)))
     kappa = jnp.array(DIFFUSION, jnp.float32)[:, None, None, None]
     gas_next = gas_state + kappa * laplacian(padded) + COUPLING * cell_sources
-    kept = jnp.where((alive_mask & (destination == 13))[:, None, None], updated, 0.0)
-    leaving = alive_mask & (destination != 13)
-    one_hot = (
-        (destination[:, None] == jnp.arange(27, dtype=jnp.int32)[None, :]) & leaving[:, None]
-    ).astype(jnp.int32)
-    slot_rank = jnp.sum(jnp.cumsum(one_hot, axis=0) * one_hot, axis=1) - 1
-    slot_index = jnp.where(leaving, destination * SLOTS + slot_rank, -1)
-    selector = (jnp.arange(27 * SLOTS, dtype=jnp.int32)[:, None] == slot_index[None, :]).astype(
-        jnp.float32
-    )
-    outbox = jnp.dot(selector, updated.reshape(blocks, -1), precision=lax.Precision.HIGHEST)
     outbox = outbox.reshape((3, 3, 3, SLOTS) + parcels.shape[1:])
     widened = with_halo(outbox, (("gx", 0), ("gy", 1), ("gz", 2)), 1)
     arrived_boxes = widened[0::2, 0::2, 0::2]

time: 175 us -> 137 us (0.78)
  Pallas kernels: 43.4 us -> 20.7 us
  waiting for transfers between devices: 29.2 us -> 21.9 us
  local copies, waits for them, and re-layouts: 20.5 us -> 14.2 us
  other arithmetic: 12.8 us -> 8.94 us
  starting transfers between devices: 64.8 us -> 67 us
    pallas_call x1, Pallas kernels: 43.4 us -> 20.7 us  [local(): pl.pallas_call(coupling_kernel, out_shape=(jax.ShapeDtypeStruct(parcels.s...]
    ppermute x6, waiting for transfers between devices: 17.7 us -> 2.78 us  [with_halo(): lax.ppermute(lax.slice_in_dim(block, 0, width, axis=dim), axis, backward)]
    ppermute x3, waiting for transfers between devices: 1.13 us -> 9.56 us  [fold_ghosts(): lax.ppermute(lax.slice_in_dim(block, 0, 1, axis=dim), axis, backward)]
    ppermute x6, waiting for transfers between devices: 7.46 us -> 1.62 us  [with_halo(): lax.ppermute(lax.slice_in_dim(block, block.shape[dim] - width, None, axis...]
    ppermute x3, waiting for transfers between devices: 2.94 us -> 7.92 us  [fold_ghosts(): lax.ppermute(lax.slice_in_dim(block, span - 1, span, axis=dim), axis, for...]
    ppermute x3, starting transfers between devices: 16.4 us -> 11.9 us  [fold_ghosts(): lax.ppermute(lax.slice_in_dim(block, span - 1, span, axis=dim), axis, for...]
    ppermute x6, starting transfers between devices: 12.5 us -> 16.9 us  [with_halo(): lax.ppermute(lax.slice_in_dim(block, 0, width, axis=dim), axis, backward)]
    ppermute x3, starting transfers between devices: 6.01 us -> 8.45 us  [fold_ghosts(): lax.ppermute(lax.slice_in_dim(block, 0, 1, axis=dim), axis, backward)]
  transfers between devices with their start and end apart: 18 -> 18, of which waited for: 10 -> 6; matrix products, arithmetic and copies ran while one was open for 12% -> 9% of each run, Pallas kernels for 0% -> 0%
where the time goes in v4:
time: 137 us; the launch traced here: 134 us
  starting transfers between devices  67 us (49%)
  waiting for transfers between devices  21.9 us (16%)
  Pallas kernels  20.7 us (15%)
  local copies, waits for them, and re-layouts  14.2 us (10%)
  other arithmetic  8.94 us (7%)
  between operations  1.69 us (1%)
    ppermute x6, starting transfers between devices, with_halo(): lax.ppermute(lax.slice_in_dim(block, block.shape[dim] - width, None, axis...  29.8 us
    pallas_call x1, Pallas kernels, local(): pl.pallas_call(coupling_kernel, out_shape=(jax.ShapeDtypeStruct(parcels.s...  20.7 us
    ppermute x6, starting transfers between devices, with_halo(): lax.ppermute(lax.slice_in_dim(block, 0, width, axis=dim), axis, backward)  16.9 us
    ppermute x3, starting transfers between devices, fold_ghosts(): lax.ppermute(lax.slice_in_dim(block, span - 1, span, axis=dim), axis, for...  11.9 us
    ppermute x3, waiting for transfers between devices, fold_ghosts(): lax.ppermute(lax.slice_in_dim(block, 0, 1, axis=dim), axis, backward)  9.56 us
    ppermute x3, starting transfers between devices, fold_ghosts(): lax.ppermute(lax.slice_in_dim(block, 0, 1, axis=dim), axis, backward)  8.45 us
    ppermute x3, waiting for transfers between devices, fold_ghosts(): lax.ppermute(lax.slice_in_dim(block, span - 1, span, axis=dim), axis, for...  7.92 us
    unnamed x16, local copies, waits for them, and re-layouts  6.45 us
  transfers between devices with their start and end apart: 18, of which 6 were waited for; matrix products, arithmetic and copies ran while one was open for 9% of the time, Pallas kernels for 0%

profile of v4, /device:TPU:58, one launch (start us, length us, event | category | flops | bytes accessed | tf_op | source)
XLA Modules:
  0.0 134.4 jit_solution(11114960163265526247)
XLA Ops:
  1.4 2.6 %collective-permute-start = (f32[5,1,16,128]{3,2,1,0:T(8,128)S(1)}, f32[5,1,16,128]{3,2,1,0:T(8,128)S(1)}, u32[]{:S(2)}, u32[]{:S(2)}) collective-permute-start(f32[5,1,16,128]{3,2,1,0:T(8,128)S(1)} %get-tuple-element.37), channel_id=1, source_target_pairs={{32,0},{64,32},{96,64},{128,96},{160,128},{192,160},{224,192},{33,... | collective-permute-start | bytes 122888 | tf_op jit(solution)/shard_map/ppermute | solution.py:25
  4.1 9.2 %collective-permute-start.1 = (f32[5,1,16,128]{3,2,1,0:T(8,128)S(1)}, f32[5,1,16,128]{3,2,1,0:T(8,128)S(1)}, u32[]{:S(2)}, u32[]{:S(2)}) collective-permute-start(f32[5,1,16,128]{3,2,1,0:T(8,128)S(1)} %get-tuple-element.38), channel_id=1, source_target_pairs={{0,32},{32,64},{64,96},{96,128},{128,160},{160,192},{192,224},{1,3... | collective-permute-start | bytes 122888 | tf_op jit(solution)/shard_map/ppermute | solution.py:22
  18.2 1.0 constant_dynamic-update-slice_fusion.1
  19.2 1.9 %collective-permute-start.3 = (f32[5,10,1,128]{3,2,1,0:T(1,128)S(1)}, f32[5,10,1,128]{3,2,1,0:T(1,128)S(1)}, u32[]{:S(2)}, u32[]{:S(2)}) collective-permute-start(f32[5,10,1,128]{3,2,1,0:T(1,128)S(1)} %get-tuple-element.35), channel_id=1, source_target_pairs={{0,4},{4,8},{8,12},{12,16},{16,20},{20,24},{24,28},{1,5},{5,9},{9,... | collective-permute-start | bytes 76808 | tf_op jit(solution)/shard_map/ppermute | solution.py:22
  21.2 3.6 %collective-permute-start.2 = (f32[5,10,1,128]{3,2,1,0:T(1,128)S(1)}, f32[5,10,1,128]{3,2,1,0:T(1,128)S(1)}, u32[]{:S(2)}, u32[]{:S(2)}) collective-permute-start(f32[5,10,1,128]{3,2,1,0:T(1,128)S(1)} %get-tuple-element.36), channel_id=1, source_target_pairs={{4,0},{8,4},{12,8},{16,12},{20,16},{24,20},{28,24},{5,1},{9,5},{13... | collective-permute-start | bytes 76808 | tf_op jit(solution)/shard_map/ppermute | solution.py:25
  25.5 0.9 collective-permute-done.2
  27.5 2.0 %collective-permute-start.4 = (f32[5,10,18,1]{2,3,1,0:T(1,128)S(1)}, f32[5,10,18,1]{2,3,1,0:T(1,128)S(1)}, u32[]{:S(2)}, u32[]{:S(2)}) collective-permute-start(f32[5,10,18,1]{2,3,1,0:T(1,128)S(1)} %copy.55), channel_id=1, source_target_pairs={{1,0},{2,1},{3,2},{5,4},{6,5},{7,6},{9,8},{10,9},{11,10},{13,12},{... | collective-permute-start | bytes 10808 | tf_op jit(solution)/shard_map/ppermute | solution.py:25
  29.5 3.8 %collective-permute-start.5 = (f32[5,10,18,1]{2,3,1,0:T(1,128)S(1)}, f32[5,10,18,1]{2,3,1,0:T(1,128)S(1)}, u32[]{:S(2)}, u32[]{:S(2)}) collective-permute-start(f32[5,10,18,1]{2,3,1,0:T(1,128)S(1)} %copy.57), channel_id=1, source_target_pairs={{0,1},{1,2},{2,3},{4,5},{5,6},{6,7},{8,9},{9,10},{10,11},{12,13},{... | collective-permute-start | bytes 10808 | tf_op jit(solution)/shard_map/ppermute | solution.py:22
  37.6 1.1 reshape.27
  38.7 1.6 %copy.76 = f32[5,130,180]{2,1,0:T(8,128)S(1)} copy(f32[5,130,180]{1,2,0:T(8,128)} %reshape.27) | data formatting | bytes 936000
  40.3 0.9 pad.28.clone
  41.2 20.7 %shard_map.94 = (f32[32,5,128]{2,1,0:T(8,128)}, f32[108,5,128]{2,1,0:T(8,128)}, f32[680,256]{1,0:T(8,128)}) custom-call(s32[1]{0:T(128)S(6)} %copy.82.live_ref, s32[32]{0:T(128)} %dest_ref.1, f32[680,256]{1,0:T(8,128)} %bitcast.57, f32[32,5,128]{2,1,0:T(8,128)} %copy.69.parcel_ref, s32[32,4,128]{2,1,0:T(4,128)} %copy.70.pair_ref, ...), custom_call_target="tpu_custom_call" | custom-call | tf_op jit(solution)/shard_map/pallas_call | solution.py:273
  61.8 2.5 %copy.75 = f32[5,130,180]{1,2,0:T(8,128)} copy(f32[5,130,180]{2,1,0:T(8,128)} %bitcast.59) | data formatting | bytes 936000
  64.3 1.3 reshape.30
  65.7 7.0 %collective-permute-start.6 = (f32[5,1,18,130]{3,2,1,0:T(8,128)S(1)}, f32[5,1,18,130]{3,2,1,0:T(8,128)S(1)}, u32[]{:S(2)}, u32[]{:S(2)}) collective-permute-start(f32[5,1,18,130]{3,2,1,0:T(8,128)S(1)} %get-tuple-element.23), channel_id=1, source_target_pairs={{0,32},{32,64},{64,96},{96,128},{128,160},{160,192},{192,224},{1,3... | collective-permute-start | bytes 140408 | tf_op jit(solution)/shard_map/ppermute | solution.py:36
  72.7 1.9 %collective-permute-start.7 = (f32[5,1,18,130]{3,2,1,0:T(8,128)S(1)}, f32[5,1,18,130]{3,2,1,0:T(8,128)S(1)}, u32[]{:S(2)}, u32[]{:S(2)}) collective-permute-start(f32[5,1,18,130]{3,2,1,0:T(8,128)S(1)} %get-tuple-element.24), channel_id=1, source_target_pairs={{32,0},{64,32},{96,64},{128,96},{160,128},{192,160},{224,192},{33,... | collective-permute-start | bytes 140408 | tf_op jit(solution)/shard_map/ppermute | solution.py:37
  74.7 1.9 %collective-permute-start.13 = (f32[1,3,3,4,5,128]{5,4,3,2,1,0:T(8,128)S(1)}, f32[1,3,3,4,5,128]{5,4,3,2,1,0:T(8,128)S(1)}, u32[]{:S(2)}, u32[]{:S(2)}) collective-permute-start(f32[1,3,3,4,5,128]{5,4,3,2,1,0:T(8,128)S(1)} %bitcast.61), channel_id=1, source_target_pairs={{32,0},{64,32},{96,64},{128,96},{160,128},{192,160},{224,192},{33,... | collective-permute-start | bytes 276488 | tf_op jit(solution)/shard_map/ppermute | solution.py:25
  76.6 9.9 %collective-permute-start.12 = (f32[1,3,3,4,5,128]{5,4,3,2,1,0:T(8,128)S(1)}, f32[1,3,3,4,5,128]{5,4,3,2,1,0:T(8,128)S(1)}, u32[]{:S(2)}, u32[]{:S(2)}) collective-permute-start(f32[1,3,3,4,5,128]{5,4,3,2,1,0:T(8,128)S(1)} %bitcast.60), channel_id=1, source_target_pairs={{0,32},{32,64},{64,96},{96,128},{128,160},{160,192},{192,224},{1,3... | collective-permute-start | bytes 276488 | tf_op jit(solution)/shard_map/ppermute | solution.py:22
  86.6 6.0 %collective-permute-done.7 = f32[5,1,18,130]{3,2,1,0:T(8,128)S(1)} collective-permute-done((f32[5,1,18,130]{3,2,1,0:T(8,128)S(1)}, f32[5,1,18,130]{3,2,1,0:T(8,128)S(1)}, u32[]{:S(2)}, u32[]{:S(2)}) %collective-permute-start.7) | collective-permute-done | bytes 46832 | tf_op jit(solution)/shard_map/ppermute | solution.py:37
  92.8 2.0 %collective-permute-start.8 = (f32[5,8,1,130]{3,2,1,0:T(1,128)S(1)}, f32[5,8,1,130]{3,2,1,0:T(1,128)S(1)}, u32[]{:S(2)}, u32[]{:S(2)}) collective-permute-start(f32[5,8,1,130]{3,2,1,0:T(1,128)S(1)} %get-tuple-element.25), channel_id=1, source_target_pairs={{0,4},{4,8},{8,12},{12,16},{16,20},{20,24},{24,28},{1,5},{5,9},{9,... | collective-permute-start | bytes 62408 | tf_op jit(solution)/shard_map/ppermute | solution.py:36
  94.8 3.6 %collective-permute-start.9 = (f32[5,8,1,130]{3,2,1,0:T(1,128)S(1)}, f32[5,8,1,130]{3,2,1,0:T(1,128)S(1)}, u32[]{:S(2)}, u32[]{:S(2)}) collective-permute-start(f32[5,8,1,130]{3,2,1,0:T(1,128)S(1)} %get-tuple-element.26), channel_id=1, source_target_pairs={{4,0},{8,4},{12,8},{16,12},{20,16},{24,20},{28,24},{5,1},{9,5},{13... | collective-permute-start | bytes 62408 | tf_op jit(solution)/shard_map/ppermute | solution.py:37
  98.4 1.9 %collective-permute-start.14 = (f32[5,1,3,4,5,128]{5,4,3,2,1,0:T(8,128)S(1)}, f32[5,1,3,4,5,128]{5,4,3,2,1,0:T(8,128)S(1)}, u32[]{:S(2)}, u32[]{:S(2)}) collective-permute-start(f32[5,1,3,4,5,128]{5,4,3,2,1,0:T(8,128)S(1)} %get-tuple-element.27), channel_id=1, source_target_pairs={{0,4},{4,8},{8,12},{12,16},{16,20},{20,24},{24,28},{1,5},{5,9},{9,... | collective-permute-start | bytes 460808 | tf_op jit(solution)/shard_map/ppermute | solution.py:22
  100.4 3.8 %collective-permute-start.15 = (f32[5,1,3,4,5,128]{5,4,3,2,1,0:T(8,128)S(1)}, f32[5,1,3,4,5,128]{5,4,3,2,1,0:T(8,128)S(1)}, u32[]{:S(2)}, u32[]{:S(2)}) collective-permute-start(f32[5,1,3,4,5,128]{5,4,3,2,1,0:T(8,128)S(1)} %get-tuple-element.28), channel_id=1, source_target_pairs={{4,0},{8,4},{12,8},{16,12},{20,16},{24,20},{28,24},{5,1},{9,5},{13... | collective-permute-start | bytes 460808 | tf_op jit(solution)/shard_map/ppermute | solution.py:25
  104.4 1.6 %collective-permute-done.14 = f32[5,1,3,4,5,128]{5,4,3,2,1,0:T(8,128)S(1)} collective-permute-done((f32[5,1,3,4,5,128]{5,4,3,2,1,0:T(8,128)S(1)}, f32[5,1,3,4,5,128]{5,4,3,2,1,0:T(8,128)S(1)}, u32[]{:S(2)}, u32[]{:S(2)}) %collective-permute-start.14) | collective-permute-done | bytes 153632 | tf_op jit(solution)/shard_map/ppermute | solution.py:22
  106.0 1.9 %collective-permute-done.15 = f32[5,1,3,4,5,128]{5,4,3,2,1,0:T(8,128)S(1)} collective-permute-done((f32[5,1,3,4,5,128]{5,4,3,2,1,0:T(8,128)S(1)}, f32[5,1,3,4,5,128]{5,4,3,2,1,0:T(8,128)S(1)}, u32[]{:S(2)}, u32[]{:S(2)}) %collective-permute-start.15) | collective-permute-done | bytes 153632 | tf_op jit(solution)/shard_map/ppermute | solution.py:25
  108.0 3.0 %collective-permute-start.16 = (f32[5,5,1,4,5,128]{5,4,3,2,1,0:T(8,128)S(1)}, f32[5,5,1,4,5,128]{5,4,3,2,1,0:T(8,128)S(1)}, u32[]{:S(2)}, u32[]{:S(2)}) collective-permute-start(f32[5,5,1,4,5,128]{5,4,3,2,1,0:T(8,128)S(1)} %get-tuple-element.21), channel_id=1, source_target_pairs={{0,1},{1,2},{2,3},{4,5},{5,6},{6,7},{8,9},{9,10},{10,11},{12,13},{... | collective-permute-start | bytes 768008 | tf_op jit(solution)/shard_map/ppermute | solution.py:22
  110.9 2.9 %collective-permute-start.17 = (f32[5,5,1,4,5,128]{5,4,3,2,1,0:T(8,128)S(1)}, f32[5,5,1,4,5,128]{5,4,3,2,1,0:T(8,128)S(1)}, u32[]{:S(2)}, u32[]{:S(2)}) collective-permute-start(f32[5,5,1,4,5,128]{5,4,3,2,1,0:T(8,128)S(1)} %get-tuple-element.22), channel_id=1, source_target_pairs={{1,0},{2,1},{3,2},{5,4},{6,5},{7,6},{9,8},{10,9},{11,10},{13,12},{... | collective-permute-start | bytes 768008 | tf_op jit(solution)/shard_map/ppermute | solution.py:25
  114.0 2.9 %collective-permute-start.10 = (f32[5,8,16,1]{3,2,1,0:T(8,128)S(1)}, f32[5,8,16,1]{3,2,1,0:T(8,128)S(1)}, u32[]{:S(2)}, u32[]{:S(2)}) collective-permute-start(f32[5,8,16,1]{3,2,1,0:T(8,128)S(1)} %get-tuple-element.29), channel_id=1, source_target_pairs={{0,1},{1,2},{2,3},{4,5},{5,6},{6,7},{8,9},{9,10},{10,11},{12,13},{... | collective-permute-start | bytes 7688 | tf_op jit(solution)/shard_map/ppermute | solution.py:36
  116.9 2.9 %collective-permute-start.11 = (f32[5,8,16,1]{3,2,1,0:T(8,128)S(1)}, f32[5,8,16,1]{3,2,1,0:T(8,128)S(1)}, u32[]{:S(2)}, u32[]{:S(2)}) collective-permute-start(f32[5,8,16,1]{3,2,1,0:T(8,128)S(1)} %get-tuple-element.30), channel_id=1, source_target_pairs={{1,0},{2,1},{3,2},{5,4},{6,5},{7,6},{9,8},{10,9},{11,10},{13,12},{... | collective-permute-start | bytes 7688 | tf_op jit(solution)/shard_map/ppermute | solution.py:37
  120.5 7.9 %collective-permute-done.10 = f32[5,8,16,1]{3,2,1,0:T(8,128)S(1)} collective-permute-done((f32[5,8,16,1]{3,2,1,0:T(8,128)S(1)}, f32[5,8,16,1]{3,2,1,0:T(8,128)S(1)}, u32[]{:S(2)}, u32[]{:S(2)}) %collective-permute-start.10) | collective-permute-done | bytes 2592 | tf_op jit(solution)/shard_map/ppermute | solution.py:36
  128.4 3.5 %collective-permute-done.11 = f32[5,8,16,1]{3,2,1,0:T(8,128)S(1)} collective-permute-done((f32[5,8,16,1]{3,2,1,0:T(8,128)S(1)}, f32[5,8,16,1]{3,2,1,0:T(8,128)S(1)}, u32[]{:S(2)}, u32[]{:S(2)}) %collective-permute-start.11) | collective-permute-done | bytes 2592 | tf_op jit(solution)/shard_map/ppermute | solution.py:37
  132.0 1.4 %fusion.4 = f32[5,8,16,128]{3,2,1,0:T(8,128)} fusion(f32[5,8,16,130]{3,2,1,0:T(8,128)S(1)} %fusion.1, f32[5,8,16,128]{3,2,1,0:T(8,128)S(1)} %copy-done.1, f32[5,10,18,1]{3,2,1,0:T(8,128)S(1)} %copy.58, f32[5,10,1,128]{3,2,1,0:T(1,128)S(1)} %collective-permute-done.2, f32[5,10,16,128]{3,2,1,0:T(8,128)S(1)} %constant_dynamic-update-slice_fusion, ...), kind=kLoop, calls=%fused_computation.15 | loop fusion | flops 1884160 | bytes 1538100 | tf_op jit(solution)/shard_map/add | solution.py:299
  (60 shorter events, 13.5 us)
Async XLA Ops:
  1.4 17.7 %collective-permute-start = (f32[5,1,16,128]{3,2,1,0:T(8,128)S(1)}, f32[5,1,16,128]{3,2,1,0:T(8,128)S(1)}, u32[]{:S(2)}, u32[]{:S(2)}) collective-permute-start(f32[5,1,16,128]{3,2,1,0:T(8,128)S(1)} %get-tuple-element.37), channel_id=1, source_target_pairs={{32,0},{64,32},{96,64},{128,96},{160,128},{192,160},{224,192},{33,... | collective-permute-start | bytes 122888 | tf_op jit(solution)/shard_map/ppermute | solution.py:25
  4.1 14.1 %collective-permute-start.1 = (f32[5,1,16,128]{3,2,1,0:T(8,128)S(1)}, f32[5,1,16,128]{3,2,1,0:T(8,128)S(1)}, u32[]{:S(2)}, u32[]{:S(2)}) collective-permute-start(f32[5,1,16,128]{3,2,1,0:T(8,128)S(1)} %get-tuple-element.38), channel_id=1, source_target_pairs={{0,32},{32,64},{64,96},{96,128},{128,160},{160,192},{192,224},{1,3... | collective-permute-start | bytes 122888 | tf_op jit(solution)/shard_map/ppermute | solution.py:22
  19.2 6.2 %collective-permute-start.3 = (f32[5,10,1,128]{3,2,1,0:T(1,128)S(1)}, f32[5,10,1,128]{3,2,1,0:T(1,128)S(1)}, u32[]{:S(2)}, u32[]{:S(2)}) collective-permute-start(f32[5,10,1,128]{3,2,1,0:T(1,128)S(1)} %get-tuple-element.35), channel_id=1, source_target_pairs={{0,4},{4,8},{8,12},{12,16},{16,20},{20,24},{24,28},{1,5},{5,9},{9,... | collective-permute-start | bytes 76808 | tf_op jit(solution)/shard_map/ppermute | solution.py:22
  21.2 5.2 %collective-permute-start.2 = (f32[5,10,1,128]{3,2,1,0:T(1,128)S(1)}, f32[5,10,1,128]{3,2,1,0:T(1,128)S(1)}, u32[]{:S(2)}, u32[]{:S(2)}) collective-permute-start(f32[5,10,1,128]{3,2,1,0:T(1,128)S(1)} %get-tuple-element.36), channel_id=1, source_target_pairs={{4,0},{8,4},{12,8},{16,12},{20,16},{24,20},{28,24},{5,1},{9,5},{13... | collective-permute-start | bytes 76808 | tf_op jit(solution)/shard_map/ppermute | solution.py:25
  26.4 7.5 %copy-start.2 = (f32[32,5,128]{2,0,1:T(8,128)S(1)}, f32[32,5,128]{2,0,1:T(8,128)}, u32[]{:S(2)}) copy-start(f32[32,5,128]{2,0,1:T(8,128)} %param.8) | copy-start | bytes 245764
  27.5 9.0 %collective-permute-start.4 = (f32[5,10,18,1]{2,3,1,0:T(1,128)S(1)}, f32[5,10,18,1]{2,3,1,0:T(1,128)S(1)}, u32[]{:S(2)}, u32[]{:S(2)}) collective-permute-start(f32[5,10,18,1]{2,3,1,0:T(1,128)S(1)} %copy.55), channel_id=1, source_target_pairs={{1,0},{2,1},{3,2},{5,4},{6,5},{7,6},{9,8},{10,9},{11,10},{13,12},{... | collective-permute-start | bytes 10808 | tf_op jit(solution)/shard_map/ppermute | solution.py:25
  29.5 6.5 %collective-permute-start.5 = (f32[5,10,18,1]{2,3,1,0:T(1,128)S(1)}, f32[5,10,18,1]{2,3,1,0:T(1,128)S(1)}, u32[]{:S(2)}, u32[]{:S(2)}) collective-permute-start(f32[5,10,18,1]{2,3,1,0:T(1,128)S(1)} %copy.57), channel_id=1, source_target_pairs={{0,1},{1,2},{2,3},{4,5},{5,6},{6,7},{8,9},{9,10},{10,11},{12,13},{... | collective-permute-start | bytes 10808 | tf_op jit(solution)/shard_map/ppermute | solution.py:22
  61.8 12.8 %copy-start = (f32[108,5,128]{2,1,0:T(8,128)S(1)}, f32[108,5,128]{2,1,0:T(8,128)}, u32[]{:S(2)}) copy-start(f32[108,5,128]{2,1,0:T(8,128)} %get-tuple-element.8) | copy-start | bytes 829444
  65.7 20.9 %collective-permute-start.6 = (f32[5,1,18,130]{3,2,1,0:T(8,128)S(1)}, f32[5,1,18,130]{3,2,1,0:T(8,128)S(1)}, u32[]{:S(2)}, u32[]{:S(2)}) collective-permute-start(f32[5,1,18,130]{3,2,1,0:T(8,128)S(1)} %get-tuple-element.23), channel_id=1, source_target_pairs={{0,32},{32,64},{64,96},{96,128},{128,160},{160,192},{192,224},{1,3... | collective-permute-start | bytes 140408 | tf_op jit(solution)/shard_map/ppermute | solution.py:36
  72.7 19.9 %collective-permute-start.7 = (f32[5,1,18,130]{3,2,1,0:T(8,128)S(1)}, f32[5,1,18,130]{3,2,1,0:T(8,128)S(1)}, u32[]{:S(2)}, u32[]{:S(2)}) collective-permute-start(f32[5,1,18,130]{3,2,1,0:T(8,128)S(1)} %get-tuple-element.24), channel_id=1, source_target_pairs={{32,0},{64,32},{96,64},{128,96},{160,128},{192,160},{224,192},{33,... | collective-permute-start | bytes 140408 | tf_op jit(solution)/shard_map/ppermute | solution.py:37
  74.7 23.7 %collective-permute-start.13 = (f32[1,3,3,4,5,128]{5,4,3,2,1,0:T(8,128)S(1)}, f32[1,3,3,4,5,128]{5,4,3,2,1,0:T(8,128)S(1)}, u32[]{:S(2)}, u32[]{:S(2)}) collective-permute-start(f32[1,3,3,4,5,128]{5,4,3,2,1,0:T(8,128)S(1)} %bitcast.61), channel_id=1, source_target_pairs={{32,0},{64,32},{96,64},{128,96},{160,128},{192,160},{224,192},{33,... | collective-permute-start | bytes 276488 | tf_op jit(solution)/shard_map/ppermute | solution.py:25
  76.6 21.8 %collective-permute-start.12 = (f32[1,3,3,4,5,128]{5,4,3,2,1,0:T(8,128)S(1)}, f32[1,3,3,4,5,128]{5,4,3,2,1,0:T(8,128)S(1)}, u32[]{:S(2)}, u32[]{:S(2)}) collective-permute-start(f32[1,3,3,4,5,128]{5,4,3,2,1,0:T(8,128)S(1)} %bitcast.60), channel_id=1, source_target_pairs={{0,32},{32,64},{64,96},{96,128},{128,160},{160,192},{192,224},{1,3... | collective-permute-start | bytes 276488 | tf_op jit(solution)/shard_map/ppermute | solution.py:22
  92.8 11.4 %collective-permute-start.8 = (f32[5,8,1,130]{3,2,1,0:T(1,128)S(1)}, f32[5,8,1,130]{3,2,1,0:T(1,128)S(1)}, u32[]{:S(2)}, u32[]{:S(2)}) collective-permute-start(f32[5,8,1,130]{3,2,1,0:T(1,128)S(1)} %get-tuple-element.25), channel_id=1, source_target_pairs={{0,4},{4,8},{8,12},{12,16},{16,20},{20,24},{24,28},{1,5},{5,9},{9,... | collective-permute-start | bytes 62408 | tf_op jit(solution)/shard_map/ppermute | solution.py:36
  94.8 9.4 %collective-permute-start.9 = (f32[5,8,1,130]{3,2,1,0:T(1,128)S(1)}, f32[5,8,1,130]{3,2,1,0:T(1,128)S(1)}, u32[]{:S(2)}, u32[]{:S(2)}) collective-permute-start(f32[5,8,1,130]{3,2,1,0:T(1,128)S(1)} %get-tuple-element.26), channel_id=1, source_target_pairs={{4,0},{8,4},{12,8},{16,12},{20,16},{24,20},{28,24},{5,1},{9,5},{13... | collective-permute-start | bytes 62408 | tf_op jit(solution)/shard_map/ppermute | solution.py:37
  98.4 7.5 %collective-permute-start.14 = (f32[5,1,3,4,5,128]{5,4,3,2,1,0:T(8,128)S(1)}, f32[5,1,3,4,5,128]{5,4,3,2,1,0:T(8,128)S(1)}, u32[]{:S(2)}, u32[]{:S(2)}) collective-permute-start(f32[5,1,3,4,5,128]{5,4,3,2,1,0:T(8,128)S(1)} %get-tuple-element.27), channel_id=1, source_target_pairs={{0,4},{4,8},{8,12},{12,16},{16,20},{20,24},{24,28},{1,5},{5,9},{9,... | collective-permute-start | bytes 460808 | tf_op jit(solution)/shard_map/ppermute | solution.py:22
  100.4 19.5 %copy-start.3 = (f32[32,5,128]{2,1,0:T(8,128)S(1)}, f32[32,5,128]{2,1,0:T(8,128)}, u32[]{:S(2)}) copy-start(f32[32,5,128]{2,1,0:T(8,128)} %get-tuple-element.19) | copy-start | bytes 245764
  100.4 7.5 %collective-permute-start.15 = (f32[5,1,3,4,5,128]{5,4,3,2,1,0:T(8,128)S(1)}, f32[5,1,3,4,5,128]{5,4,3,2,1,0:T(8,128)S(1)}, u32[]{:S(2)}, u32[]{:S(2)}) collective-permute-start(f32[5,1,3,4,5,128]{5,4,3,2,1,0:T(8,128)S(1)} %get-tuple-element.28), channel_id=1, source_target_pairs={{4,0},{8,4},{12,8},{16,12},{20,16},{24,20},{28,24},{5,1},{9,5},{13... | collective-permute-start | bytes 460808 | tf_op jit(solution)/shard_map/ppermute | solution.py:25
  104.3 27.6 %copy-start.1 = (f32[5,8,16,128]{3,2,1,0:T(8,128)S(1)}, f32[5,8,16,128]{3,2,1,0:T(8,128)}, u32[]{:S(2)}) copy-start(f32[5,8,16,128]{3,2,1,0:T(8,128)} %param.7) | copy-start | bytes 983044
  104.3 27.6 %copy-start.4 = (f32[5]{0:T(128)S(1)}, f32[5]{0:T(128)}, u32[]{:S(2)}) copy-start(f32[5]{0:T(128)} %constant.63.clone) | copy-start | bytes 64
  108.0 25.4 %collective-permute-start.16 = (f32[5,5,1,4,5,128]{5,4,3,2,1,0:T(8,128)S(1)}, f32[5,5,1,4,5,128]{5,4,3,2,1,0:T(8,128)S(1)}, u32[]{:S(2)}, u32[]{:S(2)}) collective-permute-start(f32[5,5,1,4,5,128]{5,4,3,2,1,0:T(8,128)S(1)} %get-tuple-element.21), channel_id=1, source_target_pairs={{0,1},{1,2},{2,3},{4,5},{5,6},{6,7},{8,9},{9,10},{10,11},{12,13},{... | collective-permute-start | bytes 768008 | tf_op jit(solution)/shard_map/ppermute | solution.py:22
  110.9 22.4 %collective-permute-start.17 = (f32[5,5,1,4,5,128]{5,4,3,2,1,0:T(8,128)S(1)}, f32[5,5,1,4,5,128]{5,4,3,2,1,0:T(8,128)S(1)}, u32[]{:S(2)}, u32[]{:S(2)}) collective-permute-start(f32[5,5,1,4,5,128]{5,4,3,2,1,0:T(8,128)S(1)} %get-tuple-element.22), channel_id=1, source_target_pairs={{1,0},{2,1},{3,2},{5,4},{6,5},{7,6},{9,8},{10,9},{11,10},{13,12},{... | collective-permute-start | bytes 768008 | tf_op jit(solution)/shard_map/ppermute | solution.py:25
  114.0 14.5 %collective-permute-start.10 = (f32[5,8,16,1]{3,2,1,0:T(8,128)S(1)}, f32[5,8,16,1]{3,2,1,0:T(8,128)S(1)}, u32[]{:S(2)}, u32[]{:S(2)}) collective-permute-start(f32[5,8,16,1]{3,2,1,0:T(8,128)S(1)} %get-tuple-element.29), channel_id=1, source_target_pairs={{0,1},{1,2},{2,3},{4,5},{5,6},{6,7},{8,9},{9,10},{10,11},{12,13},{... | collective-permute-start | bytes 7688 | tf_op jit(solution)/shard_map/ppermute | solution.py:36
  116.9 15.0 %collective-permute-start.11 = (f32[5,8,16,1]{3,2,1,0:T(8,128)S(1)}, f32[5,8,16,1]{3,2,1,0:T(8,128)S(1)}, u32[]{:S(2)}, u32[]{:S(2)}) collective-permute-start(f32[5,8,16,1]{3,2,1,0:T(8,128)S(1)} %get-tuple-element.30), channel_id=1, source_target_pairs={{1,0},{2,1},{3,2},{5,4},{6,5},{7,6},{9,8},{10,9},{11,10},{13,12},{... | collective-permute-start | bytes 7688 | tf_op jit(solution)/shard_map/ppermute | solution.py:37

commit v5 on v4

--- a/solution.py
+++ b/solution.py
@@ -1,3 +1,5 @@
+import functools
+
 import jax
 import jax.numpy as jnp
 from jax import lax
@@ -114,13 +116,15 @@
 
 
 def coupling_kernel(
-    live_ref, dest_ref, table_ref, parcel_ref, pair_ref, pair_share_ref,
-    depth_ref, depth_share_ref, factor_ref, kept_ref, outbox_ref, deposit_ref,
+    live_ref, dest_ref, table_ref, parcel_ref, cell_ref, offset_ref, factor_ref,
+    kept_ref, outbox_ref, deposit_ref,
     weight_scr, depth_scr, spread_scr, updated_scr, count_scr, table_high_ref, table_low_ref,
+    *, span_y, span_z,
 ):
-    fields = parcel_ref.shape[1]
-    blocks = parcel_ref.shape[0]
+    fields = parcel_ref.shape[0]
+    blocks = parcel_ref.shape[1]
     lanes = parcel_ref.shape[2]
+    plane_size = span_y * span_z
     deposit_ref[...] = jnp.zeros(deposit_ref.shape, jnp.float32)
     table_high, table_low = split_bf16(table_ref[...])
     table_high_ref[...] = table_high
@@ -130,19 +134,39 @@
     depth_iota = lax.broadcasted_iota(jnp.int32, (DEPTH_ROWS, lanes), 0)
 
     def group(g, carry):
+        first = pl.multiple_of(g * GROUP, GROUP)
+        cells = cell_ref[pl.ds(first, GROUP), :]
+        offsets = offset_ref[:, pl.ds(first, GROUP), :]
+        parcels = parcel_ref[:, pl.ds(first, GROUP), :]
+        factors = factor_ref[:, pl.ds(first, GROUP), :]
+        flat = cells.astype(jnp.float32) + 0.5
+        cell_x = jnp.floor(flat * (1.0 / plane_size))
+        rest = flat - cell_x * plane_size
+        cell_y = jnp.floor(rest * (1.0 / span_z))
+        cell_z = (rest - cell_y * span_z).astype(jnp.int32)
+        cell_x = cell_x.astype(jnp.int32)
+        cell_y = cell_y.astype(jnp.int32)
+        step_sign = jnp.where(offsets >= 0.0, 1, -1).astype(jnp.int32)
+        far_share = jnp.abs(offsets)
+        near_share = 1.0 - far_share
         for j in range(GROUP):
-            b = g * GROUP + j
-            pair = pair_ref[b]
-            pair_share = pair_share_ref[b]
             weights = jnp.zeros((PAIR_LANES, lanes), jnp.float32)
-            for c in range(4):
-                weights = weights + jnp.where(pair_iota == pair[c:c + 1], pair_share[c:c + 1], 0.0)
+            for bit_x in range(2):
+                for bit_y in range(2):
+                    share = (far_share[0, j:j + 1] if bit_x else near_share[0, j:j + 1]) * (
+                        far_share[1, j:j + 1] if bit_y else near_share[1, j:j + 1]
+                    )
+                    target = (
+                        (cell_x[j:j + 1] + bit_x * step_sign[0, j:j + 1]) * span_y
+                        + cell_y[j:j + 1]
+                        + bit_y * step_sign[1, j:j + 1]
+                    )
+                    weights = weights + jnp.where(pair_iota == target, share, 0.0)
             weight_scr[:, j * lanes:(j + 1) * lanes] = weights
-            depth = depth_ref[b]
-            depth_share = depth_share_ref[b]
-            depth_weights = jnp.where(depth_iota == depth[0:1], depth_share[0:1], 0.0)
-            depth_weights = depth_weights + jnp.where(
-                depth_iota == depth[1:2], depth_share[1:2], 0.0
+            depth_weights = jnp.where(
+                depth_iota == cell_z[j:j + 1], near_share[2, j:j + 1], 0.0
+            ) + jnp.where(
+                depth_iota == cell_z[j:j + 1] + step_sign[2, j:j + 1], far_share[2, j:j + 1], 0.0
             )
             depth_scr[:, j * lanes:(j + 1) * lanes] = depth_weights
         weight_high, weight_low = split_bf16(weight_scr[...])
@@ -153,7 +177,7 @@
             + jnp.dot(table_low_ref[...], weight_high, preferred_element_type=jnp.float32)
         )
         for j in range(GROUP):
-            b = g * GROUP + j
+            b = first + j
             depth_weights = depth_scr[:, j * lanes:(j + 1) * lanes]
             sample = [
                 jnp.sum(
@@ -164,13 +188,11 @@
                 )
                 for f in range(fields)
             ]
-            current = parcel_ref[b]
-            factors = factor_ref[b]
-            mass = current[0:1]
-            heat = current[1:2]
-            keep_velocity = factors[0:1]
-            residual_heat = factors[1:2]
-            equilibrium = factors[2:3]
+            mass = parcels[0, j:j + 1]
+            heat = parcels[1, j:j + 1]
+            keep_velocity = factors[0, j:j + 1]
+            residual_heat = factors[1, j:j + 1]
+            equilibrium = factors[2, j:j + 1]
             x = 4.0 * (equilibrium - sample[0])
             soft = jnp.maximum(x, 0.0) + jnp.log1p(jnp.exp(-jnp.abs(x)))
             share = 1.0 - jnp.exp(-0.3 * soft)
@@ -178,12 +200,14 @@
             ambient = sample[1]
             adjusted = ambient + (heat - ambient) * residual_heat - PHASE_CHANGE_COST * share
             velocity = [
-                sample[2 + d] + (current[2 + d:3 + d] - sample[2 + d]) * keep_velocity
+                sample[2 + d] + (parcels[2 + d, j:j + 1] - sample[2 + d]) * keep_velocity
                 for d in range(3)
             ]
             enthalpy = 0.5 * mass * (heat - adjusted)
-            push = [mass * (current[2 + d:3 + d] - velocity[d]) for d in range(3)]
-            updated_scr[b] = jnp.concatenate([mass - evaporated, adjusted] + velocity, axis=0)
+            push = [mass * (parcels[2 + d, j:j + 1] - velocity[d]) for d in range(3)]
+            rows = [mass - evaporated, adjusted] + velocity
+            for f in range(fields):
+                updated_scr[f, pl.ds(b, 1), :] = rows[f]
             alive = b < live
             sources = [jnp.where(alive, s, 0.0) for s in [evaporated, enthalpy] + push]
             spread_scr[:, j * lanes:(j + 1) * lanes] = jnp.concatenate(
@@ -211,13 +235,13 @@
 
         @pl.when(alive & (d == 13))
         def _():
-            kept_ref[b] = updated_scr[b]
+            kept_ref[:, pl.ds(b, 1), :] = updated_scr[:, pl.ds(b, 1), :]
 
         rank = count_scr[d]
 
         @pl.when(alive & (d != 13) & (rank < SLOTS))
         def _():
-            outbox_ref[d * SLOTS + rank] = updated_scr[b]
+            outbox_ref[:, pl.ds(d * SLOTS + rank, 1), :] = updated_scr[:, pl.ds(b, 1), :]
             count_scr[d] = rank + 1
 
         return carry
@@ -237,70 +261,51 @@
     table = jnp.transpose(padded, (0, 3, 1, 2)).reshape(fields, span_z, pair_count)
     table = jnp.pad(table, ((0, 0), (0, DEPTH_ROWS - span_z), (0, PAIR_LANES - pair_count)))
     table = table.reshape(fields * DEPTH_ROWS, PAIR_LANES)
-    cell_x = parcel_cells // plane_size
-    cell_y = parcel_cells // span_z % span_y
-    cell_z = parcel_cells % span_z
-    step_sign = jnp.where(offsets >= 0.0, 1, -1).astype(jnp.int32)
-    far_share = jnp.abs(offsets)
-    near_share = 1.0 - far_share
-    pairs = []
-    pair_shares = []
-    for bit_x in range(2):
-        for bit_y in range(2):
-            pair_shares.append(
-                (far_share[:, 0] if bit_x else near_share[:, 0])
-                * (far_share[:, 1] if bit_y else near_share[:, 1])
-            )
-            pairs.append(
-                (cell_x + bit_x * step_sign[:, 0]) * span_y + cell_y + bit_y * step_sign[:, 1]
-            )
-    pairs = jnp.stack(pairs, axis=1)
-    pair_shares = jnp.stack(pair_shares, axis=1)
-    depths = jnp.stack([cell_z, cell_z + step_sign[:, 2]], axis=1)
-    depth_shares = jnp.stack([near_share[:, 2], far_share[:, 2]], axis=1)
-    relax_time = 0.4 * parcels[:, 0] ** (2.0 / 3.0)
+    parcel_rows = jnp.transpose(parcels, (1, 0, 2))
+    offset_rows = jnp.transpose(offsets, (1, 0, 2))
+    relax_time = 0.4 * parcel_rows[0] ** (2.0 / 3.0)
     factors = jnp.stack(
         [
             jnp.exp(-TIME_STEP / relax_time),
             jnp.exp(-TIME_STEP / (1.5 * relax_time)),
-            0.4 * jnp.exp(2.0 * (parcels[:, 1] - 1.0)),
+            0.4 * jnp.exp(2.0 * (parcel_rows[1] - 1.0)),
         ],
-        axis=1,
+        axis=0,
     )
     vmem = pl.BlockSpec(memory_space=pltpu.VMEM)
     smem = pl.BlockSpec(memory_space=pltpu.SMEM)
     lanes = GROUP * block_parcels
-    kept, outbox, deposit_rows = pl.pallas_call(
-        coupling_kernel,
+    kept_rows, outbox_rows, deposit_rows = pl.pallas_call(
+        functools.partial(coupling_kernel, span_y=span_y, span_z=span_z),
         out_shape=(
-            jax.ShapeDtypeStruct(parcels.shape, jnp.float32),
-            jax.ShapeDtypeStruct((27 * SLOTS,) + parcels.shape[1:], jnp.float32),
+            jax.ShapeDtypeStruct(parcel_rows.shape, jnp.float32),
+            jax.ShapeDtypeStruct((parcel_fields, 27 * SLOTS, block_parcels), jnp.float32),
             jax.ShapeDtypeStruct((fields * DEPTH_ROWS, PAIR_LANES), jnp.float32),
         ),
-        in_specs=[smem, smem] + [vmem] * 7,
+        in_specs=[smem, smem] + [vmem] * 5,
         out_specs=(vmem, vmem, vmem),
         scratch_shapes=[
             pltpu.VMEM((PAIR_LANES, lanes), jnp.float32),
             pltpu.VMEM((DEPTH_ROWS, lanes), jnp.float32),
             pltpu.VMEM((fields * DEPTH_ROWS, lanes), jnp.float32),
-            pltpu.VMEM(parcels.shape, jnp.float32),
+            pltpu.VMEM(parcel_rows.shape, jnp.float32),
             pltpu.SMEM((32,), jnp.int32),
             pltpu.VMEM(table.shape, jnp.bfloat16),
             pltpu.VMEM(table.shape, jnp.bfloat16),
         ],
-    )(
-        live_blocks, destination, table, parcels, pairs, pair_shares, depths,
-        depth_shares, factors,
-    )
+    )(live_blocks, destination, table, parcel_rows, parcel_cells, offset_rows, factors)
+    kept = jnp.transpose(kept_rows, (1, 0, 2))
     deposit = deposit_rows.reshape(fields, DEPTH_ROWS, PAIR_LANES)[:, :span_z, :pair_count]
     deposit = jnp.transpose(deposit.reshape(fields, span_z, span_x, span_y), (0, 2, 3, 1))
     cell_sources = fold_ghosts(deposit, (("gx", 1), ("gy", 2), ("gz", 3)))
     kappa = jnp.array(DIFFUSION, jnp.float32)[:, None, None, None]
     gas_next = gas_state + kappa * laplacian(padded) + COUPLING * cell_sources
-    outbox = outbox.reshape((3, 3, 3, SLOTS) + parcels.shape[1:])
-    widened = with_halo(outbox, (("gx", 0), ("gy", 1), ("gz", 2)), 1)
-    arrived_boxes = widened[0::2, 0::2, 0::2]
-    arrived = arrived_boxes.reshape((27 * SLOTS,) + parcels.shape[1:])
+    outbox = outbox_rows.reshape((parcel_fields, 3, 3, 3, SLOTS, block_parcels))
+    widened = with_halo(outbox, (("gx", 1), ("gy", 2), ("gz", 3)), 1)
+    arrived_boxes = widened[:, 0::2, 0::2, 0::2]
+    arrived = jnp.transpose(
+        arrived_boxes.reshape((parcel_fields, 27 * SLOTS, block_parcels)), (1, 0, 2)
+    )
     return (gas_next, kept, arrived)
 
 

time: 137 us -> 126 us (0.920)
  starting transfers between devices: 67 us -> 57.9 us
  other arithmetic: 8.94 us -> 5.21 us
  waiting for transfers between devices: 21.9 us -> 25.1 us
    ppermute x6, waiting for transfers between devices: 2.78 us -> 11.8 us  [with_halo(): lax.ppermute(lax.slice_in_dim(block, 0, width, axis=dim), axis, backward)]
    ppermute x6, starting transfers between devices: 29.8 us -> 21.4 us  [with_halo(): lax.ppermute(lax.slice_in_dim(block, block.shape[dim] - width, None, axis...]
    ppermute x3, waiting for transfers between devices: 7.92 us -> 2.12 us  [fold_ghosts(): lax.ppermute(lax.slice_in_dim(block, span - 1, span, axis=dim), axis, for...]
    ppermute x3, waiting for transfers between devices: 9.56 us -> 4.33 us  [fold_ghosts(): lax.ppermute(lax.slice_in_dim(block, 0, 1, axis=dim), axis, backward)]
    ppermute x6, waiting for transfers between devices: 1.62 us -> 6.85 us  [with_halo(): lax.ppermute(lax.slice_in_dim(block, block.shape[dim] - width, None, axis...]
    ppermute x3, starting transfers between devices: 11.9 us -> 16.3 us  [fold_ghosts(): lax.ppermute(lax.slice_in_dim(block, span - 1, span, axis=dim), axis, for...]
    ppermute x3, starting transfers between devices: 8.45 us -> 5.76 us  [fold_ghosts(): lax.ppermute(lax.slice_in_dim(block, 0, 1, axis=dim), axis, backward)]
    ppermute x6, starting transfers between devices: 16.9 us -> 14.5 us  [with_halo(): lax.ppermute(lax.slice_in_dim(block, 0, width, axis=dim), axis, backward)]
  transfers between devices with their start and end apart: 18 -> 18, of which waited for: 6 -> 9; matrix products, arithmetic and copies ran while one was open for 9% -> 5% of each run, Pallas kernels for 0% -> 0%
where the time goes in v5:
time: 126 us; the launch traced here: 124 us
  starting transfers between devices  57.9 us (46%)
  waiting for transfers between devices  25.1 us (20%)
  Pallas kernels  20.6 us (16%)
  local copies, waits for them, and re-layouts  13.1 us (10%)
  other arithmetic  5.21 us (4%)
  between operations  1.66 us (1%)
    ppermute x6, starting transfers between devices, with_halo(): lax.ppermute(lax.slice_in_dim(block, block.shape[dim] - width, None, axis...  21.4 us
    pallas_call x1, Pallas kernels, local(): pl.pallas_call(functools.partial(coupling_kernel, span_y=span_y, span_z=s...  20.6 us
    ppermute x3, starting transfers between devices, fold_ghosts(): lax.ppermute(lax.slice_in_dim(block, span - 1, span, axis=dim), axis, for...  16.3 us
    ppermute x6, starting transfers between devices, with_halo(): lax.ppermute(lax.slice_in_dim(block, 0, width, axis=dim), axis, backward)  14.5 us
    ppermute x6, waiting for transfers between devices, with_halo(): lax.ppermute(lax.slice_in_dim(block, 0, width, axis=dim), axis, backward)  11.8 us
    ppermute x6, waiting for transfers between devices, with_halo(): lax.ppermute(lax.slice_in_dim(block, block.shape[dim] - width, None, axis...  6.85 us
    ppermute x3, starting transfers between devices, fold_ghosts(): lax.ppermute(lax.slice_in_dim(block, 0, 1, axis=dim), axis, backward)  5.76 us
    unnamed x16, local copies, waits for them, and re-layouts  5.08 us
  transfers between devices with their start and end apart: 18, of which 9 were waited for; matrix products, arithmetic and copies ran while one was open for 5% of the time, Pallas kernels for 0%

profile of v5, /device:TPU:58, one launch (start us, length us, event | category | flops | bytes accessed | tf_op | source)
XLA Modules:
  0.0 123.5 jit_solution(1461614855182522246)
XLA Ops:
  1.4 7.8 %collective-permute-start.1 = (f32[5,1,16,128]{3,2,1,0:T(8,128)S(1)}, f32[5,1,16,128]{3,2,1,0:T(8,128)S(1)}, u32[]{:S(2)}, u32[]{:S(2)}) collective-permute-start(f32[5,1,16,128]{3,2,1,0:T(8,128)S(1)} %get-tuple-element.24), channel_id=1, source_target_pairs={{0,32},{32,64},{64,96},{96,128},{128,160},{160,192},{192,224},{1,3... | collective-permute-start | bytes 122888 | tf_op jit(solution)/shard_map/ppermute | solution.py:24
  9.3 1.9 %collective-permute-start = (f32[5,1,16,128]{3,2,1,0:T(8,128)S(1)}, f32[5,1,16,128]{3,2,1,0:T(8,128)S(1)}, u32[]{:S(2)}, u32[]{:S(2)}) collective-permute-start(f32[5,1,16,128]{3,2,1,0:T(8,128)S(1)} %get-tuple-element.23), channel_id=1, source_target_pairs={{32,0},{64,32},{96,64},{128,96},{160,128},{192,160},{224,192},{33,... | collective-permute-start | bytes 122888 | tf_op jit(solution)/shard_map/ppermute | solution.py:27
  12.2 9.0 %collective-permute-done = f32[5,1,16,128]{3,2,1,0:T(8,128)S(1)} collective-permute-done((f32[5,1,16,128]{3,2,1,0:T(8,128)S(1)}, f32[5,1,16,128]{3,2,1,0:T(8,128)S(1)}, u32[]{:S(2)}, u32[]{:S(2)}) %collective-permute-start) | collective-permute-done | bytes 40992 | tf_op jit(solution)/shard_map/ppermute | solution.py:27
  21.3 1.9 %collective-permute-start.2 = (f32[5,10,1,128]{3,2,1,0:T(1,128)S(1)}, f32[5,10,1,128]{3,2,1,0:T(1,128)S(1)}, u32[]{:S(2)}, u32[]{:S(2)}) collective-permute-start(f32[5,10,1,128]{3,2,1,0:T(1,128)S(1)} %get-tuple-element.22), channel_id=1, source_target_pairs={{4,0},{8,4},{12,8},{16,12},{20,16},{24,20},{28,24},{5,1},{9,5},{13... | collective-permute-start | bytes 76808 | tf_op jit(solution)/shard_map/ppermute | solution.py:27
  23.2 2.4 %collective-permute-start.3 = (f32[5,10,1,128]{3,2,1,0:T(1,128)S(1)}, f32[5,10,1,128]{3,2,1,0:T(1,128)S(1)}, u32[]{:S(2)}, u32[]{:S(2)}) collective-permute-start(f32[5,10,1,128]{3,2,1,0:T(1,128)S(1)} %get-tuple-element.21), channel_id=1, source_target_pairs={{0,4},{4,8},{8,12},{12,16},{16,20},{20,24},{24,28},{1,5},{5,9},{9,... | collective-permute-start | bytes 76808 | tf_op jit(solution)/shard_map/ppermute | solution.py:24
  26.4 1.9 %collective-permute-done.3 = f32[5,10,1,128]{3,2,1,0:T(1,128)S(1)} collective-permute-done((f32[5,10,1,128]{3,2,1,0:T(1,128)S(1)}, f32[5,10,1,128]{3,2,1,0:T(1,128)S(1)}, u32[]{:S(2)}, u32[]{:S(2)}) %collective-permute-start.3) | collective-permute-done | bytes 25632 | tf_op jit(solution)/shard_map/ppermute | solution.py:24
  29.1 2.9 %collective-permute-start.4 = (f32[5,10,18,1]{2,3,1,0:T(1,128)S(1)}, f32[5,10,18,1]{2,3,1,0:T(1,128)S(1)}, u32[]{:S(2)}, u32[]{:S(2)}) collective-permute-start(f32[5,10,18,1]{2,3,1,0:T(1,128)S(1)} %copy.14), channel_id=1, source_target_pairs={{1,0},{2,1},{3,2},{5,4},{6,5},{7,6},{9,8},{10,9},{11,10},{13,12},{... | collective-permute-start | bytes 10808 | tf_op jit(solution)/shard_map/ppermute | solution.py:27
  32.4 2.9 %collective-permute-start.5 = (f32[5,10,18,1]{2,3,1,0:T(1,128)S(1)}, f32[5,10,18,1]{2,3,1,0:T(1,128)S(1)}, u32[]{:S(2)}, u32[]{:S(2)}) collective-permute-start(f32[5,10,18,1]{2,3,1,0:T(1,128)S(1)} %copy.16), channel_id=1, source_target_pairs={{0,1},{1,2},{2,3},{4,5},{5,6},{6,7},{8,9},{9,10},{10,11},{12,13},{... | collective-permute-start | bytes 10808 | tf_op jit(solution)/shard_map/ppermute | solution.py:24
  37.0 1.1 collective-permute-done.5
  39.3 1.1 reshape.25
  40.4 1.6 %copy.23 = f32[5,130,180]{2,1,0:T(8,128)S(1)} copy(f32[5,130,180]{1,2,0:T(8,128)} %reshape.25) | data formatting | bytes 936000
  42.8 20.6 %shard_map.94 = (f32[5,32,128]{2,1,0:T(8,128)}, f32[5,108,128]{2,1,0:T(8,128)}, f32[680,256]{1,0:T(8,128)}) custom-call(s32[1]{0:T(128)S(6)} %copy.28.live_ref, s32[32]{0:T(128)} %dest_ref.1, f32[680,256]{1,0:T(8,128)} %bitcast.16, f32[5,32,128]{2,1,0:T(8,128)} %bitcast.20, s32[32,128]{1,0:T(8,128)} %cell_ref.1, f32[3,32,128]{2,1,0:T(8,128)} %bitcast.21, ...), custom_call_target="tpu_custom_call" | custom-call | tf_op jit(solution)/shard_map/pallas_call | solution.py:278
  63.4 2.4 %copy.22 = f32[5,130,180]{1,2,0:T(8,128)} copy(f32[5,130,180]{2,1,0:T(8,128)} %bitcast.17) | data formatting | bytes 936000
  65.8 1.3 %reshape.28 = f32[5,130,10,18]{1,3,2,0:T(8,128)S(1)} reshape(f32[5,130,180]{1,2,0:T(8,128)} %copy.22) | data formatting | bytes 936000 | tf_op jit(solution)/shard_map/reshape | solution.py:299
  67.9 1.9 %collective-permute-start.7 = (f32[5,1,18,130]{3,2,1,0:T(8,128)}, f32[5,1,18,130]{3,2,1,0:T(8,128)}, u32[]{:S(2)}, u32[]{:S(2)}) collective-permute-start(f32[5,1,18,130]{3,2,1,0:T(8,128)} %get-tuple-element.10), channel_id=1, source_target_pairs={{32,0},{64,32},{96,64},{128,96},{160,128},{192,160},{224,192},{33,... | collective-permute-start | bytes 140408 | tf_op jit(solution)/shard_map/ppermute | solution.py:39
  69.8 9.9 %collective-permute-start.6 = (f32[5,1,18,130]{3,2,1,0:T(8,128)}, f32[5,1,18,130]{3,2,1,0:T(8,128)}, u32[]{:S(2)}, u32[]{:S(2)}) collective-permute-start(f32[5,1,18,130]{3,2,1,0:T(8,128)} %get-tuple-element.9), channel_id=1, source_target_pairs={{0,32},{32,64},{64,96},{96,128},{128,160},{160,192},{192,224},{1,3... | collective-permute-start | bytes 140408 | tf_op jit(solution)/shard_map/ppermute | solution.py:38
  79.9 1.9 %collective-permute-start.12 = (f32[5,1,3,3,4,128]{5,4,3,2,1,0:T(4,128)S(1)}, f32[5,1,3,3,4,128]{5,4,3,2,1,0:T(4,128)S(1)}, u32[]{:S(2)}, u32[]{:S(2)}) collective-permute-start(f32[5,1,3,3,4,128]{5,4,3,2,1,0:T(4,128)S(1)} %get-tuple-element.26), channel_id=1, source_target_pairs={{0,32},{32,64},{64,96},{96,128},{128,160},{160,192},{192,224},{1,3... | collective-permute-start | bytes 276488 | tf_op jit(solution)/shard_map/ppermute | solution.py:24
  81.8 3.9 %collective-permute-start.13 = (f32[5,1,3,3,4,128]{5,4,3,2,1,0:T(4,128)S(1)}, f32[5,1,3,3,4,128]{5,4,3,2,1,0:T(4,128)S(1)}, u32[]{:S(2)}, u32[]{:S(2)}) collective-permute-start(f32[5,1,3,3,4,128]{5,4,3,2,1,0:T(4,128)S(1)} %get-tuple-element.25), channel_id=1, source_target_pairs={{32,0},{64,32},{96,64},{128,96},{160,128},{192,160},{224,192},{33,... | collective-permute-start | bytes 276488 | tf_op jit(solution)/shard_map/ppermute | solution.py:27
  86.0 1.0 fusion
  87.1 1.9 %collective-permute-start.9 = (f32[5,8,1,130]{3,2,1,0:T(1,128)S(1)}, f32[5,8,1,130]{3,2,1,0:T(1,128)S(1)}, u32[]{:S(2)}, u32[]{:S(2)}) collective-permute-start(f32[5,8,1,130]{3,2,1,0:T(1,128)S(1)} %get-tuple-element.12), channel_id=1, source_target_pairs={{4,0},{8,4},{12,8},{16,12},{20,16},{24,20},{28,24},{5,1},{9,5},{13... | collective-permute-start | bytes 62408 | tf_op jit(solution)/shard_map/ppermute | solution.py:39
  89.0 2.4 %collective-permute-start.8 = (f32[5,8,1,130]{3,2,1,0:T(1,128)S(1)}, f32[5,8,1,130]{3,2,1,0:T(1,128)S(1)}, u32[]{:S(2)}, u32[]{:S(2)}) collective-permute-start(f32[5,8,1,130]{3,2,1,0:T(1,128)S(1)} %get-tuple-element.11), channel_id=1, source_target_pairs={{0,4},{4,8},{8,12},{12,16},{16,20},{20,24},{24,28},{1,5},{5,9},{9,... | collective-permute-start | bytes 62408 | tf_op jit(solution)/shard_map/ppermute | solution.py:38
  91.5 2.8 %collective-permute-done.13 = f32[5,1,3,3,4,128]{5,4,3,2,1,0:T(4,128)S(1)} collective-permute-done((f32[5,1,3,3,4,128]{5,4,3,2,1,0:T(4,128)S(1)}, f32[5,1,3,3,4,128]{5,4,3,2,1,0:T(4,128)S(1)}, u32[]{:S(2)}, u32[]{:S(2)}) %collective-permute-start.13) | collective-permute-done | bytes 92192 | tf_op jit(solution)/shard_map/ppermute | solution.py:27
  94.4 1.9 %collective-permute-start.15 = (f32[5,5,1,3,4,128]{5,4,3,2,1,0:T(4,128)S(1)}, f32[5,5,1,3,4,128]{5,4,3,2,1,0:T(4,128)S(1)}, u32[]{:S(2)}, u32[]{:S(2)}) collective-permute-start(f32[5,5,1,3,4,128]{5,4,3,2,1,0:T(4,128)S(1)} %get-tuple-element.20), channel_id=1, source_target_pairs={{4,0},{8,4},{12,8},{16,12},{20,16},{24,20},{28,24},{5,1},{9,5},{13... | collective-permute-start | bytes 460808 | tf_op jit(solution)/shard_map/ppermute | solution.py:27
  96.3 2.4 %collective-permute-start.14 = (f32[5,5,1,3,4,128]{5,4,3,2,1,0:T(4,128)S(1)}, f32[5,5,1,3,4,128]{5,4,3,2,1,0:T(4,128)S(1)}, u32[]{:S(2)}, u32[]{:S(2)}) collective-permute-start(f32[5,5,1,3,4,128]{5,4,3,2,1,0:T(4,128)S(1)} %get-tuple-element.19), channel_id=1, source_target_pairs={{0,4},{4,8},{8,12},{12,16},{16,20},{20,24},{24,28},{1,5},{5,9},{9,... | collective-permute-start | bytes 460808 | tf_op jit(solution)/shard_map/ppermute | solution.py:24
  99.0 3.8 %collective-permute-done.14 = f32[5,5,1,3,4,128]{5,4,3,2,1,0:T(4,128)S(1)} collective-permute-done((f32[5,5,1,3,4,128]{5,4,3,2,1,0:T(4,128)S(1)}, f32[5,5,1,3,4,128]{5,4,3,2,1,0:T(4,128)S(1)}, u32[]{:S(2)}, u32[]{:S(2)}) %collective-permute-start.14) | collective-permute-done | bytes 153632 | tf_op jit(solution)/shard_map/ppermute | solution.py:24
  102.9 1.9 %collective-permute-start.17 = (f32[5,5,5,1,4,128]{5,4,3,2,1,0:T(4,128)S(1)}, f32[5,5,5,1,4,128]{5,4,3,2,1,0:T(4,128)S(1)}, u32[]{:S(2)}, u32[]{:S(2)}) collective-permute-start(f32[5,5,5,1,4,128]{5,4,3,2,1,0:T(4,128)S(1)} %get-tuple-element.14), channel_id=1, source_target_pairs={{1,0},{2,1},{3,2},{5,4},{6,5},{7,6},{9,8},{10,9},{11,10},{13,12},{... | collective-permute-start | bytes 768008 | tf_op jit(solution)/shard_map/ppermute | solution.py:27
  104.9 3.9 %collective-permute-start.16 = (f32[5,5,5,1,4,128]{5,4,3,2,1,0:T(4,128)S(1)}, f32[5,5,5,1,4,128]{5,4,3,2,1,0:T(4,128)S(1)}, u32[]{:S(2)}, u32[]{:S(2)}) collective-permute-start(f32[5,5,5,1,4,128]{5,4,3,2,1,0:T(4,128)S(1)} %get-tuple-element.13), channel_id=1, source_target_pairs={{0,1},{1,2},{2,3},{4,5},{5,6},{6,7},{8,9},{9,10},{10,11},{12,13},{... | collective-permute-start | bytes 768008 | tf_op jit(solution)/shard_map/ppermute | solution.py:24
  109.0 1.9 %collective-permute-start.11 = (f32[5,8,16,1]{3,2,1,0:T(8,128)S(1)}, f32[5,8,16,1]{3,2,1,0:T(8,128)S(1)}, u32[]{:S(2)}, u32[]{:S(2)}) collective-permute-start(f32[5,8,16,1]{3,2,1,0:T(8,128)S(1)} %get-tuple-element.16), channel_id=1, source_target_pairs={{1,0},{2,1},{3,2},{5,4},{6,5},{7,6},{9,8},{10,9},{11,10},{13,12},{... | collective-permute-start | bytes 7688 | tf_op jit(solution)/shard_map/ppermute | solution.py:39
  110.9 3.9 %collective-permute-start.10 = (f32[5,8,16,1]{3,2,1,0:T(8,128)S(1)}, f32[5,8,16,1]{3,2,1,0:T(8,128)S(1)}, u32[]{:S(2)}, u32[]{:S(2)}) collective-permute-start(f32[5,8,16,1]{3,2,1,0:T(8,128)S(1)} %get-tuple-element.15), channel_id=1, source_target_pairs={{0,1},{1,2},{2,3},{4,5},{5,6},{6,7},{8,9},{9,10},{10,11},{12,13},{... | collective-permute-start | bytes 7688 | tf_op jit(solution)/shard_map/ppermute | solution.py:38
  114.8 4.3 %collective-permute-done.11 = f32[5,8,16,1]{3,2,1,0:T(8,128)S(1)} collective-permute-done((f32[5,8,16,1]{3,2,1,0:T(8,128)S(1)}, f32[5,8,16,1]{3,2,1,0:T(8,128)S(1)}, u32[]{:S(2)}, u32[]{:S(2)}) %collective-permute-start.11) | collective-permute-done | bytes 2592 | tf_op jit(solution)/shard_map/ppermute | solution.py:39
  119.1 1.9 %collective-permute-done.10 = f32[5,8,16,1]{3,2,1,0:T(8,128)S(1)} collective-permute-done((f32[5,8,16,1]{3,2,1,0:T(8,128)S(1)}, f32[5,8,16,1]{3,2,1,0:T(8,128)S(1)}, u32[]{:S(2)}, u32[]{:S(2)}) %collective-permute-start.10) | collective-permute-done | bytes 2592 | tf_op jit(solution)/shard_map/ppermute | solution.py:38
  121.0 1.3 %fusion.4 = f32[5,8,16,128]{3,2,1,0:T(8,128)} fusion(f32[5,8,16,130]{3,2,1,0:T(8,128)S(1)} %fusion.1, f32[5,8,16,128]{3,2,1,0:T(8,128)S(1)} %copy-done, f32[5,10,18,1]{3,2,1,0:T(8,128)S(1)} %copy.17, f32[5,10,1,128]{3,2,1,0:T(1,128)S(1)} %collective-permute-done.2, f32[5,10,16,128]{3,2,1,0:T(8,128)S(1)} %constant_dynamic-update-slice_fusion, ...), kind=kLoop, calls=%fused_computation.10 | loop fusion | flops 1884160 | bytes 1538100 | tf_op jit(solution)/shard_map/add | solution.py:302
  (50 shorter events, 9.8 us)
Async XLA Ops:
  1.4 9.8 %collective-permute-start.1 = (f32[5,1,16,128]{3,2,1,0:T(8,128)S(1)}, f32[5,1,16,128]{3,2,1,0:T(8,128)S(1)}, u32[]{:S(2)}, u32[]{:S(2)}) collective-permute-start(f32[5,1,16,128]{3,2,1,0:T(8,128)S(1)} %get-tuple-element.24), channel_id=1, source_target_pairs={{0,32},{32,64},{64,96},{96,128},{128,160},{160,192},{192,224},{1,3... | collective-permute-start | bytes 122888 | tf_op jit(solution)/shard_map/ppermute | solution.py:24
  9.3 11.9 %collective-permute-start = (f32[5,1,16,128]{3,2,1,0:T(8,128)S(1)}, f32[5,1,16,128]{3,2,1,0:T(8,128)S(1)}, u32[]{:S(2)}, u32[]{:S(2)}) collective-permute-start(f32[5,1,16,128]{3,2,1,0:T(8,128)S(1)} %get-tuple-element.23), channel_id=1, source_target_pairs={{32,0},{64,32},{96,64},{128,96},{160,128},{192,160},{224,192},{33,... | collective-permute-start | bytes 122888 | tf_op jit(solution)/shard_map/ppermute | solution.py:27
  21.2 5.2 %copy-start.2 = (f32[5,1,16,128]{3,2,1,0:T(8,128)}, f32[5,1,16,128]{3,2,1,0:T(8,128)S(1)}, u32[]{:S(2)}) copy-start(f32[5,1,16,128]{3,2,1,0:T(8,128)S(1)} %collective-permute-done) | copy-start | bytes 122884
  21.3 5.1 %collective-permute-start.2 = (f32[5,10,1,128]{3,2,1,0:T(1,128)S(1)}, f32[5,10,1,128]{3,2,1,0:T(1,128)S(1)}, u32[]{:S(2)}, u32[]{:S(2)}) collective-permute-start(f32[5,10,1,128]{3,2,1,0:T(1,128)S(1)} %get-tuple-element.22), channel_id=1, source_target_pairs={{4,0},{8,4},{12,8},{16,12},{20,16},{24,20},{28,24},{5,1},{9,5},{13... | collective-permute-start | bytes 76808 | tf_op jit(solution)/shard_map/ppermute | solution.py:27
  23.2 5.2 %collective-permute-start.3 = (f32[5,10,1,128]{3,2,1,0:T(1,128)S(1)}, f32[5,10,1,128]{3,2,1,0:T(1,128)S(1)}, u32[]{:S(2)}, u32[]{:S(2)}) collective-permute-start(f32[5,10,1,128]{3,2,1,0:T(1,128)S(1)} %get-tuple-element.21), channel_id=1, source_target_pairs={{0,4},{4,8},{8,12},{12,16},{16,20},{20,24},{24,28},{1,5},{5,9},{9,... | collective-permute-start | bytes 76808 | tf_op jit(solution)/shard_map/ppermute | solution.py:24
  29.1 7.5 %collective-permute-start.4 = (f32[5,10,18,1]{2,3,1,0:T(1,128)S(1)}, f32[5,10,18,1]{2,3,1,0:T(1,128)S(1)}, u32[]{:S(2)}, u32[]{:S(2)}) collective-permute-start(f32[5,10,18,1]{2,3,1,0:T(1,128)S(1)} %copy.14), channel_id=1, source_target_pairs={{1,0},{2,1},{3,2},{5,4},{6,5},{7,6},{9,8},{10,9},{11,10},{13,12},{... | collective-permute-start | bytes 10808 | tf_op jit(solution)/shard_map/ppermute | solution.py:27
  32.4 5.7 %collective-permute-start.5 = (f32[5,10,18,1]{2,3,1,0:T(1,128)S(1)}, f32[5,10,18,1]{2,3,1,0:T(1,128)S(1)}, u32[]{:S(2)}, u32[]{:S(2)}) collective-permute-start(f32[5,10,18,1]{2,3,1,0:T(1,128)S(1)} %copy.16), channel_id=1, source_target_pairs={{0,1},{1,2},{2,3},{4,5},{5,6},{6,7},{8,9},{9,10},{10,11},{12,13},{... | collective-permute-start | bytes 10808 | tf_op jit(solution)/shard_map/ppermute | solution.py:24
  65.8 13.9 %copy-start.1 = (f32[5,108,128]{2,1,0:T(8,128)S(1)}, f32[5,108,128]{2,1,0:T(8,128)}, u32[]{:S(2)}) copy-start(f32[5,108,128]{2,1,0:T(8,128)} %get-tuple-element.8) | copy-start | bytes 829444
  67.9 17.9 %collective-permute-start.7 = (f32[5,1,18,130]{3,2,1,0:T(8,128)}, f32[5,1,18,130]{3,2,1,0:T(8,128)}, u32[]{:S(2)}, u32[]{:S(2)}) collective-permute-start(f32[5,1,18,130]{3,2,1,0:T(8,128)} %get-tuple-element.10), channel_id=1, source_target_pairs={{32,0},{64,32},{96,64},{128,96},{160,128},{192,160},{224,192},{33,... | collective-permute-start | bytes 140408 | tf_op jit(solution)/shard_map/ppermute | solution.py:39
  69.8 16.2 %collective-permute-start.6 = (f32[5,1,18,130]{3,2,1,0:T(8,128)}, f32[5,1,18,130]{3,2,1,0:T(8,128)}, u32[]{:S(2)}, u32[]{:S(2)}) collective-permute-start(f32[5,1,18,130]{3,2,1,0:T(8,128)} %get-tuple-element.9), channel_id=1, source_target_pairs={{0,32},{32,64},{64,96},{96,128},{128,160},{160,192},{192,224},{1,3... | collective-permute-start | bytes 140408 | tf_op jit(solution)/shard_map/ppermute | solution.py:38
  79.9 11.6 %collective-permute-start.12 = (f32[5,1,3,3,4,128]{5,4,3,2,1,0:T(4,128)S(1)}, f32[5,1,3,3,4,128]{5,4,3,2,1,0:T(4,128)S(1)}, u32[]{:S(2)}, u32[]{:S(2)}) collective-permute-start(f32[5,1,3,3,4,128]{5,4,3,2,1,0:T(4,128)S(1)} %get-tuple-element.26), channel_id=1, source_target_pairs={{0,32},{32,64},{64,96},{96,128},{128,160},{160,192},{192,224},{1,3... | collective-permute-start | bytes 276488 | tf_op jit(solution)/shard_map/ppermute | solution.py:24
  81.8 12.5 %collective-permute-start.13 = (f32[5,1,3,3,4,128]{5,4,3,2,1,0:T(4,128)S(1)}, f32[5,1,3,3,4,128]{5,4,3,2,1,0:T(4,128)S(1)}, u32[]{:S(2)}, u32[]{:S(2)}) collective-permute-start(f32[5,1,3,3,4,128]{5,4,3,2,1,0:T(4,128)S(1)} %get-tuple-element.25), channel_id=1, source_target_pairs={{32,0},{64,32},{96,64},{128,96},{160,128},{192,160},{224,192},{33,... | collective-permute-start | bytes 276488 | tf_op jit(solution)/shard_map/ppermute | solution.py:27
  87.1 11.6 %collective-permute-start.9 = (f32[5,8,1,130]{3,2,1,0:T(1,128)S(1)}, f32[5,8,1,130]{3,2,1,0:T(1,128)S(1)}, u32[]{:S(2)}, u32[]{:S(2)}) collective-permute-start(f32[5,8,1,130]{3,2,1,0:T(1,128)S(1)} %get-tuple-element.12), channel_id=1, source_target_pairs={{4,0},{8,4},{12,8},{16,12},{20,16},{24,20},{28,24},{5,1},{9,5},{13... | collective-permute-start | bytes 62408 | tf_op jit(solution)/shard_map/ppermute | solution.py:39
  89.0 9.7 %collective-permute-start.8 = (f32[5,8,1,130]{3,2,1,0:T(1,128)S(1)}, f32[5,8,1,130]{3,2,1,0:T(1,128)S(1)}, u32[]{:S(2)}, u32[]{:S(2)}) collective-permute-start(f32[5,8,1,130]{3,2,1,0:T(1,128)S(1)} %get-tuple-element.11), channel_id=1, source_target_pairs={{0,4},{4,8},{8,12},{12,16},{16,20},{20,24},{24,28},{1,5},{5,9},{9,... | collective-permute-start | bytes 62408 | tf_op jit(solution)/shard_map/ppermute | solution.py:38
  94.4 4.6 %collective-permute-start.15 = (f32[5,5,1,3,4,128]{5,4,3,2,1,0:T(4,128)S(1)}, f32[5,5,1,3,4,128]{5,4,3,2,1,0:T(4,128)S(1)}, u32[]{:S(2)}, u32[]{:S(2)}) collective-permute-start(f32[5,5,1,3,4,128]{5,4,3,2,1,0:T(4,128)S(1)} %get-tuple-element.20), channel_id=1, source_target_pairs={{4,0},{8,4},{12,8},{16,12},{20,16},{24,20},{28,24},{5,1},{9,5},{13... | collective-permute-start | bytes 460808 | tf_op jit(solution)/shard_map/ppermute | solution.py:27
  96.3 6.5 %collective-permute-start.14 = (f32[5,5,1,3,4,128]{5,4,3,2,1,0:T(4,128)S(1)}, f32[5,5,1,3,4,128]{5,4,3,2,1,0:T(4,128)S(1)}, u32[]{:S(2)}, u32[]{:S(2)}) collective-permute-start(f32[5,5,1,3,4,128]{5,4,3,2,1,0:T(4,128)S(1)} %get-tuple-element.19), channel_id=1, source_target_pairs={{0,4},{4,8},{8,12},{12,16},{16,20},{20,24},{24,28},{1,5},{5,9},{9,... | collective-permute-start | bytes 460808 | tf_op jit(solution)/shard_map/ppermute | solution.py:24
  98.9 22.2 %copy-start = (f32[5,8,16,128]{3,2,1,0:T(8,128)S(1)}, f32[5,8,16,128]{3,2,1,0:T(8,128)}, u32[]{:S(2)}) copy-start(f32[5,8,16,128]{3,2,1,0:T(8,128)} %param.7) | copy-start | bytes 983044
  98.9 22.1 %copy-start.3 = (f32[5,1,16,128]{3,2,1,0:T(8,128)S(1)}, f32[5,1,16,128]{3,2,1,0:T(8,128)}, u32[]{:S(2)}) copy-start(f32[5,1,16,128]{3,2,1,0:T(8,128)} %copy-done.2) | copy-start | bytes 122884
  98.9 22.1 %copy-start.4 = (f32[5]{0:T(128)S(1)}, f32[5]{0:T(128)}, u32[]{:S(2)}) copy-start(f32[5]{0:T(128)} %constant.23.clone) | copy-start | bytes 64
  102.9 19.4 %collective-permute-start.17 = (f32[5,5,5,1,4,128]{5,4,3,2,1,0:T(4,128)S(1)}, f32[5,5,5,1,4,128]{5,4,3,2,1,0:T(4,128)S(1)}, u32[]{:S(2)}, u32[]{:S(2)}) collective-permute-start(f32[5,5,5,1,4,128]{5,4,3,2,1,0:T(4,128)S(1)} %get-tuple-element.14), channel_id=1, source_target_pairs={{1,0},{2,1},{3,2},{5,4},{6,5},{7,6},{9,8},{10,9},{11,10},{13,12},{... | collective-permute-start | bytes 768008 | tf_op jit(solution)/shard_map/ppermute | solution.py:27
  104.9 17.5 %collective-permute-start.16 = (f32[5,5,5,1,4,128]{5,4,3,2,1,0:T(4,128)S(1)}, f32[5,5,5,1,4,128]{5,4,3,2,1,0:T(4,128)S(1)}, u32[]{:S(2)}, u32[]{:S(2)}) collective-permute-start(f32[5,5,5,1,4,128]{5,4,3,2,1,0:T(4,128)S(1)} %get-tuple-element.13), channel_id=1, source_target_pairs={{0,1},{1,2},{2,3},{4,5},{5,6},{6,7},{8,9},{9,10},{10,11},{12,13},{... | collective-permute-start | bytes 768008 | tf_op jit(solution)/shard_map/ppermute | solution.py:24
  109.0 10.2 %collective-permute-start.11 = (f32[5,8,16,1]{3,2,1,0:T(8,128)S(1)}, f32[5,8,16,1]{3,2,1,0:T(8,128)S(1)}, u32[]{:S(2)}, u32[]{:S(2)}) collective-permute-start(f32[5,8,16,1]{3,2,1,0:T(8,128)S(1)} %get-tuple-element.16), channel_id=1, source_target_pairs={{1,0},{2,1},{3,2},{5,4},{6,5},{7,6},{9,8},{10,9},{11,10},{13,12},{... | collective-permute-start | bytes 7688 | tf_op jit(solution)/shard_map/ppermute | solution.py:39
  110.9 10.1 %collective-permute-start.10 = (f32[5,8,16,1]{3,2,1,0:T(8,128)S(1)}, f32[5,8,16,1]{3,2,1,0:T(8,128)S(1)}, u32[]{:S(2)}, u32[]{:S(2)}) collective-permute-start(f32[5,8,16,1]{3,2,1,0:T(8,128)S(1)} %get-tuple-element.15), channel_id=1, source_target_pairs={{0,1},{1,2},{2,3},{4,5},{5,6},{6,7},{8,9},{9,10},{10,11},{12,13},{... | collective-permute-start | bytes 7688 | tf_op jit(solution)/shard_map/ppermute | solution.py:38

commit v6 on v5

--- a/solution.py
+++ b/solution.py
@@ -112,7 +112,7 @@
     return out
 
 
-GROUP = 4
+GROUP = 8
 
 
 def coupling_kernel(

time: 126 us -> 125 us (level)
  no operation moved by 1% of the time
where the time goes in v6:
time: 125 us; the launch traced here: 123 us
  starting transfers between devices  57.9 us (46%)
  waiting for transfers between devices  25.1 us (20%)
  Pallas kernels  20 us (16%)
  local copies, waits for them, and re-layouts  13.1 us (10%)
  other arithmetic  5.21 us (4%)
  between operations  1.66 us (1%)
    ppermute x6, starting transfers between devices, with_halo(): lax.ppermute(lax.slice_in_dim(block, block.shape[dim] - width, None, axis...  21.4 us
    pallas_call x1, Pallas kernels, local(): pl.pallas_call(functools.partial(coupling_kernel, span_y=span_y, span_z=s...  20 us
    ppermute x3, starting transfers between devices, fold_ghosts(): lax.ppermute(lax.slice_in_dim(block, span - 1, span, axis=dim), axis, for...  16.3 us
    ppermute x6, starting transfers between devices, with_halo(): lax.ppermute(lax.slice_in_dim(block, 0, width, axis=dim), axis, backward)  14.5 us
    ppermute x6, waiting for transfers between devices, with_halo(): lax.ppermute(lax.slice_in_dim(block, 0, width, axis=dim), axis, backward)  11.8 us
    ppermute x6, waiting for transfers between devices, with_halo(): lax.ppermute(lax.slice_in_dim(block, block.shape[dim] - width, None, axis...  6.85 us
    ppermute x3, starting transfers between devices, fold_ghosts(): lax.ppermute(lax.slice_in_dim(block, 0, 1, axis=dim), axis, backward)  5.76 us
    unnamed x16, local copies, waits for them, and re-layouts  5.08 us
  transfers between devices with their start and end apart: 18, of which 9 were waited for; matrix products, arithmetic and copies ran while one was open for 5% of the time, Pallas kernels for 0%

profile of v6, /device:TPU:58, one launch (start us, length us, event | category | flops | bytes accessed | tf_op | source)
XLA Modules:
  0.0 123.0 jit_solution(502898047600686446)
XLA Ops:
  1.4 7.8 %collective-permute-start.1 = (f32[5,1,16,128]{3,2,1,0:T(8,128)S(1)}, f32[5,1,16,128]{3,2,1,0:T(8,128)S(1)}, u32[]{:S(2)}, u32[]{:S(2)}) collective-permute-start(f32[5,1,16,128]{3,2,1,0:T(8,128)S(1)} %get-tuple-element.24), channel_id=1, source_target_pairs={{0,32},{32,64},{64,96},{96,128},{128,160},{160,192},{192,224},{1,3... | collective-permute-start | bytes 122888 | tf_op jit(solution)/shard_map/ppermute | solution.py:24
  9.3 1.9 %collective-permute-start = (f32[5,1,16,128]{3,2,1,0:T(8,128)S(1)}, f32[5,1,16,128]{3,2,1,0:T(8,128)S(1)}, u32[]{:S(2)}, u32[]{:S(2)}) collective-permute-start(f32[5,1,16,128]{3,2,1,0:T(8,128)S(1)} %get-tuple-element.23), channel_id=1, source_target_pairs={{32,0},{64,32},{96,64},{128,96},{160,128},{192,160},{224,192},{33,... | collective-permute-start | bytes 122888 | tf_op jit(solution)/shard_map/ppermute | solution.py:27
  12.2 9.0 %collective-permute-done = f32[5,1,16,128]{3,2,1,0:T(8,128)S(1)} collective-permute-done((f32[5,1,16,128]{3,2,1,0:T(8,128)S(1)}, f32[5,1,16,128]{3,2,1,0:T(8,128)S(1)}, u32[]{:S(2)}, u32[]{:S(2)}) %collective-permute-start) | collective-permute-done | bytes 40992 | tf_op jit(solution)/shard_map/ppermute | solution.py:27
  21.3 1.9 %collective-permute-start.2 = (f32[5,10,1,128]{3,2,1,0:T(1,128)S(1)}, f32[5,10,1,128]{3,2,1,0:T(1,128)S(1)}, u32[]{:S(2)}, u32[]{:S(2)}) collective-permute-start(f32[5,10,1,128]{3,2,1,0:T(1,128)S(1)} %get-tuple-element.22), channel_id=1, source_target_pairs={{4,0},{8,4},{12,8},{16,12},{20,16},{24,20},{28,24},{5,1},{9,5},{13... | collective-permute-start | bytes 76808 | tf_op jit(solution)/shard_map/ppermute | solution.py:27
  23.2 2.4 %collective-permute-start.3 = (f32[5,10,1,128]{3,2,1,0:T(1,128)S(1)}, f32[5,10,1,128]{3,2,1,0:T(1,128)S(1)}, u32[]{:S(2)}, u32[]{:S(2)}) collective-permute-start(f32[5,10,1,128]{3,2,1,0:T(1,128)S(1)} %get-tuple-element.21), channel_id=1, source_target_pairs={{0,4},{4,8},{8,12},{12,16},{16,20},{20,24},{24,28},{1,5},{5,9},{9,... | collective-permute-start | bytes 76808 | tf_op jit(solution)/shard_map/ppermute | solution.py:24
  26.4 1.9 %collective-permute-done.3 = f32[5,10,1,128]{3,2,1,0:T(1,128)S(1)} collective-permute-done((f32[5,10,1,128]{3,2,1,0:T(1,128)S(1)}, f32[5,10,1,128]{3,2,1,0:T(1,128)S(1)}, u32[]{:S(2)}, u32[]{:S(2)}) %collective-permute-start.3) | collective-permute-done | bytes 25632 | tf_op jit(solution)/shard_map/ppermute | solution.py:24
  29.1 2.9 %collective-permute-start.4 = (f32[5,10,18,1]{2,3,1,0:T(1,128)S(1)}, f32[5,10,18,1]{2,3,1,0:T(1,128)S(1)}, u32[]{:S(2)}, u32[]{:S(2)}) collective-permute-start(f32[5,10,18,1]{2,3,1,0:T(1,128)S(1)} %copy.14), channel_id=1, source_target_pairs={{1,0},{2,1},{3,2},{5,4},{6,5},{7,6},{9,8},{10,9},{11,10},{13,12},{... | collective-permute-start | bytes 10808 | tf_op jit(solution)/shard_map/ppermute | solution.py:27
  32.4 2.9 %collective-permute-start.5 = (f32[5,10,18,1]{2,3,1,0:T(1,128)S(1)}, f32[5,10,18,1]{2,3,1,0:T(1,128)S(1)}, u32[]{:S(2)}, u32[]{:S(2)}) collective-permute-start(f32[5,10,18,1]{2,3,1,0:T(1,128)S(1)} %copy.16), channel_id=1, source_target_pairs={{0,1},{1,2},{2,3},{4,5},{5,6},{6,7},{8,9},{9,10},{10,11},{12,13},{... | collective-permute-start | bytes 10808 | tf_op jit(solution)/shard_map/ppermute | solution.py:24
  37.0 1.1 collective-permute-done.5
  39.3 1.1 reshape.25
  40.4 1.6 %copy.23 = f32[5,130,180]{2,1,0:T(8,128)S(1)} copy(f32[5,130,180]{1,2,0:T(8,128)} %reshape.25) | data formatting | bytes 936000
  42.8 20.0 %shard_map.94 = (f32[5,32,128]{2,1,0:T(8,128)}, f32[5,108,128]{2,1,0:T(8,128)}, f32[680,256]{1,0:T(8,128)}) custom-call(s32[1]{0:T(128)S(6)} %copy.28.live_ref, s32[32]{0:T(128)} %dest_ref.1, f32[680,256]{1,0:T(8,128)} %bitcast.16, f32[5,32,128]{2,1,0:T(8,128)} %bitcast.20, s32[32,128]{1,0:T(8,128)} %cell_ref.1, f32[3,32,128]{2,1,0:T(8,128)} %bitcast.21, ...), custom_call_target="tpu_custom_call" | custom-call | tf_op jit(solution)/shard_map/pallas_call | solution.py:278
  62.9 2.4 %copy.22 = f32[5,130,180]{1,2,0:T(8,128)} copy(f32[5,130,180]{2,1,0:T(8,128)} %bitcast.17) | data formatting | bytes 936000
  65.3 1.3 %reshape.28 = f32[5,130,10,18]{1,3,2,0:T(8,128)S(1)} reshape(f32[5,130,180]{1,2,0:T(8,128)} %copy.22) | data formatting | bytes 936000 | tf_op jit(solution)/shard_map/reshape | solution.py:299
  67.4 1.9 %collective-permute-start.7 = (f32[5,1,18,130]{3,2,1,0:T(8,128)}, f32[5,1,18,130]{3,2,1,0:T(8,128)}, u32[]{:S(2)}, u32[]{:S(2)}) collective-permute-start(f32[5,1,18,130]{3,2,1,0:T(8,128)} %get-tuple-element.10), channel_id=1, source_target_pairs={{32,0},{64,32},{96,64},{128,96},{160,128},{192,160},{224,192},{33,... | collective-permute-start | bytes 140408 | tf_op jit(solution)/shard_map/ppermute | solution.py:39
  69.3 9.9 %collective-permute-start.6 = (f32[5,1,18,130]{3,2,1,0:T(8,128)}, f32[5,1,18,130]{3,2,1,0:T(8,128)}, u32[]{:S(2)}, u32[]{:S(2)}) collective-permute-start(f32[5,1,18,130]{3,2,1,0:T(8,128)} %get-tuple-element.9), channel_id=1, source_target_pairs={{0,32},{32,64},{64,96},{96,128},{128,160},{160,192},{192,224},{1,3... | collective-permute-start | bytes 140408 | tf_op jit(solution)/shard_map/ppermute | solution.py:38
  79.4 1.9 %collective-permute-start.12 = (f32[5,1,3,3,4,128]{5,4,3,2,1,0:T(4,128)S(1)}, f32[5,1,3,3,4,128]{5,4,3,2,1,0:T(4,128)S(1)}, u32[]{:S(2)}, u32[]{:S(2)}) collective-permute-start(f32[5,1,3,3,4,128]{5,4,3,2,1,0:T(4,128)S(1)} %get-tuple-element.26), channel_id=1, source_target_pairs={{0,32},{32,64},{64,96},{96,128},{128,160},{160,192},{192,224},{1,3... | collective-permute-start | bytes 276488 | tf_op jit(solution)/shard_map/ppermute | solution.py:24
  81.3 3.9 %collective-permute-start.13 = (f32[5,1,3,3,4,128]{5,4,3,2,1,0:T(4,128)S(1)}, f32[5,1,3,3,4,128]{5,4,3,2,1,0:T(4,128)S(1)}, u32[]{:S(2)}, u32[]{:S(2)}) collective-permute-start(f32[5,1,3,3,4,128]{5,4,3,2,1,0:T(4,128)S(1)} %get-tuple-element.25), channel_id=1, source_target_pairs={{32,0},{64,32},{96,64},{128,96},{160,128},{192,160},{224,192},{33,... | collective-permute-start | bytes 276488 | tf_op jit(solution)/shard_map/ppermute | solution.py:27
  85.5 1.0 fusion
  86.6 1.9 %collective-permute-start.9 = (f32[5,8,1,130]{3,2,1,0:T(1,128)S(1)}, f32[5,8,1,130]{3,2,1,0:T(1,128)S(1)}, u32[]{:S(2)}, u32[]{:S(2)}) collective-permute-start(f32[5,8,1,130]{3,2,1,0:T(1,128)S(1)} %get-tuple-element.12), channel_id=1, source_target_pairs={{4,0},{8,4},{12,8},{16,12},{20,16},{24,20},{28,24},{5,1},{9,5},{13... | collective-permute-start | bytes 62408 | tf_op jit(solution)/shard_map/ppermute | solution.py:39
  88.5 2.4 %collective-permute-start.8 = (f32[5,8,1,130]{3,2,1,0:T(1,128)S(1)}, f32[5,8,1,130]{3,2,1,0:T(1,128)S(1)}, u32[]{:S(2)}, u32[]{:S(2)}) collective-permute-start(f32[5,8,1,130]{3,2,1,0:T(1,128)S(1)} %get-tuple-element.11), channel_id=1, source_target_pairs={{0,4},{4,8},{8,12},{12,16},{16,20},{20,24},{24,28},{1,5},{5,9},{9,... | collective-permute-start | bytes 62408 | tf_op jit(solution)/shard_map/ppermute | solution.py:38
  91.0 2.7 %collective-permute-done.13 = f32[5,1,3,3,4,128]{5,4,3,2,1,0:T(4,128)S(1)} collective-permute-done((f32[5,1,3,3,4,128]{5,4,3,2,1,0:T(4,128)S(1)}, f32[5,1,3,3,4,128]{5,4,3,2,1,0:T(4,128)S(1)}, u32[]{:S(2)}, u32[]{:S(2)}) %collective-permute-start.13) | collective-permute-done | bytes 92192 | tf_op jit(solution)/shard_map/ppermute | solution.py:27
  93.9 1.9 %collective-permute-start.15 = (f32[5,5,1,3,4,128]{5,4,3,2,1,0:T(4,128)S(1)}, f32[5,5,1,3,4,128]{5,4,3,2,1,0:T(4,128)S(1)}, u32[]{:S(2)}, u32[]{:S(2)}) collective-permute-start(f32[5,5,1,3,4,128]{5,4,3,2,1,0:T(4,128)S(1)} %get-tuple-element.20), channel_id=1, source_target_pairs={{4,0},{8,4},{12,8},{16,12},{20,16},{24,20},{28,24},{5,1},{9,5},{13... | collective-permute-start | bytes 460808 | tf_op jit(solution)/shard_map/ppermute | solution.py:27
  95.8 2.4 %collective-permute-start.14 = (f32[5,5,1,3,4,128]{5,4,3,2,1,0:T(4,128)S(1)}, f32[5,5,1,3,4,128]{5,4,3,2,1,0:T(4,128)S(1)}, u32[]{:S(2)}, u32[]{:S(2)}) collective-permute-start(f32[5,5,1,3,4,128]{5,4,3,2,1,0:T(4,128)S(1)} %get-tuple-element.19), channel_id=1, source_target_pairs={{0,4},{4,8},{8,12},{12,16},{16,20},{20,24},{24,28},{1,5},{5,9},{9,... | collective-permute-start | bytes 460808 | tf_op jit(solution)/shard_map/ppermute | solution.py:24
  98.5 3.8 %collective-permute-done.14 = f32[5,5,1,3,4,128]{5,4,3,2,1,0:T(4,128)S(1)} collective-permute-done((f32[5,5,1,3,4,128]{5,4,3,2,1,0:T(4,128)S(1)}, f32[5,5,1,3,4,128]{5,4,3,2,1,0:T(4,128)S(1)}, u32[]{:S(2)}, u32[]{:S(2)}) %collective-permute-start.14) | collective-permute-done | bytes 153632 | tf_op jit(solution)/shard_map/ppermute | solution.py:24
  102.4 1.9 %collective-permute-start.17 = (f32[5,5,5,1,4,128]{5,4,3,2,1,0:T(4,128)S(1)}, f32[5,5,5,1,4,128]{5,4,3,2,1,0:T(4,128)S(1)}, u32[]{:S(2)}, u32[]{:S(2)}) collective-permute-start(f32[5,5,5,1,4,128]{5,4,3,2,1,0:T(4,128)S(1)} %get-tuple-element.14), channel_id=1, source_target_pairs={{1,0},{2,1},{3,2},{5,4},{6,5},{7,6},{9,8},{10,9},{11,10},{13,12},{... | collective-permute-start | bytes 768008 | tf_op jit(solution)/shard_map/ppermute | solution.py:27
  104.4 3.9 %collective-permute-start.16 = (f32[5,5,5,1,4,128]{5,4,3,2,1,0:T(4,128)S(1)}, f32[5,5,5,1,4,128]{5,4,3,2,1,0:T(4,128)S(1)}, u32[]{:S(2)}, u32[]{:S(2)}) collective-permute-start(f32[5,5,5,1,4,128]{5,4,3,2,1,0:T(4,128)S(1)} %get-tuple-element.13), channel_id=1, source_target_pairs={{0,1},{1,2},{2,3},{4,5},{5,6},{6,7},{8,9},{9,10},{10,11},{12,13},{... | collective-permute-start | bytes 768008 | tf_op jit(solution)/shard_map/ppermute | solution.py:24
  108.4 1.9 %collective-permute-start.11 = (f32[5,8,16,1]{3,2,1,0:T(8,128)S(1)}, f32[5,8,16,1]{3,2,1,0:T(8,128)S(1)}, u32[]{:S(2)}, u32[]{:S(2)}) collective-permute-start(f32[5,8,16,1]{3,2,1,0:T(8,128)S(1)} %get-tuple-element.16), channel_id=1, source_target_pairs={{1,0},{2,1},{3,2},{5,4},{6,5},{7,6},{9,8},{10,9},{11,10},{13,12},{... | collective-permute-start | bytes 7688 | tf_op jit(solution)/shard_map/ppermute | solution.py:39
  110.4 3.9 %collective-permute-start.10 = (f32[5,8,16,1]{3,2,1,0:T(8,128)S(1)}, f32[5,8,16,1]{3,2,1,0:T(8,128)S(1)}, u32[]{:S(2)}, u32[]{:S(2)}) collective-permute-start(f32[5,8,16,1]{3,2,1,0:T(8,128)S(1)} %get-tuple-element.15), channel_id=1, source_target_pairs={{0,1},{1,2},{2,3},{4,5},{5,6},{6,7},{8,9},{9,10},{10,11},{12,13},{... | collective-permute-start | bytes 7688 | tf_op jit(solution)/shard_map/ppermute | solution.py:38
  114.3 4.3 %collective-permute-done.11 = f32[5,8,16,1]{3,2,1,0:T(8,128)S(1)} collective-permute-done((f32[5,8,16,1]{3,2,1,0:T(8,128)S(1)}, f32[5,8,16,1]{3,2,1,0:T(8,128)S(1)}, u32[]{:S(2)}, u32[]{:S(2)}) %collective-permute-start.11) | collective-permute-done | bytes 2592 | tf_op jit(solution)/shard_map/ppermute | solution.py:39
  118.6 1.9 %collective-permute-done.10 = f32[5,8,16,1]{3,2,1,0:T(8,128)S(1)} collective-permute-done((f32[5,8,16,1]{3,2,1,0:T(8,128)S(1)}, f32[5,8,16,1]{3,2,1,0:T(8,128)S(1)}, u32[]{:S(2)}, u32[]{:S(2)}) %collective-permute-start.10) | collective-permute-done | bytes 2592 | tf_op jit(solution)/shard_map/ppermute | solution.py:38
  120.5 1.3 %fusion.4 = f32[5,8,16,128]{3,2,1,0:T(8,128)} fusion(f32[5,8,16,130]{3,2,1,0:T(8,128)S(1)} %fusion.1, f32[5,8,16,128]{3,2,1,0:T(8,128)S(1)} %copy-done, f32[5,10,18,1]{3,2,1,0:T(8,128)S(1)} %copy.17, f32[5,10,1,128]{3,2,1,0:T(1,128)S(1)} %collective-permute-done.2, f32[5,10,16,128]{3,2,1,0:T(8,128)S(1)} %constant_dynamic-update-slice_fusion, ...), kind=kLoop, calls=%fused_computation.10 | loop fusion | flops 1884160 | bytes 1538100 | tf_op jit(solution)/shard_map/add | solution.py:302
  (50 shorter events, 9.8 us)
Async XLA Ops:
  1.4 9.8 %collective-permute-start.1 = (f32[5,1,16,128]{3,2,1,0:T(8,128)S(1)}, f32[5,1,16,128]{3,2,1,0:T(8,128)S(1)}, u32[]{:S(2)}, u32[]{:S(2)}) collective-permute-start(f32[5,1,16,128]{3,2,1,0:T(8,128)S(1)} %get-tuple-element.24), channel_id=1, source_target_pairs={{0,32},{32,64},{64,96},{96,128},{128,160},{160,192},{192,224},{1,3... | collective-permute-start | bytes 122888 | tf_op jit(solution)/shard_map/ppermute | solution.py:24
  9.3 11.9 %collective-permute-start = (f32[5,1,16,128]{3,2,1,0:T(8,128)S(1)}, f32[5,1,16,128]{3,2,1,0:T(8,128)S(1)}, u32[]{:S(2)}, u32[]{:S(2)}) collective-permute-start(f32[5,1,16,128]{3,2,1,0:T(8,128)S(1)} %get-tuple-element.23), channel_id=1, source_target_pairs={{32,0},{64,32},{96,64},{128,96},{160,128},{192,160},{224,192},{33,... | collective-permute-start | bytes 122888 | tf_op jit(solution)/shard_map/ppermute | solution.py:27
  21.2 5.2 %copy-start.2 = (f32[5,1,16,128]{3,2,1,0:T(8,128)}, f32[5,1,16,128]{3,2,1,0:T(8,128)S(1)}, u32[]{:S(2)}) copy-start(f32[5,1,16,128]{3,2,1,0:T(8,128)S(1)} %collective-permute-done) | copy-start | bytes 122884
  21.3 5.1 %collective-permute-start.2 = (f32[5,10,1,128]{3,2,1,0:T(1,128)S(1)}, f32[5,10,1,128]{3,2,1,0:T(1,128)S(1)}, u32[]{:S(2)}, u32[]{:S(2)}) collective-permute-start(f32[5,10,1,128]{3,2,1,0:T(1,128)S(1)} %get-tuple-element.22), channel_id=1, source_target_pairs={{4,0},{8,4},{12,8},{16,12},{20,16},{24,20},{28,24},{5,1},{9,5},{13... | collective-permute-start | bytes 76808 | tf_op jit(solution)/shard_map/ppermute | solution.py:27
  23.2 5.2 %collective-permute-start.3 = (f32[5,10,1,128]{3,2,1,0:T(1,128)S(1)}, f32[5,10,1,128]{3,2,1,0:T(1,128)S(1)}, u32[]{:S(2)}, u32[]{:S(2)}) collective-permute-start(f32[5,10,1,128]{3,2,1,0:T(1,128)S(1)} %get-tuple-element.21), channel_id=1, source_target_pairs={{0,4},{4,8},{8,12},{12,16},{16,20},{20,24},{24,28},{1,5},{5,9},{9,... | collective-permute-start | bytes 76808 | tf_op jit(solution)/shard_map/ppermute | solution.py:24
  29.1 7.5 %collective-permute-start.4 = (f32[5,10,18,1]{2,3,1,0:T(1,128)S(1)}, f32[5,10,18,1]{2,3,1,0:T(1,128)S(1)}, u32[]{:S(2)}, u32[]{:S(2)}) collective-permute-start(f32[5,10,18,1]{2,3,1,0:T(1,128)S(1)} %copy.14), channel_id=1, source_target_pairs={{1,0},{2,1},{3,2},{5,4},{6,5},{7,6},{9,8},{10,9},{11,10},{13,12},{... | collective-permute-start | bytes 10808 | tf_op jit(solution)/shard_map/ppermute | solution.py:27
  32.4 5.7 %collective-permute-start.5 = (f32[5,10,18,1]{2,3,1,0:T(1,128)S(1)}, f32[5,10,18,1]{2,3,1,0:T(1,128)S(1)}, u32[]{:S(2)}, u32[]{:S(2)}) collective-permute-start(f32[5,10,18,1]{2,3,1,0:T(1,128)S(1)} %copy.16), channel_id=1, source_target_pairs={{0,1},{1,2},{2,3},{4,5},{5,6},{6,7},{8,9},{9,10},{10,11},{12,13},{... | collective-permute-start | bytes 10808 | tf_op jit(solution)/shard_map/ppermute | solution.py:24
  65.3 13.9 %copy-start.1 = (f32[5,108,128]{2,1,0:T(8,128)S(1)}, f32[5,108,128]{2,1,0:T(8,128)}, u32[]{:S(2)}) copy-start(f32[5,108,128]{2,1,0:T(8,128)} %get-tuple-element.8) | copy-start | bytes 829444
  67.4 17.9 %collective-permute-start.7 = (f32[5,1,18,130]{3,2,1,0:T(8,128)}, f32[5,1,18,130]{3,2,1,0:T(8,128)}, u32[]{:S(2)}, u32[]{:S(2)}) collective-permute-start(f32[5,1,18,130]{3,2,1,0:T(8,128)} %get-tuple-element.10), channel_id=1, source_target_pairs={{32,0},{64,32},{96,64},{128,96},{160,128},{192,160},{224,192},{33,... | collective-permute-start | bytes 140408 | tf_op jit(solution)/shard_map/ppermute | solution.py:39
  69.3 16.2 %collective-permute-start.6 = (f32[5,1,18,130]{3,2,1,0:T(8,128)}, f32[5,1,18,130]{3,2,1,0:T(8,128)}, u32[]{:S(2)}, u32[]{:S(2)}) collective-permute-start(f32[5,1,18,130]{3,2,1,0:T(8,128)} %get-tuple-element.9), channel_id=1, source_target_pairs={{0,32},{32,64},{64,96},{96,128},{128,160},{160,192},{192,224},{1,3... | collective-permute-start | bytes 140408 | tf_op jit(solution)/shard_map/ppermute | solution.py:38
  79.4 11.6 %collective-permute-start.12 = (f32[5,1,3,3,4,128]{5,4,3,2,1,0:T(4,128)S(1)}, f32[5,1,3,3,4,128]{5,4,3,2,1,0:T(4,128)S(1)}, u32[]{:S(2)}, u32[]{:S(2)}) collective-permute-start(f32[5,1,3,3,4,128]{5,4,3,2,1,0:T(4,128)S(1)} %get-tuple-element.26), channel_id=1, source_target_pairs={{0,32},{32,64},{64,96},{96,128},{128,160},{160,192},{192,224},{1,3... | collective-permute-start | bytes 276488 | tf_op jit(solution)/shard_map/ppermute | solution.py:24
  81.3 12.5 %collective-permute-start.13 = (f32[5,1,3,3,4,128]{5,4,3,2,1,0:T(4,128)S(1)}, f32[5,1,3,3,4,128]{5,4,3,2,1,0:T(4,128)S(1)}, u32[]{:S(2)}, u32[]{:S(2)}) collective-permute-start(f32[5,1,3,3,4,128]{5,4,3,2,1,0:T(4,128)S(1)} %get-tuple-element.25), channel_id=1, source_target_pairs={{32,0},{64,32},{96,64},{128,96},{160,128},{192,160},{224,192},{33,... | collective-permute-start | bytes 276488 | tf_op jit(solution)/shard_map/ppermute | solution.py:27
  86.6 11.6 %collective-permute-start.9 = (f32[5,8,1,130]{3,2,1,0:T(1,128)S(1)}, f32[5,8,1,130]{3,2,1,0:T(1,128)S(1)}, u32[]{:S(2)}, u32[]{:S(2)}) collective-permute-start(f32[5,8,1,130]{3,2,1,0:T(1,128)S(1)} %get-tuple-element.12), channel_id=1, source_target_pairs={{4,0},{8,4},{12,8},{16,12},{20,16},{24,20},{28,24},{5,1},{9,5},{13... | collective-permute-start | bytes 62408 | tf_op jit(solution)/shard_map/ppermute | solution.py:39
  88.5 9.7 %collective-permute-start.8 = (f32[5,8,1,130]{3,2,1,0:T(1,128)S(1)}, f32[5,8,1,130]{3,2,1,0:T(1,128)S(1)}, u32[]{:S(2)}, u32[]{:S(2)}) collective-permute-start(f32[5,8,1,130]{3,2,1,0:T(1,128)S(1)} %get-tuple-element.11), channel_id=1, source_target_pairs={{0,4},{4,8},{8,12},{12,16},{16,20},{20,24},{24,28},{1,5},{5,9},{9,... | collective-permute-start | bytes 62408 | tf_op jit(solution)/shard_map/ppermute | solution.py:38
  93.9 4.6 %collective-permute-start.15 = (f32[5,5,1,3,4,128]{5,4,3,2,1,0:T(4,128)S(1)}, f32[5,5,1,3,4,128]{5,4,3,2,1,0:T(4,128)S(1)}, u32[]{:S(2)}, u32[]{:S(2)}) collective-permute-start(f32[5,5,1,3,4,128]{5,4,3,2,1,0:T(4,128)S(1)} %get-tuple-element.20), channel_id=1, source_target_pairs={{4,0},{8,4},{12,8},{16,12},{20,16},{24,20},{28,24},{5,1},{9,5},{13... | collective-permute-start | bytes 460808 | tf_op jit(solution)/shard_map/ppermute | solution.py:27
  95.8 6.5 %collective-permute-start.14 = (f32[5,5,1,3,4,128]{5,4,3,2,1,0:T(4,128)S(1)}, f32[5,5,1,3,4,128]{5,4,3,2,1,0:T(4,128)S(1)}, u32[]{:S(2)}, u32[]{:S(2)}) collective-permute-start(f32[5,5,1,3,4,128]{5,4,3,2,1,0:T(4,128)S(1)} %get-tuple-element.19), channel_id=1, source_target_pairs={{0,4},{4,8},{8,12},{12,16},{16,20},{20,24},{24,28},{1,5},{5,9},{9,... | collective-permute-start | bytes 460808 | tf_op jit(solution)/shard_map/ppermute | solution.py:24
  98.4 22.2 %copy-start = (f32[5,8,16,128]{3,2,1,0:T(8,128)S(1)}, f32[5,8,16,128]{3,2,1,0:T(8,128)}, u32[]{:S(2)}) copy-start(f32[5,8,16,128]{3,2,1,0:T(8,128)} %param.7) | copy-start | bytes 983044
  98.4 22.1 %copy-start.3 = (f32[5,1,16,128]{3,2,1,0:T(8,128)S(1)}, f32[5,1,16,128]{3,2,1,0:T(8,128)}, u32[]{:S(2)}) copy-start(f32[5,1,16,128]{3,2,1,0:T(8,128)} %copy-done.2) | copy-start | bytes 122884
  98.4 22.1 %copy-start.4 = (f32[5]{0:T(128)S(1)}, f32[5]{0:T(128)}, u32[]{:S(2)}) copy-start(f32[5]{0:T(128)} %constant.23.clone) | copy-start | bytes 64
  102.4 19.4 %collective-permute-start.17 = (f32[5,5,5,1,4,128]{5,4,3,2,1,0:T(4,128)S(1)}, f32[5,5,5,1,4,128]{5,4,3,2,1,0:T(4,128)S(1)}, u32[]{:S(2)}, u32[]{:S(2)}) collective-permute-start(f32[5,5,5,1,4,128]{5,4,3,2,1,0:T(4,128)S(1)} %get-tuple-element.14), channel_id=1, source_target_pairs={{1,0},{2,1},{3,2},{5,4},{6,5},{7,6},{9,8},{10,9},{11,10},{13,12},{... | collective-permute-start | bytes 768008 | tf_op jit(solution)/shard_map/ppermute | solution.py:27
  104.4 17.5 %collective-permute-start.16 = (f32[5,5,5,1,4,128]{5,4,3,2,1,0:T(4,128)S(1)}, f32[5,5,5,1,4,128]{5,4,3,2,1,0:T(4,128)S(1)}, u32[]{:S(2)}, u32[]{:S(2)}) collective-permute-start(f32[5,5,5,1,4,128]{5,4,3,2,1,0:T(4,128)S(1)} %get-tuple-element.13), channel_id=1, source_target_pairs={{0,1},{1,2},{2,3},{4,5},{5,6},{6,7},{8,9},{9,10},{10,11},{12,13},{... | collective-permute-start | bytes 768008 | tf_op jit(solution)/shard_map/ppermute | solution.py:24
  108.4 10.2 %collective-permute-start.11 = (f32[5,8,16,1]{3,2,1,0:T(8,128)S(1)}, f32[5,8,16,1]{3,2,1,0:T(8,128)S(1)}, u32[]{:S(2)}, u32[]{:S(2)}) collective-permute-start(f32[5,8,16,1]{3,2,1,0:T(8,128)S(1)} %get-tuple-element.16), channel_id=1, source_target_pairs={{1,0},{2,1},{3,2},{5,4},{6,5},{7,6},{9,8},{10,9},{11,10},{13,12},{... | collective-permute-start | bytes 7688 | tf_op jit(solution)/shard_map/ppermute | solution.py:39
  110.4 10.1 %collective-permute-start.10 = (f32[5,8,16,1]{3,2,1,0:T(8,128)S(1)}, f32[5,8,16,1]{3,2,1,0:T(8,128)S(1)}, u32[]{:S(2)}, u32[]{:S(2)}) collective-permute-start(f32[5,8,16,1]{3,2,1,0:T(8,128)S(1)} %get-tuple-element.15), channel_id=1, source_target_pairs={{0,1},{1,2},{2,3},{4,5},{5,6},{6,7},{8,9},{9,10},{10,11},{12,13},{... | collective-permute-start | bytes 7688 | tf_op jit(solution)/shard_map/ppermute | solution.py:38

commit v7 on v6

--- a/solution.py
+++ b/solution.py
@@ -46,6 +46,38 @@
     return block
 
 
+def exchange_rows(deposit, boxes, axis, dim, rows):
+    count = lax.axis_size(axis)
+    forward = [(i, i + 1) for i in range(count - 1)]
+    backward = [(target, source) for source, target in forward]
+    span = deposit.shape[dim]
+    width = boxes.shape[-1]
+    last = lax.index_in_dim(deposit, span - 1, dim, keepdims=False).reshape(-1, width)
+    first = lax.index_in_dim(deposit, 0, dim, keepdims=False).reshape(-1, width)
+    box_last = lax.index_in_dim(boxes, boxes.shape[dim] - 1, dim, keepdims=False)
+    box_first = lax.index_in_dim(boxes, 0, dim, keepdims=False)
+    up = jnp.concatenate([last, box_last.reshape(-1, width)], axis=0)
+    down = jnp.concatenate([first, box_first.reshape(-1, width)], axis=0)
+    below = lax.ppermute(up, axis, forward)
+    above = lax.ppermute(down, axis, backward)
+    layer = lax.index_in_dim(deposit, 0, dim, keepdims=True).shape
+    face = lax.index_in_dim(boxes, 0, dim, keepdims=True).shape
+    inner = lax.slice_in_dim(deposit, 1, span - 1, axis=dim)
+    low_pad = [(0, 0)] * deposit.ndim
+    high_pad = [(0, 0)] * deposit.ndim
+    low_pad[dim] = (0, span - 3)
+    high_pad[dim] = (span - 3, 0)
+    deposit = (
+        inner
+        + jnp.pad(below[:rows].reshape(layer), low_pad)
+        + jnp.pad(above[:rows].reshape(layer), high_pad)
+    )
+    boxes = jnp.concatenate(
+        [below[rows:].reshape(face), boxes, above[rows:].reshape(face)], axis=dim
+    )
+    return deposit, boxes
+
+
 def parcel_update(current_condition, local_air_sample):
     particle_weights_list = current_condition[:, 0]
     parcel_hotness_measure = current_condition[:, 1]
@@ -119,7 +151,7 @@
     live_ref, dest_ref, table_ref, parcel_ref, cell_ref, offset_ref, factor_ref,
     kept_ref, outbox_ref, deposit_ref,
     weight_scr, depth_scr, spread_scr, updated_scr, count_scr, table_high_ref, table_low_ref,
-    *, span_y, span_z,
+    *, span_y, span_z, stride,
 ):
     fields = parcel_ref.shape[0]
     blocks = parcel_ref.shape[1]
@@ -157,7 +189,7 @@
                         far_share[1, j:j + 1] if bit_y else near_share[1, j:j + 1]
                     )
                     target = (
-                        (cell_x[j:j + 1] + bit_x * step_sign[0, j:j + 1]) * span_y
+                        (cell_x[j:j + 1] + bit_x * step_sign[0, j:j + 1]) * stride
                         + cell_y[j:j + 1]
                         + bit_y * step_sign[1, j:j + 1]
                     )
@@ -216,9 +248,9 @@
         spread_high, spread_low = split_bf16(spread_scr[...])
         dims = (((1,), (1,)), ((), ()))
         deposit_ref[...] += (
-            lax.dot_general(spread_high, weight_high, dims, preferred_element_type=jnp.float32)
-            + lax.dot_general(spread_high, weight_low, dims, preferred_element_type=jnp.float32)
-            + lax.dot_general(spread_low, weight_high, dims, preferred_element_type=jnp.float32)
+            lax.dot_general(weight_high, spread_high, dims, preferred_element_type=jnp.float32)
+            + lax.dot_general(weight_low, spread_high, dims, preferred_element_type=jnp.float32)
+            + lax.dot_general(weight_high, spread_low, dims, preferred_element_type=jnp.float32)
         )
         return carry
 
@@ -241,7 +273,10 @@
 
         @pl.when(alive & (d != 13) & (rank < SLOTS))
         def _():
-            outbox_ref[:, pl.ds(d * SLOTS + rank, 1), :] = updated_scr[:, pl.ds(b, 1), :]
+            for f in range(fields):
+                outbox_ref[d * SLOTS + rank, :, f * lanes:(f + 1) * lanes] = updated_scr[
+                    f, pl.ds(b, 1), :
+                ]
             count_scr[d] = rank + 1
 
         return carry
@@ -258,7 +293,10 @@
     span_z = size_z + 2
     pair_count = span_x * span_y
     plane_size = span_y * span_z
-    table = jnp.transpose(padded, (0, 3, 1, 2)).reshape(fields, span_z, pair_count)
+    stride = -(-span_y // 8) * 8
+    pair_count = span_x * stride
+    table = jnp.pad(padded, ((0, 0), (0, 0), (0, stride - span_y), (0, 0)))
+    table = jnp.transpose(table, (0, 3, 1, 2)).reshape(fields, span_z, pair_count)
     table = jnp.pad(table, ((0, 0), (0, DEPTH_ROWS - span_z), (0, PAIR_LANES - pair_count)))
     table = table.reshape(fields * DEPTH_ROWS, PAIR_LANES)
     parcel_rows = jnp.transpose(parcels, (1, 0, 2))
@@ -276,11 +314,11 @@
     smem = pl.BlockSpec(memory_space=pltpu.SMEM)
     lanes = GROUP * block_parcels
     kept_rows, outbox_rows, deposit_rows = pl.pallas_call(
-        functools.partial(coupling_kernel, span_y=span_y, span_z=span_z),
+        functools.partial(coupling_kernel, span_y=span_y, span_z=span_z, stride=stride),
         out_shape=(
             jax.ShapeDtypeStruct(parcel_rows.shape, jnp.float32),
-            jax.ShapeDtypeStruct((parcel_fields, 27 * SLOTS, block_parcels), jnp.float32),
-            jax.ShapeDtypeStruct((fields * DEPTH_ROWS, PAIR_LANES), jnp.float32),
+            jax.ShapeDtypeStruct((27 * SLOTS, 1, fields * DEPTH_ROWS), jnp.float32),
+            jax.ShapeDtypeStruct((PAIR_LANES, fields * DEPTH_ROWS), jnp.float32),
         ),
         in_specs=[smem, smem] + [vmem] * 5,
         out_specs=(vmem, vmem, vmem),
@@ -295,17 +333,50 @@
         ],
     )(live_blocks, destination, table, parcel_rows, parcel_cells, offset_rows, factors)
     kept = jnp.transpose(kept_rows, (1, 0, 2))
-    deposit = deposit_rows.reshape(fields, DEPTH_ROWS, PAIR_LANES)[:, :span_z, :pair_count]
-    deposit = jnp.transpose(deposit.reshape(fields, span_z, span_x, span_y), (0, 2, 3, 1))
-    cell_sources = fold_ghosts(deposit, (("gx", 1), ("gy", 2), ("gz", 3)))
+    width = fields * DEPTH_ROWS
+    deposit = deposit_rows[:pair_count].reshape(span_x, stride, width)
+    boxes = outbox_rows.reshape(3, 9 * SLOTS, width)
+    deposit, boxes = exchange_rows(deposit, boxes, "gx", 0, stride)
+    boxes = boxes.reshape(boxes.shape[0], 3, 3 * SLOTS, width)
+    deposit, boxes = exchange_rows(deposit[:, :span_y], boxes, "gy", 1, size_x)
+    deposit = deposit.reshape(size_x, size_y, fields, DEPTH_ROWS)
+    boxes = boxes.reshape(boxes.shape[:2] + (3, SLOTS, width))
+    plane = size_x * size_y * fields
+    count = lax.axis_size("gz")
+    forward = [(i, i + 1) for i in range(count - 1)]
+    backward = [(target, source) for source, target in forward]
+    up = jnp.concatenate(
+        [
+            jnp.pad(deposit[..., span_z - 1].reshape(1, plane), ((0, 0), (0, width - plane))),
+            boxes[:, :, 2].reshape(-1, width),
+        ],
+        axis=0,
+    )
+    down = jnp.concatenate(
+        [
+            jnp.pad(deposit[..., 0].reshape(1, plane), ((0, 0), (0, width - plane))),
+            boxes[:, :, 0].reshape(-1, width),
+        ],
+        axis=0,
+    )
+    below = lax.ppermute(up, "gz", forward)
+    above = lax.ppermute(down, "gz", backward)
+    owned = deposit[..., 1:span_z - 1]
+    owned = owned + jnp.pad(
+        below[0, :plane].reshape(size_x, size_y, fields, 1), ((0, 0), (0, 0), (0, 0), (0, size_z - 1))
+    )
+    owned = owned + jnp.pad(
+        above[0, :plane].reshape(size_x, size_y, fields, 1), ((0, 0), (0, 0), (0, 0), (size_z - 1, 0))
+    )
+    cell_sources = jnp.transpose(owned, (2, 0, 1, 3))
+    face = boxes.shape[:2] + (1, SLOTS, width)
+    boxes = jnp.concatenate(
+        [below[1:].reshape(face), boxes, above[1:].reshape(face)], axis=2
+    )
     kappa = jnp.array(DIFFUSION, jnp.float32)[:, None, None, None]
     gas_next = gas_state + kappa * laplacian(padded) + COUPLING * cell_sources
-    outbox = outbox_rows.reshape((parcel_fields, 3, 3, 3, SLOTS, block_parcels))
-    widened = with_halo(outbox, (("gx", 1), ("gy", 2), ("gz", 3)), 1)
-    arrived_boxes = widened[:, 0::2, 0::2, 0::2]
-    arrived = jnp.transpose(
-        arrived_boxes.reshape((parcel_fields, 27 * SLOTS, block_parcels)), (1, 0, 2)
-    )
+    arrived_boxes = boxes[0::2, 0::2, 0::2][..., :parcel_fields * block_parcels]
+    arrived = arrived_boxes.reshape((27 * SLOTS, parcel_fields, block_parcels))
     return (gas_next, kept, arrived)
 
 

time: 125 us -> 141 us (1.13)
  the two profiles are of different devices: /device:TPU:58 before, /device:TPU:226 now
where the time goes in v7:
time: 141 us; the launch traced here: 140 us
  starting transfers between devices  46.6 us (33%)
  local copies, waits for them, and re-layouts  35.4 us (25%)
  waiting for transfers between devices  24.1 us (17%)
  Pallas kernels  17.3 us (12%)
  other arithmetic  14.9 us (11%)
  between operations  1.79 us (1%)
    pallas_call x1, Pallas kernels, local(): pl.pallas_call(functools.partial(coupling_kernel, span_y=span_y, span_z=s...  17.3 us
    ppermute x3, starting transfers between devices, with_halo(): lax.ppermute(lax.slice_in_dim(block, 0, width, axis=dim), axis, backward)  15.7 us
    ppermute x2, waiting for transfers between devices, exchange_rows(): below = lax.ppermute(up, axis, forward)  12 us
    ppermute x2, starting transfers between devices, exchange_rows(): above = lax.ppermute(down, axis, backward)  11.6 us
    ppermute x1, starting transfers between devices, local(): above = lax.ppermute(down, 'gz', backward)  6.99 us
    ppermute x3, starting transfers between devices, with_halo(): lax.ppermute(lax.slice_in_dim(block, block.shape[dim] - width, None, axis...  6.7 us
    unnamed x40, local copies, waits for them, and re-layouts  5.76 us
    ppermute x2, starting transfers between devices, exchange_rows(): below = lax.ppermute(up, axis, forward)  4.24 us
  transfers between devices with their start and end apart: 12, of which 10 were waited for; matrix products, arithmetic and copies ran while one was open for 10% of the time, Pallas kernels for 0%

profile of v7, /device:TPU:226, one launch (start us, length us, event | category | flops | bytes accessed | tf_op | source)
XLA Modules:
  0.0 140.1 jit_solution(17931055862191314531)
XLA Ops:
  1.8 3.5 %collective-permute-start.1 = (f32[5,1,16,128]{3,0,2,1:T(8,128)S(1)}, f32[5,1,16,128]{3,0,2,1:T(8,128)S(1)}, u32[]{:S(2)}, u32[]{:S(2)}) collective-permute-start(f32[5,1,16,128]{3,0,2,1:T(8,128)S(1)} %get-tuple-element.30), channel_id=1, source_target_pairs={{0,32},{32,64},{64,96},{96,128},{128,160},{160,192},{192,224},{1,3... | collective-permute-start | bytes 122888 | tf_op jit(solution)/shard_map/ppermute | solution.py:24
  5.3 8.4 %collective-permute-start = (f32[5,1,16,128]{3,0,2,1:T(8,128)S(1)}, f32[5,1,16,128]{3,0,2,1:T(8,128)S(1)}, u32[]{:S(2)}, u32[]{:S(2)}) collective-permute-start(f32[5,1,16,128]{3,0,2,1:T(8,128)S(1)} %get-tuple-element.29), channel_id=1, source_target_pairs={{32,0},{64,32},{96,64},{128,96},{160,128},{192,160},{224,192},{33,... | collective-permute-start | bytes 122888 | tf_op jit(solution)/shard_map/ppermute | solution.py:27
  14.0 1.2 copy_dynamic-update-slice_fusion
  15.6 1.9 %collective-permute-start.3 = (f32[5,10,1,128]{3,0,2,1:T(8,128)S(1)}, f32[5,10,1,128]{3,0,2,1:T(8,128)S(1)}, u32[]{:S(2)}, u32[]{:S(2)}) collective-permute-start(f32[5,10,1,128]{3,0,2,1:T(8,128)S(1)} %get-tuple-element.25), channel_id=1, source_target_pairs={{0,4},{4,8},{8,12},{12,16},{16,20},{20,24},{24,28},{1,5},{5,9},{9,... | collective-permute-start | bytes 76808 | tf_op jit(solution)/shard_map/ppermute | solution.py:24
  17.5 3.6 %collective-permute-start.2 = (f32[5,10,1,128]{3,0,2,1:T(8,128)S(1)}, f32[5,10,1,128]{3,0,2,1:T(8,128)S(1)}, u32[]{:S(2)}, u32[]{:S(2)}) collective-permute-start(f32[5,10,1,128]{3,0,2,1:T(8,128)S(1)} %get-tuple-element.26), channel_id=1, source_target_pairs={{4,0},{8,4},{12,8},{16,12},{20,16},{24,20},{28,24},{5,1},{9,5},{13... | collective-permute-start | bytes 76808 | tf_op jit(solution)/shard_map/ppermute | solution.py:27
  24.0 3.7 %collective-permute-start.4 = (f32[5,10,18,1]{2,3,1,0:T(1,128)S(1)}, f32[5,10,18,1]{2,3,1,0:T(1,128)S(1)}, u32[]{:S(2)}, u32[]{:S(2)}) collective-permute-start(f32[5,10,18,1]{2,3,1,0:T(1,128)S(1)} %copy.38), channel_id=1, source_target_pairs={{1,0},{2,1},{3,2},{5,4},{6,5},{7,6},{9,8},{10,9},{11,10},{13,12},{... | collective-permute-start | bytes 10808 | tf_op jit(solution)/shard_map/ppermute | solution.py:27
  27.8 1.3 collective-permute-start.5
  30.3 3.2 %collective-permute-done.5 = f32[5,10,18,1]{2,3,1,0:T(1,128)S(1)} collective-permute-done((f32[5,10,18,1]{2,3,1,0:T(1,128)S(1)}, f32[5,10,18,1]{2,3,1,0:T(1,128)S(1)}, u32[]{:S(2)}, u32[]{:S(2)}) %collective-permute-start.5) | collective-permute-done | bytes 3632 | tf_op jit(solution)/shard_map/ppermute | solution.py:24
  34.1 1.5 %copy.39 = f32[5,10,18,1]{3,0,2,1:T(8,128)} copy(f32[5,10,18,1]{2,3,1,0:T(1,128)S(1)} %collective-permute-done.4) | data formatting | bytes 7200 | tf_op jit(solution)/shard_map/ppermute | solution.py:27
  35.6 1.8 %select_maximum_fusion = f32[5,10,24,130]{3,0,2,1:T(8,128)S(1)} fusion(f32[5,10,18,1]{3,0,2,1:T(8,128)} %copy.39, f32[5,10,18,1]{3,0,2,1:T(8,128)S(1)} %copy.41, f32[5,10,1,128]{3,0,2,1:T(8,128)S(1)} %collective-permute-done.2, f32[5,10,16,128]{3,0,2,1:T(8,128)S(1)} %constant_dynamic-update-slice_fusion, f32[5,10,1,128]{3,0,2,1:T(8,128)S(1)} %collective-permute-done.3), kind=kLoop, calls=%fused_computation | loop fusion | flops 1560000 | bytes 1092000 | tf_op jit(solution)/shard_map/concatenate | solution.py:28
  37.3 1.5 %copy.46 = f32[5,130,240]{2,1,0:T(8,128)} copy(f32[5,130,240]{1,0,2:T(8,128)S(1)} %bitcast.35) | data formatting | bytes 1248000 | tf_op jit(solution)/shard_map/reshape | solution.py:299
  38.9 2.0 %pad.40 = f32[5,136,256]{2,1,0:T(8,128)} pad(f32[5,130,240]{2,1,0:T(8,128)} %copy.46, f32[]{:T(128)} %constant.5.clone.1), padding=0_0x0_6x0_16 | pad | bytes 1320324 | tf_op jit(solution)/shard_map/jit(_pad)/pad | solution.py:300
  40.9 17.3 %shard_map.94 = (f32[5,32,128]{2,1,0:T(8,128)}, f32[108,1,680]{2,1,0:T(1,128)}, f32[256,680]{1,0:T(8,128)}) custom-call(s32[1]{0:T(128)S(6)} %copy.73.live_ref, s32[32]{0:T(128)} %dest_ref.1, f32[680,256]{1,0:T(8,128)} %bitcast.36, f32[5,32,128]{2,1,0:T(8,128)} %bitcast.46, s32[32,128]{1,0:T(8,128)} %cell_ref.1, f32[3,32,128]{2,1,0:T(8,128)} %bitcast.49, ...), custom_call_target="tpu_custom_call" | custom-call | tf_op jit(solution)/shard_map/pallas_call | solution.py:316
  61.2 9.6 %collective-permute-start.7 = (f32[60,680]{1,0:T(8,128)S(1)}, f32[60,680]{1,0:T(8,128)}, u32[]{:S(2)}, u32[]{:S(2)}) collective-permute-start(f32[60,680]{1,0:T(8,128)S(1)} %pad_maximum_fusion.23), channel_id=1, source_target_pairs={{32,0},{64,32},{96,64},{128,96},{160,128},{192,160},{224,192},{33,... | collective-permute-start | bytes 489608 | tf_op jit(solution)/shard_map/ppermute | solution.py:62
  71.8 1.9 %collective-permute-start.6 = (f32[60,680]{1,0:T(8,128)S(1)}, f32[60,680]{1,0:T(8,128)S(1)}, u32[]{:S(2)}, u32[]{:S(2)}) collective-permute-start(f32[60,680]{1,0:T(8,128)S(1)} %pad_maximum_fusion.22), channel_id=1, source_target_pairs={{0,32},{32,64},{64,96},{96,128},{128,160},{160,192},{192,224},{1,3... | collective-permute-start | bytes 489608 | tf_op jit(solution)/shard_map/ppermute | solution.py:61
  77.2 9.3 %collective-permute-done.6 = f32[60,680]{1,0:T(8,128)S(1)} collective-permute-done((f32[60,680]{1,0:T(8,128)S(1)}, f32[60,680]{1,0:T(8,128)S(1)}, u32[]{:S(2)}, u32[]{:S(2)}) %collective-permute-start.6) | collective-permute-done | bytes 163232 | tf_op jit(solution)/shard_map/ppermute | solution.py:61
  88.5 2.0 %collective-permute-start.9 = (f32[68,680]{1,0:T(8,128)}, f32[68,680]{1,0:T(8,128)}, u32[]{:S(2)}, u32[]{:S(2)}) collective-permute-start(f32[68,680]{1,0:T(8,128)} %pad_maximum_fusion.21), channel_id=1, source_target_pairs={{4,0},{8,4},{12,8},{16,12},{20,16},{24,20},{28,24},{5,1},{9,5},{13... | collective-permute-start | bytes 554888 | tf_op jit(solution)/shard_map/ppermute | solution.py:62
  91.1 2.3 %collective-permute-start.8 = (f32[68,680]{1,0:T(8,128)}, f32[68,680]{1,0:T(8,128)S(1)}, u32[]{:S(2)}, u32[]{:S(2)}) collective-permute-start(f32[68,680]{1,0:T(8,128)} %pad_maximum_fusion.20), channel_id=1, source_target_pairs={{0,4},{4,8},{8,12},{12,16},{16,20},{20,24},{24,28},{1,5},{5,9},{9,... | collective-permute-start | bytes 554888 | tf_op jit(solution)/shard_map/ppermute | solution.py:61
  96.0 2.6 %collective-permute-done.8 = f32[68,680]{1,0:T(8,128)S(1)} collective-permute-done((f32[68,680]{1,0:T(8,128)}, f32[68,680]{1,0:T(8,128)S(1)}, u32[]{:S(2)}, u32[]{:S(2)}) %collective-permute-start.8) | collective-permute-done | bytes 184992 | tf_op jit(solution)/shard_map/ppermute | solution.py:61
  101.2 1.6 %fusion.17 = f32[8,16,680]{2,1,0:T(8,128)} fusion(f32[8,24,680]{2,1,0:T(8,128)S(1)} %pad_add_fusion, f32[8,1,680]{2,1,0:T(1,128)S(1)} %reshape.76, f32[8,1,680]{2,1,0:T(1,128)} %reshape.75), kind=kLoop, calls=%fused_computation.37 | loop fusion | flops 174080 | bytes 739840 | tf_op jit(solution)/shard_map/add | solution.py:71
  102.8 1.4 %reshape.77 = f32[8,16,5,136]{3,2,1,0:T(8,128)S(1)} reshape(f32[8,16,680]{2,1,0:T(8,128)} %fusion.17) | data formatting | bytes 696320 | tf_op jit(solution)/shard_map/reshape | solution.py:342
  106.2 7.0 %collective-permute-start.11 = (f32[101,680]{1,0:T(8,128)S(1)}, f32[101,680]{1,0:T(8,128)S(1)}, u32[]{:S(2)}, u32[]{:S(2)}) collective-permute-start(f32[101,680]{1,0:T(8,128)S(1)} %select_maximum_fusion.2), channel_id=1, source_target_pairs={{1,0},{2,1},{3,2},{5,4},{6,5},{7,6},{9,8},{10,9},{11,10},{13,12},{... | collective-permute-start | bytes 824168 | tf_op jit(solution)/shard_map/ppermute | solution.py:363
  113.2 1.7 %select_maximum_fusion.3 = f32[101,680]{1,0:T(8,128)} fusion(f32[1,640]{1,0:T(1,128)S(1)} %reshape_squeeze.26, f32[100,680]{1,0:T(8,128)} %reshape_squeeze.27), kind=kLoop, calls=%fused_computation.39 | loop fusion | flops 206040 | bytes 549280 | tf_op jit(solution)/shard_map/concatenate | solution.py:348
  114.9 1.3 collective-permute-start.10
  116.2 3.2 %collective-permute-done.11 = f32[101,680]{1,0:T(8,128)S(1)} collective-permute-done((f32[101,680]{1,0:T(8,128)S(1)}, f32[101,680]{1,0:T(8,128)S(1)}, u32[]{:S(2)}, u32[]{:S(2)}) %collective-permute-start.11) | collective-permute-done | bytes 274752 | tf_op jit(solution)/shard_map/ppermute | solution.py:363
  120.9 1.8 %reshape.79 = f32[5,5,1,4,680]{4,3,2,1,0:T(4,128)} reshape(f32[100,680]{1,0:T(8,128)} %slice.220) | data formatting | bytes 544000 | tf_op jit(solution)/shard_map/reshape | solution.py:374
  122.7 2.9 %collective-permute-done.10 = f32[101,680]{1,0:T(8,128)} collective-permute-done((f32[101,680]{1,0:T(8,128)}, f32[101,680]{1,0:T(8,128)}, u32[]{:S(2)}, u32[]{:S(2)}) %collective-permute-start.10) | collective-permute-done | bytes 274752 | tf_op jit(solution)/shard_map/ppermute | solution.py:362
  125.6 1.7 %slice.219 = f32[100,680]{1,0:T(8,128)} slice(f32[101,680]{1,0:T(8,128)} %collective-permute-done.10), slice={[1:101], [0:680]} | slice | bytes 544000 | tf_op jit(solution)/shard_map/slice | solution.py:374
  127.3 1.8 %reshape.78 = f32[5,5,1,4,680]{4,3,2,1,0:T(4,128)} reshape(f32[100,680]{1,0:T(8,128)} %slice.219) | data formatting | bytes 544000 | tf_op jit(solution)/shard_map/reshape | solution.py:374
  129.1 1.4 %pad_maximum_fusion = f32[5,5,5,4,680]{4,3,2,1,0:T(4,128)S(1)} fusion(f32[5,5,1,4,680]{4,3,2,1,0:T(4,128)} %reshape.79, f32[5,1,3,4,680]{4,3,2,1,0:T(4,128)S(1)} %bitcast.39, f32[1,3,3,4,680]{4,3,2,1,0:T(4,128)S(1)} %concatenate.95, f32[3,3,3,4,680]{4,3,2,1,0:T(4,128)S(1)} %concatenate.94, f32[1,3,3,4,680]{4,3,2,1,0:T(4,128)S(1)} %copy-done.6, ...), kind=kLoop, calls=%fused_computation.8 | loop fusion | flops 2040000 | bytes 2720000 | tf_op jit(solution)/shard_map/concatenate | solution.py:373
  131.5 1.8 %copy.56 = f32[108,5,128]{2,0,1:T(8,128)} copy(f32[108,5,128]{2,1,0:T(8,128)} %reshape.80) | data formatting | bytes 552960
  136.8 2.6 %fusion.8 = f32[5,8,16,128]{3,0,2,1:T(8,128)S(1)} fusion(f32[8,16,5,136]{3,2,1,0:T(8,128)S(1)} %reshape.77, f32[5,8,16,128]{3,0,2,1:T(8,128)} %copy-done.1, f32[5,10,18,1]{3,0,2,1:T(8,128)S(1)} %copy.41, f32[5,10,1,128]{3,0,2,1:T(8,128)S(1)} %copy-done.11, f32[5,10,16,128]{3,0,2,1:T(8,128)S(1)} %constant_dynamic-update-slice_fusion, ...), kind=kLoop, calls=%fused_computation.17 | loop fusion | flops 1884160 | bytes 1538100 | tf_op jit(solution)/shard_map/add | solution.py:377
  (103 shorter events, 29.5 us)
Async XLA Ops:
  1.8 11.9 %copy-start.1 = (f32[5,8,16,128]{3,0,2,1:T(8,128)}, f32[5,8,16,128]{3,0,2,1:T(8,128)S(1)}, u32[]{:S(2)}) copy-start(f32[5,8,16,128]{3,0,2,1:T(8,128)S(1)} %copy.43) | copy-start | bytes 983044
  1.8 12.2 %collective-permute-start.1 = (f32[5,1,16,128]{3,0,2,1:T(8,128)S(1)}, f32[5,1,16,128]{3,0,2,1:T(8,128)S(1)}, u32[]{:S(2)}, u32[]{:S(2)}) collective-permute-start(f32[5,1,16,128]{3,0,2,1:T(8,128)S(1)} %get-tuple-element.30), channel_id=1, source_target_pairs={{0,32},{32,64},{64,96},{96,128},{128,160},{160,192},{192,224},{1,3... | collective-permute-start | bytes 122888 | tf_op jit(solution)/shard_map/ppermute | solution.py:24
  5.3 10.3 %collective-permute-start = (f32[5,1,16,128]{3,0,2,1:T(8,128)S(1)}, f32[5,1,16,128]{3,0,2,1:T(8,128)S(1)}, u32[]{:S(2)}, u32[]{:S(2)}) collective-permute-start(f32[5,1,16,128]{3,0,2,1:T(8,128)S(1)} %get-tuple-element.29), channel_id=1, source_target_pairs={{32,0},{64,32},{96,64},{128,96},{160,128},{192,160},{224,192},{33,... | collective-permute-start | bytes 122888 | tf_op jit(solution)/shard_map/ppermute | solution.py:27
  14.0 8.8 %copy-start.13 = (f32[5,1,16,128]{3,0,2,1:T(8,128)}, f32[5,1,16,128]{3,0,2,1:T(8,128)S(1)}, u32[]{:S(2)}) copy-start(f32[5,1,16,128]{3,0,2,1:T(8,128)S(1)} %collective-permute-done.1) | copy-start | bytes 122884
  15.6 7.3 %copy-start.14 = (f32[5,1,16,128]{3,0,2,1:T(8,128)}, f32[5,1,16,128]{3,0,2,1:T(8,128)S(1)}, u32[]{:S(2)}) copy-start(f32[5,1,16,128]{3,0,2,1:T(8,128)S(1)} %collective-permute-done) | copy-start | bytes 122884
  15.6 6.4 %collective-permute-start.3 = (f32[5,10,1,128]{3,0,2,1:T(8,128)S(1)}, f32[5,10,1,128]{3,0,2,1:T(8,128)S(1)}, u32[]{:S(2)}, u32[]{:S(2)}) collective-permute-start(f32[5,10,1,128]{3,0,2,1:T(8,128)S(1)} %get-tuple-element.25), channel_id=1, source_target_pairs={{0,4},{4,8},{8,12},{12,16},{16,20},{20,24},{24,28},{1,5},{5,9},{9,... | collective-permute-start | bytes 76808 | tf_op jit(solution)/shard_map/ppermute | solution.py:24
  17.5 5.3 %collective-permute-start.2 = (f32[5,10,1,128]{3,0,2,1:T(8,128)S(1)}, f32[5,10,1,128]{3,0,2,1:T(8,128)S(1)}, u32[]{:S(2)}, u32[]{:S(2)}) collective-permute-start(f32[5,10,1,128]{3,0,2,1:T(8,128)S(1)} %get-tuple-element.26), channel_id=1, source_target_pairs={{4,0},{8,4},{12,8},{16,12},{20,16},{24,20},{28,24},{5,1},{9,5},{13... | collective-permute-start | bytes 76808 | tf_op jit(solution)/shard_map/ppermute | solution.py:27
  22.0 13.6 %copy-start.8 = (f32[5,10,1,128]{3,0,2,1:T(8,128)}, f32[5,10,1,128]{3,0,2,1:T(8,128)S(1)}, u32[]{:S(2)}) copy-start(f32[5,10,1,128]{3,0,2,1:T(8,128)S(1)} %collective-permute-done.3) | copy-start | bytes 76804
  22.9 12.7 %copy-start.10 = (f32[5,10,1,128]{3,0,2,1:T(8,128)}, f32[5,10,1,128]{3,0,2,1:T(8,128)S(1)}, u32[]{:S(2)}) copy-start(f32[5,10,1,128]{3,0,2,1:T(8,128)S(1)} %collective-permute-done.2) | copy-start | bytes 76804
  24.0 10.1 %collective-permute-start.4 = (f32[5,10,18,1]{2,3,1,0:T(1,128)S(1)}, f32[5,10,18,1]{2,3,1,0:T(1,128)S(1)}, u32[]{:S(2)}, u32[]{:S(2)}) collective-permute-start(f32[5,10,18,1]{2,3,1,0:T(1,128)S(1)} %copy.38), channel_id=1, source_target_pairs={{1,0},{2,1},{3,2},{5,4},{6,5},{7,6},{9,8},{10,9},{11,10},{13,12},{... | collective-permute-start | bytes 10808 | tf_op jit(solution)/shard_map/ppermute | solution.py:27
  27.8 5.7 %collective-permute-start.5 = (f32[5,10,18,1]{2,3,1,0:T(1,128)S(1)}, f32[5,10,18,1]{2,3,1,0:T(1,128)S(1)}, u32[]{:S(2)}, u32[]{:S(2)}) collective-permute-start(f32[5,10,18,1]{2,3,1,0:T(1,128)S(1)} %copy.40), channel_id=1, source_target_pairs={{0,1},{1,2},{2,3},{4,5},{5,6},{6,7},{8,9},{9,10},{10,11},{12,13},{... | collective-permute-start | bytes 10808 | tf_op jit(solution)/shard_map/ppermute | solution.py:24
  58.2 12.7 %copy-start.7 = (f32[256,680]{1,0:T(8,128)S(1)}, f32[256,680]{1,0:T(8,128)}, u32[]{:S(2)}) copy-start(f32[256,680]{1,0:T(8,128)} %get-tuple-element.6) | copy-start | bytes 2088964
  58.2 12.7 %copy-start.2 = (f32[108,1,680]{2,1,0:T(1,128)S(1)}, f32[108,1,680]{2,1,0:T(1,128)}, u32[]{:S(2)}) copy-start(f32[108,1,680]{2,1,0:T(1,128)} %get-tuple-element.7) | copy-start | bytes 881284
  61.2 14.2 %collective-permute-start.7 = (f32[60,680]{1,0:T(8,128)S(1)}, f32[60,680]{1,0:T(8,128)}, u32[]{:S(2)}, u32[]{:S(2)}) collective-permute-start(f32[60,680]{1,0:T(8,128)S(1)} %pad_maximum_fusion.23), channel_id=1, source_target_pairs={{32,0},{64,32},{96,64},{128,96},{160,128},{192,160},{224,192},{33,... | collective-permute-start | bytes 489608 | tf_op jit(solution)/shard_map/ppermute | solution.py:62
  71.8 14.7 %collective-permute-start.6 = (f32[60,680]{1,0:T(8,128)S(1)}, f32[60,680]{1,0:T(8,128)S(1)}, u32[]{:S(2)}, u32[]{:S(2)}) collective-permute-start(f32[60,680]{1,0:T(8,128)S(1)} %pad_maximum_fusion.22), channel_id=1, source_target_pairs={{0,32},{32,64},{64,96},{96,128},{128,160},{160,192},{192,224},{1,3... | collective-permute-start | bytes 489608 | tf_op jit(solution)/shard_map/ppermute | solution.py:61
  88.5 5.7 %collective-permute-start.9 = (f32[68,680]{1,0:T(8,128)}, f32[68,680]{1,0:T(8,128)}, u32[]{:S(2)}, u32[]{:S(2)}) collective-permute-start(f32[68,680]{1,0:T(8,128)} %pad_maximum_fusion.21), channel_id=1, source_target_pairs={{4,0},{8,4},{12,8},{16,12},{20,16},{24,20},{28,24},{5,1},{9,5},{13... | collective-permute-start | bytes 554888 | tf_op jit(solution)/shard_map/ppermute | solution.py:62
  91.1 7.5 %collective-permute-start.8 = (f32[68,680]{1,0:T(8,128)}, f32[68,680]{1,0:T(8,128)S(1)}, u32[]{:S(2)}, u32[]{:S(2)}) collective-permute-start(f32[68,680]{1,0:T(8,128)} %pad_maximum_fusion.20), channel_id=1, source_target_pairs={{0,4},{4,8},{8,12},{12,16},{16,20},{20,24},{24,28},{1,5},{5,9},{9,... | collective-permute-start | bytes 554888 | tf_op jit(solution)/shard_map/ppermute | solution.py:61
  93.7 7.5 %copy-start.5 = (f32[1,3,3,4,680]{4,3,2,1,0:T(4,128)}, f32[1,3,3,4,680]{4,3,2,1,0:T(4,128)S(1)}, u32[]{:S(2)}) copy-start(f32[1,3,3,4,680]{4,3,2,1,0:T(4,128)S(1)} %concatenate.93) | copy-start | bytes 293764
  98.7 2.5 %copy-start.3 = (f32[5,1,3,4,680]{4,3,2,0,1:T(4,128)}, f32[5,1,3,4,680]{4,3,2,0,1:T(4,128)S(1)}, u32[]{:S(2)}) copy-start(f32[5,1,3,4,680]{4,3,2,0,1:T(4,128)S(1)} %concatenate.92) | copy-start | bytes 489604
  104.7 24.4 %copy-start.4 = (f32[5,1,3,4,680]{4,3,2,0,1:T(4,128)S(1)}, f32[5,1,3,4,680]{4,3,2,0,1:T(4,128)}, u32[]{:S(2)}) copy-start(f32[5,1,3,4,680]{4,3,2,0,1:T(4,128)} %copy-done.3) | copy-start | bytes 489604
  104.7 24.3 %copy-start.6 = (f32[1,3,3,4,680]{4,3,2,1,0:T(4,128)S(1)}, f32[1,3,3,4,680]{4,3,2,1,0:T(4,128)}, u32[]{:S(2)}) copy-start(f32[1,3,3,4,680]{4,3,2,1,0:T(4,128)} %copy-done.5) | copy-start | bytes 293764
  106.2 13.3 %collective-permute-start.11 = (f32[101,680]{1,0:T(8,128)S(1)}, f32[101,680]{1,0:T(8,128)S(1)}, u32[]{:S(2)}, u32[]{:S(2)}) collective-permute-start(f32[101,680]{1,0:T(8,128)S(1)} %select_maximum_fusion.2), channel_id=1, source_target_pairs={{1,0},{2,1},{3,2},{5,4},{6,5},{7,6},{9,8},{10,9},{11,10},{13,12},{... | collective-permute-start | bytes 824168 | tf_op jit(solution)/shard_map/ppermute | solution.py:363
  114.9 10.7 %collective-permute-start.10 = (f32[101,680]{1,0:T(8,128)}, f32[101,680]{1,0:T(8,128)}, u32[]{:S(2)}, u32[]{:S(2)}) collective-permute-start(f32[101,680]{1,0:T(8,128)} %select_maximum_fusion.3), channel_id=1, source_target_pairs={{0,1},{1,2},{2,3},{4,5},{5,6},{6,7},{8,9},{9,10},{10,11},{12,13},{... | collective-permute-start | bytes 824168 | tf_op jit(solution)/shard_map/ppermute | solution.py:362
  119.4 0.7 copy-start.12
  130.5 6.3 %copy-start = (f32[5,10,18,1]{3,0,2,1:T(8,128)S(1)}, f32[5,10,18,1]{3,0,2,1:T(8,128)}, u32[]{:S(2)}) copy-start(f32[5,10,18,1]{3,0,2,1:T(8,128)} %copy.39) | copy-start | bytes 10804
  130.5 6.3 %copy-start.9 = (f32[5,10,1,128]{3,0,2,1:T(8,128)S(1)}, f32[5,10,1,128]{3,0,2,1:T(8,128)}, u32[]{:S(2)}) copy-start(f32[5,10,1,128]{3,0,2,1:T(8,128)} %copy-done.8) | copy-start | bytes 76804
  130.5 6.3 %copy-start.11 = (f32[5,10,1,128]{3,0,2,1:T(8,128)S(1)}, f32[5,10,1,128]{3,0,2,1:T(8,128)}, u32[]{:S(2)}) copy-start(f32[5,10,1,128]{3,0,2,1:T(8,128)} %copy-done.10) | copy-start | bytes 76804
  130.5 6.3 %copy-start.15 = (f32[5]{0:T(128)S(1)}, f32[5]{0:T(128)}, u32[]{:S(2)}) copy-start(f32[5]{0:T(128)} %constant.23.clone) | copy-start | bytes 64

commit v8 on v6

--- a/solution.py
+++ b/solution.py
@@ -119,7 +119,7 @@
     live_ref, dest_ref, table_ref, parcel_ref, cell_ref, offset_ref, factor_ref,
     kept_ref, outbox_ref, deposit_ref,
     weight_scr, depth_scr, spread_scr, updated_scr, count_scr, table_high_ref, table_low_ref,
-    *, span_y, span_z,
+    *, span_y, span_z, stride,
 ):
     fields = parcel_ref.shape[0]
     blocks = parcel_ref.shape[1]
@@ -157,7 +157,7 @@
                         far_share[1, j:j + 1] if bit_y else near_share[1, j:j + 1]
                     )
                     target = (
-                        (cell_x[j:j + 1] + bit_x * step_sign[0, j:j + 1]) * span_y
+                        (cell_x[j:j + 1] + bit_x * step_sign[0, j:j + 1]) * stride
                         + cell_y[j:j + 1]
                         + bit_y * step_sign[1, j:j + 1]
                     )
@@ -216,9 +216,9 @@
         spread_high, spread_low = split_bf16(spread_scr[...])
         dims = (((1,), (1,)), ((), ()))
         deposit_ref[...] += (
-            lax.dot_general(spread_high, weight_high, dims, preferred_element_type=jnp.float32)
-            + lax.dot_general(spread_high, weight_low, dims, preferred_element_type=jnp.float32)
-            + lax.dot_general(spread_low, weight_high, dims, preferred_element_type=jnp.float32)
+            lax.dot_general(weight_high, spread_high, dims, preferred_element_type=jnp.float32)
+            + lax.dot_general(weight_low, spread_high, dims, preferred_element_type=jnp.float32)
+            + lax.dot_general(weight_high, spread_low, dims, preferred_element_type=jnp.float32)
         )
         return carry
 
@@ -258,7 +258,10 @@
     span_z = size_z + 2
     pair_count = span_x * span_y
     plane_size = span_y * span_z
-    table = jnp.transpose(padded, (0, 3, 1, 2)).reshape(fields, span_z, pair_count)
+    stride = -(-span_y // 8) * 8
+    pair_count = span_x * stride
+    table = jnp.pad(padded, ((0, 0), (0, 0), (0, stride - span_y), (0, 0)))
+    table = jnp.transpose(table, (0, 3, 1, 2)).reshape(fields, span_z, pair_count)
     table = jnp.pad(table, ((0, 0), (0, DEPTH_ROWS - span_z), (0, PAIR_LANES - pair_count)))
     table = table.reshape(fields * DEPTH_ROWS, PAIR_LANES)
     parcel_rows = jnp.transpose(parcels, (1, 0, 2))
@@ -276,11 +279,11 @@
     smem = pl.BlockSpec(memory_space=pltpu.SMEM)
     lanes = GROUP * block_parcels
     kept_rows, outbox_rows, deposit_rows = pl.pallas_call(
-        functools.partial(coupling_kernel, span_y=span_y, span_z=span_z),
+        functools.partial(coupling_kernel, span_y=span_y, span_z=span_z, stride=stride),
         out_shape=(
             jax.ShapeDtypeStruct(parcel_rows.shape, jnp.float32),
             jax.ShapeDtypeStruct((parcel_fields, 27 * SLOTS, block_parcels), jnp.float32),
-            jax.ShapeDtypeStruct((fields * DEPTH_ROWS, PAIR_LANES), jnp.float32),
+            jax.ShapeDtypeStruct((PAIR_LANES, fields * DEPTH_ROWS), jnp.float32),
         ),
         in_specs=[smem, smem] + [vmem] * 5,
         out_specs=(vmem, vmem, vmem),
@@ -295,8 +298,8 @@
         ],
     )(live_blocks, destination, table, parcel_rows, parcel_cells, offset_rows, factors)
     kept = jnp.transpose(kept_rows, (1, 0, 2))
-    deposit = deposit_rows.reshape(fields, DEPTH_ROWS, PAIR_LANES)[:, :span_z, :pair_count]
-    deposit = jnp.transpose(deposit.reshape(fields, span_z, span_x, span_y), (0, 2, 3, 1))
+    deposit = deposit_rows[:pair_count].reshape(span_x, stride, fields, DEPTH_ROWS)
+    deposit = jnp.transpose(deposit[:, :span_y, :, :span_z], (2, 0, 1, 3))
     cell_sources = fold_ghosts(deposit, (("gx", 1), ("gy", 2), ("gz", 3)))
     kappa = jnp.array(DIFFUSION, jnp.float32)[:, None, None, None]
     gas_next = gas_state + kappa * laplacian(padded) + COUPLING * cell_sources

time: 125 us -> 143 us (1.14)
  the two profiles are of different devices: /device:TPU:58 before, /device:TPU:130 now
where the time goes in v8:
time: 143 us; the launch traced here: 142 us
  starting transfers between devices  73.1 us (51%)
  waiting for transfers between devices  27.2 us (19%)
  local copies, waits for them, and re-layouts  17.4 us (12%)
  Pallas kernels  17.3 us (12%)
  other arithmetic  5.87 us (4%)
  between operations  1.68 us (1%)
    ppermute x6, starting transfers between devices, with_halo(): lax.ppermute(lax.slice_in_dim(block, 0, width, axis=dim), axis, backward)  28.9 us
    ppermute x6, starting transfers between devices, with_halo(): lax.ppermute(lax.slice_in_dim(block, block.shape[dim] - width, None, axis...  18.4 us
    pallas_call x1, Pallas kernels, local(): pl.pallas_call(functools.partial(coupling_kernel, span_y=span_y, span_z=s...  17.3 us
    ppermute x3, starting transfers between devices, fold_ghosts(): lax.ppermute(lax.slice_in_dim(block, 0, 1, axis=dim), axis, backward)  15.2 us
    ppermute x6, waiting for transfers between devices, with_halo(): lax.ppermute(lax.slice_in_dim(block, block.shape[dim] - width, None, axis...  10.9 us
    ppermute x3, starting transfers between devices, fold_ghosts(): lax.ppermute(lax.slice_in_dim(block, span - 1, span, axis=dim), axis, for...  10.6 us
    ppermute x3, waiting for transfers between devices, fold_ghosts(): lax.ppermute(lax.slice_in_dim(block, span - 1, span, axis=dim), axis, for...  6.61 us
    ppermute x3, waiting for transfers between devices, fold_ghosts(): lax.ppermute(lax.slice_in_dim(block, 0, 1, axis=dim), axis, backward)  5.79 us
  transfers between devices with their start and end apart: 18, of which 10 were waited for; matrix products, arithmetic and copies ran while one was open for 4% of the time, Pallas kernels for 0%

profile of v8, /device:TPU:130, one launch (start us, length us, event | category | flops | bytes accessed | tf_op | source)
XLA Modules:
  0.0 142.4 jit_solution(1392787319939879735)
XLA Ops:
  1.8 3.5 %collective-permute-start.1 = (f32[5,1,16,128]{3,0,2,1:T(8,128)S(1)}, f32[5,1,16,128]{3,0,2,1:T(8,128)S(1)}, u32[]{:S(2)}, u32[]{:S(2)}) collective-permute-start(f32[5,1,16,128]{3,0,2,1:T(8,128)S(1)} %get-tuple-element.28), channel_id=1, source_target_pairs={{0,32},{32,64},{64,96},{96,128},{128,160},{160,192},{192,224},{1,3... | collective-permute-start | bytes 122888 | tf_op jit(solution)/shard_map/ppermute | solution.py:24
  5.3 8.4 %collective-permute-start = (f32[5,1,16,128]{3,0,2,1:T(8,128)S(1)}, f32[5,1,16,128]{3,0,2,1:T(8,128)S(1)}, u32[]{:S(2)}, u32[]{:S(2)}) collective-permute-start(f32[5,1,16,128]{3,0,2,1:T(8,128)S(1)} %get-tuple-element.27), channel_id=1, source_target_pairs={{32,0},{64,32},{96,64},{128,96},{160,128},{192,160},{224,192},{33,... | collective-permute-start | bytes 122888 | tf_op jit(solution)/shard_map/ppermute | solution.py:27
  15.6 1.9 %collective-permute-start.3 = (f32[5,10,1,128]{3,0,2,1:T(8,128)S(1)}, f32[5,10,1,128]{3,0,2,1:T(8,128)S(1)}, u32[]{:S(2)}, u32[]{:S(2)}) collective-permute-start(f32[5,10,1,128]{3,0,2,1:T(8,128)S(1)} %get-tuple-element.25), channel_id=1, source_target_pairs={{0,4},{4,8},{8,12},{12,16},{16,20},{20,24},{24,28},{1,5},{5,9},{9,... | collective-permute-start | bytes 76808 | tf_op jit(solution)/shard_map/ppermute | solution.py:24
  17.5 3.6 %collective-permute-start.2 = (f32[5,10,1,128]{3,0,2,1:T(8,128)S(1)}, f32[5,10,1,128]{3,0,2,1:T(8,128)S(1)}, u32[]{:S(2)}, u32[]{:S(2)}) collective-permute-start(f32[5,10,1,128]{3,0,2,1:T(8,128)S(1)} %get-tuple-element.26), channel_id=1, source_target_pairs={{4,0},{8,4},{12,8},{16,12},{20,16},{24,20},{28,24},{5,1},{9,5},{13... | collective-permute-start | bytes 76808 | tf_op jit(solution)/shard_map/ppermute | solution.py:27
  24.0 1.3 collective-permute-start.4
  25.3 4.5 %collective-permute-start.5 = (f32[5,10,18,1]{2,3,1,0:T(1,128)S(1)}, f32[5,10,18,1]{2,3,1,0:T(1,128)S(1)}, u32[]{:S(2)}, u32[]{:S(2)}) collective-permute-start(f32[5,10,18,1]{2,3,1,0:T(1,128)S(1)} %copy.28), channel_id=1, source_target_pairs={{0,1},{1,2},{2,3},{4,5},{5,6},{6,7},{8,9},{9,10},{10,11},{12,13},{... | collective-permute-start | bytes 10808 | tf_op jit(solution)/shard_map/ppermute | solution.py:24
  32.0 1.5 %copy.27 = f32[5,10,18,1]{3,0,2,1:T(8,128)} copy(f32[5,10,18,1]{2,3,1,0:T(1,128)S(1)} %collective-permute-done.4) | data formatting | bytes 7200 | tf_op jit(solution)/shard_map/ppermute | solution.py:27
  33.5 1.8 %select_maximum_fusion = f32[5,10,24,130]{3,0,2,1:T(8,128)S(1)} fusion(f32[5,10,18,1]{3,0,2,1:T(8,128)} %copy.27, f32[5,10,18,1]{3,0,2,1:T(8,128)S(1)} %copy.29, f32[5,10,1,128]{3,0,2,1:T(8,128)S(1)} %collective-permute-done.2, f32[5,10,16,128]{3,0,2,1:T(8,128)S(1)} %constant_dynamic-update-slice_fusion, f32[5,10,1,128]{3,0,2,1:T(8,128)S(1)} %collective-permute-done.3), kind=kLoop, calls=%fused_computation | loop fusion | flops 1560000 | bytes 1092000 | tf_op jit(solution)/shard_map/concatenate | solution.py:28
  35.2 1.5 %copy.34 = f32[5,130,240]{2,1,0:T(8,128)} copy(f32[5,130,240]{1,0,2:T(8,128)S(1)} %bitcast.10) | data formatting | bytes 1248000 | tf_op jit(solution)/shard_map/reshape | solution.py:264
  36.8 2.0 %pad.33 = f32[5,136,256]{2,1,0:T(8,128)} pad(f32[5,130,240]{2,1,0:T(8,128)} %copy.34, f32[]{:T(128)} %constant.5.clone.1), padding=0_0x0_6x0_16 | pad | bytes 1320324 | tf_op jit(solution)/shard_map/jit(_pad)/pad | solution.py:265
  38.8 17.3 %shard_map.94 = (f32[5,32,128]{2,1,0:T(8,128)}, f32[5,108,128]{2,1,0:T(8,128)}, f32[256,680]{1,0:T(8,128)}) custom-call(s32[1]{0:T(128)S(6)} %copy.41.live_ref, s32[32]{0:T(128)} %dest_ref.1, f32[680,256]{1,0:T(8,128)} %bitcast.11, f32[5,32,128]{2,1,0:T(8,128)} %bitcast.14, s32[32,128]{1,0:T(8,128)} %cell_ref.1, f32[3,32,128]{2,1,0:T(8,128)} %bitcast.15, ...), custom_call_target="tpu_custom_call" | custom-call | tf_op jit(solution)/shard_map/pallas_call | solution.py:281
  56.0 2.0 %slice.116 = f32[240,680]{1,0:T(8,128)} slice(f32[256,680]{1,0:T(8,128)} %get-tuple-element.6), slice={[0:240], [0:680]} | slice | bytes 1305600 | tf_op jit(solution)/shard_map/slice | solution.py:301
  58.1 1.9 %reshape.24 = f32[10,24,5,136]{3,2,1,0:T(8,128)S(1)} reshape(f32[240,680]{1,0:T(8,128)} %slice.116) | data formatting | bytes 1305600 | tf_op jit(solution)/shard_map/reshape | solution.py:301
  61.3 1.9 %collective-permute-start.6 = (f32[5,1,18,130]{3,0,2,1:T(8,128)S(1)}, f32[5,1,18,130]{3,0,2,1:T(8,128)S(1)}, u32[]{:S(2)}, u32[]{:S(2)}) collective-permute-start(f32[5,1,18,130]{3,0,2,1:T(8,128)S(1)} %get-tuple-element.15), channel_id=1, source_target_pairs={{0,32},{32,64},{64,96},{96,128},{128,160},{160,192},{192,224},{1,3... | collective-permute-start | bytes 140408 | tf_op jit(solution)/shard_map/ppermute | solution.py:38
  63.2 10.3 %collective-permute-start.7 = (f32[5,1,18,130]{3,0,2,1:T(8,128)S(1)}, f32[5,1,18,130]{3,0,2,1:T(8,128)S(1)}, u32[]{:S(2)}, u32[]{:S(2)}) collective-permute-start(f32[5,1,18,130]{3,0,2,1:T(8,128)S(1)} %get-tuple-element.16), channel_id=1, source_target_pairs={{32,0},{64,32},{96,64},{128,96},{160,128},{192,160},{224,192},{33,... | collective-permute-start | bytes 140408 | tf_op jit(solution)/shard_map/ppermute | solution.py:39
  74.6 1.7 %collective-permute-done.6 = f32[5,1,18,130]{3,0,2,1:T(8,128)S(1)} collective-permute-done((f32[5,1,18,130]{3,0,2,1:T(8,128)S(1)}, f32[5,1,18,130]{3,0,2,1:T(8,128)S(1)}, u32[]{:S(2)}, u32[]{:S(2)}) %collective-permute-start.6) | collective-permute-done | bytes 46832 | tf_op jit(solution)/shard_map/ppermute | solution.py:38
  76.2 1.4 collective-permute-done.7
  77.6 1.4 fusion.5
  79.0 1.9 %collective-permute-start.8 = (f32[5,8,1,130]{3,0,2,1:T(8,128)S(1)}, f32[5,8,1,130]{3,0,2,1:T(8,128)S(1)}, u32[]{:S(2)}, u32[]{:S(2)}) collective-permute-start(f32[5,8,1,130]{3,0,2,1:T(8,128)S(1)} %get-tuple-element.17), channel_id=1, source_target_pairs={{0,4},{4,8},{8,12},{12,16},{16,20},{20,24},{24,28},{1,5},{5,9},{9,... | collective-permute-start | bytes 62408 | tf_op jit(solution)/shard_map/ppermute | solution.py:38
  80.9 3.6 %collective-permute-start.9 = (f32[5,8,1,130]{3,0,2,1:T(8,128)S(1)}, f32[5,8,1,130]{3,0,2,1:T(8,128)S(1)}, u32[]{:S(2)}, u32[]{:S(2)}) collective-permute-start(f32[5,8,1,130]{3,0,2,1:T(8,128)S(1)} %get-tuple-element.18), channel_id=1, source_target_pairs={{4,0},{8,4},{12,8},{16,12},{20,16},{24,20},{28,24},{5,1},{9,5},{13... | collective-permute-start | bytes 62408 | tf_op jit(solution)/shard_map/ppermute | solution.py:39
  84.6 10.5 %collective-permute-start.13 = (f32[5,1,3,3,4,128]{5,4,3,2,1,0:T(4,128)S(1)}, f32[5,1,3,3,4,128]{5,4,3,2,1,0:T(4,128)S(1)}, u32[]{:S(2)}, u32[]{:S(2)}) collective-permute-start(f32[5,1,3,3,4,128]{5,4,3,2,1,0:T(4,128)S(1)} %get-tuple-element.31), channel_id=1, source_target_pairs={{32,0},{64,32},{96,64},{128,96},{160,128},{192,160},{224,192},{33,... | collective-permute-start | bytes 276488 | tf_op jit(solution)/shard_map/ppermute | solution.py:27
  95.1 1.9 %collective-permute-start.12 = (f32[5,1,3,3,4,128]{5,4,3,2,1,0:T(4,128)S(1)}, f32[5,1,3,3,4,128]{5,4,3,2,1,0:T(4,128)S(1)}, u32[]{:S(2)}, u32[]{:S(2)}) collective-permute-start(f32[5,1,3,3,4,128]{5,4,3,2,1,0:T(4,128)S(1)} %get-tuple-element.32), channel_id=1, source_target_pairs={{0,32},{32,64},{64,96},{96,128},{128,160},{160,192},{192,224},{1,3... | collective-permute-start | bytes 276488 | tf_op jit(solution)/shard_map/ppermute | solution.py:24
  97.2 10.4 %collective-permute-done.12 = f32[5,1,3,3,4,128]{5,4,3,2,1,0:T(4,128)S(1)} collective-permute-done((f32[5,1,3,3,4,128]{5,4,3,2,1,0:T(4,128)S(1)}, f32[5,1,3,3,4,128]{5,4,3,2,1,0:T(4,128)S(1)}, u32[]{:S(2)}, u32[]{:S(2)}) %collective-permute-start.12) | collective-permute-done | bytes 92192 | tf_op jit(solution)/shard_map/ppermute | solution.py:24
  107.7 1.9 %collective-permute-start.14 = (f32[5,5,1,3,4,128]{5,4,3,2,1,0:T(4,128)S(1)}, f32[5,5,1,3,4,128]{5,4,3,2,1,0:T(4,128)S(1)}, u32[]{:S(2)}, u32[]{:S(2)}) collective-permute-start(f32[5,5,1,3,4,128]{5,4,3,2,1,0:T(4,128)S(1)} %get-tuple-element.29), channel_id=1, source_target_pairs={{0,4},{4,8},{8,12},{12,16},{16,20},{20,24},{24,28},{1,5},{5,9},{9,... | collective-permute-start | bytes 460808 | tf_op jit(solution)/shard_map/ppermute | solution.py:24
  109.7 3.8 %collective-permute-start.15 = (f32[5,5,1,3,4,128]{5,4,3,2,1,0:T(4,128)S(1)}, f32[5,5,1,3,4,128]{5,4,3,2,1,0:T(4,128)S(1)}, u32[]{:S(2)}, u32[]{:S(2)}) collective-permute-start(f32[5,5,1,3,4,128]{5,4,3,2,1,0:T(4,128)S(1)} %get-tuple-element.30), channel_id=1, source_target_pairs={{4,0},{8,4},{12,8},{16,12},{20,16},{24,20},{28,24},{5,1},{9,5},{13... | collective-permute-start | bytes 460808 | tf_op jit(solution)/shard_map/ppermute | solution.py:27
  113.7 6.8 %collective-permute-start.10 = (f32[5,8,16,1]{3,0,2,1:T(8,128)S(1)}, f32[5,8,16,1]{3,0,2,1:T(8,128)S(1)}, u32[]{:S(2)}, u32[]{:S(2)}) collective-permute-start(f32[5,8,16,1]{3,0,2,1:T(8,128)S(1)} %get-tuple-element.19), channel_id=1, source_target_pairs={{0,1},{1,2},{2,3},{4,5},{5,6},{6,7},{8,9},{9,10},{10,11},{12,13},{... | collective-permute-start | bytes 7688 | tf_op jit(solution)/shard_map/ppermute | solution.py:38
  120.4 1.3 collective-permute-start.11
  121.9 4.6 %collective-permute-start.16 = (f32[5,5,5,1,4,128]{5,4,3,2,1,0:T(4,128)S(1)}, f32[5,5,5,1,4,128]{5,4,3,2,1,0:T(4,128)S(1)}, u32[]{:S(2)}, u32[]{:S(2)}) collective-permute-start(f32[5,5,5,1,4,128]{5,4,3,2,1,0:T(4,128)S(1)} %get-tuple-element.21), channel_id=1, source_target_pairs={{0,1},{1,2},{2,3},{4,5},{5,6},{6,7},{8,9},{9,10},{10,11},{12,13},{... | collective-permute-start | bytes 768008 | tf_op jit(solution)/shard_map/ppermute | solution.py:24
  126.5 1.3 collective-permute-start.17
  127.8 4.9 %collective-permute-done.10 = f32[5,8,16,1]{3,0,2,1:T(8,128)S(1)} collective-permute-done((f32[5,8,16,1]{3,0,2,1:T(8,128)S(1)}, f32[5,8,16,1]{3,0,2,1:T(8,128)S(1)}, u32[]{:S(2)}, u32[]{:S(2)}) %collective-permute-start.10) | collective-permute-done | bytes 2592 | tf_op jit(solution)/shard_map/ppermute | solution.py:38
  132.7 4.4 %collective-permute-done.11 = f32[5,8,16,1]{3,0,2,1:T(8,128)S(1)} collective-permute-done((f32[5,8,16,1]{3,0,2,1:T(8,128)S(1)}, f32[5,8,16,1]{3,0,2,1:T(8,128)S(1)}, u32[]{:S(2)}, u32[]{:S(2)}) %collective-permute-start.11) | collective-permute-done | bytes 2592 | tf_op jit(solution)/shard_map/ppermute | solution.py:39
  138.7 2.6 %collective-permute-done.17 = f32[5,5,5,1,4,128]{5,4,3,2,1,0:T(4,128)S(1)} collective-permute-done((f32[5,5,5,1,4,128]{5,4,3,2,1,0:T(4,128)S(1)}, f32[5,5,5,1,4,128]{5,4,3,2,1,0:T(4,128)S(1)}, u32[]{:S(2)}, u32[]{:S(2)}) %collective-permute-start.17) | collective-permute-done | bytes 256032 | tf_op jit(solution)/shard_map/ppermute | solution.py:27
  (56 shorter events, 12.9 us)
Async XLA Ops:
  1.8 11.9 %copy-start.2 = (f32[5,8,16,128]{3,0,2,1:T(8,128)}, f32[5,8,16,128]{3,0,2,1:T(8,128)S(1)}, u32[]{:S(2)}) copy-start(f32[5,8,16,128]{3,0,2,1:T(8,128)S(1)} %copy.31) | copy-start | bytes 983044
  1.8 12.2 %collective-permute-start.1 = (f32[5,1,16,128]{3,0,2,1:T(8,128)S(1)}, f32[5,1,16,128]{3,0,2,1:T(8,128)S(1)}, u32[]{:S(2)}, u32[]{:S(2)}) collective-permute-start(f32[5,1,16,128]{3,0,2,1:T(8,128)S(1)} %get-tuple-element.28), channel_id=1, source_target_pairs={{0,32},{32,64},{64,96},{96,128},{128,160},{160,192},{192,224},{1,3... | collective-permute-start | bytes 122888 | tf_op jit(solution)/shard_map/ppermute | solution.py:24
  5.3 10.3 %collective-permute-start = (f32[5,1,16,128]{3,0,2,1:T(8,128)S(1)}, f32[5,1,16,128]{3,0,2,1:T(8,128)S(1)}, u32[]{:S(2)}, u32[]{:S(2)}) collective-permute-start(f32[5,1,16,128]{3,0,2,1:T(8,128)S(1)} %get-tuple-element.27), channel_id=1, source_target_pairs={{32,0},{64,32},{96,64},{128,96},{160,128},{192,160},{224,192},{33,... | collective-permute-start | bytes 122888 | tf_op jit(solution)/shard_map/ppermute | solution.py:27
  15.6 7.3 %copy-start.4 = (f32[5,1,16,128]{3,0,2,1:T(8,128)}, f32[5,1,16,128]{3,0,2,1:T(8,128)S(1)}, u32[]{:S(2)}) copy-start(f32[5,1,16,128]{3,0,2,1:T(8,128)S(1)} %collective-permute-done) | copy-start | bytes 122884
  15.6 6.4 %collective-permute-start.3 = (f32[5,10,1,128]{3,0,2,1:T(8,128)S(1)}, f32[5,10,1,128]{3,0,2,1:T(8,128)S(1)}, u32[]{:S(2)}, u32[]{:S(2)}) collective-permute-start(f32[5,10,1,128]{3,0,2,1:T(8,128)S(1)} %get-tuple-element.25), channel_id=1, source_target_pairs={{0,4},{4,8},{8,12},{12,16},{16,20},{20,24},{24,28},{1,5},{5,9},{9,... | collective-permute-start | bytes 76808 | tf_op jit(solution)/shard_map/ppermute | solution.py:24
  17.5 5.3 %collective-permute-start.2 = (f32[5,10,1,128]{3,0,2,1:T(8,128)S(1)}, f32[5,10,1,128]{3,0,2,1:T(8,128)S(1)}, u32[]{:S(2)}, u32[]{:S(2)}) collective-permute-start(f32[5,10,1,128]{3,0,2,1:T(8,128)S(1)} %get-tuple-element.26), channel_id=1, source_target_pairs={{4,0},{8,4},{12,8},{16,12},{20,16},{24,20},{28,24},{5,1},{9,5},{13... | collective-permute-start | bytes 76808 | tf_op jit(solution)/shard_map/ppermute | solution.py:27
  24.0 8.0 %collective-permute-start.4 = (f32[5,10,18,1]{2,3,1,0:T(1,128)S(1)}, f32[5,10,18,1]{2,3,1,0:T(1,128)S(1)}, u32[]{:S(2)}, u32[]{:S(2)}) collective-permute-start(f32[5,10,18,1]{2,3,1,0:T(1,128)S(1)} %copy.26), channel_id=1, source_target_pairs={{1,0},{2,1},{3,2},{5,4},{6,5},{7,6},{9,8},{10,9},{11,10},{13,12},{... | collective-permute-start | bytes 10808 | tf_op jit(solution)/shard_map/ppermute | solution.py:27
  25.3 6.1 %collective-permute-start.5 = (f32[5,10,18,1]{2,3,1,0:T(1,128)S(1)}, f32[5,10,18,1]{2,3,1,0:T(1,128)S(1)}, u32[]{:S(2)}, u32[]{:S(2)}) collective-permute-start(f32[5,10,18,1]{2,3,1,0:T(1,128)S(1)} %copy.28), channel_id=1, source_target_pairs={{0,1},{1,2},{2,3},{4,5},{5,6},{6,7},{8,9},{9,10},{10,11},{12,13},{... | collective-permute-start | bytes 10808 | tf_op jit(solution)/shard_map/ppermute | solution.py:24
  60.1 1.1 copy-start.1
  61.3 14.9 %collective-permute-start.6 = (f32[5,1,18,130]{3,0,2,1:T(8,128)S(1)}, f32[5,1,18,130]{3,0,2,1:T(8,128)S(1)}, u32[]{:S(2)}, u32[]{:S(2)}) collective-permute-start(f32[5,1,18,130]{3,0,2,1:T(8,128)S(1)} %get-tuple-element.15), channel_id=1, source_target_pairs={{0,32},{32,64},{64,96},{96,128},{128,160},{160,192},{192,224},{1,3... | collective-permute-start | bytes 140408 | tf_op jit(solution)/shard_map/ppermute | solution.py:38
  63.2 14.4 %collective-permute-start.7 = (f32[5,1,18,130]{3,0,2,1:T(8,128)S(1)}, f32[5,1,18,130]{3,0,2,1:T(8,128)S(1)}, u32[]{:S(2)}, u32[]{:S(2)}) collective-permute-start(f32[5,1,18,130]{3,0,2,1:T(8,128)S(1)} %get-tuple-element.16), channel_id=1, source_target_pairs={{32,0},{64,32},{96,64},{128,96},{160,128},{192,160},{224,192},{33,... | collective-permute-start | bytes 140408 | tf_op jit(solution)/shard_map/ppermute | solution.py:39
  79.0 18.1 %collective-permute-start.8 = (f32[5,8,1,130]{3,0,2,1:T(8,128)S(1)}, f32[5,8,1,130]{3,0,2,1:T(8,128)S(1)}, u32[]{:S(2)}, u32[]{:S(2)}) collective-permute-start(f32[5,8,1,130]{3,0,2,1:T(8,128)S(1)} %get-tuple-element.17), channel_id=1, source_target_pairs={{0,4},{4,8},{8,12},{12,16},{16,20},{20,24},{24,28},{1,5},{5,9},{9,... | collective-permute-start | bytes 62408 | tf_op jit(solution)/shard_map/ppermute | solution.py:38
  80.9 16.1 %collective-permute-start.9 = (f32[5,8,1,130]{3,0,2,1:T(8,128)S(1)}, f32[5,8,1,130]{3,0,2,1:T(8,128)S(1)}, u32[]{:S(2)}, u32[]{:S(2)}) collective-permute-start(f32[5,8,1,130]{3,0,2,1:T(8,128)S(1)} %get-tuple-element.18), channel_id=1, source_target_pairs={{4,0},{8,4},{12,8},{16,12},{20,16},{24,20},{28,24},{5,1},{9,5},{13... | collective-permute-start | bytes 62408 | tf_op jit(solution)/shard_map/ppermute | solution.py:39
  84.6 23.0 %collective-permute-start.13 = (f32[5,1,3,3,4,128]{5,4,3,2,1,0:T(4,128)S(1)}, f32[5,1,3,3,4,128]{5,4,3,2,1,0:T(4,128)S(1)}, u32[]{:S(2)}, u32[]{:S(2)}) collective-permute-start(f32[5,1,3,3,4,128]{5,4,3,2,1,0:T(4,128)S(1)} %get-tuple-element.31), channel_id=1, source_target_pairs={{32,0},{64,32},{96,64},{128,96},{160,128},{192,160},{224,192},{33,... | collective-permute-start | bytes 276488 | tf_op jit(solution)/shard_map/ppermute | solution.py:27
  95.1 12.5 %collective-permute-start.12 = (f32[5,1,3,3,4,128]{5,4,3,2,1,0:T(4,128)S(1)}, f32[5,1,3,3,4,128]{5,4,3,2,1,0:T(4,128)S(1)}, u32[]{:S(2)}, u32[]{:S(2)}) collective-permute-start(f32[5,1,3,3,4,128]{5,4,3,2,1,0:T(4,128)S(1)} %get-tuple-element.32), channel_id=1, source_target_pairs={{0,32},{32,64},{64,96},{96,128},{128,160},{160,192},{192,224},{1,3... | collective-permute-start | bytes 276488 | tf_op jit(solution)/shard_map/ppermute | solution.py:24
  107.7 14.0 %collective-permute-start.14 = (f32[5,5,1,3,4,128]{5,4,3,2,1,0:T(4,128)S(1)}, f32[5,5,1,3,4,128]{5,4,3,2,1,0:T(4,128)S(1)}, u32[]{:S(2)}, u32[]{:S(2)}) collective-permute-start(f32[5,5,1,3,4,128]{5,4,3,2,1,0:T(4,128)S(1)} %get-tuple-element.29), channel_id=1, source_target_pairs={{0,4},{4,8},{8,12},{12,16},{16,20},{20,24},{24,28},{1,5},{5,9},{9,... | collective-permute-start | bytes 460808 | tf_op jit(solution)/shard_map/ppermute | solution.py:24
  109.7 27.5 %copy-start = (f32[5,10,18,1]{3,0,2,1:T(8,128)S(1)}, f32[5,10,18,1]{3,0,2,1:T(8,128)}, u32[]{:S(2)}) copy-start(f32[5,10,18,1]{3,0,2,1:T(8,128)} %copy.27) | copy-start | bytes 10804
  109.7 27.5 %copy-start.3 = (f32[5,8,16,128]{3,0,2,1:T(8,128)S(1)}, f32[5,8,16,128]{3,0,2,1:T(8,128)}, u32[]{:S(2)}) copy-start(f32[5,8,16,128]{3,0,2,1:T(8,128)} %copy-done.2) | copy-start | bytes 983044
  109.7 27.5 %copy-start.5 = (f32[5,1,16,128]{3,0,2,1:T(8,128)S(1)}, f32[5,1,16,128]{3,0,2,1:T(8,128)}, u32[]{:S(2)}) copy-start(f32[5,1,16,128]{3,0,2,1:T(8,128)} %copy-done.4) | copy-start | bytes 122884
  109.7 27.5 %copy-start.6 = (f32[5]{0:T(128)S(1)}, f32[5]{0:T(128)}, u32[]{:S(2)}) copy-start(f32[5]{0:T(128)} %constant.23.clone) | copy-start | bytes 64
  109.7 12.1 %collective-permute-start.15 = (f32[5,5,1,3,4,128]{5,4,3,2,1,0:T(4,128)S(1)}, f32[5,5,1,3,4,128]{5,4,3,2,1,0:T(4,128)S(1)}, u32[]{:S(2)}, u32[]{:S(2)}) collective-permute-start(f32[5,5,1,3,4,128]{5,4,3,2,1,0:T(4,128)S(1)} %get-tuple-element.30), channel_id=1, source_target_pairs={{4,0},{8,4},{12,8},{16,12},{20,16},{24,20},{28,24},{5,1},{9,5},{13... | collective-permute-start | bytes 460808 | tf_op jit(solution)/shard_map/ppermute | solution.py:27
  113.7 19.0 %collective-permute-start.10 = (f32[5,8,16,1]{3,0,2,1:T(8,128)S(1)}, f32[5,8,16,1]{3,0,2,1:T(8,128)S(1)}, u32[]{:S(2)}, u32[]{:S(2)}) collective-permute-start(f32[5,8,16,1]{3,0,2,1:T(8,128)S(1)} %get-tuple-element.19), channel_id=1, source_target_pairs={{0,1},{1,2},{2,3},{4,5},{5,6},{6,7},{8,9},{9,10},{10,11},{12,13},{... | collective-permute-start | bytes 7688 | tf_op jit(solution)/shard_map/ppermute | solution.py:38
  120.4 16.7 %collective-permute-start.11 = (f32[5,8,16,1]{3,0,2,1:T(8,128)S(1)}, f32[5,8,16,1]{3,0,2,1:T(8,128)S(1)}, u32[]{:S(2)}, u32[]{:S(2)}) collective-permute-start(f32[5,8,16,1]{3,0,2,1:T(8,128)S(1)} %get-tuple-element.20), channel_id=1, source_target_pairs={{1,0},{2,1},{3,2},{5,4},{6,5},{7,6},{9,8},{10,9},{11,10},{13,12},{... | collective-permute-start | bytes 7688 | tf_op jit(solution)/shard_map/ppermute | solution.py:39
  121.9 16.8 %collective-permute-start.16 = (f32[5,5,5,1,4,128]{5,4,3,2,1,0:T(4,128)S(1)}, f32[5,5,5,1,4,128]{5,4,3,2,1,0:T(4,128)S(1)}, u32[]{:S(2)}, u32[]{:S(2)}) collective-permute-start(f32[5,5,5,1,4,128]{5,4,3,2,1,0:T(4,128)S(1)} %get-tuple-element.21), channel_id=1, source_target_pairs={{0,1},{1,2},{2,3},{4,5},{5,6},{6,7},{8,9},{9,10},{10,11},{12,13},{... | collective-permute-start | bytes 768008 | tf_op jit(solution)/shard_map/ppermute | solution.py:24
  126.5 14.8 %collective-permute-start.17 = (f32[5,5,5,1,4,128]{5,4,3,2,1,0:T(4,128)S(1)}, f32[5,5,5,1,4,128]{5,4,3,2,1,0:T(4,128)S(1)}, u32[]{:S(2)}, u32[]{:S(2)}) collective-permute-start(f32[5,5,5,1,4,128]{5,4,3,2,1,0:T(4,128)S(1)} %get-tuple-element.22), channel_id=1, source_target_pairs={{1,0},{2,1},{3,2},{5,4},{6,5},{7,6},{9,8},{10,9},{11,10},{13,12},{... | collective-permute-start | bytes 768008 | tf_op jit(solution)/shard_map/ppermute | solution.py:27

commit v9 on v6

--- a/solution.py
+++ b/solution.py
@@ -44,6 +44,39 @@
         high_pad[dim] = (span - 3, 0)
         block = inner + jnp.pad(below, low_pad) + jnp.pad(above, high_pad)
     return block
+
+
+def fold_and_widen(block, boxes, sides):
+    for axis, dim, box_dim in sides:
+        count = lax.axis_size(axis)
+        forward = [(i, i + 1) for i in range(count - 1)]
+        backward = [(target, source) for source, target in forward]
+        span = block.shape[dim]
+        width = boxes.shape[box_dim]
+        sends = lax.optimization_barrier(
+            (
+                lax.slice_in_dim(block, span - 1, span, axis=dim),
+                lax.slice_in_dim(block, 0, 1, axis=dim),
+                lax.slice_in_dim(boxes, width - 1, width, axis=box_dim),
+                lax.slice_in_dim(boxes, 0, 1, axis=box_dim),
+            )
+        )
+        below, above, box_below, box_above = lax.optimization_barrier(
+            (
+                lax.ppermute(sends[0], axis, forward),
+                lax.ppermute(sends[1], axis, backward),
+                lax.ppermute(sends[2], axis, forward),
+                lax.ppermute(sends[3], axis, backward),
+            )
+        )
+        inner = lax.slice_in_dim(block, 1, span - 1, axis=dim)
+        low_pad = [(0, 0)] * block.ndim
+        high_pad = [(0, 0)] * block.ndim
+        low_pad[dim] = (0, span - 3)
+        high_pad[dim] = (span - 3, 0)
+        block = inner + jnp.pad(below, low_pad) + jnp.pad(above, high_pad)
+        boxes = jnp.concatenate([box_below, boxes, box_above], axis=box_dim)
+    return block, boxes
 
 
 def parcel_update(current_condition, local_air_sample):
@@ -297,11 +330,12 @@
     kept = jnp.transpose(kept_rows, (1, 0, 2))
     deposit = deposit_rows.reshape(fields, DEPTH_ROWS, PAIR_LANES)[:, :span_z, :pair_count]
     deposit = jnp.transpose(deposit.reshape(fields, span_z, span_x, span_y), (0, 2, 3, 1))
-    cell_sources = fold_ghosts(deposit, (("gx", 1), ("gy", 2), ("gz", 3)))
+    outbox = outbox_rows.reshape((parcel_fields, 3, 3, 3, SLOTS, block_parcels))
+    cell_sources, widened = fold_and_widen(
+        deposit, outbox, (("gx", 1, 1), ("gy", 2, 2), ("gz", 3, 3))
+    )
     kappa = jnp.array(DIFFUSION, jnp.float32)[:, None, None, None]
     gas_next = gas_state + kappa * laplacian(padded) + COUPLING * cell_sources
-    outbox = outbox_rows.reshape((parcel_fields, 3, 3, 3, SLOTS, block_parcels))
-    widened = with_halo(outbox, (("gx", 1), ("gy", 2), ("gz", 3)), 1)
     arrived_boxes = widened[:, 0::2, 0::2, 0::2]
     arrived = jnp.transpose(
         arrived_boxes.reshape((parcel_fields, 27 * SLOTS, block_parcels)), (1, 0, 2)

time: 125 us -> 137 us (1.096)
  waiting for transfers between devices: 25.1 us -> 35.6 us
  starting transfers between devices: 57.9 us -> 59.8 us
    ppermute x6 -> x12, waiting for transfers between devices: 6.46 us -> 24.4 us  [the longest x3 14.7 us: fold_and_widen(): lax.ppermute(sends[1], axis, backward)]
    ppermute x6 -> x12, starting transfers between devices: 22 us -> 38.7 us  [the longest x3 12.8 us: fold_and_widen(): lax.ppermute(sends[0], axis, forward)]
    ppermute x6 -> x3, starting transfers between devices: 21.4 us -> 12.7 us  [with_halo(): lax.ppermute(lax.slice_in_dim(block, block.shape[dim] - width, None, axis...]
    ppermute x6 -> x3, starting transfers between devices: 14.5 us -> 8.47 us  [with_halo(): lax.ppermute(lax.slice_in_dim(block, 0, width, axis=dim), axis, backward)]
    ppermute x6 -> x3, waiting for transfers between devices: 6.85 us -> 1.53 us  [with_halo(): lax.ppermute(lax.slice_in_dim(block, block.shape[dim] - width, None, axis...]
    ppermute x6 -> x3, waiting for transfers between devices: 11.8 us -> 9.65 us  [with_halo(): lax.ppermute(lax.slice_in_dim(block, 0, width, axis=dim), axis, backward)]
    unnamed x16 -> x18, local copies, waits for them, and re-layouts: 5.08 us -> 5.12 us
  transfers between devices with their start and end apart: 18 -> 18, of which waited for: 9 -> 8; matrix products, arithmetic and copies ran while one was open for 5% -> 2% of each run, Pallas kernels for 0% -> 0%
where the time goes in v9:
time: 137 us; the launch traced here: 135 us
  starting transfers between devices  59.8 us (44%)
  waiting for transfers between devices  35.6 us (26%)
  Pallas kernels  20 us (15%)
  local copies, waits for them, and re-layouts  12.4 us (9%)
  other arithmetic  5.09 us (4%)
  between operations  1.63 us (1%)
    pallas_call x1, Pallas kernels, local(): pl.pallas_call(functools.partial(coupling_kernel, span_y=span_y, span_z=s...  20 us
    ppermute x3, waiting for transfers between devices, fold_and_widen(): lax.ppermute(sends[1], axis, backward)  14.7 us
    ppermute x3, starting transfers between devices, fold_and_widen(): lax.ppermute(sends[0], axis, forward)  12.8 us
    ppermute x3, starting transfers between devices, with_halo(): lax.ppermute(lax.slice_in_dim(block, block.shape[dim] - width, None, axis...  12.7 us
    ppermute x3, starting transfers between devices, fold_and_widen(): lax.ppermute(sends[3], axis, backward)  10.5 us
    ppermute x3, waiting for transfers between devices, fold_and_widen(): lax.ppermute(sends[0], axis, forward)  9.66 us
    ppermute x3, waiting for transfers between devices, with_halo(): lax.ppermute(lax.slice_in_dim(block, 0, width, axis=dim), axis, backward)  9.65 us
    ppermute x3, starting transfers between devices, with_halo(): lax.ppermute(lax.slice_in_dim(block, 0, width, axis=dim), axis, backward)  8.47 us
  transfers between devices with their start and end apart: 18, of which 8 were waited for; matrix products, arithmetic and copies ran while one was open for 2% of the time, Pallas kernels for 0%

profile of v9, /device:TPU:58, one launch (start us, length us, event | category | flops | bytes accessed | tf_op | source)
XLA Modules:
  0.0 134.5 jit_solution(13301239910298115257)
XLA Ops:
  1.4 7.8 %collective-permute-start.1 = (f32[5,1,16,128]{3,2,1,0:T(8,128)S(1)}, f32[5,1,16,128]{3,2,1,0:T(8,128)S(1)}, u32[]{:S(2)}, u32[]{:S(2)}) collective-permute-start(f32[5,1,16,128]{3,2,1,0:T(8,128)S(1)} %get-tuple-element.72), channel_id=1, source_target_pairs={{0,32},{32,64},{64,96},{96,128},{128,160},{160,192},{192,224},{1,3... | collective-permute-start | bytes 122888 | tf_op jit(solution)/shard_map/ppermute | solution.py:24
  9.3 1.9 %collective-permute-start = (f32[5,1,16,128]{3,2,1,0:T(8,128)S(1)}, f32[5,1,16,128]{3,2,1,0:T(8,128)S(1)}, u32[]{:S(2)}, u32[]{:S(2)}) collective-permute-start(f32[5,1,16,128]{3,2,1,0:T(8,128)S(1)} %get-tuple-element.71), channel_id=1, source_target_pairs={{32,0},{64,32},{96,64},{128,96},{160,128},{192,160},{224,192},{33,... | collective-permute-start | bytes 122888 | tf_op jit(solution)/shard_map/ppermute | solution.py:27
  11.3 1.0 constant_dynamic-update-slice_fusion.1
  12.3 8.9 %collective-permute-done = f32[5,1,16,128]{3,2,1,0:T(8,128)S(1)} collective-permute-done((f32[5,1,16,128]{3,2,1,0:T(8,128)S(1)}, f32[5,1,16,128]{3,2,1,0:T(8,128)S(1)}, u32[]{:S(2)}, u32[]{:S(2)}) %collective-permute-start) | collective-permute-done | bytes 40992 | tf_op jit(solution)/shard_map/ppermute | solution.py:27
  21.3 1.9 %collective-permute-start.3 = (f32[5,10,1,128]{3,2,1,0:T(1,128)S(1)}, f32[5,10,1,128]{3,2,1,0:T(1,128)S(1)}, u32[]{:S(2)}, u32[]{:S(2)}) collective-permute-start(f32[5,10,1,128]{3,2,1,0:T(1,128)S(1)} %get-tuple-element.69), channel_id=1, source_target_pairs={{0,4},{4,8},{8,12},{12,16},{16,20},{20,24},{24,28},{1,5},{5,9},{9,... | collective-permute-start | bytes 76808 | tf_op jit(solution)/shard_map/ppermute | solution.py:24
  23.2 3.6 %collective-permute-start.2 = (f32[5,10,1,128]{3,2,1,0:T(1,128)S(1)}, f32[5,10,1,128]{3,2,1,0:T(1,128)S(1)}, u32[]{:S(2)}, u32[]{:S(2)}) collective-permute-start(f32[5,10,1,128]{3,2,1,0:T(1,128)S(1)} %get-tuple-element.70), channel_id=1, source_target_pairs={{4,0},{8,4},{12,8},{16,12},{20,16},{24,20},{28,24},{5,1},{9,5},{13... | collective-permute-start | bytes 76808 | tf_op jit(solution)/shard_map/ppermute | solution.py:27
  29.5 2.9 %collective-permute-start.4 = (f32[5,10,18,1]{2,3,1,0:T(1,128)S(1)}, f32[5,10,18,1]{2,3,1,0:T(1,128)S(1)}, u32[]{:S(2)}, u32[]{:S(2)}) collective-permute-start(f32[5,10,18,1]{2,3,1,0:T(1,128)S(1)} %copy.14), channel_id=1, source_target_pairs={{1,0},{2,1},{3,2},{5,4},{6,5},{7,6},{9,8},{10,9},{11,10},{13,12},{... | collective-permute-start | bytes 10808 | tf_op jit(solution)/shard_map/ppermute | solution.py:27
  32.4 2.9 %collective-permute-start.5 = (f32[5,10,18,1]{2,3,1,0:T(1,128)S(1)}, f32[5,10,18,1]{2,3,1,0:T(1,128)S(1)}, u32[]{:S(2)}, u32[]{:S(2)}) collective-permute-start(f32[5,10,18,1]{2,3,1,0:T(1,128)S(1)} %copy.16), channel_id=1, source_target_pairs={{0,1},{1,2},{2,3},{4,5},{5,6},{6,7},{8,9},{9,10},{10,11},{12,13},{... | collective-permute-start | bytes 10808 | tf_op jit(solution)/shard_map/ppermute | solution.py:24
  36.6 1.5 %collective-permute-done.5 = f32[5,10,18,1]{2,3,1,0:T(1,128)S(1)} collective-permute-done((f32[5,10,18,1]{2,3,1,0:T(1,128)S(1)}, f32[5,10,18,1]{2,3,1,0:T(1,128)S(1)}, u32[]{:S(2)}, u32[]{:S(2)}) %collective-permute-start.5) | collective-permute-done | bytes 3632 | tf_op jit(solution)/shard_map/ppermute | solution.py:24
  39.7 1.1 reshape.25
  40.8 1.6 %copy.23 = f32[5,130,180]{2,1,0:T(8,128)S(1)} copy(f32[5,130,180]{1,2,0:T(8,128)} %reshape.25) | data formatting | bytes 936000
  43.3 20.0 %shard_map.94 = (f32[5,32,128]{2,1,0:T(8,128)}, f32[5,108,128]{2,1,0:T(8,128)}, f32[680,256]{1,0:T(8,128)}) custom-call(s32[1]{0:T(128)S(6)} %copy.28.live_ref, s32[32]{0:T(128)} %dest_ref.1, f32[680,256]{1,0:T(8,128)} %bitcast.16, f32[5,32,128]{2,1,0:T(8,128)} %bitcast.20, s32[32,128]{1,0:T(8,128)} %cell_ref.1, f32[3,32,128]{2,1,0:T(8,128)} %bitcast.21, ...), custom_call_target="tpu_custom_call" | custom-call | tf_op jit(solution)/shard_map/pallas_call | solution.py:311
  63.3 2.5 %copy.22 = f32[5,130,180]{1,2,0:T(8,128)} copy(f32[5,130,180]{2,1,0:T(8,128)} %bitcast.17) | data formatting | bytes 936000
  65.9 1.3 reshape.28
  67.3 1.9 %collective-permute-start.8 = (f32[5,1,3,3,4,128]{5,4,3,2,1,0:T(4,128)S(1)}, f32[5,1,3,3,4,128]{5,4,3,2,1,0:T(4,128)S(1)}, u32[]{:S(2)}, u32[]{:S(2)}) collective-permute-start(f32[5,1,3,3,4,128]{5,4,3,2,1,0:T(4,128)S(1)} %get-tuple-element.34), channel_id=1, source_target_pairs={{0,32},{32,64},{64,96},{96,128},{128,160},{160,192},{192,224},{1,3... | collective-permute-start | bytes 276488 | tf_op jit(solution)/shard_map/ppermute | solution.py:68
  69.2 3.9 %collective-permute-start.9 = (f32[5,1,3,3,4,128]{5,4,3,2,1,0:T(4,128)S(1)}, f32[5,1,3,3,4,128]{5,4,3,2,1,0:T(4,128)S(1)}, u32[]{:S(2)}, u32[]{:S(2)}) collective-permute-start(f32[5,1,3,3,4,128]{5,4,3,2,1,0:T(4,128)S(1)} %get-tuple-element.35), channel_id=1, source_target_pairs={{32,0},{64,32},{96,64},{128,96},{160,128},{192,160},{224,192},{33,... | collective-permute-start | bytes 276488 | tf_op jit(solution)/shard_map/ppermute | solution.py:69
  73.1 7.9 %collective-permute-start.6 = (f32[5,1,18,130]{3,2,1,0:T(8,128)S(1)}, f32[5,1,18,130]{3,2,1,0:T(8,128)S(1)}, u32[]{:S(2)}, u32[]{:S(2)}) collective-permute-start(f32[5,1,18,130]{3,2,1,0:T(8,128)S(1)} %get-tuple-element.32), channel_id=1, source_target_pairs={{0,32},{32,64},{64,96},{96,128},{128,160},{160,192},{192,224},{1,3... | collective-permute-start | bytes 140408 | tf_op jit(solution)/shard_map/ppermute | solution.py:66
  81.1 1.9 %collective-permute-start.7 = (f32[5,1,18,130]{3,2,1,0:T(8,128)S(1)}, f32[5,1,18,130]{3,2,1,0:T(8,128)S(1)}, u32[]{:S(2)}, u32[]{:S(2)}) collective-permute-start(f32[5,1,18,130]{3,2,1,0:T(8,128)S(1)} %get-tuple-element.33), channel_id=1, source_target_pairs={{32,0},{64,32},{96,64},{128,96},{160,128},{192,160},{224,192},{33,... | collective-permute-start | bytes 140408 | tf_op jit(solution)/shard_map/ppermute | solution.py:67
  83.0 3.3 %collective-permute-done.6 = f32[5,1,18,130]{3,2,1,0:T(8,128)S(1)} collective-permute-done((f32[5,1,18,130]{3,2,1,0:T(8,128)S(1)}, f32[5,1,18,130]{3,2,1,0:T(8,128)S(1)}, u32[]{:S(2)}, u32[]{:S(2)}) %collective-permute-start.6) | collective-permute-done | bytes 46832 | tf_op jit(solution)/shard_map/ppermute | solution.py:66
  86.3 10.1 %collective-permute-done.7 = f32[5,1,18,130]{3,2,1,0:T(8,128)S(1)} collective-permute-done((f32[5,1,18,130]{3,2,1,0:T(8,128)S(1)}, f32[5,1,18,130]{3,2,1,0:T(8,128)S(1)}, u32[]{:S(2)}, u32[]{:S(2)}) %collective-permute-start.7) | collective-permute-done | bytes 46832 | tf_op jit(solution)/shard_map/ppermute | solution.py:67
  96.8 1.9 %collective-permute-start.12 = (f32[5,5,1,3,4,128]{5,4,3,2,1,0:T(4,128)S(1)}, f32[5,5,1,3,4,128]{5,4,3,2,1,0:T(4,128)S(1)}, u32[]{:S(2)}, u32[]{:S(2)}) collective-permute-start(f32[5,5,1,3,4,128]{5,4,3,2,1,0:T(4,128)S(1)} %get-tuple-element.42), channel_id=1, source_target_pairs={{0,4},{4,8},{8,12},{12,16},{16,20},{20,24},{24,28},{1,5},{5,9},{9,... | collective-permute-start | bytes 460808 | tf_op jit(solution)/shard_map/ppermute | solution.py:68
  98.7 3.6 %collective-permute-start.13 = (f32[5,5,1,3,4,128]{5,4,3,2,1,0:T(4,128)S(1)}, f32[5,5,1,3,4,128]{5,4,3,2,1,0:T(4,128)S(1)}, u32[]{:S(2)}, u32[]{:S(2)}) collective-permute-start(f32[5,5,1,3,4,128]{5,4,3,2,1,0:T(4,128)S(1)} %get-tuple-element.43), channel_id=1, source_target_pairs={{4,0},{8,4},{12,8},{16,12},{20,16},{24,20},{28,24},{5,1},{9,5},{13... | collective-permute-start | bytes 460808 | tf_op jit(solution)/shard_map/ppermute | solution.py:69
  102.3 2.0 %collective-permute-start.10 = (f32[5,8,1,130]{3,2,1,0:T(1,128)S(1)}, f32[5,8,1,130]{3,2,1,0:T(1,128)S(1)}, u32[]{:S(2)}, u32[]{:S(2)}) collective-permute-start(f32[5,8,1,130]{3,2,1,0:T(1,128)S(1)} %get-tuple-element.40), channel_id=1, source_target_pairs={{0,4},{4,8},{8,12},{12,16},{16,20},{20,24},{24,28},{1,5},{5,9},{9,... | collective-permute-start | bytes 62408 | tf_op jit(solution)/shard_map/ppermute | solution.py:66
  104.3 3.6 %collective-permute-start.11 = (f32[5,8,1,130]{3,2,1,0:T(1,128)S(1)}, f32[5,8,1,130]{3,2,1,0:T(1,128)S(1)}, u32[]{:S(2)}, u32[]{:S(2)}) collective-permute-start(f32[5,8,1,130]{3,2,1,0:T(1,128)S(1)} %get-tuple-element.41), channel_id=1, source_target_pairs={{4,0},{8,4},{12,8},{16,12},{20,16},{24,20},{28,24},{5,1},{9,5},{13... | collective-permute-start | bytes 62408 | tf_op jit(solution)/shard_map/ppermute | solution.py:67
  107.9 1.6 %collective-permute-done.11 = f32[5,8,1,130]{3,2,1,0:T(1,128)S(1)} collective-permute-done((f32[5,8,1,130]{3,2,1,0:T(1,128)S(1)}, f32[5,8,1,130]{3,2,1,0:T(1,128)S(1)}, u32[]{:S(2)}, u32[]{:S(2)}) %collective-permute-start.11) | collective-permute-done | bytes 20832 | tf_op jit(solution)/shard_map/ppermute | solution.py:67
  110.0 3.1 %collective-permute-start.16 = (f32[5,5,5,1,4,128]{5,4,3,2,1,0:T(4,128)S(1)}, f32[5,5,5,1,4,128]{5,4,3,2,1,0:T(4,128)S(1)}, u32[]{:S(2)}, u32[]{:S(2)}) collective-permute-start(f32[5,5,5,1,4,128]{5,4,3,2,1,0:T(4,128)S(1)} %get-tuple-element.50), channel_id=1, source_target_pairs={{0,1},{1,2},{2,3},{4,5},{5,6},{6,7},{8,9},{9,10},{10,11},{12,13},{... | collective-permute-start | bytes 768008 | tf_op jit(solution)/shard_map/ppermute | solution.py:68
  113.1 2.9 %collective-permute-start.17 = (f32[5,5,5,1,4,128]{5,4,3,2,1,0:T(4,128)S(1)}, f32[5,5,5,1,4,128]{5,4,3,2,1,0:T(4,128)S(1)}, u32[]{:S(2)}, u32[]{:S(2)}) collective-permute-start(f32[5,5,5,1,4,128]{5,4,3,2,1,0:T(4,128)S(1)} %get-tuple-element.51), channel_id=1, source_target_pairs={{1,0},{2,1},{3,2},{5,4},{6,5},{7,6},{9,8},{10,9},{11,10},{13,12},{... | collective-permute-start | bytes 768008 | tf_op jit(solution)/shard_map/ppermute | solution.py:69
  116.0 2.9 %collective-permute-start.14 = (f32[5,8,16,1]{3,2,1,0:T(8,128)S(1)}, f32[5,8,16,1]{3,2,1,0:T(8,128)S(1)}, u32[]{:S(2)}, u32[]{:S(2)}) collective-permute-start(f32[5,8,16,1]{3,2,1,0:T(8,128)S(1)} %get-tuple-element.48), channel_id=1, source_target_pairs={{0,1},{1,2},{2,3},{4,5},{5,6},{6,7},{8,9},{9,10},{10,11},{12,13},{... | collective-permute-start | bytes 7688 | tf_op jit(solution)/shard_map/ppermute | solution.py:66
  118.9 2.9 %collective-permute-start.15 = (f32[5,8,16,1]{3,2,1,0:T(8,128)S(1)}, f32[5,8,16,1]{3,2,1,0:T(8,128)S(1)}, u32[]{:S(2)}, u32[]{:S(2)}) collective-permute-start(f32[5,8,16,1]{3,2,1,0:T(8,128)S(1)} %get-tuple-element.49), channel_id=1, source_target_pairs={{1,0},{2,1},{3,2},{5,4},{6,5},{7,6},{9,8},{10,9},{11,10},{13,12},{... | collective-permute-start | bytes 7688 | tf_op jit(solution)/shard_map/ppermute | solution.py:67
  121.9 6.3 %collective-permute-done.14 = f32[5,8,16,1]{3,2,1,0:T(8,128)S(1)} collective-permute-done((f32[5,8,16,1]{3,2,1,0:T(8,128)S(1)}, f32[5,8,16,1]{3,2,1,0:T(8,128)S(1)}, u32[]{:S(2)}, u32[]{:S(2)}) %collective-permute-start.14) | collective-permute-done | bytes 2592 | tf_op jit(solution)/shard_map/ppermute | solution.py:66
  128.2 2.9 %collective-permute-done.15 = f32[5,8,16,1]{3,2,1,0:T(8,128)S(1)} collective-permute-done((f32[5,8,16,1]{3,2,1,0:T(8,128)S(1)}, f32[5,8,16,1]{3,2,1,0:T(8,128)S(1)}, u32[]{:S(2)}, u32[]{:S(2)}) %collective-permute-start.15) | collective-permute-done | bytes 2592 | tf_op jit(solution)/shard_map/ppermute | solution.py:67
  132.3 2.2 %fusion.4 = f32[5,8,16,128]{3,2,1,0:T(8,128)} fusion(f32[5,8,16,130]{3,2,1,0:T(8,128)S(1)} %fusion.1, f32[5,8,16,128]{3,2,1,0:T(8,128)S(1)} %copy-done, f32[5,10,18,1]{3,2,1,0:T(8,128)S(1)} %copy.17, f32[5,10,1,128]{3,2,1,0:T(1,128)} %copy-done.3, f32[5,10,16,128]{3,2,1,0:T(8,128)S(1)} %constant_dynamic-update-slice_fusion, f32[5,10,1,128]{3,2,1,0:T(1,128)} %copy-done.2, ...), kind=kLoop, calls=%fused_computation.10 | loop fusion | flops 1884160 | bytes 1538100 | tf_op jit(solution)/shard_map/add | solution.py:338
  (52 shorter events, 8.6 us)
Async XLA Ops:
  1.4 9.8 %collective-permute-start.1 = (f32[5,1,16,128]{3,2,1,0:T(8,128)S(1)}, f32[5,1,16,128]{3,2,1,0:T(8,128)S(1)}, u32[]{:S(2)}, u32[]{:S(2)}) collective-permute-start(f32[5,1,16,128]{3,2,1,0:T(8,128)S(1)} %get-tuple-element.72), channel_id=1, source_target_pairs={{0,32},{32,64},{64,96},{96,128},{128,160},{160,192},{192,224},{1,3... | collective-permute-start | bytes 122888 | tf_op jit(solution)/shard_map/ppermute | solution.py:24
  9.3 11.9 %collective-permute-start = (f32[5,1,16,128]{3,2,1,0:T(8,128)S(1)}, f32[5,1,16,128]{3,2,1,0:T(8,128)S(1)}, u32[]{:S(2)}, u32[]{:S(2)}) collective-permute-start(f32[5,1,16,128]{3,2,1,0:T(8,128)S(1)} %get-tuple-element.71), channel_id=1, source_target_pairs={{32,0},{64,32},{96,64},{128,96},{160,128},{192,160},{224,192},{33,... | collective-permute-start | bytes 122888 | tf_op jit(solution)/shard_map/ppermute | solution.py:27
  11.2 17.1 %copy-start.4 = (f32[5,1,16,128]{3,2,1,0:T(8,128)}, f32[5,1,16,128]{3,2,1,0:T(8,128)S(1)}, u32[]{:S(2)}) copy-start(f32[5,1,16,128]{3,2,1,0:T(8,128)S(1)} %collective-permute-done.1) | copy-start | bytes 122884
  21.2 7.1 %copy-start.5 = (f32[5,1,16,128]{3,2,1,0:T(8,128)}, f32[5,1,16,128]{3,2,1,0:T(8,128)S(1)}, u32[]{:S(2)}) copy-start(f32[5,1,16,128]{3,2,1,0:T(8,128)S(1)} %collective-permute-done) | copy-start | bytes 122884
  21.3 6.4 %collective-permute-start.3 = (f32[5,10,1,128]{3,2,1,0:T(1,128)S(1)}, f32[5,10,1,128]{3,2,1,0:T(1,128)S(1)}, u32[]{:S(2)}, u32[]{:S(2)}) collective-permute-start(f32[5,10,1,128]{3,2,1,0:T(1,128)S(1)} %get-tuple-element.69), channel_id=1, source_target_pairs={{0,4},{4,8},{8,12},{12,16},{16,20},{20,24},{24,28},{1,5},{5,9},{9,... | collective-permute-start | bytes 76808 | tf_op jit(solution)/shard_map/ppermute | solution.py:24
  23.2 5.2 %collective-permute-start.2 = (f32[5,10,1,128]{3,2,1,0:T(1,128)S(1)}, f32[5,10,1,128]{3,2,1,0:T(1,128)S(1)}, u32[]{:S(2)}, u32[]{:S(2)}) collective-permute-start(f32[5,10,1,128]{3,2,1,0:T(1,128)S(1)} %get-tuple-element.70), channel_id=1, source_target_pairs={{4,0},{8,4},{12,8},{16,12},{20,16},{24,20},{28,24},{5,1},{9,5},{13... | collective-permute-start | bytes 76808 | tf_op jit(solution)/shard_map/ppermute | solution.py:27
  27.6 11.3 %copy-start.2 = (f32[5,10,1,128]{3,2,1,0:T(1,128)}, f32[5,10,1,128]{3,2,1,0:T(1,128)S(1)}, u32[]{:S(2)}) copy-start(f32[5,10,1,128]{3,2,1,0:T(1,128)S(1)} %collective-permute-done.3) | copy-start | bytes 76804
  28.3 10.6 %copy-start.3 = (f32[5,10,1,128]{3,2,1,0:T(1,128)}, f32[5,10,1,128]{3,2,1,0:T(1,128)S(1)}, u32[]{:S(2)}) copy-start(f32[5,10,1,128]{3,2,1,0:T(1,128)S(1)} %collective-permute-done.2) | copy-start | bytes 76804
  29.5 9.1 %collective-permute-start.4 = (f32[5,10,18,1]{2,3,1,0:T(1,128)S(1)}, f32[5,10,18,1]{2,3,1,0:T(1,128)S(1)}, u32[]{:S(2)}, u32[]{:S(2)}) collective-permute-start(f32[5,10,18,1]{2,3,1,0:T(1,128)S(1)} %copy.14), channel_id=1, source_target_pairs={{1,0},{2,1},{3,2},{5,4},{6,5},{7,6},{9,8},{10,9},{11,10},{13,12},{... | collective-permute-start | bytes 10808 | tf_op jit(solution)/shard_map/ppermute | solution.py:27
  32.4 5.7 %collective-permute-start.5 = (f32[5,10,18,1]{2,3,1,0:T(1,128)S(1)}, f32[5,10,18,1]{2,3,1,0:T(1,128)S(1)}, u32[]{:S(2)}, u32[]{:S(2)}) collective-permute-start(f32[5,10,18,1]{2,3,1,0:T(1,128)S(1)} %copy.16), channel_id=1, source_target_pairs={{0,1},{1,2},{2,3},{4,5},{5,6},{6,7},{8,9},{9,10},{10,11},{12,13},{... | collective-permute-start | bytes 10808 | tf_op jit(solution)/shard_map/ppermute | solution.py:24
  63.3 2.5 %copy-start.1 = (f32[5,108,128]{2,1,0:T(8,128)S(1)}, f32[5,108,128]{2,1,0:T(8,128)}, u32[]{:S(2)}) copy-start(f32[5,108,128]{2,1,0:T(8,128)} %get-tuple-element.31) | copy-start | bytes 829444
  67.3 29.2 %collective-permute-start.8 = (f32[5,1,3,3,4,128]{5,4,3,2,1,0:T(4,128)S(1)}, f32[5,1,3,3,4,128]{5,4,3,2,1,0:T(4,128)S(1)}, u32[]{:S(2)}, u32[]{:S(2)}) collective-permute-start(f32[5,1,3,3,4,128]{5,4,3,2,1,0:T(4,128)S(1)} %get-tuple-element.34), channel_id=1, source_target_pairs={{0,32},{32,64},{64,96},{96,128},{128,160},{160,192},{192,224},{1,3... | collective-permute-start | bytes 276488 | tf_op jit(solution)/shard_map/ppermute | solution.py:68
  69.2 27.3 %collective-permute-start.9 = (f32[5,1,3,3,4,128]{5,4,3,2,1,0:T(4,128)S(1)}, f32[5,1,3,3,4,128]{5,4,3,2,1,0:T(4,128)S(1)}, u32[]{:S(2)}, u32[]{:S(2)}) collective-permute-start(f32[5,1,3,3,4,128]{5,4,3,2,1,0:T(4,128)S(1)} %get-tuple-element.35), channel_id=1, source_target_pairs={{32,0},{64,32},{96,64},{128,96},{160,128},{192,160},{224,192},{33,... | collective-permute-start | bytes 276488 | tf_op jit(solution)/shard_map/ppermute | solution.py:69
  73.1 13.2 %collective-permute-start.6 = (f32[5,1,18,130]{3,2,1,0:T(8,128)S(1)}, f32[5,1,18,130]{3,2,1,0:T(8,128)S(1)}, u32[]{:S(2)}, u32[]{:S(2)}) collective-permute-start(f32[5,1,18,130]{3,2,1,0:T(8,128)S(1)} %get-tuple-element.32), channel_id=1, source_target_pairs={{0,32},{32,64},{64,96},{96,128},{128,160},{160,192},{192,224},{1,3... | collective-permute-start | bytes 140408 | tf_op jit(solution)/shard_map/ppermute | solution.py:66
  81.1 15.4 %collective-permute-start.7 = (f32[5,1,18,130]{3,2,1,0:T(8,128)S(1)}, f32[5,1,18,130]{3,2,1,0:T(8,128)S(1)}, u32[]{:S(2)}, u32[]{:S(2)}) collective-permute-start(f32[5,1,18,130]{3,2,1,0:T(8,128)S(1)} %get-tuple-element.33), channel_id=1, source_target_pairs={{32,0},{64,32},{96,64},{128,96},{160,128},{192,160},{224,192},{33,... | collective-permute-start | bytes 140408 | tf_op jit(solution)/shard_map/ppermute | solution.py:67
  96.8 12.8 %collective-permute-start.12 = (f32[5,5,1,3,4,128]{5,4,3,2,1,0:T(4,128)S(1)}, f32[5,5,1,3,4,128]{5,4,3,2,1,0:T(4,128)S(1)}, u32[]{:S(2)}, u32[]{:S(2)}) collective-permute-start(f32[5,5,1,3,4,128]{5,4,3,2,1,0:T(4,128)S(1)} %get-tuple-element.42), channel_id=1, source_target_pairs={{0,4},{4,8},{8,12},{12,16},{16,20},{20,24},{24,28},{1,5},{5,9},{9,... | collective-permute-start | bytes 460808 | tf_op jit(solution)/shard_map/ppermute | solution.py:68
  98.7 10.9 %collective-permute-start.13 = (f32[5,5,1,3,4,128]{5,4,3,2,1,0:T(4,128)S(1)}, f32[5,5,1,3,4,128]{5,4,3,2,1,0:T(4,128)S(1)}, u32[]{:S(2)}, u32[]{:S(2)}) collective-permute-start(f32[5,5,1,3,4,128]{5,4,3,2,1,0:T(4,128)S(1)} %get-tuple-element.43), channel_id=1, source_target_pairs={{4,0},{8,4},{12,8},{16,12},{20,16},{24,20},{28,24},{5,1},{9,5},{13... | collective-permute-start | bytes 460808 | tf_op jit(solution)/shard_map/ppermute | solution.py:69
  102.3 5.6 %collective-permute-start.10 = (f32[5,8,1,130]{3,2,1,0:T(1,128)S(1)}, f32[5,8,1,130]{3,2,1,0:T(1,128)S(1)}, u32[]{:S(2)}, u32[]{:S(2)}) collective-permute-start(f32[5,8,1,130]{3,2,1,0:T(1,128)S(1)} %get-tuple-element.40), channel_id=1, source_target_pairs={{0,4},{4,8},{8,12},{12,16},{16,20},{20,24},{24,28},{1,5},{5,9},{9,... | collective-permute-start | bytes 62408 | tf_op jit(solution)/shard_map/ppermute | solution.py:66
  104.3 5.3 %collective-permute-start.11 = (f32[5,8,1,130]{3,2,1,0:T(1,128)S(1)}, f32[5,8,1,130]{3,2,1,0:T(1,128)S(1)}, u32[]{:S(2)}, u32[]{:S(2)}) collective-permute-start(f32[5,8,1,130]{3,2,1,0:T(1,128)S(1)} %get-tuple-element.41), channel_id=1, source_target_pairs={{4,0},{8,4},{12,8},{16,12},{20,16},{24,20},{28,24},{5,1},{9,5},{13... | collective-permute-start | bytes 62408 | tf_op jit(solution)/shard_map/ppermute | solution.py:67
  110.0 22.3 %copy-start = (f32[5,8,16,128]{3,2,1,0:T(8,128)S(1)}, f32[5,8,16,128]{3,2,1,0:T(8,128)}, u32[]{:S(2)}) copy-start(f32[5,8,16,128]{3,2,1,0:T(8,128)} %param.7) | copy-start | bytes 983044
  110.0 21.2 %collective-permute-start.16 = (f32[5,5,5,1,4,128]{5,4,3,2,1,0:T(4,128)S(1)}, f32[5,5,5,1,4,128]{5,4,3,2,1,0:T(4,128)S(1)}, u32[]{:S(2)}, u32[]{:S(2)}) collective-permute-start(f32[5,5,5,1,4,128]{5,4,3,2,1,0:T(4,128)S(1)} %get-tuple-element.50), channel_id=1, source_target_pairs={{0,1},{1,2},{2,3},{4,5},{5,6},{6,7},{8,9},{9,10},{10,11},{12,13},{... | collective-permute-start | bytes 768008 | tf_op jit(solution)/shard_map/ppermute | solution.py:68
  113.1 18.1 %collective-permute-start.17 = (f32[5,5,5,1,4,128]{5,4,3,2,1,0:T(4,128)S(1)}, f32[5,5,5,1,4,128]{5,4,3,2,1,0:T(4,128)S(1)}, u32[]{:S(2)}, u32[]{:S(2)}) collective-permute-start(f32[5,5,5,1,4,128]{5,4,3,2,1,0:T(4,128)S(1)} %get-tuple-element.51), channel_id=1, source_target_pairs={{1,0},{2,1},{3,2},{5,4},{6,5},{7,6},{9,8},{10,9},{11,10},{13,12},{... | collective-permute-start | bytes 768008 | tf_op jit(solution)/shard_map/ppermute | solution.py:69
  116.0 12.2 %collective-permute-start.14 = (f32[5,8,16,1]{3,2,1,0:T(8,128)S(1)}, f32[5,8,16,1]{3,2,1,0:T(8,128)S(1)}, u32[]{:S(2)}, u32[]{:S(2)}) collective-permute-start(f32[5,8,16,1]{3,2,1,0:T(8,128)S(1)} %get-tuple-element.48), channel_id=1, source_target_pairs={{0,1},{1,2},{2,3},{4,5},{5,6},{6,7},{8,9},{9,10},{10,11},{12,13},{... | collective-permute-start | bytes 7688 | tf_op jit(solution)/shard_map/ppermute | solution.py:66
  118.9 12.2 %collective-permute-start.15 = (f32[5,8,16,1]{3,2,1,0:T(8,128)S(1)}, f32[5,8,16,1]{3,2,1,0:T(8,128)S(1)}, u32[]{:S(2)}, u32[]{:S(2)}) collective-permute-start(f32[5,8,16,1]{3,2,1,0:T(8,128)S(1)} %get-tuple-element.49), channel_id=1, source_target_pairs={{1,0},{2,1},{3,2},{5,4},{6,5},{7,6},{9,8},{10,9},{11,10},{13,12},{... | collective-permute-start | bytes 7688 | tf_op jit(solution)/shard_map/ppermute | solution.py:67

commit v10 on v6

--- a/solution.py
+++ b/solution.py
@@ -44,6 +44,50 @@
         high_pad[dim] = (span - 3, 0)
         block = inner + jnp.pad(below, low_pad) + jnp.pad(above, high_pad)
     return block
+
+
+def fold_and_widen(block, boxes, sides):
+    for axis, dim in sides:
+        count = lax.axis_size(axis)
+        forward = [(i, i + 1) for i in range(count - 1)]
+        backward = [(target, source) for source, target in forward]
+        span = block.shape[dim]
+        width = boxes.shape[dim]
+        fields = block.shape[0]
+        lanes = block.shape[-1]
+        layer = lax.index_in_dim(block, 0, dim, keepdims=True).shape
+        face = lax.index_in_dim(boxes, 0, dim, keepdims=True).shape
+        rows = 1
+        for n in layer[1:-1]:
+            rows *= n
+
+        def payload(block_layer, box_face):
+            return jnp.concatenate(
+                [block_layer.reshape(fields, -1, lanes), box_face.reshape(fields, -1, lanes)],
+                axis=1,
+            )
+
+        up = payload(
+            lax.slice_in_dim(block, span - 1, span, axis=dim),
+            lax.slice_in_dim(boxes, width - 1, width, axis=dim),
+        )
+        down = payload(lax.slice_in_dim(block, 0, 1, axis=dim), lax.slice_in_dim(boxes, 0, 1, axis=dim))
+        below = lax.ppermute(up, axis, forward)
+        above = lax.ppermute(down, axis, backward)
+        inner = lax.slice_in_dim(block, 1, span - 1, axis=dim)
+        low_pad = [(0, 0)] * block.ndim
+        high_pad = [(0, 0)] * block.ndim
+        low_pad[dim] = (0, span - 3)
+        high_pad[dim] = (span - 3, 0)
+        block = (
+            inner
+            + jnp.pad(below[:, :rows].reshape(layer), low_pad)
+            + jnp.pad(above[:, :rows].reshape(layer), high_pad)
+        )
+        boxes = jnp.concatenate(
+            [below[:, rows:].reshape(face), boxes, above[:, rows:].reshape(face)], axis=dim
+        )
+    return block, boxes
 
 
 def parcel_update(current_condition, local_air_sample):
@@ -297,12 +341,14 @@
     kept = jnp.transpose(kept_rows, (1, 0, 2))
     deposit = deposit_rows.reshape(fields, DEPTH_ROWS, PAIR_LANES)[:, :span_z, :pair_count]
     deposit = jnp.transpose(deposit.reshape(fields, span_z, span_x, span_y), (0, 2, 3, 1))
-    cell_sources = fold_ghosts(deposit, (("gx", 1), ("gy", 2), ("gz", 3)))
+    boxes = jnp.pad(outbox_rows, ((0, 0), (0, 0), (0, span_z - block_parcels)))
+    boxes = boxes.reshape((parcel_fields, 3, 3, 3, SLOTS, span_z))
+    deposit, boxes = fold_and_widen(deposit, boxes, (("gx", 1), ("gy", 2)))
+    cell_sources = fold_ghosts(deposit, (("gz", 3),))
     kappa = jnp.array(DIFFUSION, jnp.float32)[:, None, None, None]
     gas_next = gas_state + kappa * laplacian(padded) + COUPLING * cell_sources
-    outbox = outbox_rows.reshape((parcel_fields, 3, 3, 3, SLOTS, block_parcels))
-    widened = with_halo(outbox, (("gx", 1), ("gy", 2), ("gz", 3)), 1)
-    arrived_boxes = widened[:, 0::2, 0::2, 0::2]
+    widened = with_halo(boxes, (("gz", 3),), 1)
+    arrived_boxes = widened[:, 0::2, 0::2, 0::2, :, :block_parcels]
     arrived = jnp.transpose(
         arrived_boxes.reshape((parcel_fields, 27 * SLOTS, block_parcels)), (1, 0, 2)
     )

time: 125 us -> 160 us (1.28)
  the two profiles are of different devices: /device:TPU:58 before, /device:TPU:133 now
where the time goes in v10:
time: 160 us; the launch traced here: 159 us
  starting transfers between devices  56.9 us (36%)
  local copies, waits for them, and re-layouts  37.8 us (24%)
  waiting for transfers between devices  32.1 us (20%)
  Pallas kernels  20.1 us (13%)
  other arithmetic  10.3 us (6%)
  between operations  1.78 us (1%)
    ppermute x4, starting transfers between devices, with_halo(): lax.ppermute(lax.slice_in_dim(block, block.shape[dim] - width, None, axis...  21.4 us
    pallas_call x1, Pallas kernels, local(): pl.pallas_call(functools.partial(coupling_kernel, span_y=span_y, span_z=s...  20.1 us
    ppermute x2, starting transfers between devices, fold_and_widen(): above = lax.ppermute(down, axis, backward)  13.1 us
    ppermute x4, starting transfers between devices, with_halo(): lax.ppermute(lax.slice_in_dim(block, 0, width, axis=dim), axis, backward)  12.6 us
    ppermute x1, waiting for transfers between devices, fold_ghosts(): lax.ppermute(lax.slice_in_dim(block, span - 1, span, axis=dim), axis, for...  11 us
    ppermute x2, waiting for transfers between devices, fold_and_widen(): below = lax.ppermute(up, axis, forward)  8.76 us
    unnamed x48, local copies, waits for them, and re-layouts  6.78 us
    ppermute x2, waiting for transfers between devices, fold_and_widen(): above = lax.ppermute(down, axis, backward)  5.51 us
  transfers between devices with their start and end apart: 14, of which 6 were waited for; matrix products, arithmetic and copies ran while one was open for 9% of the time, Pallas kernels for 0%

profile of v10, /device:TPU:133, one launch (start us, length us, event | category | flops | bytes accessed | tf_op | source)
XLA Modules:
  0.0 159.0 jit_solution(4211745557686972394)
XLA Ops:
  1.4 3.2 %collective-permute-start.1 = (f32[5,1,16,128]{3,2,1,0:T(8,128)S(1)}, f32[5,1,16,128]{3,2,1,0:T(8,128)S(1)}, u32[]{:S(2)}, u32[]{:S(2)}) collective-permute-start(f32[5,1,16,128]{3,2,1,0:T(8,128)S(1)} %get-tuple-element.29), channel_id=1, source_target_pairs={{0,32},{32,64},{64,96},{96,128},{128,160},{160,192},{192,224},{1,3... | collective-permute-start | bytes 122888 | tf_op jit(solution)/shard_map/ppermute | solution.py:24
  4.6 8.1 %collective-permute-start = (f32[5,1,16,128]{3,2,1,0:T(8,128)S(1)}, f32[5,1,16,128]{3,2,1,0:T(8,128)S(1)}, u32[]{:S(2)}, u32[]{:S(2)}) collective-permute-start(f32[5,1,16,128]{3,2,1,0:T(8,128)S(1)} %get-tuple-element.28), channel_id=1, source_target_pairs={{32,0},{64,32},{96,64},{128,96},{160,128},{192,160},{224,192},{33,... | collective-permute-start | bytes 122888 | tf_op jit(solution)/shard_map/ppermute | solution.py:27
  13.9 4.5 %collective-permute-start.3 = (f32[5,10,1,128]{3,2,1,0:T(1,128)S(1)}, f32[5,10,1,128]{3,2,1,0:T(1,128)S(1)}, u32[]{:S(2)}, u32[]{:S(2)}) collective-permute-start(f32[5,10,1,128]{3,2,1,0:T(1,128)S(1)} %get-tuple-element.26), channel_id=1, source_target_pairs={{0,4},{4,8},{8,12},{12,16},{16,20},{20,24},{24,28},{1,5},{5,9},{9,... | collective-permute-start | bytes 76808 | tf_op jit(solution)/shard_map/ppermute | solution.py:24
  18.4 1.9 %collective-permute-start.2 = (f32[5,10,1,128]{3,2,1,0:T(1,128)S(1)}, f32[5,10,1,128]{3,2,1,0:T(1,128)S(1)}, u32[]{:S(2)}, u32[]{:S(2)}) collective-permute-start(f32[5,10,1,128]{3,2,1,0:T(1,128)S(1)} %get-tuple-element.27), channel_id=1, source_target_pairs={{4,0},{8,4},{12,8},{16,12},{20,16},{24,20},{28,24},{5,1},{9,5},{13... | collective-permute-start | bytes 76808 | tf_op jit(solution)/shard_map/ppermute | solution.py:27
  21.2 2.4 %collective-permute-done.2 = f32[5,10,1,128]{3,2,1,0:T(1,128)S(1)} collective-permute-done((f32[5,10,1,128]{3,2,1,0:T(1,128)S(1)}, f32[5,10,1,128]{3,2,1,0:T(1,128)S(1)}, u32[]{:S(2)}, u32[]{:S(2)}) %collective-permute-start.2) | collective-permute-done | bytes 25632 | tf_op jit(solution)/shard_map/ppermute | solution.py:27
  26.0 4.0 %collective-permute-start.5 = (f32[5,10,18,1]{2,3,1,0:T(1,128)S(1)}, f32[5,10,18,1]{2,3,1,0:T(1,128)S(1)}, u32[]{:S(2)}, u32[]{:S(2)}) collective-permute-start(f32[5,10,18,1]{2,3,1,0:T(1,128)S(1)} %copy.42), channel_id=1, source_target_pairs={{0,1},{1,2},{2,3},{4,5},{5,6},{6,7},{8,9},{9,10},{10,11},{12,13},{... | collective-permute-start | bytes 10808 | tf_op jit(solution)/shard_map/ppermute | solution.py:24
  33.9 1.6 copy.55
  36.4 20.1 %shard_map.94 = (f32[5,32,128]{2,1,0:T(8,128)}, f32[5,108,128]{2,1,0:T(8,128)}, f32[680,256]{1,0:T(8,128)}) custom-call(s32[1]{0:T(128)S(6)} %copy.62.live_ref, s32[32]{0:T(128)} %dest_ref.1, f32[680,256]{1,0:T(8,128)} %bitcast.40, f32[5,32,128]{2,1,0:T(8,128)} %bitcast.46, s32[32,128]{1,0:T(8,128)} %cell_ref.1, f32[3,32,128]{2,1,0:T(8,128)} %bitcast.47, ...), custom_call_target="tpu_custom_call" | custom-call | tf_op jit(solution)/shard_map/pallas_call | solution.py:322
  56.5 2.5 %copy.54 = f32[5,130,180]{1,2,0:T(8,128)} copy(f32[5,130,180]{2,1,0:T(8,128)} %bitcast.41) | data formatting | bytes 936000
  63.8 1.7 %reshape.79 = f32[5,36,130]{2,1,0:T(8,128)} reshape(f32[5,1,3,3,4,130]{5,4,3,2,1,0:T(4,128)} %get-tuple-element.24) | data formatting | bytes 187200 | tf_op jit(solution)/shard_map/reshape | solution.py:66
  65.4 1.7 %reshape.82 = f32[5,36,130]{2,1,0:T(8,128)} reshape(f32[5,1,3,3,4,130]{5,4,3,2,1,0:T(4,128)} %get-tuple-element.25) | data formatting | bytes 187200 | tf_op jit(solution)/shard_map/reshape | solution.py:66
  68.1 10.0 %collective-permute-start.7 = (f32[5,54,130]{2,1,0:T(8,128)S(1)}, f32[5,54,130]{2,1,0:T(8,128)S(1)}, u32[]{:S(2)}, u32[]{:S(2)}) collective-permute-start(f32[5,54,130]{2,1,0:T(8,128)S(1)} %pad_maximum_fusion.23), channel_id=1, source_target_pairs={{32,0},{64,32},{96,64},{128,96},{160,128},{192,160},{224,192},{33,... | collective-permute-start | bytes 421208 | tf_op jit(solution)/shard_map/ppermute | solution.py:76
  78.1 1.7 %pad_maximum_fusion.22 = f32[5,54,130]{2,1,0:T(8,128)} fusion(f32[5,36,130]{2,1,0:T(8,128)} %reshape.79, f32[5,18,130]{2,1,0:T(8,128)S(1)} %get-tuple-element.14), kind=kLoop, calls=%fused_computation.39 | loop fusion | flops 35100 | bytes 280800 | tf_op jit(solution)/shard_map/concatenate | solution.py:65
  79.8 1.9 %collective-permute-start.6 = (f32[5,54,130]{2,1,0:T(8,128)}, f32[5,54,130]{2,1,0:T(8,128)}, u32[]{:S(2)}, u32[]{:S(2)}) collective-permute-start(f32[5,54,130]{2,1,0:T(8,128)} %pad_maximum_fusion.22), channel_id=1, source_target_pairs={{0,32},{32,64},{64,96},{96,128},{128,160},{160,192},{192,224},{1,3... | collective-permute-start | bytes 421208 | tf_op jit(solution)/shard_map/ppermute | solution.py:75
  81.7 2.5 %collective-permute-done.7 = f32[5,54,130]{2,1,0:T(8,128)S(1)} collective-permute-done((f32[5,54,130]{2,1,0:T(8,128)S(1)}, f32[5,54,130]{2,1,0:T(8,128)S(1)}, u32[]{:S(2)}, u32[]{:S(2)}) %collective-permute-start.7) | collective-permute-done | bytes 140432 | tf_op jit(solution)/shard_map/ppermute | solution.py:76
  85.7 1.7 %reshape.86 = f32[5,1,3,3,4,130]{5,4,3,2,1,0:T(4,128)} reshape(f32[5,36,130]{2,1,0:T(8,128)} %slice.179) | data formatting | bytes 187200 | tf_op jit(solution)/shard_map/reshape | solution.py:88
  87.3 8.8 %collective-permute-done.6 = f32[5,54,130]{2,1,0:T(8,128)} collective-permute-done((f32[5,54,130]{2,1,0:T(8,128)}, f32[5,54,130]{2,1,0:T(8,128)}, u32[]{:S(2)}, u32[]{:S(2)}) %collective-permute-start.6) | collective-permute-done | bytes 140432 | tf_op jit(solution)/shard_map/ppermute | solution.py:75
  96.1 1.6 %slice.178 = f32[5,36,130]{2,1,0:T(8,128)} slice(f32[5,54,130]{2,1,0:T(8,128)} %collective-permute-done.6), slice={[0:5], [18:54], [0:130]} | slice | bytes 187200 | tf_op jit(solution)/shard_map/slice | solution.py:88
  97.7 1.7 %reshape.85 = f32[5,1,3,3,4,130]{5,4,3,2,0,1:T(4,128)} reshape(f32[5,36,130]{2,1,0:T(8,128)} %slice.178) | data formatting | bytes 187200 | tf_op jit(solution)/shard_map/reshape | solution.py:88
  103.5 3.2 %collective-permute-start.9 = (f32[5,68,130]{2,1,0:T(8,128)}, f32[5,68,130]{2,1,0:T(8,128)}, u32[]{:S(2)}, u32[]{:S(2)}) collective-permute-start(f32[5,68,130]{2,1,0:T(8,128)} %pad_maximum_fusion.8), channel_id=1, source_target_pairs={{4,0},{8,4},{12,8},{16,12},{20,16},{24,20},{28,24},{5,1},{9,5},{13... | collective-permute-start | bytes 530408 | tf_op jit(solution)/shard_map/ppermute | solution.py:76
  107.6 2.4 %collective-permute-start.8 = (f32[5,68,130]{2,1,0:T(8,128)}, f32[5,68,130]{2,1,0:T(8,128)}, u32[]{:S(2)}, u32[]{:S(2)}) collective-permute-start(f32[5,68,130]{2,1,0:T(8,128)} %pad_maximum_fusion.7), channel_id=1, source_target_pairs={{0,4},{4,8},{8,12},{12,16},{16,20},{20,24},{24,28},{1,5},{5,9},{9,... | collective-permute-start | bytes 530408 | tf_op jit(solution)/shard_map/ppermute | solution.py:75
  110.0 3.0 %collective-permute-done.9 = f32[5,68,130]{2,1,0:T(8,128)} collective-permute-done((f32[5,68,130]{2,1,0:T(8,128)}, f32[5,68,130]{2,1,0:T(8,128)}, u32[]{:S(2)}, u32[]{:S(2)}) %collective-permute-start.9) | collective-permute-done | bytes 176832 | tf_op jit(solution)/shard_map/ppermute | solution.py:76
  112.9 1.7 %slice.187 = f32[5,60,130]{2,1,0:T(8,128)} slice(f32[5,68,130]{2,1,0:T(8,128)} %collective-permute-done.9), slice={[0:5], [8:68], [0:130]} | slice | bytes 312000 | tf_op jit(solution)/shard_map/slice | solution.py:88
  114.7 1.9 %reshape.93 = f32[5,5,1,3,4,130]{5,4,3,2,1,0:T(4,128)} reshape(f32[5,60,130]{2,1,0:T(8,128)} %slice.187) | data formatting | bytes 312000 | tf_op jit(solution)/shard_map/reshape | solution.py:88
  118.0 1.7 %slice.186 = f32[5,60,130]{2,1,0:T(8,128)} slice(f32[5,68,130]{2,1,0:T(8,128)} %collective-permute-done.8), slice={[0:5], [8:68], [0:130]} | slice | bytes 312000 | tf_op jit(solution)/shard_map/slice | solution.py:88
  119.7 1.8 %reshape.92 = f32[5,5,1,3,4,130]{5,4,3,2,1,0:T(4,128)} reshape(f32[5,60,130]{2,1,0:T(8,128)} %slice.186) | data formatting | bytes 312000 | tf_op jit(solution)/shard_map/reshape | solution.py:88
  122.5 1.3 pad_maximum_fusion.6
  123.8 9.7 %collective-permute-start.12 = (f32[5,5,5,1,4,130]{5,4,3,2,1,0:T(4,128)S(1)}, f32[5,5,5,1,4,130]{5,4,3,2,1,0:T(4,128)S(1)}, u32[]{:S(2)}, u32[]{:S(2)}) collective-permute-start(f32[5,5,5,1,4,130]{5,4,3,2,1,0:T(4,128)S(1)} %get-tuple-element.12), channel_id=1, source_target_pairs={{0,1},{1,2},{2,3},{4,5},{5,6},{6,7},{8,9},{9,10},{10,11},{12,13},{... | collective-permute-start | bytes 780008 | tf_op jit(solution)/shard_map/ppermute | solution.py:24
  135.2 4.1 %collective-permute-start.10 = (f32[5,8,16,1]{3,2,1,0:T(8,128)S(1)}, f32[5,8,16,1]{3,2,1,0:T(8,128)S(1)}, u32[]{:S(2)}, u32[]{:S(2)}) collective-permute-start(f32[5,8,16,1]{3,2,1,0:T(8,128)S(1)} %get-tuple-element.20), channel_id=1, source_target_pairs={{0,1},{1,2},{2,3},{4,5},{5,6},{6,7},{8,9},{9,10},{10,11},{12,13},{... | collective-permute-start | bytes 7688 | tf_op jit(solution)/shard_map/ppermute | solution.py:38
  140.6 11.0 %collective-permute-done.10 = f32[5,8,16,1]{3,2,1,0:T(8,128)S(1)} collective-permute-done((f32[5,8,16,1]{3,2,1,0:T(8,128)S(1)}, f32[5,8,16,1]{3,2,1,0:T(8,128)S(1)}, u32[]{:S(2)}, u32[]{:S(2)}) %collective-permute-start.10) | collective-permute-done | bytes 2592 | tf_op jit(solution)/shard_map/ppermute | solution.py:38
  151.6 4.4 %collective-permute-done.11 = f32[5,8,16,1]{3,2,1,0:T(8,128)S(1)} collective-permute-done((f32[5,8,16,1]{3,2,1,0:T(8,128)S(1)}, f32[5,8,16,1]{3,2,1,0:T(8,128)S(1)}, u32[]{:S(2)}, u32[]{:S(2)}) %collective-permute-start.11) | collective-permute-done | bytes 2592 | tf_op jit(solution)/shard_map/ppermute | solution.py:39
  156.0 1.4 fusion.4
  (96 shorter events, 28.3 us)
Async XLA Ops:
  1.4 11.3 %collective-permute-start.1 = (f32[5,1,16,128]{3,2,1,0:T(8,128)S(1)}, f32[5,1,16,128]{3,2,1,0:T(8,128)S(1)}, u32[]{:S(2)}, u32[]{:S(2)}) collective-permute-start(f32[5,1,16,128]{3,2,1,0:T(8,128)S(1)} %get-tuple-element.29), channel_id=1, source_target_pairs={{0,32},{32,64},{64,96},{96,128},{128,160},{160,192},{192,224},{1,3... | collective-permute-start | bytes 122888 | tf_op jit(solution)/shard_map/ppermute | solution.py:24
  4.6 9.2 %collective-permute-start = (f32[5,1,16,128]{3,2,1,0:T(8,128)S(1)}, f32[5,1,16,128]{3,2,1,0:T(8,128)S(1)}, u32[]{:S(2)}, u32[]{:S(2)}) collective-permute-start(f32[5,1,16,128]{3,2,1,0:T(8,128)S(1)} %get-tuple-element.28), channel_id=1, source_target_pairs={{32,0},{64,32},{96,64},{128,96},{160,128},{192,160},{224,192},{33,... | collective-permute-start | bytes 122888 | tf_op jit(solution)/shard_map/ppermute | solution.py:27
  12.8 8.4 %copy-start.16 = (f32[5,1,16,128]{3,2,1,0:T(8,128)}, f32[5,1,16,128]{3,2,1,0:T(8,128)S(1)}, u32[]{:S(2)}) copy-start(f32[5,1,16,128]{3,2,1,0:T(8,128)S(1)} %collective-permute-done.1) | copy-start | bytes 122884
  13.8 7.3 %copy-start.18 = (f32[5,1,16,128]{3,2,1,0:T(8,128)}, f32[5,1,16,128]{3,2,1,0:T(8,128)S(1)}, u32[]{:S(2)}) copy-start(f32[5,1,16,128]{3,2,1,0:T(8,128)S(1)} %collective-permute-done) | copy-start | bytes 122884
  13.9 7.2 %collective-permute-start.3 = (f32[5,10,1,128]{3,2,1,0:T(1,128)S(1)}, f32[5,10,1,128]{3,2,1,0:T(1,128)S(1)}, u32[]{:S(2)}, u32[]{:S(2)}) collective-permute-start(f32[5,10,1,128]{3,2,1,0:T(1,128)S(1)} %get-tuple-element.26), channel_id=1, source_target_pairs={{0,4},{4,8},{8,12},{12,16},{16,20},{20,24},{24,28},{1,5},{5,9},{9,... | collective-permute-start | bytes 76808 | tf_op jit(solution)/shard_map/ppermute | solution.py:24
  18.4 5.2 %collective-permute-start.2 = (f32[5,10,1,128]{3,2,1,0:T(1,128)S(1)}, f32[5,10,1,128]{3,2,1,0:T(1,128)S(1)}, u32[]{:S(2)}, u32[]{:S(2)}) collective-permute-start(f32[5,10,1,128]{3,2,1,0:T(1,128)S(1)} %get-tuple-element.27), channel_id=1, source_target_pairs={{4,0},{8,4},{12,8},{16,12},{20,16},{24,20},{28,24},{5,1},{9,5},{13... | collective-permute-start | bytes 76808 | tf_op jit(solution)/shard_map/ppermute | solution.py:27
  21.1 11.0 %copy-start.11 = (f32[5,10,1,128]{3,2,1,0:T(1,128)}, f32[5,10,1,128]{3,2,1,0:T(1,128)S(1)}, u32[]{:S(2)}) copy-start(f32[5,10,1,128]{3,2,1,0:T(1,128)S(1)} %collective-permute-done.3) | copy-start | bytes 76804
  23.6 8.6 %copy-start.13 = (f32[5,10,1,128]{3,2,1,0:T(1,128)}, f32[5,10,1,128]{3,2,1,0:T(1,128)S(1)}, u32[]{:S(2)}) copy-start(f32[5,10,1,128]{3,2,1,0:T(1,128)S(1)} %collective-permute-done.2) | copy-start | bytes 76804
  24.7 7.0 %collective-permute-start.4 = (f32[5,10,18,1]{2,3,1,0:T(1,128)S(1)}, f32[5,10,18,1]{2,3,1,0:T(1,128)S(1)}, u32[]{:S(2)}, u32[]{:S(2)}) collective-permute-start(f32[5,10,18,1]{2,3,1,0:T(1,128)S(1)} %copy.40), channel_id=1, source_target_pairs={{1,0},{2,1},{3,2},{5,4},{6,5},{7,6},{9,8},{10,9},{11,10},{13,12},{... | collective-permute-start | bytes 10808 | tf_op jit(solution)/shard_map/ppermute | solution.py:27
  26.0 5.3 %collective-permute-start.5 = (f32[5,10,18,1]{2,3,1,0:T(1,128)S(1)}, f32[5,10,18,1]{2,3,1,0:T(1,128)S(1)}, u32[]{:S(2)}, u32[]{:S(2)}) collective-permute-start(f32[5,10,18,1]{2,3,1,0:T(1,128)S(1)} %copy.42), channel_id=1, source_target_pairs={{0,1},{1,2},{2,3},{4,5},{5,6},{6,7},{8,9},{9,10},{10,11},{12,13},{... | collective-permute-start | bytes 10808 | tf_op jit(solution)/shard_map/ppermute | solution.py:24
  56.5 4.4 %copy-start.10 = (f32[5,108,128]{2,1,0:T(8,128)S(1)}, f32[5,108,128]{2,1,0:T(8,128)}, u32[]{:S(2)}) copy-start(f32[5,108,128]{2,1,0:T(8,128)} %get-tuple-element.7) | copy-start | bytes 829444
  68.1 16.1 %collective-permute-start.7 = (f32[5,54,130]{2,1,0:T(8,128)S(1)}, f32[5,54,130]{2,1,0:T(8,128)S(1)}, u32[]{:S(2)}, u32[]{:S(2)}) collective-permute-start(f32[5,54,130]{2,1,0:T(8,128)S(1)} %pad_maximum_fusion.23), channel_id=1, source_target_pairs={{32,0},{64,32},{96,64},{128,96},{160,128},{192,160},{224,192},{33,... | collective-permute-start | bytes 421208 | tf_op jit(solution)/shard_map/ppermute | solution.py:76
  79.8 16.3 %collective-permute-start.6 = (f32[5,54,130]{2,1,0:T(8,128)}, f32[5,54,130]{2,1,0:T(8,128)}, u32[]{:S(2)}, u32[]{:S(2)}) collective-permute-start(f32[5,54,130]{2,1,0:T(8,128)} %pad_maximum_fusion.22), channel_id=1, source_target_pairs={{0,32},{32,64},{64,96},{96,128},{128,160},{160,192},{192,224},{1,3... | collective-permute-start | bytes 421208 | tf_op jit(solution)/shard_map/ppermute | solution.py:75
  99.4 3.0 %copy-start.4 = (f32[5,1,3,3,4,130]{5,4,3,2,0,1:T(4,128)S(1)}, f32[5,1,3,3,4,130]{5,4,3,2,0,1:T(4,128)}, u32[]{:S(2)}) copy-start(f32[5,1,3,3,4,130]{5,4,3,2,0,1:T(4,128)} %reshape.85) | copy-start | bytes 280804
  102.7 19.7 %copy-start.3 = (f32[5,1,3,3,4,130]{5,4,3,2,1,0:T(4,128)S(1)}, f32[5,1,3,3,4,130]{5,4,3,2,1,0:T(4,128)}, u32[]{:S(2)}) copy-start(f32[5,1,3,3,4,130]{5,4,3,2,1,0:T(4,128)} %reshape.86) | copy-start | bytes 280804
  102.7 19.7 %copy-start.5 = (f32[5,1,3,3,4,130]{5,4,3,2,0,1:T(4,128)S(1)}, f32[5,1,3,3,4,130]{5,4,3,2,0,1:T(4,128)}, u32[]{:S(2)}) copy-start(f32[5,1,3,3,4,130]{5,4,3,2,0,1:T(4,128)} %reshape.85) | copy-start | bytes 280804
  103.5 9.4 %collective-permute-start.9 = (f32[5,68,130]{2,1,0:T(8,128)}, f32[5,68,130]{2,1,0:T(8,128)}, u32[]{:S(2)}, u32[]{:S(2)}) collective-permute-start(f32[5,68,130]{2,1,0:T(8,128)} %pad_maximum_fusion.8), channel_id=1, source_target_pairs={{4,0},{8,4},{12,8},{16,12},{20,16},{24,20},{28,24},{5,1},{9,5},{13... | collective-permute-start | bytes 530408 | tf_op jit(solution)/shard_map/ppermute | solution.py:76
  107.6 10.4 %collective-permute-start.8 = (f32[5,68,130]{2,1,0:T(8,128)}, f32[5,68,130]{2,1,0:T(8,128)}, u32[]{:S(2)}, u32[]{:S(2)}) collective-permute-start(f32[5,68,130]{2,1,0:T(8,128)} %pad_maximum_fusion.7), channel_id=1, source_target_pairs={{0,4},{4,8},{8,12},{12,16},{16,20},{20,24},{24,28},{1,5},{5,9},{9,... | collective-permute-start | bytes 530408 | tf_op jit(solution)/shard_map/ppermute | solution.py:75
  114.7 20.2 %copy-start.1 = (f32[5,8,18,130]{3,2,1,0:T(8,128)S(1)}, f32[5,8,18,130]{3,2,1,0:T(8,128)}, u32[]{:S(2)}) copy-start(f32[5,8,18,130]{3,2,1,0:T(8,128)} %copy-done) | copy-start | bytes 1123204
  121.5 13.3 %copy-start.15 = (f32[5,8,1,130]{3,2,1,0:T(1,128)S(1)}, f32[5,8,1,130]{3,2,1,0:T(1,128)}, u32[]{:S(2)}) copy-start(f32[5,8,1,130]{3,2,1,0:T(1,128)} %copy.51) | copy-start | bytes 62404
  122.4 33.6 %copy-start.8 = (f32[5,8,16,128]{3,2,1,0:T(8,128)S(1)}, f32[5,8,16,128]{3,2,1,0:T(8,128)}, u32[]{:S(2)}) copy-start(f32[5,8,16,128]{3,2,1,0:T(8,128)} %param.7) | copy-start | bytes 983044
  122.4 33.6 %copy-start.12 = (f32[5,10,1,128]{3,2,1,0:T(1,128)S(1)}, f32[5,10,1,128]{3,2,1,0:T(1,128)}, u32[]{:S(2)}) copy-start(f32[5,10,1,128]{3,2,1,0:T(1,128)} %copy-done.11) | copy-start | bytes 76804
  122.4 33.6 %copy-start.14 = (f32[5,10,1,128]{3,2,1,0:T(1,128)S(1)}, f32[5,10,1,128]{3,2,1,0:T(1,128)}, u32[]{:S(2)}) copy-start(f32[5,10,1,128]{3,2,1,0:T(1,128)} %copy-done.13) | copy-start | bytes 76804
  122.4 33.6 %copy-start.17 = (f32[5,1,16,128]{3,2,1,0:T(8,128)S(1)}, f32[5,1,16,128]{3,2,1,0:T(8,128)}, u32[]{:S(2)}) copy-start(f32[5,1,16,128]{3,2,1,0:T(8,128)} %copy-done.16) | copy-start | bytes 122884
  122.4 33.6 %copy-start.19 = (f32[5,1,16,128]{3,2,1,0:T(8,128)S(1)}, f32[5,1,16,128]{3,2,1,0:T(8,128)}, u32[]{:S(2)}) copy-start(f32[5,1,16,128]{3,2,1,0:T(8,128)} %copy-done.18) | copy-start | bytes 122884
  122.5 33.6 %copy-start.20 = (f32[5]{0:T(128)S(1)}, f32[5]{0:T(128)}, u32[]{:S(2)}) copy-start(f32[5]{0:T(128)} %constant.23.clone) | copy-start | bytes 64
  123.8 33.6 %collective-permute-start.12 = (f32[5,5,5,1,4,130]{5,4,3,2,1,0:T(4,128)S(1)}, f32[5,5,5,1,4,130]{5,4,3,2,1,0:T(4,128)S(1)}, u32[]{:S(2)}, u32[]{:S(2)}) collective-permute-start(f32[5,5,5,1,4,130]{5,4,3,2,1,0:T(4,128)S(1)} %get-tuple-element.12), channel_id=1, source_target_pairs={{0,1},{1,2},{2,3},{4,5},{5,6},{6,7},{8,9},{9,10},{10,11},{12,13},{... | collective-permute-start | bytes 780008 | tf_op jit(solution)/shard_map/ppermute | solution.py:24
  133.5 23.9 %collective-permute-start.13 = (f32[5,5,5,1,4,130]{5,4,3,2,1,0:T(4,128)S(1)}, f32[5,5,5,1,4,130]{5,4,3,2,1,0:T(4,128)S(1)}, u32[]{:S(2)}, u32[]{:S(2)}) collective-permute-start(f32[5,5,5,1,4,130]{5,4,3,2,1,0:T(4,128)S(1)} %get-tuple-element.13), channel_id=1, source_target_pairs={{1,0},{2,1},{3,2},{5,4},{6,5},{7,6},{9,8},{10,9},{11,10},{13,12},{... | collective-permute-start | bytes 780008 | tf_op jit(solution)/shard_map/ppermute | solution.py:27
  135.0 22.4 %copy-start.6 = (f32[5,5,1,3,4,130]{5,4,3,2,1,0:T(4,128)S(1)}, f32[5,5,1,3,4,130]{5,4,3,2,1,0:T(4,128)}, u32[]{:S(2)}) copy-start(f32[5,5,1,3,4,130]{5,4,3,2,1,0:T(4,128)} %reshape.93) | copy-start | bytes 468004
  135.0 22.4 %copy-start.7 = (f32[5,5,1,3,4,130]{5,4,3,2,1,0:T(4,128)S(1)}, f32[5,5,1,3,4,130]{5,4,3,2,1,0:T(4,128)}, u32[]{:S(2)}) copy-start(f32[5,5,1,3,4,130]{5,4,3,2,1,0:T(4,128)} %reshape.92) | copy-start | bytes 468004
  135.2 16.5 %collective-permute-start.10 = (f32[5,8,16,1]{3,2,1,0:T(8,128)S(1)}, f32[5,8,16,1]{3,2,1,0:T(8,128)S(1)}, u32[]{:S(2)}, u32[]{:S(2)}) collective-permute-start(f32[5,8,16,1]{3,2,1,0:T(8,128)S(1)} %get-tuple-element.20), channel_id=1, source_target_pairs={{0,1},{1,2},{2,3},{4,5},{5,6},{6,7},{8,9},{9,10},{10,11},{12,13},{... | collective-permute-start | bytes 7688 | tf_op jit(solution)/shard_map/ppermute | solution.py:38
  139.3 16.7 %collective-permute-start.11 = (f32[5,8,16,1]{3,2,1,0:T(8,128)S(1)}, f32[5,8,16,1]{3,2,1,0:T(8,128)S(1)}, u32[]{:S(2)}, u32[]{:S(2)}) collective-permute-start(f32[5,8,16,1]{3,2,1,0:T(8,128)S(1)} %get-tuple-element.21), channel_id=1, source_target_pairs={{1,0},{2,1},{3,2},{5,4},{6,5},{7,6},{9,8},{10,9},{11,10},{13,12},{... | collective-permute-start | bytes 7688 | tf_op jit(solution)/shard_map/ppermute | solution.py:39
  (3 other events, 4.7 us)

commit v11 on v6

--- a/solution.py
+++ b/solution.py
@@ -119,13 +119,13 @@
     live_ref, dest_ref, table_ref, parcel_ref, cell_ref, offset_ref, factor_ref,
     kept_ref, outbox_ref, deposit_ref,
     weight_scr, depth_scr, spread_scr, updated_scr, count_scr, table_high_ref, table_low_ref,
-    *, span_y, span_z,
+    total_scr, *, span_y, span_z,
 ):
     fields = parcel_ref.shape[0]
     blocks = parcel_ref.shape[1]
     lanes = parcel_ref.shape[2]
     plane_size = span_y * span_z
-    deposit_ref[...] = jnp.zeros(deposit_ref.shape, jnp.float32)
+    total_scr[...] = jnp.zeros(total_scr.shape, jnp.float32)
     table_high, table_low = split_bf16(table_ref[...])
     table_high_ref[...] = table_high
     table_low_ref[...] = table_low
@@ -215,14 +215,15 @@
             )
         spread_high, spread_low = split_bf16(spread_scr[...])
         dims = (((1,), (1,)), ((), ()))
-        deposit_ref[...] += (
-            lax.dot_general(spread_high, weight_high, dims, preferred_element_type=jnp.float32)
-            + lax.dot_general(spread_high, weight_low, dims, preferred_element_type=jnp.float32)
-            + lax.dot_general(spread_low, weight_high, dims, preferred_element_type=jnp.float32)
+        total_scr[...] += (
+            lax.dot_general(weight_high, spread_high, dims, preferred_element_type=jnp.float32)
+            + lax.dot_general(weight_low, spread_high, dims, preferred_element_type=jnp.float32)
+            + lax.dot_general(weight_high, spread_low, dims, preferred_element_type=jnp.float32)
         )
         return carry
 
     lax.fori_loop(0, blocks // GROUP, group, 0)
+    deposit_ref[...] = total_scr[...].T
 
     kept_ref[...] = jnp.zeros(kept_ref.shape, jnp.float32)
     outbox_ref[...] = jnp.zeros(outbox_ref.shape, jnp.float32)
@@ -292,6 +293,7 @@
             pltpu.SMEM((32,), jnp.int32),
             pltpu.VMEM(table.shape, jnp.bfloat16),
             pltpu.VMEM(table.shape, jnp.bfloat16),
+            pltpu.VMEM((PAIR_LANES, fields * DEPTH_ROWS), jnp.float32),
         ],
     )(live_blocks, destination, table, parcel_rows, parcel_cells, offset_rows, factors)
     kept = jnp.transpose(kept_rows, (1, 0, 2))

time: 125 us -> 123 us (0.984)
  Pallas kernels: 20 us -> 17.5 us
    pallas_call x1, Pallas kernels: 20 us -> 17.5 us  [local(): pl.pallas_call(functools.partial(coupling_kernel, span_y=span_y, span_z=s...]
where the time goes in v11:
time: 123 us; the launch traced here: 120 us
  starting transfers between devices  57.9 us (47%)
  waiting for transfers between devices  25.1 us (20%)
  Pallas kernels  17.5 us (14%)
  local copies, waits for them, and re-layouts  13.1 us (11%)
  other arithmetic  5.21 us (4%)
  between operations  1.66 us (1%)
    ppermute x6, starting transfers between devices, with_halo(): lax.ppermute(lax.slice_in_dim(block, block.shape[dim] - width, None, axis...  21.4 us
    pallas_call x1, Pallas kernels, local(): pl.pallas_call(functools.partial(coupling_kernel, span_y=span_y, span_z=s...  17.5 us
    ppermute x3, starting transfers between devices, fold_ghosts(): lax.ppermute(lax.slice_in_dim(block, span - 1, span, axis=dim), axis, for...  16.3 us
    ppermute x6, starting transfers between devices, with_halo(): lax.ppermute(lax.slice_in_dim(block, 0, width, axis=dim), axis, backward)  14.5 us
    ppermute x6, waiting for transfers between devices, with_halo(): lax.ppermute(lax.slice_in_dim(block, 0, width, axis=dim), axis, backward)  11.8 us
    ppermute x6, waiting for transfers between devices, with_halo(): lax.ppermute(lax.slice_in_dim(block, block.shape[dim] - width, None, axis...  6.85 us
    ppermute x3, starting transfers between devices, fold_ghosts(): lax.ppermute(lax.slice_in_dim(block, 0, 1, axis=dim), axis, backward)  5.76 us
    unnamed x16, local copies, waits for them, and re-layouts  5.08 us
  transfers between devices with their start and end apart: 18, of which 9 were waited for; matrix products, arithmetic and copies ran while one was open for 5% of the time, Pallas kernels for 0%

profile of v11, /device:TPU:58, one launch (start us, length us, event | category | flops | bytes accessed | tf_op | source)
XLA Modules:
  0.0 120.5 jit_solution(976946453128240524)
XLA Ops:
  1.4 7.8 %collective-permute-start.1 = (f32[5,1,16,128]{3,2,1,0:T(8,128)S(1)}, f32[5,1,16,128]{3,2,1,0:T(8,128)S(1)}, u32[]{:S(2)}, u32[]{:S(2)}) collective-permute-start(f32[5,1,16,128]{3,2,1,0:T(8,128)S(1)} %get-tuple-element.24), channel_id=1, source_target_pairs={{0,32},{32,64},{64,96},{96,128},{128,160},{160,192},{192,224},{1,3... | collective-permute-start | bytes 122888 | tf_op jit(solution)/shard_map/ppermute | solution.py:24
  9.3 1.9 %collective-permute-start = (f32[5,1,16,128]{3,2,1,0:T(8,128)S(1)}, f32[5,1,16,128]{3,2,1,0:T(8,128)S(1)}, u32[]{:S(2)}, u32[]{:S(2)}) collective-permute-start(f32[5,1,16,128]{3,2,1,0:T(8,128)S(1)} %get-tuple-element.23), channel_id=1, source_target_pairs={{32,0},{64,32},{96,64},{128,96},{160,128},{192,160},{224,192},{33,... | collective-permute-start | bytes 122888 | tf_op jit(solution)/shard_map/ppermute | solution.py:27
  12.2 9.0 %collective-permute-done = f32[5,1,16,128]{3,2,1,0:T(8,128)S(1)} collective-permute-done((f32[5,1,16,128]{3,2,1,0:T(8,128)S(1)}, f32[5,1,16,128]{3,2,1,0:T(8,128)S(1)}, u32[]{:S(2)}, u32[]{:S(2)}) %collective-permute-start) | collective-permute-done | bytes 40992 | tf_op jit(solution)/shard_map/ppermute | solution.py:27
  21.3 1.9 %collective-permute-start.2 = (f32[5,10,1,128]{3,2,1,0:T(1,128)S(1)}, f32[5,10,1,128]{3,2,1,0:T(1,128)S(1)}, u32[]{:S(2)}, u32[]{:S(2)}) collective-permute-start(f32[5,10,1,128]{3,2,1,0:T(1,128)S(1)} %get-tuple-element.22), channel_id=1, source_target_pairs={{4,0},{8,4},{12,8},{16,12},{20,16},{24,20},{28,24},{5,1},{9,5},{13... | collective-permute-start | bytes 76808 | tf_op jit(solution)/shard_map/ppermute | solution.py:27
  23.2 2.4 %collective-permute-start.3 = (f32[5,10,1,128]{3,2,1,0:T(1,128)S(1)}, f32[5,10,1,128]{3,2,1,0:T(1,128)S(1)}, u32[]{:S(2)}, u32[]{:S(2)}) collective-permute-start(f32[5,10,1,128]{3,2,1,0:T(1,128)S(1)} %get-tuple-element.21), channel_id=1, source_target_pairs={{0,4},{4,8},{8,12},{12,16},{16,20},{20,24},{24,28},{1,5},{5,9},{9,... | collective-permute-start | bytes 76808 | tf_op jit(solution)/shard_map/ppermute | solution.py:24
  26.4 1.9 %collective-permute-done.3 = f32[5,10,1,128]{3,2,1,0:T(1,128)S(1)} collective-permute-done((f32[5,10,1,128]{3,2,1,0:T(1,128)S(1)}, f32[5,10,1,128]{3,2,1,0:T(1,128)S(1)}, u32[]{:S(2)}, u32[]{:S(2)}) %collective-permute-start.3) | collective-permute-done | bytes 25632 | tf_op jit(solution)/shard_map/ppermute | solution.py:24
  29.1 2.9 %collective-permute-start.4 = (f32[5,10,18,1]{2,3,1,0:T(1,128)S(1)}, f32[5,10,18,1]{2,3,1,0:T(1,128)S(1)}, u32[]{:S(2)}, u32[]{:S(2)}) collective-permute-start(f32[5,10,18,1]{2,3,1,0:T(1,128)S(1)} %copy.14), channel_id=1, source_target_pairs={{1,0},{2,1},{3,2},{5,4},{6,5},{7,6},{9,8},{10,9},{11,10},{13,12},{... | collective-permute-start | bytes 10808 | tf_op jit(solution)/shard_map/ppermute | solution.py:27
  32.4 2.9 %collective-permute-start.5 = (f32[5,10,18,1]{2,3,1,0:T(1,128)S(1)}, f32[5,10,18,1]{2,3,1,0:T(1,128)S(1)}, u32[]{:S(2)}, u32[]{:S(2)}) collective-permute-start(f32[5,10,18,1]{2,3,1,0:T(1,128)S(1)} %copy.16), channel_id=1, source_target_pairs={{0,1},{1,2},{2,3},{4,5},{5,6},{6,7},{8,9},{9,10},{10,11},{12,13},{... | collective-permute-start | bytes 10808 | tf_op jit(solution)/shard_map/ppermute | solution.py:24
  37.0 1.1 collective-permute-done.5
  39.3 1.1 reshape.25
  40.4 1.6 %copy.23 = f32[5,130,180]{2,1,0:T(8,128)S(1)} copy(f32[5,130,180]{1,2,0:T(8,128)} %reshape.25) | data formatting | bytes 936000
  42.8 17.5 %shard_map.94 = (f32[5,32,128]{2,1,0:T(8,128)}, f32[5,108,128]{2,1,0:T(8,128)}, f32[680,256]{1,0:T(8,128)}) custom-call(s32[1]{0:T(128)S(6)} %copy.28.live_ref, s32[32]{0:T(128)} %dest_ref.1, f32[680,256]{1,0:T(8,128)} %bitcast.16, f32[5,32,128]{2,1,0:T(8,128)} %bitcast.20, s32[32,128]{1,0:T(8,128)} %cell_ref.1, f32[3,32,128]{2,1,0:T(8,128)} %bitcast.21, ...), custom_call_target="tpu_custom_call" | custom-call | tf_op jit(solution)/shard_map/pallas_call | solution.py:279
  60.3 2.4 %copy.22 = f32[5,130,180]{1,2,0:T(8,128)} copy(f32[5,130,180]{2,1,0:T(8,128)} %bitcast.17) | data formatting | bytes 936000
  62.7 1.3 %reshape.28 = f32[5,130,10,18]{1,3,2,0:T(8,128)S(1)} reshape(f32[5,130,180]{1,2,0:T(8,128)} %copy.22) | data formatting | bytes 936000 | tf_op jit(solution)/shard_map/reshape | solution.py:301
  64.8 1.9 %collective-permute-start.7 = (f32[5,1,18,130]{3,2,1,0:T(8,128)}, f32[5,1,18,130]{3,2,1,0:T(8,128)}, u32[]{:S(2)}, u32[]{:S(2)}) collective-permute-start(f32[5,1,18,130]{3,2,1,0:T(8,128)} %get-tuple-element.10), channel_id=1, source_target_pairs={{32,0},{64,32},{96,64},{128,96},{160,128},{192,160},{224,192},{33,... | collective-permute-start | bytes 140408 | tf_op jit(solution)/shard_map/ppermute | solution.py:39
  66.7 9.9 %collective-permute-start.6 = (f32[5,1,18,130]{3,2,1,0:T(8,128)}, f32[5,1,18,130]{3,2,1,0:T(8,128)}, u32[]{:S(2)}, u32[]{:S(2)}) collective-permute-start(f32[5,1,18,130]{3,2,1,0:T(8,128)} %get-tuple-element.9), channel_id=1, source_target_pairs={{0,32},{32,64},{64,96},{96,128},{128,160},{160,192},{192,224},{1,3... | collective-permute-start | bytes 140408 | tf_op jit(solution)/shard_map/ppermute | solution.py:38
  76.8 1.9 %collective-permute-start.12 = (f32[5,1,3,3,4,128]{5,4,3,2,1,0:T(4,128)S(1)}, f32[5,1,3,3,4,128]{5,4,3,2,1,0:T(4,128)S(1)}, u32[]{:S(2)}, u32[]{:S(2)}) collective-permute-start(f32[5,1,3,3,4,128]{5,4,3,2,1,0:T(4,128)S(1)} %get-tuple-element.26), channel_id=1, source_target_pairs={{0,32},{32,64},{64,96},{96,128},{128,160},{160,192},{192,224},{1,3... | collective-permute-start | bytes 276488 | tf_op jit(solution)/shard_map/ppermute | solution.py:24
  78.7 3.9 %collective-permute-start.13 = (f32[5,1,3,3,4,128]{5,4,3,2,1,0:T(4,128)S(1)}, f32[5,1,3,3,4,128]{5,4,3,2,1,0:T(4,128)S(1)}, u32[]{:S(2)}, u32[]{:S(2)}) collective-permute-start(f32[5,1,3,3,4,128]{5,4,3,2,1,0:T(4,128)S(1)} %get-tuple-element.25), channel_id=1, source_target_pairs={{32,0},{64,32},{96,64},{128,96},{160,128},{192,160},{224,192},{33,... | collective-permute-start | bytes 276488 | tf_op jit(solution)/shard_map/ppermute | solution.py:27
  82.9 1.0 fusion
  84.0 1.9 %collective-permute-start.9 = (f32[5,8,1,130]{3,2,1,0:T(1,128)S(1)}, f32[5,8,1,130]{3,2,1,0:T(1,128)S(1)}, u32[]{:S(2)}, u32[]{:S(2)}) collective-permute-start(f32[5,8,1,130]{3,2,1,0:T(1,128)S(1)} %get-tuple-element.12), channel_id=1, source_target_pairs={{4,0},{8,4},{12,8},{16,12},{20,16},{24,20},{28,24},{5,1},{9,5},{13... | collective-permute-start | bytes 62408 | tf_op jit(solution)/shard_map/ppermute | solution.py:39
  86.0 2.4 %collective-permute-start.8 = (f32[5,8,1,130]{3,2,1,0:T(1,128)S(1)}, f32[5,8,1,130]{3,2,1,0:T(1,128)S(1)}, u32[]{:S(2)}, u32[]{:S(2)}) collective-permute-start(f32[5,8,1,130]{3,2,1,0:T(1,128)S(1)} %get-tuple-element.11), channel_id=1, source_target_pairs={{0,4},{4,8},{8,12},{12,16},{16,20},{20,24},{24,28},{1,5},{5,9},{9,... | collective-permute-start | bytes 62408 | tf_op jit(solution)/shard_map/ppermute | solution.py:38
  88.5 2.7 %collective-permute-done.13 = f32[5,1,3,3,4,128]{5,4,3,2,1,0:T(4,128)S(1)} collective-permute-done((f32[5,1,3,3,4,128]{5,4,3,2,1,0:T(4,128)S(1)}, f32[5,1,3,3,4,128]{5,4,3,2,1,0:T(4,128)S(1)}, u32[]{:S(2)}, u32[]{:S(2)}) %collective-permute-start.13) | collective-permute-done | bytes 92192 | tf_op jit(solution)/shard_map/ppermute | solution.py:27
  91.3 1.9 %collective-permute-start.15 = (f32[5,5,1,3,4,128]{5,4,3,2,1,0:T(4,128)S(1)}, f32[5,5,1,3,4,128]{5,4,3,2,1,0:T(4,128)S(1)}, u32[]{:S(2)}, u32[]{:S(2)}) collective-permute-start(f32[5,5,1,3,4,128]{5,4,3,2,1,0:T(4,128)S(1)} %get-tuple-element.20), channel_id=1, source_target_pairs={{4,0},{8,4},{12,8},{16,12},{20,16},{24,20},{28,24},{5,1},{9,5},{13... | collective-permute-start | bytes 460808 | tf_op jit(solution)/shard_map/ppermute | solution.py:27
  93.2 2.4 %collective-permute-start.14 = (f32[5,5,1,3,4,128]{5,4,3,2,1,0:T(4,128)S(1)}, f32[5,5,1,3,4,128]{5,4,3,2,1,0:T(4,128)S(1)}, u32[]{:S(2)}, u32[]{:S(2)}) collective-permute-start(f32[5,5,1,3,4,128]{5,4,3,2,1,0:T(4,128)S(1)} %get-tuple-element.19), channel_id=1, source_target_pairs={{0,4},{4,8},{8,12},{12,16},{16,20},{20,24},{24,28},{1,5},{5,9},{9,... | collective-permute-start | bytes 460808 | tf_op jit(solution)/shard_map/ppermute | solution.py:24
  95.9 3.8 %collective-permute-done.14 = f32[5,5,1,3,4,128]{5,4,3,2,1,0:T(4,128)S(1)} collective-permute-done((f32[5,5,1,3,4,128]{5,4,3,2,1,0:T(4,128)S(1)}, f32[5,5,1,3,4,128]{5,4,3,2,1,0:T(4,128)S(1)}, u32[]{:S(2)}, u32[]{:S(2)}) %collective-permute-start.14) | collective-permute-done | bytes 153632 | tf_op jit(solution)/shard_map/ppermute | solution.py:24
  99.8 1.9 %collective-permute-start.17 = (f32[5,5,5,1,4,128]{5,4,3,2,1,0:T(4,128)S(1)}, f32[5,5,5,1,4,128]{5,4,3,2,1,0:T(4,128)S(1)}, u32[]{:S(2)}, u32[]{:S(2)}) collective-permute-start(f32[5,5,5,1,4,128]{5,4,3,2,1,0:T(4,128)S(1)} %get-tuple-element.14), channel_id=1, source_target_pairs={{1,0},{2,1},{3,2},{5,4},{6,5},{7,6},{9,8},{10,9},{11,10},{13,12},{... | collective-permute-start | bytes 768008 | tf_op jit(solution)/shard_map/ppermute | solution.py:27
  101.8 3.9 %collective-permute-start.16 = (f32[5,5,5,1,4,128]{5,4,3,2,1,0:T(4,128)S(1)}, f32[5,5,5,1,4,128]{5,4,3,2,1,0:T(4,128)S(1)}, u32[]{:S(2)}, u32[]{:S(2)}) collective-permute-start(f32[5,5,5,1,4,128]{5,4,3,2,1,0:T(4,128)S(1)} %get-tuple-element.13), channel_id=1, source_target_pairs={{0,1},{1,2},{2,3},{4,5},{5,6},{6,7},{8,9},{9,10},{10,11},{12,13},{... | collective-permute-start | bytes 768008 | tf_op jit(solution)/shard_map/ppermute | solution.py:24
  105.9 1.9 %collective-permute-start.11 = (f32[5,8,16,1]{3,2,1,0:T(8,128)S(1)}, f32[5,8,16,1]{3,2,1,0:T(8,128)S(1)}, u32[]{:S(2)}, u32[]{:S(2)}) collective-permute-start(f32[5,8,16,1]{3,2,1,0:T(8,128)S(1)} %get-tuple-element.16), channel_id=1, source_target_pairs={{1,0},{2,1},{3,2},{5,4},{6,5},{7,6},{9,8},{10,9},{11,10},{13,12},{... | collective-permute-start | bytes 7688 | tf_op jit(solution)/shard_map/ppermute | solution.py:39
  107.8 3.9 %collective-permute-start.10 = (f32[5,8,16,1]{3,2,1,0:T(8,128)S(1)}, f32[5,8,16,1]{3,2,1,0:T(8,128)S(1)}, u32[]{:S(2)}, u32[]{:S(2)}) collective-permute-start(f32[5,8,16,1]{3,2,1,0:T(8,128)S(1)} %get-tuple-element.15), channel_id=1, source_target_pairs={{0,1},{1,2},{2,3},{4,5},{5,6},{6,7},{8,9},{9,10},{10,11},{12,13},{... | collective-permute-start | bytes 7688 | tf_op jit(solution)/shard_map/ppermute | solution.py:38
  111.7 4.3 %collective-permute-done.11 = f32[5,8,16,1]{3,2,1,0:T(8,128)S(1)} collective-permute-done((f32[5,8,16,1]{3,2,1,0:T(8,128)S(1)}, f32[5,8,16,1]{3,2,1,0:T(8,128)S(1)}, u32[]{:S(2)}, u32[]{:S(2)}) %collective-permute-start.11) | collective-permute-done | bytes 2592 | tf_op jit(solution)/shard_map/ppermute | solution.py:39
  116.0 1.9 %collective-permute-done.10 = f32[5,8,16,1]{3,2,1,0:T(8,128)S(1)} collective-permute-done((f32[5,8,16,1]{3,2,1,0:T(8,128)S(1)}, f32[5,8,16,1]{3,2,1,0:T(8,128)S(1)}, u32[]{:S(2)}, u32[]{:S(2)}) %collective-permute-start.10) | collective-permute-done | bytes 2592 | tf_op jit(solution)/shard_map/ppermute | solution.py:38
  117.9 1.3 %fusion.4 = f32[5,8,16,128]{3,2,1,0:T(8,128)} fusion(f32[5,8,16,130]{3,2,1,0:T(8,128)S(1)} %fusion.1, f32[5,8,16,128]{3,2,1,0:T(8,128)S(1)} %copy-done, f32[5,10,18,1]{3,2,1,0:T(8,128)S(1)} %copy.17, f32[5,10,1,128]{3,2,1,0:T(1,128)S(1)} %collective-permute-done.2, f32[5,10,16,128]{3,2,1,0:T(8,128)S(1)} %constant_dynamic-update-slice_fusion, ...), kind=kLoop, calls=%fused_computation.10 | loop fusion | flops 1884160 | bytes 1538100 | tf_op jit(solution)/shard_map/add | solution.py:304
  (50 shorter events, 9.8 us)
Async XLA Ops:
  1.4 9.8 %collective-permute-start.1 = (f32[5,1,16,128]{3,2,1,0:T(8,128)S(1)}, f32[5,1,16,128]{3,2,1,0:T(8,128)S(1)}, u32[]{:S(2)}, u32[]{:S(2)}) collective-permute-start(f32[5,1,16,128]{3,2,1,0:T(8,128)S(1)} %get-tuple-element.24), channel_id=1, source_target_pairs={{0,32},{32,64},{64,96},{96,128},{128,160},{160,192},{192,224},{1,3... | collective-permute-start | bytes 122888 | tf_op jit(solution)/shard_map/ppermute | solution.py:24
  9.3 11.9 %collective-permute-start = (f32[5,1,16,128]{3,2,1,0:T(8,128)S(1)}, f32[5,1,16,128]{3,2,1,0:T(8,128)S(1)}, u32[]{:S(2)}, u32[]{:S(2)}) collective-permute-start(f32[5,1,16,128]{3,2,1,0:T(8,128)S(1)} %get-tuple-element.23), channel_id=1, source_target_pairs={{32,0},{64,32},{96,64},{128,96},{160,128},{192,160},{224,192},{33,... | collective-permute-start | bytes 122888 | tf_op jit(solution)/shard_map/ppermute | solution.py:27
  21.2 5.2 %copy-start.2 = (f32[5,1,16,128]{3,2,1,0:T(8,128)}, f32[5,1,16,128]{3,2,1,0:T(8,128)S(1)}, u32[]{:S(2)}) copy-start(f32[5,1,16,128]{3,2,1,0:T(8,128)S(1)} %collective-permute-done) | copy-start | bytes 122884
  21.3 5.1 %collective-permute-start.2 = (f32[5,10,1,128]{3,2,1,0:T(1,128)S(1)}, f32[5,10,1,128]{3,2,1,0:T(1,128)S(1)}, u32[]{:S(2)}, u32[]{:S(2)}) collective-permute-start(f32[5,10,1,128]{3,2,1,0:T(1,128)S(1)} %get-tuple-element.22), channel_id=1, source_target_pairs={{4,0},{8,4},{12,8},{16,12},{20,16},{24,20},{28,24},{5,1},{9,5},{13... | collective-permute-start | bytes 76808 | tf_op jit(solution)/shard_map/ppermute | solution.py:27
  23.2 5.2 %collective-permute-start.3 = (f32[5,10,1,128]{3,2,1,0:T(1,128)S(1)}, f32[5,10,1,128]{3,2,1,0:T(1,128)S(1)}, u32[]{:S(2)}, u32[]{:S(2)}) collective-permute-start(f32[5,10,1,128]{3,2,1,0:T(1,128)S(1)} %get-tuple-element.21), channel_id=1, source_target_pairs={{0,4},{4,8},{8,12},{12,16},{16,20},{20,24},{24,28},{1,5},{5,9},{9,... | collective-permute-start | bytes 76808 | tf_op jit(solution)/shard_map/ppermute | solution.py:24
  29.1 7.5 %collective-permute-start.4 = (f32[5,10,18,1]{2,3,1,0:T(1,128)S(1)}, f32[5,10,18,1]{2,3,1,0:T(1,128)S(1)}, u32[]{:S(2)}, u32[]{:S(2)}) collective-permute-start(f32[5,10,18,1]{2,3,1,0:T(1,128)S(1)} %copy.14), channel_id=1, source_target_pairs={{1,0},{2,1},{3,2},{5,4},{6,5},{7,6},{9,8},{10,9},{11,10},{13,12},{... | collective-permute-start | bytes 10808 | tf_op jit(solution)/shard_map/ppermute | solution.py:27
  32.4 5.7 %collective-permute-start.5 = (f32[5,10,18,1]{2,3,1,0:T(1,128)S(1)}, f32[5,10,18,1]{2,3,1,0:T(1,128)S(1)}, u32[]{:S(2)}, u32[]{:S(2)}) collective-permute-start(f32[5,10,18,1]{2,3,1,0:T(1,128)S(1)} %copy.16), channel_id=1, source_target_pairs={{0,1},{1,2},{2,3},{4,5},{5,6},{6,7},{8,9},{9,10},{10,11},{12,13},{... | collective-permute-start | bytes 10808 | tf_op jit(solution)/shard_map/ppermute | solution.py:24
  62.7 13.9 %copy-start.1 = (f32[5,108,128]{2,1,0:T(8,128)S(1)}, f32[5,108,128]{2,1,0:T(8,128)}, u32[]{:S(2)}) copy-start(f32[5,108,128]{2,1,0:T(8,128)} %get-tuple-element.8) | copy-start | bytes 829444
  64.8 17.9 %collective-permute-start.7 = (f32[5,1,18,130]{3,2,1,0:T(8,128)}, f32[5,1,18,130]{3,2,1,0:T(8,128)}, u32[]{:S(2)}, u32[]{:S(2)}) collective-permute-start(f32[5,1,18,130]{3,2,1,0:T(8,128)} %get-tuple-element.10), channel_id=1, source_target_pairs={{32,0},{64,32},{96,64},{128,96},{160,128},{192,160},{224,192},{33,... | collective-permute-start | bytes 140408 | tf_op jit(solution)/shard_map/ppermute | solution.py:39
  66.7 16.2 %collective-permute-start.6 = (f32[5,1,18,130]{3,2,1,0:T(8,128)}, f32[5,1,18,130]{3,2,1,0:T(8,128)}, u32[]{:S(2)}, u32[]{:S(2)}) collective-permute-start(f32[5,1,18,130]{3,2,1,0:T(8,128)} %get-tuple-element.9), channel_id=1, source_target_pairs={{0,32},{32,64},{64,96},{96,128},{128,160},{160,192},{192,224},{1,3... | collective-permute-start | bytes 140408 | tf_op jit(solution)/shard_map/ppermute | solution.py:38
  76.8 11.6 %collective-permute-start.12 = (f32[5,1,3,3,4,128]{5,4,3,2,1,0:T(4,128)S(1)}, f32[5,1,3,3,4,128]{5,4,3,2,1,0:T(4,128)S(1)}, u32[]{:S(2)}, u32[]{:S(2)}) collective-permute-start(f32[5,1,3,3,4,128]{5,4,3,2,1,0:T(4,128)S(1)} %get-tuple-element.26), channel_id=1, source_target_pairs={{0,32},{32,64},{64,96},{96,128},{128,160},{160,192},{192,224},{1,3... | collective-permute-start | bytes 276488 | tf_op jit(solution)/shard_map/ppermute | solution.py:24
  78.7 12.5 %collective-permute-start.13 = (f32[5,1,3,3,4,128]{5,4,3,2,1,0:T(4,128)S(1)}, f32[5,1,3,3,4,128]{5,4,3,2,1,0:T(4,128)S(1)}, u32[]{:S(2)}, u32[]{:S(2)}) collective-permute-start(f32[5,1,3,3,4,128]{5,4,3,2,1,0:T(4,128)S(1)} %get-tuple-element.25), channel_id=1, source_target_pairs={{32,0},{64,32},{96,64},{128,96},{160,128},{192,160},{224,192},{33,... | collective-permute-start | bytes 276488 | tf_op jit(solution)/shard_map/ppermute | solution.py:27
  84.0 11.6 %collective-permute-start.9 = (f32[5,8,1,130]{3,2,1,0:T(1,128)S(1)}, f32[5,8,1,130]{3,2,1,0:T(1,128)S(1)}, u32[]{:S(2)}, u32[]{:S(2)}) collective-permute-start(f32[5,8,1,130]{3,2,1,0:T(1,128)S(1)} %get-tuple-element.12), channel_id=1, source_target_pairs={{4,0},{8,4},{12,8},{16,12},{20,16},{24,20},{28,24},{5,1},{9,5},{13... | collective-permute-start | bytes 62408 | tf_op jit(solution)/shard_map/ppermute | solution.py:39
  86.0 9.7 %collective-permute-start.8 = (f32[5,8,1,130]{3,2,1,0:T(1,128)S(1)}, f32[5,8,1,130]{3,2,1,0:T(1,128)S(1)}, u32[]{:S(2)}, u32[]{:S(2)}) collective-permute-start(f32[5,8,1,130]{3,2,1,0:T(1,128)S(1)} %get-tuple-element.11), channel_id=1, source_target_pairs={{0,4},{4,8},{8,12},{12,16},{16,20},{20,24},{24,28},{1,5},{5,9},{9,... | collective-permute-start | bytes 62408 | tf_op jit(solution)/shard_map/ppermute | solution.py:38
  91.3 4.6 %collective-permute-start.15 = (f32[5,5,1,3,4,128]{5,4,3,2,1,0:T(4,128)S(1)}, f32[5,5,1,3,4,128]{5,4,3,2,1,0:T(4,128)S(1)}, u32[]{:S(2)}, u32[]{:S(2)}) collective-permute-start(f32[5,5,1,3,4,128]{5,4,3,2,1,0:T(4,128)S(1)} %get-tuple-element.20), channel_id=1, source_target_pairs={{4,0},{8,4},{12,8},{16,12},{20,16},{24,20},{28,24},{5,1},{9,5},{13... | collective-permute-start | bytes 460808 | tf_op jit(solution)/shard_map/ppermute | solution.py:27
  93.2 6.5 %collective-permute-start.14 = (f32[5,5,1,3,4,128]{5,4,3,2,1,0:T(4,128)S(1)}, f32[5,5,1,3,4,128]{5,4,3,2,1,0:T(4,128)S(1)}, u32[]{:S(2)}, u32[]{:S(2)}) collective-permute-start(f32[5,5,1,3,4,128]{5,4,3,2,1,0:T(4,128)S(1)} %get-tuple-element.19), channel_id=1, source_target_pairs={{0,4},{4,8},{8,12},{12,16},{16,20},{20,24},{24,28},{1,5},{5,9},{9,... | collective-permute-start | bytes 460808 | tf_op jit(solution)/shard_map/ppermute | solution.py:24
  95.8 22.2 %copy-start = (f32[5,8,16,128]{3,2,1,0:T(8,128)S(1)}, f32[5,8,16,128]{3,2,1,0:T(8,128)}, u32[]{:S(2)}) copy-start(f32[5,8,16,128]{3,2,1,0:T(8,128)} %param.7) | copy-start | bytes 983044
  95.8 22.1 %copy-start.3 = (f32[5,1,16,128]{3,2,1,0:T(8,128)S(1)}, f32[5,1,16,128]{3,2,1,0:T(8,128)}, u32[]{:S(2)}) copy-start(f32[5,1,16,128]{3,2,1,0:T(8,128)} %copy-done.2) | copy-start | bytes 122884
  95.8 22.1 %copy-start.4 = (f32[5]{0:T(128)S(1)}, f32[5]{0:T(128)}, u32[]{:S(2)}) copy-start(f32[5]{0:T(128)} %constant.23.clone) | copy-start | bytes 64
  99.8 19.4 %collective-permute-start.17 = (f32[5,5,5,1,4,128]{5,4,3,2,1,0:T(4,128)S(1)}, f32[5,5,5,1,4,128]{5,4,3,2,1,0:T(4,128)S(1)}, u32[]{:S(2)}, u32[]{:S(2)}) collective-permute-start(f32[5,5,5,1,4,128]{5,4,3,2,1,0:T(4,128)S(1)} %get-tuple-element.14), channel_id=1, source_target_pairs={{1,0},{2,1},{3,2},{5,4},{6,5},{7,6},{9,8},{10,9},{11,10},{13,12},{... | collective-permute-start | bytes 768008 | tf_op jit(solution)/shard_map/ppermute | solution.py:27
  101.8 17.5 %collective-permute-start.16 = (f32[5,5,5,1,4,128]{5,4,3,2,1,0:T(4,128)S(1)}, f32[5,5,5,1,4,128]{5,4,3,2,1,0:T(4,128)S(1)}, u32[]{:S(2)}, u32[]{:S(2)}) collective-permute-start(f32[5,5,5,1,4,128]{5,4,3,2,1,0:T(4,128)S(1)} %get-tuple-element.13), channel_id=1, source_target_pairs={{0,1},{1,2},{2,3},{4,5},{5,6},{6,7},{8,9},{9,10},{10,11},{12,13},{... | collective-permute-start | bytes 768008 | tf_op jit(solution)/shard_map/ppermute | solution.py:24
  105.9 10.2 %collective-permute-start.11 = (f32[5,8,16,1]{3,2,1,0:T(8,128)S(1)}, f32[5,8,16,1]{3,2,1,0:T(8,128)S(1)}, u32[]{:S(2)}, u32[]{:S(2)}) collective-permute-start(f32[5,8,16,1]{3,2,1,0:T(8,128)S(1)} %get-tuple-element.16), channel_id=1, source_target_pairs={{1,0},{2,1},{3,2},{5,4},{6,5},{7,6},{9,8},{10,9},{11,10},{13,12},{... | collective-permute-start | bytes 7688 | tf_op jit(solution)/shard_map/ppermute | solution.py:39
  107.8 10.1 %collective-permute-start.10 = (f32[5,8,16,1]{3,2,1,0:T(8,128)S(1)}, f32[5,8,16,1]{3,2,1,0:T(8,128)S(1)}, u32[]{:S(2)}, u32[]{:S(2)}) collective-permute-start(f32[5,8,16,1]{3,2,1,0:T(8,128)S(1)} %get-tuple-element.15), channel_id=1, source_target_pairs={{0,1},{1,2},{2,3},{4,5},{5,6},{6,7},{8,9},{9,10},{10,11},{12,13},{... | collective-permute-start | bytes 7688 | tf_op jit(solution)/shard_map/ppermute | solution.py:38

commit v12 on v11

--- a/solution.py
+++ b/solution.py
@@ -119,7 +119,7 @@
     live_ref, dest_ref, table_ref, parcel_ref, cell_ref, offset_ref, factor_ref,
     kept_ref, outbox_ref, deposit_ref,
     weight_scr, depth_scr, spread_scr, updated_scr, count_scr, table_high_ref, table_low_ref,
-    total_scr, *, span_y, span_z,
+    total_scr, stack_scr, weight_rows_scr, spread_rows_scr, *, span_y, span_z,
 ):
     fields = parcel_ref.shape[0]
     blocks = parcel_ref.shape[1]
@@ -127,8 +127,9 @@
     plane_size = span_y * span_z
     total_scr[...] = jnp.zeros(total_scr.shape, jnp.float32)
     table_high, table_low = split_bf16(table_ref[...])
-    table_high_ref[...] = table_high
-    table_low_ref[...] = table_low
+    stack_scr[:, 0:PAIR_LANES] = table_high
+    stack_scr[:, PAIR_LANES:2 * PAIR_LANES] = table_high
+    stack_scr[:, 2 * PAIR_LANES:3 * PAIR_LANES] = table_low
     live = live_ref[0]
     pair_iota = lax.broadcasted_iota(jnp.int32, (PAIR_LANES, lanes), 0)
     depth_iota = lax.broadcasted_iota(jnp.int32, (DEPTH_ROWS, lanes), 0)
@@ -170,12 +171,11 @@
             )
             depth_scr[:, j * lanes:(j + 1) * lanes] = depth_weights
         weight_high, weight_low = split_bf16(weight_scr[...])
-        table_high = table_high_ref[...]
-        mixed = (
-            jnp.dot(table_high, weight_high, preferred_element_type=jnp.float32)
-            + jnp.dot(table_high, weight_low, preferred_element_type=jnp.float32)
-            + jnp.dot(table_low_ref[...], weight_high, preferred_element_type=jnp.float32)
-        )
+        width = GROUP * lanes
+        weight_rows_scr[0:PAIR_LANES, :] = weight_high
+        weight_rows_scr[PAIR_LANES:2 * PAIR_LANES, :] = weight_low
+        weight_rows_scr[2 * PAIR_LANES:3 * PAIR_LANES, :] = weight_high
+        mixed = jnp.dot(stack_scr[...], weight_rows_scr[...], preferred_element_type=jnp.float32)
         for j in range(GROUP):
             b = first + j
             depth_weights = depth_scr[:, j * lanes:(j + 1) * lanes]
@@ -214,11 +214,13 @@
                 [s * depth_weights for s in sources], axis=0
             )
         spread_high, spread_low = split_bf16(spread_scr[...])
+        spread_rows_scr[:, 0:width] = spread_high
+        spread_rows_scr[:, width:2 * width] = spread_high
+        spread_rows_scr[:, 2 * width:3 * width] = spread_low
+        weight_cols = jnp.concatenate([weight_high, weight_low, weight_high], axis=1)
         dims = (((1,), (1,)), ((), ()))
-        total_scr[...] += (
-            lax.dot_general(weight_high, spread_high, dims, preferred_element_type=jnp.float32)
-            + lax.dot_general(weight_low, spread_high, dims, preferred_element_type=jnp.float32)
-            + lax.dot_general(weight_high, spread_low, dims, preferred_element_type=jnp.float32)
+        total_scr[...] += lax.dot_general(
+            weight_cols, spread_rows_scr[...], dims, preferred_element_type=jnp.float32
         )
         return carry
 
@@ -294,6 +296,9 @@
             pltpu.VMEM(table.shape, jnp.bfloat16),
             pltpu.VMEM(table.shape, jnp.bfloat16),
             pltpu.VMEM((PAIR_LANES, fields * DEPTH_ROWS), jnp.float32),
+            pltpu.VMEM((fields * DEPTH_ROWS, 3 * PAIR_LANES), jnp.bfloat16),
+            pltpu.VMEM((3 * PAIR_LANES, lanes), jnp.bfloat16),
+            pltpu.VMEM((fields * DEPTH_ROWS, 3 * lanes), jnp.bfloat16),
         ],
     )(live_blocks, destination, table, parcel_rows, parcel_cells, offset_rows, factors)
     kept = jnp.transpose(kept_rows, (1, 0, 2))

time: 123 us -> 123 us (level)
  no operation moved by 1% of the time
where the time goes in v12:
time: 123 us; the launch traced here: 120 us
  starting transfers between devices  57.9 us (47%)
  waiting for transfers between devices  25.1 us (20%)
  Pallas kernels  17.2 us (14%)
  local copies, waits for them, and re-layouts  13.1 us (11%)
  other arithmetic  5.21 us (4%)
  between operations  1.66 us (1%)
    ppermute x6, starting transfers between devices, with_halo(): lax.ppermute(lax.slice_in_dim(block, block.shape[dim] - width, None, axis...  21.4 us
    pallas_call x1, Pallas kernels, local(): pl.pallas_call(functools.partial(coupling_kernel, span_y=span_y, span_z=s...  17.2 us
    ppermute x3, starting transfers between devices, fold_ghosts(): lax.ppermute(lax.slice_in_dim(block, span - 1, span, axis=dim), axis, for...  16.3 us
    ppermute x6, starting transfers between devices, with_halo(): lax.ppermute(lax.slice_in_dim(block, 0, width, axis=dim), axis, backward)  14.5 us
    ppermute x6, waiting for transfers between devices, with_halo(): lax.ppermute(lax.slice_in_dim(block, 0, width, axis=dim), axis, backward)  11.8 us
    ppermute x6, waiting for transfers between devices, with_halo(): lax.ppermute(lax.slice_in_dim(block, block.shape[dim] - width, None, axis...  6.85 us
    ppermute x3, starting transfers between devices, fold_ghosts(): lax.ppermute(lax.slice_in_dim(block, 0, 1, axis=dim), axis, backward)  5.76 us
    unnamed x16, local copies, waits for them, and re-layouts  5.08 us
  transfers between devices with their start and end apart: 18, of which 9 were waited for; matrix products, arithmetic and copies ran while one was open for 5% of the time, Pallas kernels for 0%

profile of v12, /device:TPU:58, one launch (start us, length us, event | category | flops | bytes accessed | tf_op | source)
XLA Modules:
  0.0 120.2 jit_solution(15637506930605228404)
XLA Ops:
  1.4 7.8 %collective-permute-start.1 = (f32[5,1,16,128]{3,2,1,0:T(8,128)S(1)}, f32[5,1,16,128]{3,2,1,0:T(8,128)S(1)}, u32[]{:S(2)}, u32[]{:S(2)}) collective-permute-start(f32[5,1,16,128]{3,2,1,0:T(8,128)S(1)} %get-tuple-element.24), channel_id=1, source_target_pairs={{0,32},{32,64},{64,96},{96,128},{128,160},{160,192},{192,224},{1,3... | collective-permute-start | bytes 122888 | tf_op jit(solution)/shard_map/ppermute | solution.py:24
  9.3 1.9 %collective-permute-start = (f32[5,1,16,128]{3,2,1,0:T(8,128)S(1)}, f32[5,1,16,128]{3,2,1,0:T(8,128)S(1)}, u32[]{:S(2)}, u32[]{:S(2)}) collective-permute-start(f32[5,1,16,128]{3,2,1,0:T(8,128)S(1)} %get-tuple-element.23), channel_id=1, source_target_pairs={{32,0},{64,32},{96,64},{128,96},{160,128},{192,160},{224,192},{33,... | collective-permute-start | bytes 122888 | tf_op jit(solution)/shard_map/ppermute | solution.py:27
  12.2 9.0 %collective-permute-done = f32[5,1,16,128]{3,2,1,0:T(8,128)S(1)} collective-permute-done((f32[5,1,16,128]{3,2,1,0:T(8,128)S(1)}, f32[5,1,16,128]{3,2,1,0:T(8,128)S(1)}, u32[]{:S(2)}, u32[]{:S(2)}) %collective-permute-start) | collective-permute-done | bytes 40992 | tf_op jit(solution)/shard_map/ppermute | solution.py:27
  21.3 1.9 %collective-permute-start.2 = (f32[5,10,1,128]{3,2,1,0:T(1,128)S(1)}, f32[5,10,1,128]{3,2,1,0:T(1,128)S(1)}, u32[]{:S(2)}, u32[]{:S(2)}) collective-permute-start(f32[5,10,1,128]{3,2,1,0:T(1,128)S(1)} %get-tuple-element.22), channel_id=1, source_target_pairs={{4,0},{8,4},{12,8},{16,12},{20,16},{24,20},{28,24},{5,1},{9,5},{13... | collective-permute-start | bytes 76808 | tf_op jit(solution)/shard_map/ppermute | solution.py:27
  23.2 2.4 %collective-permute-start.3 = (f32[5,10,1,128]{3,2,1,0:T(1,128)S(1)}, f32[5,10,1,128]{3,2,1,0:T(1,128)S(1)}, u32[]{:S(2)}, u32[]{:S(2)}) collective-permute-start(f32[5,10,1,128]{3,2,1,0:T(1,128)S(1)} %get-tuple-element.21), channel_id=1, source_target_pairs={{0,4},{4,8},{8,12},{12,16},{16,20},{20,24},{24,28},{1,5},{5,9},{9,... | collective-permute-start | bytes 76808 | tf_op jit(solution)/shard_map/ppermute | solution.py:24
  26.4 1.9 %collective-permute-done.3 = f32[5,10,1,128]{3,2,1,0:T(1,128)S(1)} collective-permute-done((f32[5,10,1,128]{3,2,1,0:T(1,128)S(1)}, f32[5,10,1,128]{3,2,1,0:T(1,128)S(1)}, u32[]{:S(2)}, u32[]{:S(2)}) %collective-permute-start.3) | collective-permute-done | bytes 25632 | tf_op jit(solution)/shard_map/ppermute | solution.py:24
  29.1 2.9 %collective-permute-start.4 = (f32[5,10,18,1]{2,3,1,0:T(1,128)S(1)}, f32[5,10,18,1]{2,3,1,0:T(1,128)S(1)}, u32[]{:S(2)}, u32[]{:S(2)}) collective-permute-start(f32[5,10,18,1]{2,3,1,0:T(1,128)S(1)} %copy.14), channel_id=1, source_target_pairs={{1,0},{2,1},{3,2},{5,4},{6,5},{7,6},{9,8},{10,9},{11,10},{13,12},{... | collective-permute-start | bytes 10808 | tf_op jit(solution)/shard_map/ppermute | solution.py:27
  32.4 2.9 %collective-permute-start.5 = (f32[5,10,18,1]{2,3,1,0:T(1,128)S(1)}, f32[5,10,18,1]{2,3,1,0:T(1,128)S(1)}, u32[]{:S(2)}, u32[]{:S(2)}) collective-permute-start(f32[5,10,18,1]{2,3,1,0:T(1,128)S(1)} %copy.16), channel_id=1, source_target_pairs={{0,1},{1,2},{2,3},{4,5},{5,6},{6,7},{8,9},{9,10},{10,11},{12,13},{... | collective-permute-start | bytes 10808 | tf_op jit(solution)/shard_map/ppermute | solution.py:24
  37.0 1.1 collective-permute-done.5
  39.3 1.1 reshape.25
  40.4 1.6 %copy.23 = f32[5,130,180]{2,1,0:T(8,128)S(1)} copy(f32[5,130,180]{1,2,0:T(8,128)} %reshape.25) | data formatting | bytes 936000
  42.8 17.2 %shard_map.94 = (f32[5,32,128]{2,1,0:T(8,128)}, f32[5,108,128]{2,1,0:T(8,128)}, f32[680,256]{1,0:T(8,128)}) custom-call(s32[1]{0:T(128)S(6)} %copy.28.live_ref, s32[32]{0:T(128)} %dest_ref.1, f32[680,256]{1,0:T(8,128)} %bitcast.16, f32[5,32,128]{2,1,0:T(8,128)} %bitcast.20, s32[32,128]{1,0:T(8,128)} %cell_ref.1, f32[3,32,128]{2,1,0:T(8,128)} %bitcast.21, ...), custom_call_target="tpu_custom_call" | custom-call | tf_op jit(solution)/shard_map/pallas_call | solution.py:281
  60.1 2.4 %copy.22 = f32[5,130,180]{1,2,0:T(8,128)} copy(f32[5,130,180]{2,1,0:T(8,128)} %bitcast.17) | data formatting | bytes 936000
  62.5 1.3 %reshape.28 = f32[5,130,10,18]{1,3,2,0:T(8,128)S(1)} reshape(f32[5,130,180]{1,2,0:T(8,128)} %copy.22) | data formatting | bytes 936000 | tf_op jit(solution)/shard_map/reshape | solution.py:306
  64.6 1.9 %collective-permute-start.7 = (f32[5,1,18,130]{3,2,1,0:T(8,128)}, f32[5,1,18,130]{3,2,1,0:T(8,128)}, u32[]{:S(2)}, u32[]{:S(2)}) collective-permute-start(f32[5,1,18,130]{3,2,1,0:T(8,128)} %get-tuple-element.10), channel_id=1, source_target_pairs={{32,0},{64,32},{96,64},{128,96},{160,128},{192,160},{224,192},{33,... | collective-permute-start | bytes 140408 | tf_op jit(solution)/shard_map/ppermute | solution.py:39
  66.5 9.9 %collective-permute-start.6 = (f32[5,1,18,130]{3,2,1,0:T(8,128)}, f32[5,1,18,130]{3,2,1,0:T(8,128)}, u32[]{:S(2)}, u32[]{:S(2)}) collective-permute-start(f32[5,1,18,130]{3,2,1,0:T(8,128)} %get-tuple-element.9), channel_id=1, source_target_pairs={{0,32},{32,64},{64,96},{96,128},{128,160},{160,192},{192,224},{1,3... | collective-permute-start | bytes 140408 | tf_op jit(solution)/shard_map/ppermute | solution.py:38
  76.5 1.9 %collective-permute-start.12 = (f32[5,1,3,3,4,128]{5,4,3,2,1,0:T(4,128)S(1)}, f32[5,1,3,3,4,128]{5,4,3,2,1,0:T(4,128)S(1)}, u32[]{:S(2)}, u32[]{:S(2)}) collective-permute-start(f32[5,1,3,3,4,128]{5,4,3,2,1,0:T(4,128)S(1)} %get-tuple-element.26), channel_id=1, source_target_pairs={{0,32},{32,64},{64,96},{96,128},{128,160},{160,192},{192,224},{1,3... | collective-permute-start | bytes 276488 | tf_op jit(solution)/shard_map/ppermute | solution.py:24
  78.5 3.9 %collective-permute-start.13 = (f32[5,1,3,3,4,128]{5,4,3,2,1,0:T(4,128)S(1)}, f32[5,1,3,3,4,128]{5,4,3,2,1,0:T(4,128)S(1)}, u32[]{:S(2)}, u32[]{:S(2)}) collective-permute-start(f32[5,1,3,3,4,128]{5,4,3,2,1,0:T(4,128)S(1)} %get-tuple-element.25), channel_id=1, source_target_pairs={{32,0},{64,32},{96,64},{128,96},{160,128},{192,160},{224,192},{33,... | collective-permute-start | bytes 276488 | tf_op jit(solution)/shard_map/ppermute | solution.py:27
  82.7 1.0 fusion
  83.8 1.9 %collective-permute-start.9 = (f32[5,8,1,130]{3,2,1,0:T(1,128)S(1)}, f32[5,8,1,130]{3,2,1,0:T(1,128)S(1)}, u32[]{:S(2)}, u32[]{:S(2)}) collective-permute-start(f32[5,8,1,130]{3,2,1,0:T(1,128)S(1)} %get-tuple-element.12), channel_id=1, source_target_pairs={{4,0},{8,4},{12,8},{16,12},{20,16},{24,20},{28,24},{5,1},{9,5},{13... | collective-permute-start | bytes 62408 | tf_op jit(solution)/shard_map/ppermute | solution.py:39
  85.7 2.4 %collective-permute-start.8 = (f32[5,8,1,130]{3,2,1,0:T(1,128)S(1)}, f32[5,8,1,130]{3,2,1,0:T(1,128)S(1)}, u32[]{:S(2)}, u32[]{:S(2)}) collective-permute-start(f32[5,8,1,130]{3,2,1,0:T(1,128)S(1)} %get-tuple-element.11), channel_id=1, source_target_pairs={{0,4},{4,8},{8,12},{12,16},{16,20},{20,24},{24,28},{1,5},{5,9},{9,... | collective-permute-start | bytes 62408 | tf_op jit(solution)/shard_map/ppermute | solution.py:38
  88.2 2.7 %collective-permute-done.13 = f32[5,1,3,3,4,128]{5,4,3,2,1,0:T(4,128)S(1)} collective-permute-done((f32[5,1,3,3,4,128]{5,4,3,2,1,0:T(4,128)S(1)}, f32[5,1,3,3,4,128]{5,4,3,2,1,0:T(4,128)S(1)}, u32[]{:S(2)}, u32[]{:S(2)}) %collective-permute-start.13) | collective-permute-done | bytes 92192 | tf_op jit(solution)/shard_map/ppermute | solution.py:27
  91.0 1.9 %collective-permute-start.15 = (f32[5,5,1,3,4,128]{5,4,3,2,1,0:T(4,128)S(1)}, f32[5,5,1,3,4,128]{5,4,3,2,1,0:T(4,128)S(1)}, u32[]{:S(2)}, u32[]{:S(2)}) collective-permute-start(f32[5,5,1,3,4,128]{5,4,3,2,1,0:T(4,128)S(1)} %get-tuple-element.20), channel_id=1, source_target_pairs={{4,0},{8,4},{12,8},{16,12},{20,16},{24,20},{28,24},{5,1},{9,5},{13... | collective-permute-start | bytes 460808 | tf_op jit(solution)/shard_map/ppermute | solution.py:27
  92.9 2.4 %collective-permute-start.14 = (f32[5,5,1,3,4,128]{5,4,3,2,1,0:T(4,128)S(1)}, f32[5,5,1,3,4,128]{5,4,3,2,1,0:T(4,128)S(1)}, u32[]{:S(2)}, u32[]{:S(2)}) collective-permute-start(f32[5,5,1,3,4,128]{5,4,3,2,1,0:T(4,128)S(1)} %get-tuple-element.19), channel_id=1, source_target_pairs={{0,4},{4,8},{8,12},{12,16},{16,20},{20,24},{24,28},{1,5},{5,9},{9,... | collective-permute-start | bytes 460808 | tf_op jit(solution)/shard_map/ppermute | solution.py:24
  95.7 3.8 %collective-permute-done.14 = f32[5,5,1,3,4,128]{5,4,3,2,1,0:T(4,128)S(1)} collective-permute-done((f32[5,5,1,3,4,128]{5,4,3,2,1,0:T(4,128)S(1)}, f32[5,5,1,3,4,128]{5,4,3,2,1,0:T(4,128)S(1)}, u32[]{:S(2)}, u32[]{:S(2)}) %collective-permute-start.14) | collective-permute-done | bytes 153632 | tf_op jit(solution)/shard_map/ppermute | solution.py:24
  99.6 1.9 %collective-permute-start.17 = (f32[5,5,5,1,4,128]{5,4,3,2,1,0:T(4,128)S(1)}, f32[5,5,5,1,4,128]{5,4,3,2,1,0:T(4,128)S(1)}, u32[]{:S(2)}, u32[]{:S(2)}) collective-permute-start(f32[5,5,5,1,4,128]{5,4,3,2,1,0:T(4,128)S(1)} %get-tuple-element.14), channel_id=1, source_target_pairs={{1,0},{2,1},{3,2},{5,4},{6,5},{7,6},{9,8},{10,9},{11,10},{13,12},{... | collective-permute-start | bytes 768008 | tf_op jit(solution)/shard_map/ppermute | solution.py:27
  101.5 3.9 %collective-permute-start.16 = (f32[5,5,5,1,4,128]{5,4,3,2,1,0:T(4,128)S(1)}, f32[5,5,5,1,4,128]{5,4,3,2,1,0:T(4,128)S(1)}, u32[]{:S(2)}, u32[]{:S(2)}) collective-permute-start(f32[5,5,5,1,4,128]{5,4,3,2,1,0:T(4,128)S(1)} %get-tuple-element.13), channel_id=1, source_target_pairs={{0,1},{1,2},{2,3},{4,5},{5,6},{6,7},{8,9},{9,10},{10,11},{12,13},{... | collective-permute-start | bytes 768008 | tf_op jit(solution)/shard_map/ppermute | solution.py:24
  105.6 1.9 %collective-permute-start.11 = (f32[5,8,16,1]{3,2,1,0:T(8,128)S(1)}, f32[5,8,16,1]{3,2,1,0:T(8,128)S(1)}, u32[]{:S(2)}, u32[]{:S(2)}) collective-permute-start(f32[5,8,16,1]{3,2,1,0:T(8,128)S(1)} %get-tuple-element.16), channel_id=1, source_target_pairs={{1,0},{2,1},{3,2},{5,4},{6,5},{7,6},{9,8},{10,9},{11,10},{13,12},{... | collective-permute-start | bytes 7688 | tf_op jit(solution)/shard_map/ppermute | solution.py:39
  107.5 3.9 %collective-permute-start.10 = (f32[5,8,16,1]{3,2,1,0:T(8,128)S(1)}, f32[5,8,16,1]{3,2,1,0:T(8,128)S(1)}, u32[]{:S(2)}, u32[]{:S(2)}) collective-permute-start(f32[5,8,16,1]{3,2,1,0:T(8,128)S(1)} %get-tuple-element.15), channel_id=1, source_target_pairs={{0,1},{1,2},{2,3},{4,5},{5,6},{6,7},{8,9},{9,10},{10,11},{12,13},{... | collective-permute-start | bytes 7688 | tf_op jit(solution)/shard_map/ppermute | solution.py:38
  111.5 4.3 %collective-permute-done.11 = f32[5,8,16,1]{3,2,1,0:T(8,128)S(1)} collective-permute-done((f32[5,8,16,1]{3,2,1,0:T(8,128)S(1)}, f32[5,8,16,1]{3,2,1,0:T(8,128)S(1)}, u32[]{:S(2)}, u32[]{:S(2)}) %collective-permute-start.11) | collective-permute-done | bytes 2592 | tf_op jit(solution)/shard_map/ppermute | solution.py:39
  115.8 1.9 %collective-permute-done.10 = f32[5,8,16,1]{3,2,1,0:T(8,128)S(1)} collective-permute-done((f32[5,8,16,1]{3,2,1,0:T(8,128)S(1)}, f32[5,8,16,1]{3,2,1,0:T(8,128)S(1)}, u32[]{:S(2)}, u32[]{:S(2)}) %collective-permute-start.10) | collective-permute-done | bytes 2592 | tf_op jit(solution)/shard_map/ppermute | solution.py:38
  117.7 1.3 %fusion.4 = f32[5,8,16,128]{3,2,1,0:T(8,128)} fusion(f32[5,8,16,130]{3,2,1,0:T(8,128)S(1)} %fusion.1, f32[5,8,16,128]{3,2,1,0:T(8,128)S(1)} %copy-done, f32[5,10,18,1]{3,2,1,0:T(8,128)S(1)} %copy.17, f32[5,10,1,128]{3,2,1,0:T(1,128)S(1)} %collective-permute-done.2, f32[5,10,16,128]{3,2,1,0:T(8,128)S(1)} %constant_dynamic-update-slice_fusion, ...), kind=kLoop, calls=%fused_computation.10 | loop fusion | flops 1884160 | bytes 1538100 | tf_op jit(solution)/shard_map/add | solution.py:309
  (50 shorter events, 9.8 us)
Async XLA Ops:
  1.4 9.8 %collective-permute-start.1 = (f32[5,1,16,128]{3,2,1,0:T(8,128)S(1)}, f32[5,1,16,128]{3,2,1,0:T(8,128)S(1)}, u32[]{:S(2)}, u32[]{:S(2)}) collective-permute-start(f32[5,1,16,128]{3,2,1,0:T(8,128)S(1)} %get-tuple-element.24), channel_id=1, source_target_pairs={{0,32},{32,64},{64,96},{96,128},{128,160},{160,192},{192,224},{1,3... | collective-permute-start | bytes 122888 | tf_op jit(solution)/shard_map/ppermute | solution.py:24
  9.3 11.9 %collective-permute-start = (f32[5,1,16,128]{3,2,1,0:T(8,128)S(1)}, f32[5,1,16,128]{3,2,1,0:T(8,128)S(1)}, u32[]{:S(2)}, u32[]{:S(2)}) collective-permute-start(f32[5,1,16,128]{3,2,1,0:T(8,128)S(1)} %get-tuple-element.23), channel_id=1, source_target_pairs={{32,0},{64,32},{96,64},{128,96},{160,128},{192,160},{224,192},{33,... | collective-permute-start | bytes 122888 | tf_op jit(solution)/shard_map/ppermute | solution.py:27
  21.2 5.2 %copy-start.2 = (f32[5,1,16,128]{3,2,1,0:T(8,128)}, f32[5,1,16,128]{3,2,1,0:T(8,128)S(1)}, u32[]{:S(2)}) copy-start(f32[5,1,16,128]{3,2,1,0:T(8,128)S(1)} %collective-permute-done) | copy-start | bytes 122884
  21.3 5.1 %collective-permute-start.2 = (f32[5,10,1,128]{3,2,1,0:T(1,128)S(1)}, f32[5,10,1,128]{3,2,1,0:T(1,128)S(1)}, u32[]{:S(2)}, u32[]{:S(2)}) collective-permute-start(f32[5,10,1,128]{3,2,1,0:T(1,128)S(1)} %get-tuple-element.22), channel_id=1, source_target_pairs={{4,0},{8,4},{12,8},{16,12},{20,16},{24,20},{28,24},{5,1},{9,5},{13... | collective-permute-start | bytes 76808 | tf_op jit(solution)/shard_map/ppermute | solution.py:27
  23.2 5.2 %collective-permute-start.3 = (f32[5,10,1,128]{3,2,1,0:T(1,128)S(1)}, f32[5,10,1,128]{3,2,1,0:T(1,128)S(1)}, u32[]{:S(2)}, u32[]{:S(2)}) collective-permute-start(f32[5,10,1,128]{3,2,1,0:T(1,128)S(1)} %get-tuple-element.21), channel_id=1, source_target_pairs={{0,4},{4,8},{8,12},{12,16},{16,20},{20,24},{24,28},{1,5},{5,9},{9,... | collective-permute-start | bytes 76808 | tf_op jit(solution)/shard_map/ppermute | solution.py:24
  29.1 7.5 %collective-permute-start.4 = (f32[5,10,18,1]{2,3,1,0:T(1,128)S(1)}, f32[5,10,18,1]{2,3,1,0:T(1,128)S(1)}, u32[]{:S(2)}, u32[]{:S(2)}) collective-permute-start(f32[5,10,18,1]{2,3,1,0:T(1,128)S(1)} %copy.14), channel_id=1, source_target_pairs={{1,0},{2,1},{3,2},{5,4},{6,5},{7,6},{9,8},{10,9},{11,10},{13,12},{... | collective-permute-start | bytes 10808 | tf_op jit(solution)/shard_map/ppermute | solution.py:27
  32.4 5.7 %collective-permute-start.5 = (f32[5,10,18,1]{2,3,1,0:T(1,128)S(1)}, f32[5,10,18,1]{2,3,1,0:T(1,128)S(1)}, u32[]{:S(2)}, u32[]{:S(2)}) collective-permute-start(f32[5,10,18,1]{2,3,1,0:T(1,128)S(1)} %copy.16), channel_id=1, source_target_pairs={{0,1},{1,2},{2,3},{4,5},{5,6},{6,7},{8,9},{9,10},{10,11},{12,13},{... | collective-permute-start | bytes 10808 | tf_op jit(solution)/shard_map/ppermute | solution.py:24
  62.5 13.9 %copy-start.1 = (f32[5,108,128]{2,1,0:T(8,128)S(1)}, f32[5,108,128]{2,1,0:T(8,128)}, u32[]{:S(2)}) copy-start(f32[5,108,128]{2,1,0:T(8,128)} %get-tuple-element.8) | copy-start | bytes 829444
  64.6 17.9 %collective-permute-start.7 = (f32[5,1,18,130]{3,2,1,0:T(8,128)}, f32[5,1,18,130]{3,2,1,0:T(8,128)}, u32[]{:S(2)}, u32[]{:S(2)}) collective-permute-start(f32[5,1,18,130]{3,2,1,0:T(8,128)} %get-tuple-element.10), channel_id=1, source_target_pairs={{32,0},{64,32},{96,64},{128,96},{160,128},{192,160},{224,192},{33,... | collective-permute-start | bytes 140408 | tf_op jit(solution)/shard_map/ppermute | solution.py:39
  66.5 16.2 %collective-permute-start.6 = (f32[5,1,18,130]{3,2,1,0:T(8,128)}, f32[5,1,18,130]{3,2,1,0:T(8,128)}, u32[]{:S(2)}, u32[]{:S(2)}) collective-permute-start(f32[5,1,18,130]{3,2,1,0:T(8,128)} %get-tuple-element.9), channel_id=1, source_target_pairs={{0,32},{32,64},{64,96},{96,128},{128,160},{160,192},{192,224},{1,3... | collective-permute-start | bytes 140408 | tf_op jit(solution)/shard_map/ppermute | solution.py:38
  76.5 11.6 %collective-permute-start.12 = (f32[5,1,3,3,4,128]{5,4,3,2,1,0:T(4,128)S(1)}, f32[5,1,3,3,4,128]{5,4,3,2,1,0:T(4,128)S(1)}, u32[]{:S(2)}, u32[]{:S(2)}) collective-permute-start(f32[5,1,3,3,4,128]{5,4,3,2,1,0:T(4,128)S(1)} %get-tuple-element.26), channel_id=1, source_target_pairs={{0,32},{32,64},{64,96},{96,128},{128,160},{160,192},{192,224},{1,3... | collective-permute-start | bytes 276488 | tf_op jit(solution)/shard_map/ppermute | solution.py:24
  78.5 12.5 %collective-permute-start.13 = (f32[5,1,3,3,4,128]{5,4,3,2,1,0:T(4,128)S(1)}, f32[5,1,3,3,4,128]{5,4,3,2,1,0:T(4,128)S(1)}, u32[]{:S(2)}, u32[]{:S(2)}) collective-permute-start(f32[5,1,3,3,4,128]{5,4,3,2,1,0:T(4,128)S(1)} %get-tuple-element.25), channel_id=1, source_target_pairs={{32,0},{64,32},{96,64},{128,96},{160,128},{192,160},{224,192},{33,... | collective-permute-start | bytes 276488 | tf_op jit(solution)/shard_map/ppermute | solution.py:27
  83.8 11.6 %collective-permute-start.9 = (f32[5,8,1,130]{3,2,1,0:T(1,128)S(1)}, f32[5,8,1,130]{3,2,1,0:T(1,128)S(1)}, u32[]{:S(2)}, u32[]{:S(2)}) collective-permute-start(f32[5,8,1,130]{3,2,1,0:T(1,128)S(1)} %get-tuple-element.12), channel_id=1, source_target_pairs={{4,0},{8,4},{12,8},{16,12},{20,16},{24,20},{28,24},{5,1},{9,5},{13... | collective-permute-start | bytes 62408 | tf_op jit(solution)/shard_map/ppermute | solution.py:39
  85.7 9.7 %collective-permute-start.8 = (f32[5,8,1,130]{3,2,1,0:T(1,128)S(1)}, f32[5,8,1,130]{3,2,1,0:T(1,128)S(1)}, u32[]{:S(2)}, u32[]{:S(2)}) collective-permute-start(f32[5,8,1,130]{3,2,1,0:T(1,128)S(1)} %get-tuple-element.11), channel_id=1, source_target_pairs={{0,4},{4,8},{8,12},{12,16},{16,20},{20,24},{24,28},{1,5},{5,9},{9,... | collective-permute-start | bytes 62408 | tf_op jit(solution)/shard_map/ppermute | solution.py:38
  91.0 4.6 %collective-permute-start.15 = (f32[5,5,1,3,4,128]{5,4,3,2,1,0:T(4,128)S(1)}, f32[5,5,1,3,4,128]{5,4,3,2,1,0:T(4,128)S(1)}, u32[]{:S(2)}, u32[]{:S(2)}) collective-permute-start(f32[5,5,1,3,4,128]{5,4,3,2,1,0:T(4,128)S(1)} %get-tuple-element.20), channel_id=1, source_target_pairs={{4,0},{8,4},{12,8},{16,12},{20,16},{24,20},{28,24},{5,1},{9,5},{13... | collective-permute-start | bytes 460808 | tf_op jit(solution)/shard_map/ppermute | solution.py:27
  92.9 6.5 %collective-permute-start.14 = (f32[5,5,1,3,4,128]{5,4,3,2,1,0:T(4,128)S(1)}, f32[5,5,1,3,4,128]{5,4,3,2,1,0:T(4,128)S(1)}, u32[]{:S(2)}, u32[]{:S(2)}) collective-permute-start(f32[5,5,1,3,4,128]{5,4,3,2,1,0:T(4,128)S(1)} %get-tuple-element.19), channel_id=1, source_target_pairs={{0,4},{4,8},{8,12},{12,16},{16,20},{20,24},{24,28},{1,5},{5,9},{9,... | collective-permute-start | bytes 460808 | tf_op jit(solution)/shard_map/ppermute | solution.py:24
  95.5 22.2 %copy-start = (f32[5,8,16,128]{3,2,1,0:T(8,128)S(1)}, f32[5,8,16,128]{3,2,1,0:T(8,128)}, u32[]{:S(2)}) copy-start(f32[5,8,16,128]{3,2,1,0:T(8,128)} %param.7) | copy-start | bytes 983044
  95.5 22.1 %copy-start.3 = (f32[5,1,16,128]{3,2,1,0:T(8,128)S(1)}, f32[5,1,16,128]{3,2,1,0:T(8,128)}, u32[]{:S(2)}) copy-start(f32[5,1,16,128]{3,2,1,0:T(8,128)} %copy-done.2) | copy-start | bytes 122884
  95.5 22.1 %copy-start.4 = (f32[5]{0:T(128)S(1)}, f32[5]{0:T(128)}, u32[]{:S(2)}) copy-start(f32[5]{0:T(128)} %constant.23.clone) | copy-start | bytes 64
  99.6 19.4 %collective-permute-start.17 = (f32[5,5,5,1,4,128]{5,4,3,2,1,0:T(4,128)S(1)}, f32[5,5,5,1,4,128]{5,4,3,2,1,0:T(4,128)S(1)}, u32[]{:S(2)}, u32[]{:S(2)}) collective-permute-start(f32[5,5,5,1,4,128]{5,4,3,2,1,0:T(4,128)S(1)} %get-tuple-element.14), channel_id=1, source_target_pairs={{1,0},{2,1},{3,2},{5,4},{6,5},{7,6},{9,8},{10,9},{11,10},{13,12},{... | collective-permute-start | bytes 768008 | tf_op jit(solution)/shard_map/ppermute | solution.py:27
  101.5 17.5 %collective-permute-start.16 = (f32[5,5,5,1,4,128]{5,4,3,2,1,0:T(4,128)S(1)}, f32[5,5,5,1,4,128]{5,4,3,2,1,0:T(4,128)S(1)}, u32[]{:S(2)}, u32[]{:S(2)}) collective-permute-start(f32[5,5,5,1,4,128]{5,4,3,2,1,0:T(4,128)S(1)} %get-tuple-element.13), channel_id=1, source_target_pairs={{0,1},{1,2},{2,3},{4,5},{5,6},{6,7},{8,9},{9,10},{10,11},{12,13},{... | collective-permute-start | bytes 768008 | tf_op jit(solution)/shard_map/ppermute | solution.py:24
  105.6 10.2 %collective-permute-start.11 = (f32[5,8,16,1]{3,2,1,0:T(8,128)S(1)}, f32[5,8,16,1]{3,2,1,0:T(8,128)S(1)}, u32[]{:S(2)}, u32[]{:S(2)}) collective-permute-start(f32[5,8,16,1]{3,2,1,0:T(8,128)S(1)} %get-tuple-element.16), channel_id=1, source_target_pairs={{1,0},{2,1},{3,2},{5,4},{6,5},{7,6},{9,8},{10,9},{11,10},{13,12},{... | collective-permute-start | bytes 7688 | tf_op jit(solution)/shard_map/ppermute | solution.py:39
  107.5 10.1 %collective-permute-start.10 = (f32[5,8,16,1]{3,2,1,0:T(8,128)S(1)}, f32[5,8,16,1]{3,2,1,0:T(8,128)S(1)}, u32[]{:S(2)}, u32[]{:S(2)}) collective-permute-start(f32[5,8,16,1]{3,2,1,0:T(8,128)S(1)} %get-tuple-element.15), channel_id=1, source_target_pairs={{0,1},{1,2},{2,3},{4,5},{5,6},{6,7},{8,9},{9,10},{10,11},{12,13},{... | collective-permute-start | bytes 7688 | tf_op jit(solution)/shard_map/ppermute | solution.py:38

commit v13 on v12

--- a/solution.py
+++ b/solution.py
@@ -93,6 +93,7 @@
 
 
 PAIR_LANES = 256
+PAIR_ROWS = 192
 DEPTH_ROWS = 136
 
 
@@ -131,7 +132,8 @@
     stack_scr[:, PAIR_LANES:2 * PAIR_LANES] = table_high
     stack_scr[:, 2 * PAIR_LANES:3 * PAIR_LANES] = table_low
     live = live_ref[0]
-    pair_iota = lax.broadcasted_iota(jnp.int32, (PAIR_LANES, lanes), 0)
+    pair_iota = lax.broadcasted_iota(jnp.int32, (PAIR_ROWS, lanes), 0)
+    weight_rows_scr[...] = jnp.zeros(weight_rows_scr.shape, jnp.bfloat16)
     depth_iota = lax.broadcasted_iota(jnp.int32, (DEPTH_ROWS, lanes), 0)
 
     def group(g, carry):
@@ -151,7 +153,7 @@
         far_share = jnp.abs(offsets)
         near_share = 1.0 - far_share
         for j in range(GROUP):
-            weights = jnp.zeros((PAIR_LANES, lanes), jnp.float32)
+            weights = jnp.zeros((PAIR_ROWS, lanes), jnp.float32)
             for bit_x in range(2):
                 for bit_y in range(2):
                     share = (far_share[0, j:j + 1] if bit_x else near_share[0, j:j + 1]) * (
@@ -172,9 +174,9 @@
             depth_scr[:, j * lanes:(j + 1) * lanes] = depth_weights
         weight_high, weight_low = split_bf16(weight_scr[...])
         width = GROUP * lanes
-        weight_rows_scr[0:PAIR_LANES, :] = weight_high
-        weight_rows_scr[PAIR_LANES:2 * PAIR_LANES, :] = weight_low
-        weight_rows_scr[2 * PAIR_LANES:3 * PAIR_LANES, :] = weight_high
+        weight_rows_scr[0:PAIR_ROWS, :] = weight_high
+        weight_rows_scr[PAIR_LANES:PAIR_LANES + PAIR_ROWS, :] = weight_low
+        weight_rows_scr[2 * PAIR_LANES:2 * PAIR_LANES + PAIR_ROWS, :] = weight_high
         mixed = jnp.dot(stack_scr[...], weight_rows_scr[...], preferred_element_type=jnp.float32)
         for j in range(GROUP):
             b = first + j
@@ -225,7 +227,8 @@
         return carry
 
     lax.fori_loop(0, blocks // GROUP, group, 0)
-    deposit_ref[...] = total_scr[...].T
+    deposit_ref[...] = jnp.zeros(deposit_ref.shape, jnp.float32)
+    deposit_ref[:, 0:PAIR_ROWS] = total_scr[...].T
 
     kept_ref[...] = jnp.zeros(kept_ref.shape, jnp.float32)
     outbox_ref[...] = jnp.zeros(outbox_ref.shape, jnp.float32)
@@ -260,6 +263,7 @@
     span_y = size_y + 2
     span_z = size_z + 2
     pair_count = span_x * span_y
+    assert pair_count <= PAIR_ROWS and span_z <= DEPTH_ROWS
     plane_size = span_y * span_z
     table = jnp.transpose(padded, (0, 3, 1, 2)).reshape(fields, span_z, pair_count)
     table = jnp.pad(table, ((0, 0), (0, DEPTH_ROWS - span_z), (0, PAIR_LANES - pair_count)))
@@ -288,14 +292,14 @@
         in_specs=[smem, smem] + [vmem] * 5,
         out_specs=(vmem, vmem, vmem),
         scratch_shapes=[
-            pltpu.VMEM((PAIR_LANES, lanes), jnp.float32),
+            pltpu.VMEM((PAIR_ROWS, lanes), jnp.float32),
             pltpu.VMEM((DEPTH_ROWS, lanes), jnp.float32),
             pltpu.VMEM((fields * DEPTH_ROWS, lanes), jnp.float32),
             pltpu.VMEM(parcel_rows.shape, jnp.float32),
             pltpu.SMEM((32,), jnp.int32),
             pltpu.VMEM(table.shape, jnp.bfloat16),
             pltpu.VMEM(table.shape, jnp.bfloat16),
-            pltpu.VMEM((PAIR_LANES, fields * DEPTH_ROWS), jnp.float32),
+            pltpu.VMEM((PAIR_ROWS, fields * DEPTH_ROWS), jnp.float32),
             pltpu.VMEM((fields * DEPTH_ROWS, 3 * PAIR_LANES), jnp.bfloat16),
             pltpu.VMEM((3 * PAIR_LANES, lanes), jnp.bfloat16),
             pltpu.VMEM((fields * DEPTH_ROWS, 3 * lanes), jnp.bfloat16),

time: 123 us -> 122 us (level)
  no operation moved by 1% of the time
where the time goes in v13:
time: 122 us; the launch traced here: 119 us
  starting transfers between devices  57.9 us (47%)
  waiting for transfers between devices  25.1 us (21%)
  Pallas kernels  16.4 us (13%)
  local copies, waits for them, and re-layouts  13.1 us (11%)
  other arithmetic  5.21 us (4%)
  between operations  1.66 us (1%)
    ppermute x6, starting transfers between devices, with_halo(): lax.ppermute(lax.slice_in_dim(block, block.shape[dim] - width, None, axis...  21.4 us
    pallas_call x1, Pallas kernels, local(): pl.pallas_call(functools.partial(coupling_kernel, span_y=span_y, span_z=s...  16.4 us
    ppermute x3, starting transfers between devices, fold_ghosts(): lax.ppermute(lax.slice_in_dim(block, span - 1, span, axis=dim), axis, for...  16.3 us
    ppermute x6, starting transfers between devices, with_halo(): lax.ppermute(lax.slice_in_dim(block, 0, width, axis=dim), axis, backward)  14.5 us
    ppermute x6, waiting for transfers between devices, with_halo(): lax.ppermute(lax.slice_in_dim(block, 0, width, axis=dim), axis, backward)  11.8 us
    ppermute x6, waiting for transfers between devices, with_halo(): lax.ppermute(lax.slice_in_dim(block, block.shape[dim] - width, None, axis...  6.85 us
    ppermute x3, starting transfers between devices, fold_ghosts(): lax.ppermute(lax.slice_in_dim(block, 0, 1, axis=dim), axis, backward)  5.76 us
    unnamed x16, local copies, waits for them, and re-layouts  5.08 us
  transfers between devices with their start and end apart: 18, of which 9 were waited for; matrix products, arithmetic and copies ran while one was open for 5% of the time, Pallas kernels for 0%

profile of v13, /device:TPU:58, one launch (start us, length us, event | category | flops | bytes accessed | tf_op | source)
XLA Modules:
  0.0 119.4 jit_solution(3270045527732135961)
XLA Ops:
  1.4 7.8 %collective-permute-start.1 = (f32[5,1,16,128]{3,2,1,0:T(8,128)S(1)}, f32[5,1,16,128]{3,2,1,0:T(8,128)S(1)}, u32[]{:S(2)}, u32[]{:S(2)}) collective-permute-start(f32[5,1,16,128]{3,2,1,0:T(8,128)S(1)} %get-tuple-element.24), channel_id=1, source_target_pairs={{0,32},{32,64},{64,96},{96,128},{128,160},{160,192},{192,224},{1,3... | collective-permute-start | bytes 122888 | tf_op jit(solution)/shard_map/ppermute | solution.py:24
  9.3 1.9 %collective-permute-start = (f32[5,1,16,128]{3,2,1,0:T(8,128)S(1)}, f32[5,1,16,128]{3,2,1,0:T(8,128)S(1)}, u32[]{:S(2)}, u32[]{:S(2)}) collective-permute-start(f32[5,1,16,128]{3,2,1,0:T(8,128)S(1)} %get-tuple-element.23), channel_id=1, source_target_pairs={{32,0},{64,32},{96,64},{128,96},{160,128},{192,160},{224,192},{33,... | collective-permute-start | bytes 122888 | tf_op jit(solution)/shard_map/ppermute | solution.py:27
  12.2 9.0 %collective-permute-done = f32[5,1,16,128]{3,2,1,0:T(8,128)S(1)} collective-permute-done((f32[5,1,16,128]{3,2,1,0:T(8,128)S(1)}, f32[5,1,16,128]{3,2,1,0:T(8,128)S(1)}, u32[]{:S(2)}, u32[]{:S(2)}) %collective-permute-start) | collective-permute-done | bytes 40992 | tf_op jit(solution)/shard_map/ppermute | solution.py:27
  21.3 1.9 %collective-permute-start.2 = (f32[5,10,1,128]{3,2,1,0:T(1,128)S(1)}, f32[5,10,1,128]{3,2,1,0:T(1,128)S(1)}, u32[]{:S(2)}, u32[]{:S(2)}) collective-permute-start(f32[5,10,1,128]{3,2,1,0:T(1,128)S(1)} %get-tuple-element.22), channel_id=1, source_target_pairs={{4,0},{8,4},{12,8},{16,12},{20,16},{24,20},{28,24},{5,1},{9,5},{13... | collective-permute-start | bytes 76808 | tf_op jit(solution)/shard_map/ppermute | solution.py:27
  23.2 2.4 %collective-permute-start.3 = (f32[5,10,1,128]{3,2,1,0:T(1,128)S(1)}, f32[5,10,1,128]{3,2,1,0:T(1,128)S(1)}, u32[]{:S(2)}, u32[]{:S(2)}) collective-permute-start(f32[5,10,1,128]{3,2,1,0:T(1,128)S(1)} %get-tuple-element.21), channel_id=1, source_target_pairs={{0,4},{4,8},{8,12},{12,16},{16,20},{20,24},{24,28},{1,5},{5,9},{9,... | collective-permute-start | bytes 76808 | tf_op jit(solution)/shard_map/ppermute | solution.py:24
  26.4 1.9 %collective-permute-done.3 = f32[5,10,1,128]{3,2,1,0:T(1,128)S(1)} collective-permute-done((f32[5,10,1,128]{3,2,1,0:T(1,128)S(1)}, f32[5,10,1,128]{3,2,1,0:T(1,128)S(1)}, u32[]{:S(2)}, u32[]{:S(2)}) %collective-permute-start.3) | collective-permute-done | bytes 25632 | tf_op jit(solution)/shard_map/ppermute | solution.py:24
  29.1 2.9 %collective-permute-start.4 = (f32[5,10,18,1]{2,3,1,0:T(1,128)S(1)}, f32[5,10,18,1]{2,3,1,0:T(1,128)S(1)}, u32[]{:S(2)}, u32[]{:S(2)}) collective-permute-start(f32[5,10,18,1]{2,3,1,0:T(1,128)S(1)} %copy.14), channel_id=1, source_target_pairs={{1,0},{2,1},{3,2},{5,4},{6,5},{7,6},{9,8},{10,9},{11,10},{13,12},{... | collective-permute-start | bytes 10808 | tf_op jit(solution)/shard_map/ppermute | solution.py:27
  32.4 2.9 %collective-permute-start.5 = (f32[5,10,18,1]{2,3,1,0:T(1,128)S(1)}, f32[5,10,18,1]{2,3,1,0:T(1,128)S(1)}, u32[]{:S(2)}, u32[]{:S(2)}) collective-permute-start(f32[5,10,18,1]{2,3,1,0:T(1,128)S(1)} %copy.16), channel_id=1, source_target_pairs={{0,1},{1,2},{2,3},{4,5},{5,6},{6,7},{8,9},{9,10},{10,11},{12,13},{... | collective-permute-start | bytes 10808 | tf_op jit(solution)/shard_map/ppermute | solution.py:24
  37.0 1.1 collective-permute-done.5
  39.3 1.1 reshape.25
  40.4 1.6 %copy.23 = f32[5,130,180]{2,1,0:T(8,128)S(1)} copy(f32[5,130,180]{1,2,0:T(8,128)} %reshape.25) | data formatting | bytes 936000
  42.8 16.4 %shard_map.94 = (f32[5,32,128]{2,1,0:T(8,128)}, f32[5,108,128]{2,1,0:T(8,128)}, f32[680,256]{1,0:T(8,128)}) custom-call(s32[1]{0:T(128)S(6)} %copy.28.live_ref, s32[32]{0:T(128)} %dest_ref.1, f32[680,256]{1,0:T(8,128)} %bitcast.16, f32[5,32,128]{2,1,0:T(8,128)} %bitcast.20, s32[32,128]{1,0:T(8,128)} %cell_ref.1, f32[3,32,128]{2,1,0:T(8,128)} %bitcast.21, ...), custom_call_target="tpu_custom_call" | custom-call | tf_op jit(solution)/shard_map/pallas_call | solution.py:285
  59.3 2.4 %copy.22 = f32[5,130,180]{1,2,0:T(8,128)} copy(f32[5,130,180]{2,1,0:T(8,128)} %bitcast.17) | data formatting | bytes 936000
  61.7 1.3 %reshape.28 = f32[5,130,10,18]{1,3,2,0:T(8,128)S(1)} reshape(f32[5,130,180]{1,2,0:T(8,128)} %copy.22) | data formatting | bytes 936000 | tf_op jit(solution)/shard_map/reshape | solution.py:310
  63.8 1.9 %collective-permute-start.7 = (f32[5,1,18,130]{3,2,1,0:T(8,128)}, f32[5,1,18,130]{3,2,1,0:T(8,128)}, u32[]{:S(2)}, u32[]{:S(2)}) collective-permute-start(f32[5,1,18,130]{3,2,1,0:T(8,128)} %get-tuple-element.10), channel_id=1, source_target_pairs={{32,0},{64,32},{96,64},{128,96},{160,128},{192,160},{224,192},{33,... | collective-permute-start | bytes 140408 | tf_op jit(solution)/shard_map/ppermute | solution.py:39
  65.7 9.9 %collective-permute-start.6 = (f32[5,1,18,130]{3,2,1,0:T(8,128)}, f32[5,1,18,130]{3,2,1,0:T(8,128)}, u32[]{:S(2)}, u32[]{:S(2)}) collective-permute-start(f32[5,1,18,130]{3,2,1,0:T(8,128)} %get-tuple-element.9), channel_id=1, source_target_pairs={{0,32},{32,64},{64,96},{96,128},{128,160},{160,192},{192,224},{1,3... | collective-permute-start | bytes 140408 | tf_op jit(solution)/shard_map/ppermute | solution.py:38
  75.8 1.9 %collective-permute-start.12 = (f32[5,1,3,3,4,128]{5,4,3,2,1,0:T(4,128)S(1)}, f32[5,1,3,3,4,128]{5,4,3,2,1,0:T(4,128)S(1)}, u32[]{:S(2)}, u32[]{:S(2)}) collective-permute-start(f32[5,1,3,3,4,128]{5,4,3,2,1,0:T(4,128)S(1)} %get-tuple-element.26), channel_id=1, source_target_pairs={{0,32},{32,64},{64,96},{96,128},{128,160},{160,192},{192,224},{1,3... | collective-permute-start | bytes 276488 | tf_op jit(solution)/shard_map/ppermute | solution.py:24
  77.7 3.9 %collective-permute-start.13 = (f32[5,1,3,3,4,128]{5,4,3,2,1,0:T(4,128)S(1)}, f32[5,1,3,3,4,128]{5,4,3,2,1,0:T(4,128)S(1)}, u32[]{:S(2)}, u32[]{:S(2)}) collective-permute-start(f32[5,1,3,3,4,128]{5,4,3,2,1,0:T(4,128)S(1)} %get-tuple-element.25), channel_id=1, source_target_pairs={{32,0},{64,32},{96,64},{128,96},{160,128},{192,160},{224,192},{33,... | collective-permute-start | bytes 276488 | tf_op jit(solution)/shard_map/ppermute | solution.py:27
  81.9 1.0 fusion
  83.0 1.9 %collective-permute-start.9 = (f32[5,8,1,130]{3,2,1,0:T(1,128)S(1)}, f32[5,8,1,130]{3,2,1,0:T(1,128)S(1)}, u32[]{:S(2)}, u32[]{:S(2)}) collective-permute-start(f32[5,8,1,130]{3,2,1,0:T(1,128)S(1)} %get-tuple-element.12), channel_id=1, source_target_pairs={{4,0},{8,4},{12,8},{16,12},{20,16},{24,20},{28,24},{5,1},{9,5},{13... | collective-permute-start | bytes 62408 | tf_op jit(solution)/shard_map/ppermute | solution.py:39
  84.9 2.4 %collective-permute-start.8 = (f32[5,8,1,130]{3,2,1,0:T(1,128)S(1)}, f32[5,8,1,130]{3,2,1,0:T(1,128)S(1)}, u32[]{:S(2)}, u32[]{:S(2)}) collective-permute-start(f32[5,8,1,130]{3,2,1,0:T(1,128)S(1)} %get-tuple-element.11), channel_id=1, source_target_pairs={{0,4},{4,8},{8,12},{12,16},{16,20},{20,24},{24,28},{1,5},{5,9},{9,... | collective-permute-start | bytes 62408 | tf_op jit(solution)/shard_map/ppermute | solution.py:38
  87.4 2.7 %collective-permute-done.13 = f32[5,1,3,3,4,128]{5,4,3,2,1,0:T(4,128)S(1)} collective-permute-done((f32[5,1,3,3,4,128]{5,4,3,2,1,0:T(4,128)S(1)}, f32[5,1,3,3,4,128]{5,4,3,2,1,0:T(4,128)S(1)}, u32[]{:S(2)}, u32[]{:S(2)}) %collective-permute-start.13) | collective-permute-done | bytes 92192 | tf_op jit(solution)/shard_map/ppermute | solution.py:27
  90.2 1.9 %collective-permute-start.15 = (f32[5,5,1,3,4,128]{5,4,3,2,1,0:T(4,128)S(1)}, f32[5,5,1,3,4,128]{5,4,3,2,1,0:T(4,128)S(1)}, u32[]{:S(2)}, u32[]{:S(2)}) collective-permute-start(f32[5,5,1,3,4,128]{5,4,3,2,1,0:T(4,128)S(1)} %get-tuple-element.20), channel_id=1, source_target_pairs={{4,0},{8,4},{12,8},{16,12},{20,16},{24,20},{28,24},{5,1},{9,5},{13... | collective-permute-start | bytes 460808 | tf_op jit(solution)/shard_map/ppermute | solution.py:27
  92.2 2.4 %collective-permute-start.14 = (f32[5,5,1,3,4,128]{5,4,3,2,1,0:T(4,128)S(1)}, f32[5,5,1,3,4,128]{5,4,3,2,1,0:T(4,128)S(1)}, u32[]{:S(2)}, u32[]{:S(2)}) collective-permute-start(f32[5,5,1,3,4,128]{5,4,3,2,1,0:T(4,128)S(1)} %get-tuple-element.19), channel_id=1, source_target_pairs={{0,4},{4,8},{8,12},{12,16},{16,20},{20,24},{24,28},{1,5},{5,9},{9,... | collective-permute-start | bytes 460808 | tf_op jit(solution)/shard_map/ppermute | solution.py:24
  94.9 3.8 %collective-permute-done.14 = f32[5,5,1,3,4,128]{5,4,3,2,1,0:T(4,128)S(1)} collective-permute-done((f32[5,5,1,3,4,128]{5,4,3,2,1,0:T(4,128)S(1)}, f32[5,5,1,3,4,128]{5,4,3,2,1,0:T(4,128)S(1)}, u32[]{:S(2)}, u32[]{:S(2)}) %collective-permute-start.14) | collective-permute-done | bytes 153632 | tf_op jit(solution)/shard_map/ppermute | solution.py:24
  98.8 1.9 %collective-permute-start.17 = (f32[5,5,5,1,4,128]{5,4,3,2,1,0:T(4,128)S(1)}, f32[5,5,5,1,4,128]{5,4,3,2,1,0:T(4,128)S(1)}, u32[]{:S(2)}, u32[]{:S(2)}) collective-permute-start(f32[5,5,5,1,4,128]{5,4,3,2,1,0:T(4,128)S(1)} %get-tuple-element.14), channel_id=1, source_target_pairs={{1,0},{2,1},{3,2},{5,4},{6,5},{7,6},{9,8},{10,9},{11,10},{13,12},{... | collective-permute-start | bytes 768008 | tf_op jit(solution)/shard_map/ppermute | solution.py:27
  100.7 3.9 %collective-permute-start.16 = (f32[5,5,5,1,4,128]{5,4,3,2,1,0:T(4,128)S(1)}, f32[5,5,5,1,4,128]{5,4,3,2,1,0:T(4,128)S(1)}, u32[]{:S(2)}, u32[]{:S(2)}) collective-permute-start(f32[5,5,5,1,4,128]{5,4,3,2,1,0:T(4,128)S(1)} %get-tuple-element.13), channel_id=1, source_target_pairs={{0,1},{1,2},{2,3},{4,5},{5,6},{6,7},{8,9},{9,10},{10,11},{12,13},{... | collective-permute-start | bytes 768008 | tf_op jit(solution)/shard_map/ppermute | solution.py:24
  104.8 1.9 %collective-permute-start.11 = (f32[5,8,16,1]{3,2,1,0:T(8,128)S(1)}, f32[5,8,16,1]{3,2,1,0:T(8,128)S(1)}, u32[]{:S(2)}, u32[]{:S(2)}) collective-permute-start(f32[5,8,16,1]{3,2,1,0:T(8,128)S(1)} %get-tuple-element.16), channel_id=1, source_target_pairs={{1,0},{2,1},{3,2},{5,4},{6,5},{7,6},{9,8},{10,9},{11,10},{13,12},{... | collective-permute-start | bytes 7688 | tf_op jit(solution)/shard_map/ppermute | solution.py:39
  106.8 3.9 %collective-permute-start.10 = (f32[5,8,16,1]{3,2,1,0:T(8,128)S(1)}, f32[5,8,16,1]{3,2,1,0:T(8,128)S(1)}, u32[]{:S(2)}, u32[]{:S(2)}) collective-permute-start(f32[5,8,16,1]{3,2,1,0:T(8,128)S(1)} %get-tuple-element.15), channel_id=1, source_target_pairs={{0,1},{1,2},{2,3},{4,5},{5,6},{6,7},{8,9},{9,10},{10,11},{12,13},{... | collective-permute-start | bytes 7688 | tf_op jit(solution)/shard_map/ppermute | solution.py:38
  110.7 4.3 %collective-permute-done.11 = f32[5,8,16,1]{3,2,1,0:T(8,128)S(1)} collective-permute-done((f32[5,8,16,1]{3,2,1,0:T(8,128)S(1)}, f32[5,8,16,1]{3,2,1,0:T(8,128)S(1)}, u32[]{:S(2)}, u32[]{:S(2)}) %collective-permute-start.11) | collective-permute-done | bytes 2592 | tf_op jit(solution)/shard_map/ppermute | solution.py:39
  115.0 1.9 %collective-permute-done.10 = f32[5,8,16,1]{3,2,1,0:T(8,128)S(1)} collective-permute-done((f32[5,8,16,1]{3,2,1,0:T(8,128)S(1)}, f32[5,8,16,1]{3,2,1,0:T(8,128)S(1)}, u32[]{:S(2)}, u32[]{:S(2)}) %collective-permute-start.10) | collective-permute-done | bytes 2592 | tf_op jit(solution)/shard_map/ppermute | solution.py:38
  116.9 1.3 %fusion.4 = f32[5,8,16,128]{3,2,1,0:T(8,128)} fusion(f32[5,8,16,130]{3,2,1,0:T(8,128)S(1)} %fusion.1, f32[5,8,16,128]{3,2,1,0:T(8,128)S(1)} %copy-done, f32[5,10,18,1]{3,2,1,0:T(8,128)S(1)} %copy.17, f32[5,10,1,128]{3,2,1,0:T(1,128)S(1)} %collective-permute-done.2, f32[5,10,16,128]{3,2,1,0:T(8,128)S(1)} %constant_dynamic-update-slice_fusion, ...), kind=kLoop, calls=%fused_computation.10 | loop fusion | flops 1884160 | bytes 1538100 | tf_op jit(solution)/shard_map/add | solution.py:313
  (50 shorter events, 9.8 us)
Async XLA Ops:
  1.4 9.8 %collective-permute-start.1 = (f32[5,1,16,128]{3,2,1,0:T(8,128)S(1)}, f32[5,1,16,128]{3,2,1,0:T(8,128)S(1)}, u32[]{:S(2)}, u32[]{:S(2)}) collective-permute-start(f32[5,1,16,128]{3,2,1,0:T(8,128)S(1)} %get-tuple-element.24), channel_id=1, source_target_pairs={{0,32},{32,64},{64,96},{96,128},{128,160},{160,192},{192,224},{1,3... | collective-permute-start | bytes 122888 | tf_op jit(solution)/shard_map/ppermute | solution.py:24
  9.3 11.9 %collective-permute-start = (f32[5,1,16,128]{3,2,1,0:T(8,128)S(1)}, f32[5,1,16,128]{3,2,1,0:T(8,128)S(1)}, u32[]{:S(2)}, u32[]{:S(2)}) collective-permute-start(f32[5,1,16,128]{3,2,1,0:T(8,128)S(1)} %get-tuple-element.23), channel_id=1, source_target_pairs={{32,0},{64,32},{96,64},{128,96},{160,128},{192,160},{224,192},{33,... | collective-permute-start | bytes 122888 | tf_op jit(solution)/shard_map/ppermute | solution.py:27
  21.2 5.2 %copy-start.2 = (f32[5,1,16,128]{3,2,1,0:T(8,128)}, f32[5,1,16,128]{3,2,1,0:T(8,128)S(1)}, u32[]{:S(2)}) copy-start(f32[5,1,16,128]{3,2,1,0:T(8,128)S(1)} %collective-permute-done) | copy-start | bytes 122884
  21.3 5.1 %collective-permute-start.2 = (f32[5,10,1,128]{3,2,1,0:T(1,128)S(1)}, f32[5,10,1,128]{3,2,1,0:T(1,128)S(1)}, u32[]{:S(2)}, u32[]{:S(2)}) collective-permute-start(f32[5,10,1,128]{3,2,1,0:T(1,128)S(1)} %get-tuple-element.22), channel_id=1, source_target_pairs={{4,0},{8,4},{12,8},{16,12},{20,16},{24,20},{28,24},{5,1},{9,5},{13... | collective-permute-start | bytes 76808 | tf_op jit(solution)/shard_map/ppermute | solution.py:27
  23.2 5.2 %collective-permute-start.3 = (f32[5,10,1,128]{3,2,1,0:T(1,128)S(1)}, f32[5,10,1,128]{3,2,1,0:T(1,128)S(1)}, u32[]{:S(2)}, u32[]{:S(2)}) collective-permute-start(f32[5,10,1,128]{3,2,1,0:T(1,128)S(1)} %get-tuple-element.21), channel_id=1, source_target_pairs={{0,4},{4,8},{8,12},{12,16},{16,20},{20,24},{24,28},{1,5},{5,9},{9,... | collective-permute-start | bytes 76808 | tf_op jit(solution)/shard_map/ppermute | solution.py:24
  29.1 7.5 %collective-permute-start.4 = (f32[5,10,18,1]{2,3,1,0:T(1,128)S(1)}, f32[5,10,18,1]{2,3,1,0:T(1,128)S(1)}, u32[]{:S(2)}, u32[]{:S(2)}) collective-permute-start(f32[5,10,18,1]{2,3,1,0:T(1,128)S(1)} %copy.14), channel_id=1, source_target_pairs={{1,0},{2,1},{3,2},{5,4},{6,5},{7,6},{9,8},{10,9},{11,10},{13,12},{... | collective-permute-start | bytes 10808 | tf_op jit(solution)/shard_map/ppermute | solution.py:27
  32.4 5.7 %collective-permute-start.5 = (f32[5,10,18,1]{2,3,1,0:T(1,128)S(1)}, f32[5,10,18,1]{2,3,1,0:T(1,128)S(1)}, u32[]{:S(2)}, u32[]{:S(2)}) collective-permute-start(f32[5,10,18,1]{2,3,1,0:T(1,128)S(1)} %copy.16), channel_id=1, source_target_pairs={{0,1},{1,2},{2,3},{4,5},{5,6},{6,7},{8,9},{9,10},{10,11},{12,13},{... | collective-permute-start | bytes 10808 | tf_op jit(solution)/shard_map/ppermute | solution.py:24
  61.7 13.9 %copy-start.1 = (f32[5,108,128]{2,1,0:T(8,128)S(1)}, f32[5,108,128]{2,1,0:T(8,128)}, u32[]{:S(2)}) copy-start(f32[5,108,128]{2,1,0:T(8,128)} %get-tuple-element.8) | copy-start | bytes 829444
  63.8 17.9 %collective-permute-start.7 = (f32[5,1,18,130]{3,2,1,0:T(8,128)}, f32[5,1,18,130]{3,2,1,0:T(8,128)}, u32[]{:S(2)}, u32[]{:S(2)}) collective-permute-start(f32[5,1,18,130]{3,2,1,0:T(8,128)} %get-tuple-element.10), channel_id=1, source_target_pairs={{32,0},{64,32},{96,64},{128,96},{160,128},{192,160},{224,192},{33,... | collective-permute-start | bytes 140408 | tf_op jit(solution)/shard_map/ppermute | solution.py:39
  65.7 16.2 %collective-permute-start.6 = (f32[5,1,18,130]{3,2,1,0:T(8,128)}, f32[5,1,18,130]{3,2,1,0:T(8,128)}, u32[]{:S(2)}, u32[]{:S(2)}) collective-permute-start(f32[5,1,18,130]{3,2,1,0:T(8,128)} %get-tuple-element.9), channel_id=1, source_target_pairs={{0,32},{32,64},{64,96},{96,128},{128,160},{160,192},{192,224},{1,3... | collective-permute-start | bytes 140408 | tf_op jit(solution)/shard_map/ppermute | solution.py:38
  75.8 11.6 %collective-permute-start.12 = (f32[5,1,3,3,4,128]{5,4,3,2,1,0:T(4,128)S(1)}, f32[5,1,3,3,4,128]{5,4,3,2,1,0:T(4,128)S(1)}, u32[]{:S(2)}, u32[]{:S(2)}) collective-permute-start(f32[5,1,3,3,4,128]{5,4,3,2,1,0:T(4,128)S(1)} %get-tuple-element.26), channel_id=1, source_target_pairs={{0,32},{32,64},{64,96},{96,128},{128,160},{160,192},{192,224},{1,3... | collective-permute-start | bytes 276488 | tf_op jit(solution)/shard_map/ppermute | solution.py:24
  77.7 12.5 %collective-permute-start.13 = (f32[5,1,3,3,4,128]{5,4,3,2,1,0:T(4,128)S(1)}, f32[5,1,3,3,4,128]{5,4,3,2,1,0:T(4,128)S(1)}, u32[]{:S(2)}, u32[]{:S(2)}) collective-permute-start(f32[5,1,3,3,4,128]{5,4,3,2,1,0:T(4,128)S(1)} %get-tuple-element.25), channel_id=1, source_target_pairs={{32,0},{64,32},{96,64},{128,96},{160,128},{192,160},{224,192},{33,... | collective-permute-start | bytes 276488 | tf_op jit(solution)/shard_map/ppermute | solution.py:27
  83.0 11.6 %collective-permute-start.9 = (f32[5,8,1,130]{3,2,1,0:T(1,128)S(1)}, f32[5,8,1,130]{3,2,1,0:T(1,128)S(1)}, u32[]{:S(2)}, u32[]{:S(2)}) collective-permute-start(f32[5,8,1,130]{3,2,1,0:T(1,128)S(1)} %get-tuple-element.12), channel_id=1, source_target_pairs={{4,0},{8,4},{12,8},{16,12},{20,16},{24,20},{28,24},{5,1},{9,5},{13... | collective-permute-start | bytes 62408 | tf_op jit(solution)/shard_map/ppermute | solution.py:39
  84.9 9.7 %collective-permute-start.8 = (f32[5,8,1,130]{3,2,1,0:T(1,128)S(1)}, f32[5,8,1,130]{3,2,1,0:T(1,128)S(1)}, u32[]{:S(2)}, u32[]{:S(2)}) collective-permute-start(f32[5,8,1,130]{3,2,1,0:T(1,128)S(1)} %get-tuple-element.11), channel_id=1, source_target_pairs={{0,4},{4,8},{8,12},{12,16},{16,20},{20,24},{24,28},{1,5},{5,9},{9,... | collective-permute-start | bytes 62408 | tf_op jit(solution)/shard_map/ppermute | solution.py:38
  90.2 4.6 %collective-permute-start.15 = (f32[5,5,1,3,4,128]{5,4,3,2,1,0:T(4,128)S(1)}, f32[5,5,1,3,4,128]{5,4,3,2,1,0:T(4,128)S(1)}, u32[]{:S(2)}, u32[]{:S(2)}) collective-permute-start(f32[5,5,1,3,4,128]{5,4,3,2,1,0:T(4,128)S(1)} %get-tuple-element.20), channel_id=1, source_target_pairs={{4,0},{8,4},{12,8},{16,12},{20,16},{24,20},{28,24},{5,1},{9,5},{13... | collective-permute-start | bytes 460808 | tf_op jit(solution)/shard_map/ppermute | solution.py:27
  92.2 6.5 %collective-permute-start.14 = (f32[5,5,1,3,4,128]{5,4,3,2,1,0:T(4,128)S(1)}, f32[5,5,1,3,4,128]{5,4,3,2,1,0:T(4,128)S(1)}, u32[]{:S(2)}, u32[]{:S(2)}) collective-permute-start(f32[5,5,1,3,4,128]{5,4,3,2,1,0:T(4,128)S(1)} %get-tuple-element.19), channel_id=1, source_target_pairs={{0,4},{4,8},{8,12},{12,16},{16,20},{20,24},{24,28},{1,5},{5,9},{9,... | collective-permute-start | bytes 460808 | tf_op jit(solution)/shard_map/ppermute | solution.py:24
  94.7 22.2 %copy-start = (f32[5,8,16,128]{3,2,1,0:T(8,128)S(1)}, f32[5,8,16,128]{3,2,1,0:T(8,128)}, u32[]{:S(2)}) copy-start(f32[5,8,16,128]{3,2,1,0:T(8,128)} %param.7) | copy-start | bytes 983044
  94.8 22.1 %copy-start.3 = (f32[5,1,16,128]{3,2,1,0:T(8,128)S(1)}, f32[5,1,16,128]{3,2,1,0:T(8,128)}, u32[]{:S(2)}) copy-start(f32[5,1,16,128]{3,2,1,0:T(8,128)} %copy-done.2) | copy-start | bytes 122884
  94.8 22.1 %copy-start.4 = (f32[5]{0:T(128)S(1)}, f32[5]{0:T(128)}, u32[]{:S(2)}) copy-start(f32[5]{0:T(128)} %constant.23.clone) | copy-start | bytes 64
  98.8 19.4 %collective-permute-start.17 = (f32[5,5,5,1,4,128]{5,4,3,2,1,0:T(4,128)S(1)}, f32[5,5,5,1,4,128]{5,4,3,2,1,0:T(4,128)S(1)}, u32[]{:S(2)}, u32[]{:S(2)}) collective-permute-start(f32[5,5,5,1,4,128]{5,4,3,2,1,0:T(4,128)S(1)} %get-tuple-element.14), channel_id=1, source_target_pairs={{1,0},{2,1},{3,2},{5,4},{6,5},{7,6},{9,8},{10,9},{11,10},{13,12},{... | collective-permute-start | bytes 768008 | tf_op jit(solution)/shard_map/ppermute | solution.py:27
  100.7 17.5 %collective-permute-start.16 = (f32[5,5,5,1,4,128]{5,4,3,2,1,0:T(4,128)S(1)}, f32[5,5,5,1,4,128]{5,4,3,2,1,0:T(4,128)S(1)}, u32[]{:S(2)}, u32[]{:S(2)}) collective-permute-start(f32[5,5,5,1,4,128]{5,4,3,2,1,0:T(4,128)S(1)} %get-tuple-element.13), channel_id=1, source_target_pairs={{0,1},{1,2},{2,3},{4,5},{5,6},{6,7},{8,9},{9,10},{10,11},{12,13},{... | collective-permute-start | bytes 768008 | tf_op jit(solution)/shard_map/ppermute | solution.py:24
  104.8 10.2 %collective-permute-start.11 = (f32[5,8,16,1]{3,2,1,0:T(8,128)S(1)}, f32[5,8,16,1]{3,2,1,0:T(8,128)S(1)}, u32[]{:S(2)}, u32[]{:S(2)}) collective-permute-start(f32[5,8,16,1]{3,2,1,0:T(8,128)S(1)} %get-tuple-element.16), channel_id=1, source_target_pairs={{1,0},{2,1},{3,2},{5,4},{6,5},{7,6},{9,8},{10,9},{11,10},{13,12},{... | collective-permute-start | bytes 7688 | tf_op jit(solution)/shard_map/ppermute | solution.py:39
  106.8 10.1 %collective-permute-start.10 = (f32[5,8,16,1]{3,2,1,0:T(8,128)S(1)}, f32[5,8,16,1]{3,2,1,0:T(8,128)S(1)}, u32[]{:S(2)}, u32[]{:S(2)}) collective-permute-start(f32[5,8,16,1]{3,2,1,0:T(8,128)S(1)} %get-tuple-element.15), channel_id=1, source_target_pairs={{0,1},{1,2},{2,3},{4,5},{5,6},{6,7},{8,9},{9,10},{10,11},{12,13},{... | collective-permute-start | bytes 7688 | tf_op jit(solution)/shard_map/ppermute | solution.py:38

commit v14 on v13

--- a/solution.py
+++ b/solution.py
@@ -113,7 +113,7 @@
     return out
 
 
-GROUP = 8
+GROUP = 16
 
 
 def coupling_kernel(

time: 122 us -> 121 us (level)
  no operation moved by 1% of the time
where the time goes in v14:
time: 121 us; the launch traced here: 119 us
  starting transfers between devices  57.9 us (48%)
  waiting for transfers between devices  25.1 us (21%)
  Pallas kernels  15.8 us (13%)
  local copies, waits for them, and re-layouts  13.1 us (11%)
  other arithmetic  5.21 us (4%)
  between operations  1.66 us (1%)
    ppermute x6, starting transfers between devices, with_halo(): lax.ppermute(lax.slice_in_dim(block, block.shape[dim] - width, None, axis...  21.4 us
    ppermute x3, starting transfers between devices, fold_ghosts(): lax.ppermute(lax.slice_in_dim(block, span - 1, span, axis=dim), axis, for...  16.3 us
    pallas_call x1, Pallas kernels, local(): pl.pallas_call(functools.partial(coupling_kernel, span_y=span_y, span_z=s...  15.8 us
    ppermute x6, starting transfers between devices, with_halo(): lax.ppermute(lax.slice_in_dim(block, 0, width, axis=dim), axis, backward)  14.5 us
    ppermute x6, waiting for transfers between devices, with_halo(): lax.ppermute(lax.slice_in_dim(block, 0, width, axis=dim), axis, backward)  11.8 us
    ppermute x6, waiting for transfers between devices, with_halo(): lax.ppermute(lax.slice_in_dim(block, block.shape[dim] - width, None, axis...  6.85 us
    ppermute x3, starting transfers between devices, fold_ghosts(): lax.ppermute(lax.slice_in_dim(block, 0, 1, axis=dim), axis, backward)  5.76 us
    unnamed x16, local copies, waits for them, and re-layouts  5.08 us
  transfers between devices with their start and end apart: 18, of which 9 were waited for; matrix products, arithmetic and copies ran while one was open for 5% of the time, Pallas kernels for 0%

profile of v14, /device:TPU:58, one launch (start us, length us, event | category | flops | bytes accessed | tf_op | source)
XLA Modules:
  0.0 118.8 jit_solution(15254283626445996240)
XLA Ops:
  1.4 7.8 %collective-permute-start.1 = (f32[5,1,16,128]{3,2,1,0:T(8,128)S(1)}, f32[5,1,16,128]{3,2,1,0:T(8,128)S(1)}, u32[]{:S(2)}, u32[]{:S(2)}) collective-permute-start(f32[5,1,16,128]{3,2,1,0:T(8,128)S(1)} %get-tuple-element.24), channel_id=1, source_target_pairs={{0,32},{32,64},{64,96},{96,128},{128,160},{160,192},{192,224},{1,3... | collective-permute-start | bytes 122888 | tf_op jit(solution)/shard_map/ppermute | solution.py:24
  9.3 1.9 %collective-permute-start = (f32[5,1,16,128]{3,2,1,0:T(8,128)S(1)}, f32[5,1,16,128]{3,2,1,0:T(8,128)S(1)}, u32[]{:S(2)}, u32[]{:S(2)}) collective-permute-start(f32[5,1,16,128]{3,2,1,0:T(8,128)S(1)} %get-tuple-element.23), channel_id=1, source_target_pairs={{32,0},{64,32},{96,64},{128,96},{160,128},{192,160},{224,192},{33,... | collective-permute-start | bytes 122888 | tf_op jit(solution)/shard_map/ppermute | solution.py:27
  12.2 9.0 %collective-permute-done = f32[5,1,16,128]{3,2,1,0:T(8,128)S(1)} collective-permute-done((f32[5,1,16,128]{3,2,1,0:T(8,128)S(1)}, f32[5,1,16,128]{3,2,1,0:T(8,128)S(1)}, u32[]{:S(2)}, u32[]{:S(2)}) %collective-permute-start) | collective-permute-done | bytes 40992 | tf_op jit(solution)/shard_map/ppermute | solution.py:27
  21.3 1.9 %collective-permute-start.2 = (f32[5,10,1,128]{3,2,1,0:T(1,128)S(1)}, f32[5,10,1,128]{3,2,1,0:T(1,128)S(1)}, u32[]{:S(2)}, u32[]{:S(2)}) collective-permute-start(f32[5,10,1,128]{3,2,1,0:T(1,128)S(1)} %get-tuple-element.22), channel_id=1, source_target_pairs={{4,0},{8,4},{12,8},{16,12},{20,16},{24,20},{28,24},{5,1},{9,5},{13... | collective-permute-start | bytes 76808 | tf_op jit(solution)/shard_map/ppermute | solution.py:27
  23.2 2.4 %collective-permute-start.3 = (f32[5,10,1,128]{3,2,1,0:T(1,128)S(1)}, f32[5,10,1,128]{3,2,1,0:T(1,128)S(1)}, u32[]{:S(2)}, u32[]{:S(2)}) collective-permute-start(f32[5,10,1,128]{3,2,1,0:T(1,128)S(1)} %get-tuple-element.21), channel_id=1, source_target_pairs={{0,4},{4,8},{8,12},{12,16},{16,20},{20,24},{24,28},{1,5},{5,9},{9,... | collective-permute-start | bytes 76808 | tf_op jit(solution)/shard_map/ppermute | solution.py:24
  26.4 1.9 %collective-permute-done.3 = f32[5,10,1,128]{3,2,1,0:T(1,128)S(1)} collective-permute-done((f32[5,10,1,128]{3,2,1,0:T(1,128)S(1)}, f32[5,10,1,128]{3,2,1,0:T(1,128)S(1)}, u32[]{:S(2)}, u32[]{:S(2)}) %collective-permute-start.3) | collective-permute-done | bytes 25632 | tf_op jit(solution)/shard_map/ppermute | solution.py:24
  29.1 2.9 %collective-permute-start.4 = (f32[5,10,18,1]{2,3,1,0:T(1,128)S(1)}, f32[5,10,18,1]{2,3,1,0:T(1,128)S(1)}, u32[]{:S(2)}, u32[]{:S(2)}) collective-permute-start(f32[5,10,18,1]{2,3,1,0:T(1,128)S(1)} %copy.14), channel_id=1, source_target_pairs={{1,0},{2,1},{3,2},{5,4},{6,5},{7,6},{9,8},{10,9},{11,10},{13,12},{... | collective-permute-start | bytes 10808 | tf_op jit(solution)/shard_map/ppermute | solution.py:27
  32.4 2.9 %collective-permute-start.5 = (f32[5,10,18,1]{2,3,1,0:T(1,128)S(1)}, f32[5,10,18,1]{2,3,1,0:T(1,128)S(1)}, u32[]{:S(2)}, u32[]{:S(2)}) collective-permute-start(f32[5,10,18,1]{2,3,1,0:T(1,128)S(1)} %copy.16), channel_id=1, source_target_pairs={{0,1},{1,2},{2,3},{4,5},{5,6},{6,7},{8,9},{9,10},{10,11},{12,13},{... | collective-permute-start | bytes 10808 | tf_op jit(solution)/shard_map/ppermute | solution.py:24
  37.0 1.1 collective-permute-done.5
  39.3 1.1 reshape.25
  40.4 1.6 %copy.23 = f32[5,130,180]{2,1,0:T(8,128)S(1)} copy(f32[5,130,180]{1,2,0:T(8,128)} %reshape.25) | data formatting | bytes 936000
  42.8 15.8 %shard_map.94 = (f32[5,32,128]{2,1,0:T(8,128)}, f32[5,108,128]{2,1,0:T(8,128)}, f32[680,256]{1,0:T(8,128)}) custom-call(s32[1]{0:T(128)S(6)} %copy.28.live_ref, s32[32]{0:T(128)} %dest_ref.1, f32[680,256]{1,0:T(8,128)} %bitcast.16, f32[5,32,128]{2,1,0:T(8,128)} %bitcast.20, s32[32,128]{1,0:T(8,128)} %cell_ref.1, f32[3,32,128]{2,1,0:T(8,128)} %bitcast.21, ...), custom_call_target="tpu_custom_call" | custom-call | tf_op jit(solution)/shard_map/pallas_call | solution.py:285
  58.7 2.4 %copy.22 = f32[5,130,180]{1,2,0:T(8,128)} copy(f32[5,130,180]{2,1,0:T(8,128)} %bitcast.17) | data formatting | bytes 936000
  61.1 1.3 %reshape.28 = f32[5,130,10,18]{1,3,2,0:T(8,128)S(1)} reshape(f32[5,130,180]{1,2,0:T(8,128)} %copy.22) | data formatting | bytes 936000 | tf_op jit(solution)/shard_map/reshape | solution.py:310
  63.2 1.9 %collective-permute-start.7 = (f32[5,1,18,130]{3,2,1,0:T(8,128)}, f32[5,1,18,130]{3,2,1,0:T(8,128)}, u32[]{:S(2)}, u32[]{:S(2)}) collective-permute-start(f32[5,1,18,130]{3,2,1,0:T(8,128)} %get-tuple-element.10), channel_id=1, source_target_pairs={{32,0},{64,32},{96,64},{128,96},{160,128},{192,160},{224,192},{33,... | collective-permute-start | bytes 140408 | tf_op jit(solution)/shard_map/ppermute | solution.py:39
  65.1 9.9 %collective-permute-start.6 = (f32[5,1,18,130]{3,2,1,0:T(8,128)}, f32[5,1,18,130]{3,2,1,0:T(8,128)}, u32[]{:S(2)}, u32[]{:S(2)}) collective-permute-start(f32[5,1,18,130]{3,2,1,0:T(8,128)} %get-tuple-element.9), channel_id=1, source_target_pairs={{0,32},{32,64},{64,96},{96,128},{128,160},{160,192},{192,224},{1,3... | collective-permute-start | bytes 140408 | tf_op jit(solution)/shard_map/ppermute | solution.py:38
  75.2 1.9 %collective-permute-start.12 = (f32[5,1,3,3,4,128]{5,4,3,2,1,0:T(4,128)S(1)}, f32[5,1,3,3,4,128]{5,4,3,2,1,0:T(4,128)S(1)}, u32[]{:S(2)}, u32[]{:S(2)}) collective-permute-start(f32[5,1,3,3,4,128]{5,4,3,2,1,0:T(4,128)S(1)} %get-tuple-element.26), channel_id=1, source_target_pairs={{0,32},{32,64},{64,96},{96,128},{128,160},{160,192},{192,224},{1,3... | collective-permute-start | bytes 276488 | tf_op jit(solution)/shard_map/ppermute | solution.py:24
  77.1 3.9 %collective-permute-start.13 = (f32[5,1,3,3,4,128]{5,4,3,2,1,0:T(4,128)S(1)}, f32[5,1,3,3,4,128]{5,4,3,2,1,0:T(4,128)S(1)}, u32[]{:S(2)}, u32[]{:S(2)}) collective-permute-start(f32[5,1,3,3,4,128]{5,4,3,2,1,0:T(4,128)S(1)} %get-tuple-element.25), channel_id=1, source_target_pairs={{32,0},{64,32},{96,64},{128,96},{160,128},{192,160},{224,192},{33,... | collective-permute-start | bytes 276488 | tf_op jit(solution)/shard_map/ppermute | solution.py:27
  81.3 1.0 fusion
  82.4 1.9 %collective-permute-start.9 = (f32[5,8,1,130]{3,2,1,0:T(1,128)S(1)}, f32[5,8,1,130]{3,2,1,0:T(1,128)S(1)}, u32[]{:S(2)}, u32[]{:S(2)}) collective-permute-start(f32[5,8,1,130]{3,2,1,0:T(1,128)S(1)} %get-tuple-element.12), channel_id=1, source_target_pairs={{4,0},{8,4},{12,8},{16,12},{20,16},{24,20},{28,24},{5,1},{9,5},{13... | collective-permute-start | bytes 62408 | tf_op jit(solution)/shard_map/ppermute | solution.py:39
  84.3 2.4 %collective-permute-start.8 = (f32[5,8,1,130]{3,2,1,0:T(1,128)S(1)}, f32[5,8,1,130]{3,2,1,0:T(1,128)S(1)}, u32[]{:S(2)}, u32[]{:S(2)}) collective-permute-start(f32[5,8,1,130]{3,2,1,0:T(1,128)S(1)} %get-tuple-element.11), channel_id=1, source_target_pairs={{0,4},{4,8},{8,12},{12,16},{16,20},{20,24},{24,28},{1,5},{5,9},{9,... | collective-permute-start | bytes 62408 | tf_op jit(solution)/shard_map/ppermute | solution.py:38
  86.8 2.8 %collective-permute-done.13 = f32[5,1,3,3,4,128]{5,4,3,2,1,0:T(4,128)S(1)} collective-permute-done((f32[5,1,3,3,4,128]{5,4,3,2,1,0:T(4,128)S(1)}, f32[5,1,3,3,4,128]{5,4,3,2,1,0:T(4,128)S(1)}, u32[]{:S(2)}, u32[]{:S(2)}) %collective-permute-start.13) | collective-permute-done | bytes 92192 | tf_op jit(solution)/shard_map/ppermute | solution.py:27
  89.6 1.9 %collective-permute-start.15 = (f32[5,5,1,3,4,128]{5,4,3,2,1,0:T(4,128)S(1)}, f32[5,5,1,3,4,128]{5,4,3,2,1,0:T(4,128)S(1)}, u32[]{:S(2)}, u32[]{:S(2)}) collective-permute-start(f32[5,5,1,3,4,128]{5,4,3,2,1,0:T(4,128)S(1)} %get-tuple-element.20), channel_id=1, source_target_pairs={{4,0},{8,4},{12,8},{16,12},{20,16},{24,20},{28,24},{5,1},{9,5},{13... | collective-permute-start | bytes 460808 | tf_op jit(solution)/shard_map/ppermute | solution.py:27
  91.6 2.4 %collective-permute-start.14 = (f32[5,5,1,3,4,128]{5,4,3,2,1,0:T(4,128)S(1)}, f32[5,5,1,3,4,128]{5,4,3,2,1,0:T(4,128)S(1)}, u32[]{:S(2)}, u32[]{:S(2)}) collective-permute-start(f32[5,5,1,3,4,128]{5,4,3,2,1,0:T(4,128)S(1)} %get-tuple-element.19), channel_id=1, source_target_pairs={{0,4},{4,8},{8,12},{12,16},{16,20},{20,24},{24,28},{1,5},{5,9},{9,... | collective-permute-start | bytes 460808 | tf_op jit(solution)/shard_map/ppermute | solution.py:24
  94.3 3.8 %collective-permute-done.14 = f32[5,5,1,3,4,128]{5,4,3,2,1,0:T(4,128)S(1)} collective-permute-done((f32[5,5,1,3,4,128]{5,4,3,2,1,0:T(4,128)S(1)}, f32[5,5,1,3,4,128]{5,4,3,2,1,0:T(4,128)S(1)}, u32[]{:S(2)}, u32[]{:S(2)}) %collective-permute-start.14) | collective-permute-done | bytes 153632 | tf_op jit(solution)/shard_map/ppermute | solution.py:24
  98.2 1.9 %collective-permute-start.17 = (f32[5,5,5,1,4,128]{5,4,3,2,1,0:T(4,128)S(1)}, f32[5,5,5,1,4,128]{5,4,3,2,1,0:T(4,128)S(1)}, u32[]{:S(2)}, u32[]{:S(2)}) collective-permute-start(f32[5,5,5,1,4,128]{5,4,3,2,1,0:T(4,128)S(1)} %get-tuple-element.14), channel_id=1, source_target_pairs={{1,0},{2,1},{3,2},{5,4},{6,5},{7,6},{9,8},{10,9},{11,10},{13,12},{... | collective-permute-start | bytes 768008 | tf_op jit(solution)/shard_map/ppermute | solution.py:27
  100.1 3.9 %collective-permute-start.16 = (f32[5,5,5,1,4,128]{5,4,3,2,1,0:T(4,128)S(1)}, f32[5,5,5,1,4,128]{5,4,3,2,1,0:T(4,128)S(1)}, u32[]{:S(2)}, u32[]{:S(2)}) collective-permute-start(f32[5,5,5,1,4,128]{5,4,3,2,1,0:T(4,128)S(1)} %get-tuple-element.13), channel_id=1, source_target_pairs={{0,1},{1,2},{2,3},{4,5},{5,6},{6,7},{8,9},{9,10},{10,11},{12,13},{... | collective-permute-start | bytes 768008 | tf_op jit(solution)/shard_map/ppermute | solution.py:24
  104.2 1.9 %collective-permute-start.11 = (f32[5,8,16,1]{3,2,1,0:T(8,128)S(1)}, f32[5,8,16,1]{3,2,1,0:T(8,128)S(1)}, u32[]{:S(2)}, u32[]{:S(2)}) collective-permute-start(f32[5,8,16,1]{3,2,1,0:T(8,128)S(1)} %get-tuple-element.16), channel_id=1, source_target_pairs={{1,0},{2,1},{3,2},{5,4},{6,5},{7,6},{9,8},{10,9},{11,10},{13,12},{... | collective-permute-start | bytes 7688 | tf_op jit(solution)/shard_map/ppermute | solution.py:39
  106.2 3.9 %collective-permute-start.10 = (f32[5,8,16,1]{3,2,1,0:T(8,128)S(1)}, f32[5,8,16,1]{3,2,1,0:T(8,128)S(1)}, u32[]{:S(2)}, u32[]{:S(2)}) collective-permute-start(f32[5,8,16,1]{3,2,1,0:T(8,128)S(1)} %get-tuple-element.15), channel_id=1, source_target_pairs={{0,1},{1,2},{2,3},{4,5},{5,6},{6,7},{8,9},{9,10},{10,11},{12,13},{... | collective-permute-start | bytes 7688 | tf_op jit(solution)/shard_map/ppermute | solution.py:38
  110.1 4.3 %collective-permute-done.11 = f32[5,8,16,1]{3,2,1,0:T(8,128)S(1)} collective-permute-done((f32[5,8,16,1]{3,2,1,0:T(8,128)S(1)}, f32[5,8,16,1]{3,2,1,0:T(8,128)S(1)}, u32[]{:S(2)}, u32[]{:S(2)}) %collective-permute-start.11) | collective-permute-done | bytes 2592 | tf_op jit(solution)/shard_map/ppermute | solution.py:39
  114.4 1.9 %collective-permute-done.10 = f32[5,8,16,1]{3,2,1,0:T(8,128)S(1)} collective-permute-done((f32[5,8,16,1]{3,2,1,0:T(8,128)S(1)}, f32[5,8,16,1]{3,2,1,0:T(8,128)S(1)}, u32[]{:S(2)}, u32[]{:S(2)}) %collective-permute-start.10) | collective-permute-done | bytes 2592 | tf_op jit(solution)/shard_map/ppermute | solution.py:38
  116.3 1.3 %fusion.4 = f32[5,8,16,128]{3,2,1,0:T(8,128)} fusion(f32[5,8,16,130]{3,2,1,0:T(8,128)S(1)} %fusion.1, f32[5,8,16,128]{3,2,1,0:T(8,128)S(1)} %copy-done, f32[5,10,18,1]{3,2,1,0:T(8,128)S(1)} %copy.17, f32[5,10,1,128]{3,2,1,0:T(1,128)S(1)} %collective-permute-done.2, f32[5,10,16,128]{3,2,1,0:T(8,128)S(1)} %constant_dynamic-update-slice_fusion, ...), kind=kLoop, calls=%fused_computation.10 | loop fusion | flops 1884160 | bytes 1538100 | tf_op jit(solution)/shard_map/add | solution.py:313
  (50 shorter events, 9.8 us)
Async XLA Ops:
  1.4 9.8 %collective-permute-start.1 = (f32[5,1,16,128]{3,2,1,0:T(8,128)S(1)}, f32[5,1,16,128]{3,2,1,0:T(8,128)S(1)}, u32[]{:S(2)}, u32[]{:S(2)}) collective-permute-start(f32[5,1,16,128]{3,2,1,0:T(8,128)S(1)} %get-tuple-element.24), channel_id=1, source_target_pairs={{0,32},{32,64},{64,96},{96,128},{128,160},{160,192},{192,224},{1,3... | collective-permute-start | bytes 122888 | tf_op jit(solution)/shard_map/ppermute | solution.py:24
  9.3 11.9 %collective-permute-start = (f32[5,1,16,128]{3,2,1,0:T(8,128)S(1)}, f32[5,1,16,128]{3,2,1,0:T(8,128)S(1)}, u32[]{:S(2)}, u32[]{:S(2)}) collective-permute-start(f32[5,1,16,128]{3,2,1,0:T(8,128)S(1)} %get-tuple-element.23), channel_id=1, source_target_pairs={{32,0},{64,32},{96,64},{128,96},{160,128},{192,160},{224,192},{33,... | collective-permute-start | bytes 122888 | tf_op jit(solution)/shard_map/ppermute | solution.py:27
  21.2 5.2 %copy-start.2 = (f32[5,1,16,128]{3,2,1,0:T(8,128)}, f32[5,1,16,128]{3,2,1,0:T(8,128)S(1)}, u32[]{:S(2)}) copy-start(f32[5,1,16,128]{3,2,1,0:T(8,128)S(1)} %collective-permute-done) | copy-start | bytes 122884
  21.3 5.1 %collective-permute-start.2 = (f32[5,10,1,128]{3,2,1,0:T(1,128)S(1)}, f32[5,10,1,128]{3,2,1,0:T(1,128)S(1)}, u32[]{:S(2)}, u32[]{:S(2)}) collective-permute-start(f32[5,10,1,128]{3,2,1,0:T(1,128)S(1)} %get-tuple-element.22), channel_id=1, source_target_pairs={{4,0},{8,4},{12,8},{16,12},{20,16},{24,20},{28,24},{5,1},{9,5},{13... | collective-permute-start | bytes 76808 | tf_op jit(solution)/shard_map/ppermute | solution.py:27
  23.2 5.2 %collective-permute-start.3 = (f32[5,10,1,128]{3,2,1,0:T(1,128)S(1)}, f32[5,10,1,128]{3,2,1,0:T(1,128)S(1)}, u32[]{:S(2)}, u32[]{:S(2)}) collective-permute-start(f32[5,10,1,128]{3,2,1,0:T(1,128)S(1)} %get-tuple-element.21), channel_id=1, source_target_pairs={{0,4},{4,8},{8,12},{12,16},{16,20},{20,24},{24,28},{1,5},{5,9},{9,... | collective-permute-start | bytes 76808 | tf_op jit(solution)/shard_map/ppermute | solution.py:24
  29.1 7.5 %collective-permute-start.4 = (f32[5,10,18,1]{2,3,1,0:T(1,128)S(1)}, f32[5,10,18,1]{2,3,1,0:T(1,128)S(1)}, u32[]{:S(2)}, u32[]{:S(2)}) collective-permute-start(f32[5,10,18,1]{2,3,1,0:T(1,128)S(1)} %copy.14), channel_id=1, source_target_pairs={{1,0},{2,1},{3,2},{5,4},{6,5},{7,6},{9,8},{10,9},{11,10},{13,12},{... | collective-permute-start | bytes 10808 | tf_op jit(solution)/shard_map/ppermute | solution.py:27
  32.4 5.7 %collective-permute-start.5 = (f32[5,10,18,1]{2,3,1,0:T(1,128)S(1)}, f32[5,10,18,1]{2,3,1,0:T(1,128)S(1)}, u32[]{:S(2)}, u32[]{:S(2)}) collective-permute-start(f32[5,10,18,1]{2,3,1,0:T(1,128)S(1)} %copy.16), channel_id=1, source_target_pairs={{0,1},{1,2},{2,3},{4,5},{5,6},{6,7},{8,9},{9,10},{10,11},{12,13},{... | collective-permute-start | bytes 10808 | tf_op jit(solution)/shard_map/ppermute | solution.py:24
  61.1 13.9 %copy-start.1 = (f32[5,108,128]{2,1,0:T(8,128)S(1)}, f32[5,108,128]{2,1,0:T(8,128)}, u32[]{:S(2)}) copy-start(f32[5,108,128]{2,1,0:T(8,128)} %get-tuple-element.8) | copy-start | bytes 829444
  63.2 17.9 %collective-permute-start.7 = (f32[5,1,18,130]{3,2,1,0:T(8,128)}, f32[5,1,18,130]{3,2,1,0:T(8,128)}, u32[]{:S(2)}, u32[]{:S(2)}) collective-permute-start(f32[5,1,18,130]{3,2,1,0:T(8,128)} %get-tuple-element.10), channel_id=1, source_target_pairs={{32,0},{64,32},{96,64},{128,96},{160,128},{192,160},{224,192},{33,... | collective-permute-start | bytes 140408 | tf_op jit(solution)/shard_map/ppermute | solution.py:39
  65.1 16.2 %collective-permute-start.6 = (f32[5,1,18,130]{3,2,1,0:T(8,128)}, f32[5,1,18,130]{3,2,1,0:T(8,128)}, u32[]{:S(2)}, u32[]{:S(2)}) collective-permute-start(f32[5,1,18,130]{3,2,1,0:T(8,128)} %get-tuple-element.9), channel_id=1, source_target_pairs={{0,32},{32,64},{64,96},{96,128},{128,160},{160,192},{192,224},{1,3... | collective-permute-start | bytes 140408 | tf_op jit(solution)/shard_map/ppermute | solution.py:38
  75.2 11.6 %collective-permute-start.12 = (f32[5,1,3,3,4,128]{5,4,3,2,1,0:T(4,128)S(1)}, f32[5,1,3,3,4,128]{5,4,3,2,1,0:T(4,128)S(1)}, u32[]{:S(2)}, u32[]{:S(2)}) collective-permute-start(f32[5,1,3,3,4,128]{5,4,3,2,1,0:T(4,128)S(1)} %get-tuple-element.26), channel_id=1, source_target_pairs={{0,32},{32,64},{64,96},{96,128},{128,160},{160,192},{192,224},{1,3... | collective-permute-start | bytes 276488 | tf_op jit(solution)/shard_map/ppermute | solution.py:24
  77.1 12.5 %collective-permute-start.13 = (f32[5,1,3,3,4,128]{5,4,3,2,1,0:T(4,128)S(1)}, f32[5,1,3,3,4,128]{5,4,3,2,1,0:T(4,128)S(1)}, u32[]{:S(2)}, u32[]{:S(2)}) collective-permute-start(f32[5,1,3,3,4,128]{5,4,3,2,1,0:T(4,128)S(1)} %get-tuple-element.25), channel_id=1, source_target_pairs={{32,0},{64,32},{96,64},{128,96},{160,128},{192,160},{224,192},{33,... | collective-permute-start | bytes 276488 | tf_op jit(solution)/shard_map/ppermute | solution.py:27
  82.4 11.6 %collective-permute-start.9 = (f32[5,8,1,130]{3,2,1,0:T(1,128)S(1)}, f32[5,8,1,130]{3,2,1,0:T(1,128)S(1)}, u32[]{:S(2)}, u32[]{:S(2)}) collective-permute-start(f32[5,8,1,130]{3,2,1,0:T(1,128)S(1)} %get-tuple-element.12), channel_id=1, source_target_pairs={{4,0},{8,4},{12,8},{16,12},{20,16},{24,20},{28,24},{5,1},{9,5},{13... | collective-permute-start | bytes 62408 | tf_op jit(solution)/shard_map/ppermute | solution.py:39
  84.3 9.7 %collective-permute-start.8 = (f32[5,8,1,130]{3,2,1,0:T(1,128)S(1)}, f32[5,8,1,130]{3,2,1,0:T(1,128)S(1)}, u32[]{:S(2)}, u32[]{:S(2)}) collective-permute-start(f32[5,8,1,130]{3,2,1,0:T(1,128)S(1)} %get-tuple-element.11), channel_id=1, source_target_pairs={{0,4},{4,8},{8,12},{12,16},{16,20},{20,24},{24,28},{1,5},{5,9},{9,... | collective-permute-start | bytes 62408 | tf_op jit(solution)/shard_map/ppermute | solution.py:38
  89.6 4.6 %collective-permute-start.15 = (f32[5,5,1,3,4,128]{5,4,3,2,1,0:T(4,128)S(1)}, f32[5,5,1,3,4,128]{5,4,3,2,1,0:T(4,128)S(1)}, u32[]{:S(2)}, u32[]{:S(2)}) collective-permute-start(f32[5,5,1,3,4,128]{5,4,3,2,1,0:T(4,128)S(1)} %get-tuple-element.20), channel_id=1, source_target_pairs={{4,0},{8,4},{12,8},{16,12},{20,16},{24,20},{28,24},{5,1},{9,5},{13... | collective-permute-start | bytes 460808 | tf_op jit(solution)/shard_map/ppermute | solution.py:27
  91.6 6.5 %collective-permute-start.14 = (f32[5,5,1,3,4,128]{5,4,3,2,1,0:T(4,128)S(1)}, f32[5,5,1,3,4,128]{5,4,3,2,1,0:T(4,128)S(1)}, u32[]{:S(2)}, u32[]{:S(2)}) collective-permute-start(f32[5,5,1,3,4,128]{5,4,3,2,1,0:T(4,128)S(1)} %get-tuple-element.19), channel_id=1, source_target_pairs={{0,4},{4,8},{8,12},{12,16},{16,20},{20,24},{24,28},{1,5},{5,9},{9,... | collective-permute-start | bytes 460808 | tf_op jit(solution)/shard_map/ppermute | solution.py:24
  94.1 22.2 %copy-start = (f32[5,8,16,128]{3,2,1,0:T(8,128)S(1)}, f32[5,8,16,128]{3,2,1,0:T(8,128)}, u32[]{:S(2)}) copy-start(f32[5,8,16,128]{3,2,1,0:T(8,128)} %param.7) | copy-start | bytes 983044
  94.1 22.1 %copy-start.3 = (f32[5,1,16,128]{3,2,1,0:T(8,128)S(1)}, f32[5,1,16,128]{3,2,1,0:T(8,128)}, u32[]{:S(2)}) copy-start(f32[5,1,16,128]{3,2,1,0:T(8,128)} %copy-done.2) | copy-start | bytes 122884
  94.2 22.1 %copy-start.4 = (f32[5]{0:T(128)S(1)}, f32[5]{0:T(128)}, u32[]{:S(2)}) copy-start(f32[5]{0:T(128)} %constant.23.clone) | copy-start | bytes 64
  98.2 19.4 %collective-permute-start.17 = (f32[5,5,5,1,4,128]{5,4,3,2,1,0:T(4,128)S(1)}, f32[5,5,5,1,4,128]{5,4,3,2,1,0:T(4,128)S(1)}, u32[]{:S(2)}, u32[]{:S(2)}) collective-permute-start(f32[5,5,5,1,4,128]{5,4,3,2,1,0:T(4,128)S(1)} %get-tuple-element.14), channel_id=1, source_target_pairs={{1,0},{2,1},{3,2},{5,4},{6,5},{7,6},{9,8},{10,9},{11,10},{13,12},{... | collective-permute-start | bytes 768008 | tf_op jit(solution)/shard_map/ppermute | solution.py:27
  100.1 17.5 %collective-permute-start.16 = (f32[5,5,5,1,4,128]{5,4,3,2,1,0:T(4,128)S(1)}, f32[5,5,5,1,4,128]{5,4,3,2,1,0:T(4,128)S(1)}, u32[]{:S(2)}, u32[]{:S(2)}) collective-permute-start(f32[5,5,5,1,4,128]{5,4,3,2,1,0:T(4,128)S(1)} %get-tuple-element.13), channel_id=1, source_target_pairs={{0,1},{1,2},{2,3},{4,5},{5,6},{6,7},{8,9},{9,10},{10,11},{12,13},{... | collective-permute-start | bytes 768008 | tf_op jit(solution)/shard_map/ppermute | solution.py:24
  104.2 10.2 %collective-permute-start.11 = (f32[5,8,16,1]{3,2,1,0:T(8,128)S(1)}, f32[5,8,16,1]{3,2,1,0:T(8,128)S(1)}, u32[]{:S(2)}, u32[]{:S(2)}) collective-permute-start(f32[5,8,16,1]{3,2,1,0:T(8,128)S(1)} %get-tuple-element.16), channel_id=1, source_target_pairs={{1,0},{2,1},{3,2},{5,4},{6,5},{7,6},{9,8},{10,9},{11,10},{13,12},{... | collective-permute-start | bytes 7688 | tf_op jit(solution)/shard_map/ppermute | solution.py:39
  106.2 10.1 %collective-permute-start.10 = (f32[5,8,16,1]{3,2,1,0:T(8,128)S(1)}, f32[5,8,16,1]{3,2,1,0:T(8,128)S(1)}, u32[]{:S(2)}, u32[]{:S(2)}) collective-permute-start(f32[5,8,16,1]{3,2,1,0:T(8,128)S(1)} %get-tuple-element.15), channel_id=1, source_target_pairs={{0,1},{1,2},{2,3},{4,5},{5,6},{6,7},{8,9},{9,10},{10,11},{12,13},{... | collective-permute-start | bytes 7688 | tf_op jit(solution)/shard_map/ppermute | solution.py:38

commit v15 on v14

--- a/solution.py
+++ b/solution.py
@@ -113,7 +113,7 @@
     return out
 
 
-GROUP = 16
+GROUP = 32
 
 
 def coupling_kernel(

time: 121 us -> 120 us (level)
  transfers between devices with their start and end apart: 18 -> 18, of which waited for: 9 -> 8; matrix products, arithmetic and copies ran while one was open for 5% -> 5% of each run, Pallas kernels for 0% -> 0%
where the time goes in v15:
time: 120 us; the launch traced here: 118 us
  starting transfers between devices  58.1 us (48%)
  waiting for transfers between devices  25.1 us (21%)
  Pallas kernels  15 us (12%)
  local copies, waits for them, and re-layouts  13.1 us (11%)
  other arithmetic  5.21 us (4%)
  between operations  1.66 us (1%)
    ppermute x6, starting transfers between devices, with_halo(): lax.ppermute(lax.slice_in_dim(block, block.shape[dim] - width, None, axis...  21.4 us
    ppermute x3, starting transfers between devices, fold_ghosts(): lax.ppermute(lax.slice_in_dim(block, span - 1, span, axis=dim), axis, for...  16.4 us
    pallas_call x1, Pallas kernels, local(): pl.pallas_call(functools.partial(coupling_kernel, span_y=span_y, span_z=s...  15 us
    ppermute x6, starting transfers between devices, with_halo(): lax.ppermute(lax.slice_in_dim(block, 0, width, axis=dim), axis, backward)  14.5 us
    ppermute x6, waiting for transfers between devices, with_halo(): lax.ppermute(lax.slice_in_dim(block, 0, width, axis=dim), axis, backward)  12 us
    ppermute x6, waiting for transfers between devices, with_halo(): lax.ppermute(lax.slice_in_dim(block, block.shape[dim] - width, None, axis...  6.85 us
    ppermute x3, starting transfers between devices, fold_ghosts(): lax.ppermute(lax.slice_in_dim(block, 0, 1, axis=dim), axis, backward)  5.76 us
    unnamed x16, local copies, waits for them, and re-layouts  5.08 us
  transfers between devices with their start and end apart: 18, of which 8 were waited for; matrix products, arithmetic and copies ran while one was open for 5% of the time, Pallas kernels for 0%

profile of v15, /device:TPU:58, one launch (start us, length us, event | category | flops | bytes accessed | tf_op | source)
XLA Modules:
  0.0 118.1 jit_solution(12313412001968055991)
XLA Ops:
  1.4 7.8 %collective-permute-start.1 = (f32[5,1,16,128]{3,2,1,0:T(8,128)S(1)}, f32[5,1,16,128]{3,2,1,0:T(8,128)S(1)}, u32[]{:S(2)}, u32[]{:S(2)}) collective-permute-start(f32[5,1,16,128]{3,2,1,0:T(8,128)S(1)} %get-tuple-element.24), channel_id=1, source_target_pairs={{0,32},{32,64},{64,96},{96,128},{128,160},{160,192},{192,224},{1,3... | collective-permute-start | bytes 122888 | tf_op jit(solution)/shard_map/ppermute | solution.py:24
  9.3 1.9 %collective-permute-start = (f32[5,1,16,128]{3,2,1,0:T(8,128)S(1)}, f32[5,1,16,128]{3,2,1,0:T(8,128)S(1)}, u32[]{:S(2)}, u32[]{:S(2)}) collective-permute-start(f32[5,1,16,128]{3,2,1,0:T(8,128)S(1)} %get-tuple-element.23), channel_id=1, source_target_pairs={{32,0},{64,32},{96,64},{128,96},{160,128},{192,160},{224,192},{33,... | collective-permute-start | bytes 122888 | tf_op jit(solution)/shard_map/ppermute | solution.py:27
  12.2 9.0 %collective-permute-done = f32[5,1,16,128]{3,2,1,0:T(8,128)S(1)} collective-permute-done((f32[5,1,16,128]{3,2,1,0:T(8,128)S(1)}, f32[5,1,16,128]{3,2,1,0:T(8,128)S(1)}, u32[]{:S(2)}, u32[]{:S(2)}) %collective-permute-start) | collective-permute-done | bytes 40992 | tf_op jit(solution)/shard_map/ppermute | solution.py:27
  21.3 1.9 %collective-permute-start.2 = (f32[5,10,1,128]{3,2,1,0:T(1,128)S(1)}, f32[5,10,1,128]{3,2,1,0:T(1,128)S(1)}, u32[]{:S(2)}, u32[]{:S(2)}) collective-permute-start(f32[5,10,1,128]{3,2,1,0:T(1,128)S(1)} %get-tuple-element.22), channel_id=1, source_target_pairs={{4,0},{8,4},{12,8},{16,12},{20,16},{24,20},{28,24},{5,1},{9,5},{13... | collective-permute-start | bytes 76808 | tf_op jit(solution)/shard_map/ppermute | solution.py:27
  23.2 2.4 %collective-permute-start.3 = (f32[5,10,1,128]{3,2,1,0:T(1,128)S(1)}, f32[5,10,1,128]{3,2,1,0:T(1,128)S(1)}, u32[]{:S(2)}, u32[]{:S(2)}) collective-permute-start(f32[5,10,1,128]{3,2,1,0:T(1,128)S(1)} %get-tuple-element.21), channel_id=1, source_target_pairs={{0,4},{4,8},{8,12},{12,16},{16,20},{20,24},{24,28},{1,5},{5,9},{9,... | collective-permute-start | bytes 76808 | tf_op jit(solution)/shard_map/ppermute | solution.py:24
  26.4 1.9 %collective-permute-done.3 = f32[5,10,1,128]{3,2,1,0:T(1,128)S(1)} collective-permute-done((f32[5,10,1,128]{3,2,1,0:T(1,128)S(1)}, f32[5,10,1,128]{3,2,1,0:T(1,128)S(1)}, u32[]{:S(2)}, u32[]{:S(2)}) %collective-permute-start.3) | collective-permute-done | bytes 25632 | tf_op jit(solution)/shard_map/ppermute | solution.py:24
  29.1 2.9 %collective-permute-start.4 = (f32[5,10,18,1]{2,3,1,0:T(1,128)S(1)}, f32[5,10,18,1]{2,3,1,0:T(1,128)S(1)}, u32[]{:S(2)}, u32[]{:S(2)}) collective-permute-start(f32[5,10,18,1]{2,3,1,0:T(1,128)S(1)} %copy.14), channel_id=1, source_target_pairs={{1,0},{2,1},{3,2},{5,4},{6,5},{7,6},{9,8},{10,9},{11,10},{13,12},{... | collective-permute-start | bytes 10808 | tf_op jit(solution)/shard_map/ppermute | solution.py:27
  32.4 2.9 %collective-permute-start.5 = (f32[5,10,18,1]{2,3,1,0:T(1,128)S(1)}, f32[5,10,18,1]{2,3,1,0:T(1,128)S(1)}, u32[]{:S(2)}, u32[]{:S(2)}) collective-permute-start(f32[5,10,18,1]{2,3,1,0:T(1,128)S(1)} %copy.16), channel_id=1, source_target_pairs={{0,1},{1,2},{2,3},{4,5},{5,6},{6,7},{8,9},{9,10},{10,11},{12,13},{... | collective-permute-start | bytes 10808 | tf_op jit(solution)/shard_map/ppermute | solution.py:24
  37.0 1.1 collective-permute-done.5
  39.3 1.1 reshape.25
  40.4 1.6 %copy.23 = f32[5,130,180]{2,1,0:T(8,128)S(1)} copy(f32[5,130,180]{1,2,0:T(8,128)} %reshape.25) | data formatting | bytes 936000
  42.8 15.0 %shard_map.94 = (f32[5,32,128]{2,1,0:T(8,128)}, f32[5,108,128]{2,1,0:T(8,128)}, f32[680,256]{1,0:T(8,128)}) custom-call(s32[1]{0:T(128)S(6)} %copy.28.live_ref, s32[32]{0:T(128)} %dest_ref.1, f32[680,256]{1,0:T(8,128)} %bitcast.16, f32[5,32,128]{2,1,0:T(8,128)} %bitcast.20, s32[32,128]{1,0:T(8,128)} %cell_ref.1, f32[3,32,128]{2,1,0:T(8,128)} %bitcast.21, ...), custom_call_target="tpu_custom_call" | custom-call | tf_op jit(solution)/shard_map/pallas_call | solution.py:285
  57.8 2.4 %copy.22 = f32[5,130,180]{1,2,0:T(8,128)} copy(f32[5,130,180]{2,1,0:T(8,128)} %bitcast.17) | data formatting | bytes 936000
  60.2 1.3 %reshape.28 = f32[5,130,10,18]{1,3,2,0:T(8,128)S(1)} reshape(f32[5,130,180]{1,2,0:T(8,128)} %copy.22) | data formatting | bytes 936000 | tf_op jit(solution)/shard_map/reshape | solution.py:310
  62.3 1.9 %collective-permute-start.7 = (f32[5,1,18,130]{3,2,1,0:T(8,128)}, f32[5,1,18,130]{3,2,1,0:T(8,128)}, u32[]{:S(2)}, u32[]{:S(2)}) collective-permute-start(f32[5,1,18,130]{3,2,1,0:T(8,128)} %get-tuple-element.10), channel_id=1, source_target_pairs={{32,0},{64,32},{96,64},{128,96},{160,128},{192,160},{224,192},{33,... | collective-permute-start | bytes 140408 | tf_op jit(solution)/shard_map/ppermute | solution.py:39
  64.2 10.1 %collective-permute-start.6 = (f32[5,1,18,130]{3,2,1,0:T(8,128)}, f32[5,1,18,130]{3,2,1,0:T(8,128)}, u32[]{:S(2)}, u32[]{:S(2)}) collective-permute-start(f32[5,1,18,130]{3,2,1,0:T(8,128)} %get-tuple-element.9), channel_id=1, source_target_pairs={{0,32},{32,64},{64,96},{96,128},{128,160},{160,192},{192,224},{1,3... | collective-permute-start | bytes 140408 | tf_op jit(solution)/shard_map/ppermute | solution.py:38
  74.5 1.9 %collective-permute-start.12 = (f32[5,1,3,3,4,128]{5,4,3,2,1,0:T(4,128)S(1)}, f32[5,1,3,3,4,128]{5,4,3,2,1,0:T(4,128)S(1)}, u32[]{:S(2)}, u32[]{:S(2)}) collective-permute-start(f32[5,1,3,3,4,128]{5,4,3,2,1,0:T(4,128)S(1)} %get-tuple-element.26), channel_id=1, source_target_pairs={{0,32},{32,64},{64,96},{96,128},{128,160},{160,192},{192,224},{1,3... | collective-permute-start | bytes 276488 | tf_op jit(solution)/shard_map/ppermute | solution.py:24
  76.4 3.9 %collective-permute-start.13 = (f32[5,1,3,3,4,128]{5,4,3,2,1,0:T(4,128)S(1)}, f32[5,1,3,3,4,128]{5,4,3,2,1,0:T(4,128)S(1)}, u32[]{:S(2)}, u32[]{:S(2)}) collective-permute-start(f32[5,1,3,3,4,128]{5,4,3,2,1,0:T(4,128)S(1)} %get-tuple-element.25), channel_id=1, source_target_pairs={{32,0},{64,32},{96,64},{128,96},{160,128},{192,160},{224,192},{33,... | collective-permute-start | bytes 276488 | tf_op jit(solution)/shard_map/ppermute | solution.py:27
  80.4 1.0 fusion
  81.5 1.9 %collective-permute-start.9 = (f32[5,8,1,130]{3,2,1,0:T(1,128)S(1)}, f32[5,8,1,130]{3,2,1,0:T(1,128)S(1)}, u32[]{:S(2)}, u32[]{:S(2)}) collective-permute-start(f32[5,8,1,130]{3,2,1,0:T(1,128)S(1)} %get-tuple-element.12), channel_id=1, source_target_pairs={{4,0},{8,4},{12,8},{16,12},{20,16},{24,20},{28,24},{5,1},{9,5},{13... | collective-permute-start | bytes 62408 | tf_op jit(solution)/shard_map/ppermute | solution.py:39
  83.4 2.4 %collective-permute-start.8 = (f32[5,8,1,130]{3,2,1,0:T(1,128)S(1)}, f32[5,8,1,130]{3,2,1,0:T(1,128)S(1)}, u32[]{:S(2)}, u32[]{:S(2)}) collective-permute-start(f32[5,8,1,130]{3,2,1,0:T(1,128)S(1)} %get-tuple-element.11), channel_id=1, source_target_pairs={{0,4},{4,8},{8,12},{12,16},{16,20},{20,24},{24,28},{1,5},{5,9},{9,... | collective-permute-start | bytes 62408 | tf_op jit(solution)/shard_map/ppermute | solution.py:38
  85.9 2.9 %collective-permute-done.13 = f32[5,1,3,3,4,128]{5,4,3,2,1,0:T(4,128)S(1)} collective-permute-done((f32[5,1,3,3,4,128]{5,4,3,2,1,0:T(4,128)S(1)}, f32[5,1,3,3,4,128]{5,4,3,2,1,0:T(4,128)S(1)}, u32[]{:S(2)}, u32[]{:S(2)}) %collective-permute-start.13) | collective-permute-done | bytes 92192 | tf_op jit(solution)/shard_map/ppermute | solution.py:27
  88.9 1.9 %collective-permute-start.15 = (f32[5,5,1,3,4,128]{5,4,3,2,1,0:T(4,128)S(1)}, f32[5,5,1,3,4,128]{5,4,3,2,1,0:T(4,128)S(1)}, u32[]{:S(2)}, u32[]{:S(2)}) collective-permute-start(f32[5,5,1,3,4,128]{5,4,3,2,1,0:T(4,128)S(1)} %get-tuple-element.20), channel_id=1, source_target_pairs={{4,0},{8,4},{12,8},{16,12},{20,16},{24,20},{28,24},{5,1},{9,5},{13... | collective-permute-start | bytes 460808 | tf_op jit(solution)/shard_map/ppermute | solution.py:27
  90.9 2.4 %collective-permute-start.14 = (f32[5,5,1,3,4,128]{5,4,3,2,1,0:T(4,128)S(1)}, f32[5,5,1,3,4,128]{5,4,3,2,1,0:T(4,128)S(1)}, u32[]{:S(2)}, u32[]{:S(2)}) collective-permute-start(f32[5,5,1,3,4,128]{5,4,3,2,1,0:T(4,128)S(1)} %get-tuple-element.19), channel_id=1, source_target_pairs={{0,4},{4,8},{8,12},{12,16},{16,20},{20,24},{24,28},{1,5},{5,9},{9,... | collective-permute-start | bytes 460808 | tf_op jit(solution)/shard_map/ppermute | solution.py:24
  93.6 3.8 %collective-permute-done.14 = f32[5,5,1,3,4,128]{5,4,3,2,1,0:T(4,128)S(1)} collective-permute-done((f32[5,5,1,3,4,128]{5,4,3,2,1,0:T(4,128)S(1)}, f32[5,5,1,3,4,128]{5,4,3,2,1,0:T(4,128)S(1)}, u32[]{:S(2)}, u32[]{:S(2)}) %collective-permute-start.14) | collective-permute-done | bytes 153632 | tf_op jit(solution)/shard_map/ppermute | solution.py:24
  97.5 1.9 %collective-permute-start.17 = (f32[5,5,5,1,4,128]{5,4,3,2,1,0:T(4,128)S(1)}, f32[5,5,5,1,4,128]{5,4,3,2,1,0:T(4,128)S(1)}, u32[]{:S(2)}, u32[]{:S(2)}) collective-permute-start(f32[5,5,5,1,4,128]{5,4,3,2,1,0:T(4,128)S(1)} %get-tuple-element.14), channel_id=1, source_target_pairs={{1,0},{2,1},{3,2},{5,4},{6,5},{7,6},{9,8},{10,9},{11,10},{13,12},{... | collective-permute-start | bytes 768008 | tf_op jit(solution)/shard_map/ppermute | solution.py:27
  99.5 3.9 %collective-permute-start.16 = (f32[5,5,5,1,4,128]{5,4,3,2,1,0:T(4,128)S(1)}, f32[5,5,5,1,4,128]{5,4,3,2,1,0:T(4,128)S(1)}, u32[]{:S(2)}, u32[]{:S(2)}) collective-permute-start(f32[5,5,5,1,4,128]{5,4,3,2,1,0:T(4,128)S(1)} %get-tuple-element.13), channel_id=1, source_target_pairs={{0,1},{1,2},{2,3},{4,5},{5,6},{6,7},{8,9},{9,10},{10,11},{12,13},{... | collective-permute-start | bytes 768008 | tf_op jit(solution)/shard_map/ppermute | solution.py:24
  103.5 1.9 %collective-permute-start.11 = (f32[5,8,16,1]{3,2,1,0:T(8,128)S(1)}, f32[5,8,16,1]{3,2,1,0:T(8,128)S(1)}, u32[]{:S(2)}, u32[]{:S(2)}) collective-permute-start(f32[5,8,16,1]{3,2,1,0:T(8,128)S(1)} %get-tuple-element.16), channel_id=1, source_target_pairs={{1,0},{2,1},{3,2},{5,4},{6,5},{7,6},{9,8},{10,9},{11,10},{13,12},{... | collective-permute-start | bytes 7688 | tf_op jit(solution)/shard_map/ppermute | solution.py:39
  105.5 3.9 %collective-permute-start.10 = (f32[5,8,16,1]{3,2,1,0:T(8,128)S(1)}, f32[5,8,16,1]{3,2,1,0:T(8,128)S(1)}, u32[]{:S(2)}, u32[]{:S(2)}) collective-permute-start(f32[5,8,16,1]{3,2,1,0:T(8,128)S(1)} %get-tuple-element.15), channel_id=1, source_target_pairs={{0,1},{1,2},{2,3},{4,5},{5,6},{6,7},{8,9},{9,10},{10,11},{12,13},{... | collective-permute-start | bytes 7688 | tf_op jit(solution)/shard_map/ppermute | solution.py:38
  109.4 4.3 %collective-permute-done.11 = f32[5,8,16,1]{3,2,1,0:T(8,128)S(1)} collective-permute-done((f32[5,8,16,1]{3,2,1,0:T(8,128)S(1)}, f32[5,8,16,1]{3,2,1,0:T(8,128)S(1)}, u32[]{:S(2)}, u32[]{:S(2)}) %collective-permute-start.11) | collective-permute-done | bytes 2592 | tf_op jit(solution)/shard_map/ppermute | solution.py:39
  113.7 1.9 %collective-permute-done.10 = f32[5,8,16,1]{3,2,1,0:T(8,128)S(1)} collective-permute-done((f32[5,8,16,1]{3,2,1,0:T(8,128)S(1)}, f32[5,8,16,1]{3,2,1,0:T(8,128)S(1)}, u32[]{:S(2)}, u32[]{:S(2)}) %collective-permute-start.10) | collective-permute-done | bytes 2592 | tf_op jit(solution)/shard_map/ppermute | solution.py:38
  115.6 1.3 %fusion.4 = f32[5,8,16,128]{3,2,1,0:T(8,128)} fusion(f32[5,8,16,130]{3,2,1,0:T(8,128)S(1)} %fusion.1, f32[5,8,16,128]{3,2,1,0:T(8,128)S(1)} %copy-done, f32[5,10,18,1]{3,2,1,0:T(8,128)S(1)} %copy.17, f32[5,10,1,128]{3,2,1,0:T(1,128)S(1)} %collective-permute-done.2, f32[5,10,16,128]{3,2,1,0:T(8,128)S(1)} %constant_dynamic-update-slice_fusion, ...), kind=kLoop, calls=%fused_computation.10 | loop fusion | flops 1884160 | bytes 1538100 | tf_op jit(solution)/shard_map/add | solution.py:313
  (50 shorter events, 9.6 us)
Async XLA Ops:
  1.4 9.8 %collective-permute-start.1 = (f32[5,1,16,128]{3,2,1,0:T(8,128)S(1)}, f32[5,1,16,128]{3,2,1,0:T(8,128)S(1)}, u32[]{:S(2)}, u32[]{:S(2)}) collective-permute-start(f32[5,1,16,128]{3,2,1,0:T(8,128)S(1)} %get-tuple-element.24), channel_id=1, source_target_pairs={{0,32},{32,64},{64,96},{96,128},{128,160},{160,192},{192,224},{1,3... | collective-permute-start | bytes 122888 | tf_op jit(solution)/shard_map/ppermute | solution.py:24
  9.3 11.9 %collective-permute-start = (f32[5,1,16,128]{3,2,1,0:T(8,128)S(1)}, f32[5,1,16,128]{3,2,1,0:T(8,128)S(1)}, u32[]{:S(2)}, u32[]{:S(2)}) collective-permute-start(f32[5,1,16,128]{3,2,1,0:T(8,128)S(1)} %get-tuple-element.23), channel_id=1, source_target_pairs={{32,0},{64,32},{96,64},{128,96},{160,128},{192,160},{224,192},{33,... | collective-permute-start | bytes 122888 | tf_op jit(solution)/shard_map/ppermute | solution.py:27
  21.2 5.2 %copy-start.2 = (f32[5,1,16,128]{3,2,1,0:T(8,128)}, f32[5,1,16,128]{3,2,1,0:T(8,128)S(1)}, u32[]{:S(2)}) copy-start(f32[5,1,16,128]{3,2,1,0:T(8,128)S(1)} %collective-permute-done) | copy-start | bytes 122884
  21.3 5.1 %collective-permute-start.2 = (f32[5,10,1,128]{3,2,1,0:T(1,128)S(1)}, f32[5,10,1,128]{3,2,1,0:T(1,128)S(1)}, u32[]{:S(2)}, u32[]{:S(2)}) collective-permute-start(f32[5,10,1,128]{3,2,1,0:T(1,128)S(1)} %get-tuple-element.22), channel_id=1, source_target_pairs={{4,0},{8,4},{12,8},{16,12},{20,16},{24,20},{28,24},{5,1},{9,5},{13... | collective-permute-start | bytes 76808 | tf_op jit(solution)/shard_map/ppermute | solution.py:27
  23.2 5.2 %collective-permute-start.3 = (f32[5,10,1,128]{3,2,1,0:T(1,128)S(1)}, f32[5,10,1,128]{3,2,1,0:T(1,128)S(1)}, u32[]{:S(2)}, u32[]{:S(2)}) collective-permute-start(f32[5,10,1,128]{3,2,1,0:T(1,128)S(1)} %get-tuple-element.21), channel_id=1, source_target_pairs={{0,4},{4,8},{8,12},{12,16},{16,20},{20,24},{24,28},{1,5},{5,9},{9,... | collective-permute-start | bytes 76808 | tf_op jit(solution)/shard_map/ppermute | solution.py:24
  29.1 7.5 %collective-permute-start.4 = (f32[5,10,18,1]{2,3,1,0:T(1,128)S(1)}, f32[5,10,18,1]{2,3,1,0:T(1,128)S(1)}, u32[]{:S(2)}, u32[]{:S(2)}) collective-permute-start(f32[5,10,18,1]{2,3,1,0:T(1,128)S(1)} %copy.14), channel_id=1, source_target_pairs={{1,0},{2,1},{3,2},{5,4},{6,5},{7,6},{9,8},{10,9},{11,10},{13,12},{... | collective-permute-start | bytes 10808 | tf_op jit(solution)/shard_map/ppermute | solution.py:27
  32.4 5.7 %collective-permute-start.5 = (f32[5,10,18,1]{2,3,1,0:T(1,128)S(1)}, f32[5,10,18,1]{2,3,1,0:T(1,128)S(1)}, u32[]{:S(2)}, u32[]{:S(2)}) collective-permute-start(f32[5,10,18,1]{2,3,1,0:T(1,128)S(1)} %copy.16), channel_id=1, source_target_pairs={{0,1},{1,2},{2,3},{4,5},{5,6},{6,7},{8,9},{9,10},{10,11},{12,13},{... | collective-permute-start | bytes 10808 | tf_op jit(solution)/shard_map/ppermute | solution.py:24
  60.2 14.1 %copy-start.1 = (f32[5,108,128]{2,1,0:T(8,128)S(1)}, f32[5,108,128]{2,1,0:T(8,128)}, u32[]{:S(2)}) copy-start(f32[5,108,128]{2,1,0:T(8,128)} %get-tuple-element.8) | copy-start | bytes 829444
  62.3 18.0 %collective-permute-start.7 = (f32[5,1,18,130]{3,2,1,0:T(8,128)}, f32[5,1,18,130]{3,2,1,0:T(8,128)}, u32[]{:S(2)}, u32[]{:S(2)}) collective-permute-start(f32[5,1,18,130]{3,2,1,0:T(8,128)} %get-tuple-element.10), channel_id=1, source_target_pairs={{32,0},{64,32},{96,64},{128,96},{160,128},{192,160},{224,192},{33,... | collective-permute-start | bytes 140408 | tf_op jit(solution)/shard_map/ppermute | solution.py:39
  64.2 16.2 %collective-permute-start.6 = (f32[5,1,18,130]{3,2,1,0:T(8,128)}, f32[5,1,18,130]{3,2,1,0:T(8,128)}, u32[]{:S(2)}, u32[]{:S(2)}) collective-permute-start(f32[5,1,18,130]{3,2,1,0:T(8,128)} %get-tuple-element.9), channel_id=1, source_target_pairs={{0,32},{32,64},{64,96},{96,128},{128,160},{160,192},{192,224},{1,3... | collective-permute-start | bytes 140408 | tf_op jit(solution)/shard_map/ppermute | solution.py:38
  74.5 11.4 %collective-permute-start.12 = (f32[5,1,3,3,4,128]{5,4,3,2,1,0:T(4,128)S(1)}, f32[5,1,3,3,4,128]{5,4,3,2,1,0:T(4,128)S(1)}, u32[]{:S(2)}, u32[]{:S(2)}) collective-permute-start(f32[5,1,3,3,4,128]{5,4,3,2,1,0:T(4,128)S(1)} %get-tuple-element.26), channel_id=1, source_target_pairs={{0,32},{32,64},{64,96},{96,128},{128,160},{160,192},{192,224},{1,3... | collective-permute-start | bytes 276488 | tf_op jit(solution)/shard_map/ppermute | solution.py:24
  76.4 12.5 %collective-permute-start.13 = (f32[5,1,3,3,4,128]{5,4,3,2,1,0:T(4,128)S(1)}, f32[5,1,3,3,4,128]{5,4,3,2,1,0:T(4,128)S(1)}, u32[]{:S(2)}, u32[]{:S(2)}) collective-permute-start(f32[5,1,3,3,4,128]{5,4,3,2,1,0:T(4,128)S(1)} %get-tuple-element.25), channel_id=1, source_target_pairs={{32,0},{64,32},{96,64},{128,96},{160,128},{192,160},{224,192},{33,... | collective-permute-start | bytes 276488 | tf_op jit(solution)/shard_map/ppermute | solution.py:27
  81.5 11.8 %collective-permute-start.9 = (f32[5,8,1,130]{3,2,1,0:T(1,128)S(1)}, f32[5,8,1,130]{3,2,1,0:T(1,128)S(1)}, u32[]{:S(2)}, u32[]{:S(2)}) collective-permute-start(f32[5,8,1,130]{3,2,1,0:T(1,128)S(1)} %get-tuple-element.12), channel_id=1, source_target_pairs={{4,0},{8,4},{12,8},{16,12},{20,16},{24,20},{28,24},{5,1},{9,5},{13... | collective-permute-start | bytes 62408 | tf_op jit(solution)/shard_map/ppermute | solution.py:39
  83.4 9.9 %collective-permute-start.8 = (f32[5,8,1,130]{3,2,1,0:T(1,128)S(1)}, f32[5,8,1,130]{3,2,1,0:T(1,128)S(1)}, u32[]{:S(2)}, u32[]{:S(2)}) collective-permute-start(f32[5,8,1,130]{3,2,1,0:T(1,128)S(1)} %get-tuple-element.11), channel_id=1, source_target_pairs={{0,4},{4,8},{8,12},{12,16},{16,20},{20,24},{24,28},{1,5},{5,9},{9,... | collective-permute-start | bytes 62408 | tf_op jit(solution)/shard_map/ppermute | solution.py:38
  88.9 4.6 %collective-permute-start.15 = (f32[5,5,1,3,4,128]{5,4,3,2,1,0:T(4,128)S(1)}, f32[5,5,1,3,4,128]{5,4,3,2,1,0:T(4,128)S(1)}, u32[]{:S(2)}, u32[]{:S(2)}) collective-permute-start(f32[5,5,1,3,4,128]{5,4,3,2,1,0:T(4,128)S(1)} %get-tuple-element.20), channel_id=1, source_target_pairs={{4,0},{8,4},{12,8},{16,12},{20,16},{24,20},{28,24},{5,1},{9,5},{13... | collective-permute-start | bytes 460808 | tf_op jit(solution)/shard_map/ppermute | solution.py:27
  90.9 6.5 %collective-permute-start.14 = (f32[5,5,1,3,4,128]{5,4,3,2,1,0:T(4,128)S(1)}, f32[5,5,1,3,4,128]{5,4,3,2,1,0:T(4,128)S(1)}, u32[]{:S(2)}, u32[]{:S(2)}) collective-permute-start(f32[5,5,1,3,4,128]{5,4,3,2,1,0:T(4,128)S(1)} %get-tuple-element.19), channel_id=1, source_target_pairs={{0,4},{4,8},{8,12},{12,16},{16,20},{20,24},{24,28},{1,5},{5,9},{9,... | collective-permute-start | bytes 460808 | tf_op jit(solution)/shard_map/ppermute | solution.py:24
  93.4 22.2 %copy-start = (f32[5,8,16,128]{3,2,1,0:T(8,128)S(1)}, f32[5,8,16,128]{3,2,1,0:T(8,128)}, u32[]{:S(2)}) copy-start(f32[5,8,16,128]{3,2,1,0:T(8,128)} %param.7) | copy-start | bytes 983044
  93.5 22.1 %copy-start.3 = (f32[5,1,16,128]{3,2,1,0:T(8,128)S(1)}, f32[5,1,16,128]{3,2,1,0:T(8,128)}, u32[]{:S(2)}) copy-start(f32[5,1,16,128]{3,2,1,0:T(8,128)} %copy-done.2) | copy-start | bytes 122884
  93.5 22.1 %copy-start.4 = (f32[5]{0:T(128)S(1)}, f32[5]{0:T(128)}, u32[]{:S(2)}) copy-start(f32[5]{0:T(128)} %constant.23.clone) | copy-start | bytes 64
  97.5 19.4 %collective-permute-start.17 = (f32[5,5,5,1,4,128]{5,4,3,2,1,0:T(4,128)S(1)}, f32[5,5,5,1,4,128]{5,4,3,2,1,0:T(4,128)S(1)}, u32[]{:S(2)}, u32[]{:S(2)}) collective-permute-start(f32[5,5,5,1,4,128]{5,4,3,2,1,0:T(4,128)S(1)} %get-tuple-element.14), channel_id=1, source_target_pairs={{1,0},{2,1},{3,2},{5,4},{6,5},{7,6},{9,8},{10,9},{11,10},{13,12},{... | collective-permute-start | bytes 768008 | tf_op jit(solution)/shard_map/ppermute | solution.py:27
  99.5 17.5 %collective-permute-start.16 = (f32[5,5,5,1,4,128]{5,4,3,2,1,0:T(4,128)S(1)}, f32[5,5,5,1,4,128]{5,4,3,2,1,0:T(4,128)S(1)}, u32[]{:S(2)}, u32[]{:S(2)}) collective-permute-start(f32[5,5,5,1,4,128]{5,4,3,2,1,0:T(4,128)S(1)} %get-tuple-element.13), channel_id=1, source_target_pairs={{0,1},{1,2},{2,3},{4,5},{5,6},{6,7},{8,9},{9,10},{10,11},{12,13},{... | collective-permute-start | bytes 768008 | tf_op jit(solution)/shard_map/ppermute | solution.py:24
  103.5 10.2 %collective-permute-start.11 = (f32[5,8,16,1]{3,2,1,0:T(8,128)S(1)}, f32[5,8,16,1]{3,2,1,0:T(8,128)S(1)}, u32[]{:S(2)}, u32[]{:S(2)}) collective-permute-start(f32[5,8,16,1]{3,2,1,0:T(8,128)S(1)} %get-tuple-element.16), channel_id=1, source_target_pairs={{1,0},{2,1},{3,2},{5,4},{6,5},{7,6},{9,8},{10,9},{11,10},{13,12},{... | collective-permute-start | bytes 7688 | tf_op jit(solution)/shard_map/ppermute | solution.py:39
  105.5 10.1 %collective-permute-start.10 = (f32[5,8,16,1]{3,2,1,0:T(8,128)S(1)}, f32[5,8,16,1]{3,2,1,0:T(8,128)S(1)}, u32[]{:S(2)}, u32[]{:S(2)}) collective-permute-start(f32[5,8,16,1]{3,2,1,0:T(8,128)S(1)} %get-tuple-element.15), channel_id=1, source_target_pairs={{0,1},{1,2},{2,3},{4,5},{5,6},{6,7},{8,9},{9,10},{10,11},{12,13},{... | collective-permute-start | bytes 7688 | tf_op jit(solution)/shard_map/ppermute | solution.py:38
